TPU v7x, 512 devices: a whole 4x4x16 slice. The times are simulated.
512 devices in a mesh: ctx: 64 (over z, y_lo, core), head: 8 (over y_hi, x).
Axes of the slice: x: 4, y: 4 (y_hi: 2, y_lo: 2; y = y_hi * 2 + y_lo), z: 16, core: 2. Of those that a mesh axis runs over, the one named last changes fastest.
Arguments:
- events: bfloat16 [16384, 1024], P('ctx'), may hold values from -16 to 16
- ssm_input: bfloat16 [16384, 2048], P('ctx', 'head'), may hold values from -1.5 to 1.5
- gate_input: bfloat16 [16384, 2048], P('ctx', 'head'), may hold values from -6 to 6
- grad_out: bfloat16 [16384, 2048], P('ctx', 'head'), may hold values from -0.015625 to 0.015625
- shared_b: bfloat16 [16384, 128], P('ctx'), may hold values from -6 to 6
- shared_c: bfloat16 [16384, 128], P('ctx'), may hold values from -6 to 6
- log_decay: float32 [32, 16384], P('head', 'ctx'), may hold values from -1 to 0, as said below
- entry_state: float32 [64, 32, 128, 64], P('ctx', 'head'), may hold values from -48 to 48
- w_gate: bfloat16 [1024, 2048], P(None, 'head'), may hold values from -0.1875 to 0.1875
- w_value: bfloat16 [1024, 2048], P(None, 'head'), may hold values from -0.1875 to 0.1875
- w_shared: bfloat16 [1024, 256], P(None, 'head'), may hold values from -0.1875 to 0.1875
Outputs:
- grad_input: bfloat16 [16384, 1024], P('ctx', 'head')
- grad_w_gate: float32 [1024, 2048], P('ctx', 'head')
- grad_w_value: float32 [1024, 2048], P('ctx', 'head')
- grad_w_shared: float32 [1024, 256], P('ctx', 'head')
Inputs may be any that keep to these rules, and one draw needn't show every extreme that they name: `log_decay`: every entry is negative.
All inputs are finite; a program needn't handle non-finite values.
Results may differ from a plain program's by a relative error of at most 0.015.
Values may be sent and summed in bfloat16 or wider, within the bound.
No kernel may reach another device: no remote copies, remote signals or barrier semaphores. Data moves between devices by JAX's collectives and lax.ppermute only.
A program may use at most 64 MiB of HBM per device.

v0:
```python
import math

import jax
import jax.numpy as jnp
from jax import lax
from jax.sharding import PartitionSpec as P

SPAN = 256


highest = lax.Precision.HIGHEST


def entering(part, axis, combine, identity):
    count = lax.axis_size(axis)
    place = lax.axis_index(axis)
    ahead = count - 1 - place
    gathered = jax.tree.map(lambda a: lax.all_gather(a, axis), part)
    state = jax.tree.map(lambda a, e: jnp.zeros_like(a) + jnp.asarray(e, a.dtype), part, identity)

    def one(lap, state):
        source = count - 1 - lap
        return combine(
            state, jax.tree.map(lambda a: lax.dynamic_index_in_dim(a, source, 0, False), gathered)
        )

    return lax.fori_loop(0, ahead, one, state)


def ssd_partials(ssm_input, gate_input, grad_out, shared_b, shared_c, log_decay, entry, block_len):
    head_count, length = log_decay.shape
    head_width = ssm_input.shape[1] // head_count
    span_count = length // block_len
    values_f = ssm_input.astype(jnp.float32).reshape(span_count, block_len, head_count, head_width)
    gates_f = gate_input.astype(jnp.float32).reshape(span_count, block_len, head_count, head_width)
    grad_f = grad_out.astype(jnp.float32).reshape(span_count, block_len, head_count, head_width)
    shared_bf = shared_b.astype(jnp.float32).reshape(span_count, block_len, shared_b.shape[1])
    shared_cf = shared_c.astype(jnp.float32).reshape(span_count, block_len, shared_c.shape[1])
    cumlog = jnp.cumsum(log_decay.reshape(head_count, span_count, block_len), axis=2)
    totals = cumlog[:, :, -1]
    causal = jnp.arange(block_len)[:, None] >= jnp.arange(block_len)[None, :]
    spread = cumlog[:, :, :, None] - cumlog[:, :, None, :]
    decay_mat = jnp.where(causal, jnp.exp(jnp.minimum(spread, 0.0)), 0.0)
    shared_c_blocks = shared_c.reshape(span_count, block_len, shared_c.shape[1])
    shared_b_blocks = shared_b.reshape(span_count, block_len, shared_b.shape[1])
    scores = jnp.einsum(
        "ktn,ksn->kts", shared_c_blocks, shared_b_blocks, preferred_element_type=jnp.float32
    )
    weighted = decay_mat * scores[None]
    to_end = jnp.exp(totals[:, :, None] - cumlog).transpose(1, 2, 0)
    from_start = jnp.exp(cumlog).transpose(1, 2, 0)
    scaled_x = values_f * to_end[..., None]
    local_states = jnp.einsum("ksn,kshp->khnp", shared_bf, scaled_x, precision=highest)
    span_decay = jnp.exp(totals).T

    def forward_step(running, inputs):
        decay_k, local_k = inputs
        return (decay_k[:, None, None] * running + local_k, running)

    _, entries = lax.scan(forward_step, entry, (span_decay, local_states))
    ssm_out = jnp.einsum("hkts,kshp->kthp", weighted, values_f, precision=highest)
    ssm_out = ssm_out + from_start[..., None] * jnp.einsum(
        "ktn,khnp->kthp", shared_cf, entries, precision=highest
    )
    gate_sig = jax.nn.sigmoid(gates_f)
    grad_y = grad_f * gates_f * gate_sig
    grad_z = grad_f * ssm_out * gate_sig * (1.0 + gates_f * (1.0 - gate_sig))
    products = decay_mat * jnp.einsum("kthp,kshp->hkts", grad_y, values_f, precision=highest)
    scaled_dy = grad_y * from_start[..., None]
    grad_c = jnp.einsum("hkts,ksn->ktn", products, shared_bf, precision=highest)
    grad_c = grad_c + jnp.einsum("kthp,khnp->ktn", scaled_dy, entries, precision=highest)
    grad_b = jnp.einsum("hkst,ksn->ktn", products, shared_cf, precision=highest)
    grad_x = jnp.einsum("hkst,kshp->kthp", weighted, grad_y, precision=highest)
    block_terms = jnp.einsum("ksn,kshp->khnp", shared_cf, scaled_dy, precision=highest)

    def backward_step(running, inputs):
        decay_k, term_k = inputs
        return (term_k + decay_k[:, None, None] * running, running)

    block_sum, later_sums = lax.scan(
        backward_step, jnp.zeros_like(entry), (span_decay, block_terms), reverse=True
    )
    block_log = jnp.sum(totals, axis=1)
    suffix = block_log[None, :] - jnp.cumsum(totals, axis=1).T
    grad_z_out = grad_z.reshape(length, head_count * head_width).astype(jnp.bfloat16)
    return (
        grad_z_out,
        grad_x,
        grad_b,
        grad_c,
        later_sums,
        suffix,
        to_end,
        scaled_x,
        shared_bf,
        block_sum,
        block_log,
    )


def finish_block(partials, incoming):
    (
        grad_z_out,
        grad_x,
        grad_b,
        grad_c,
        later_sums,
        suffix,
        to_end,
        scaled_x,
        shared_bf,
        block_sum,
        block_log,
    ) = partials
    carried = later_sums + jnp.exp(suffix)[:, :, None, None] * incoming[None]
    grad_x = grad_x + to_end[..., None] * jnp.einsum(
        "ktn,khnp->kthp", shared_bf, carried, precision=highest
    )
    grad_b = grad_b + jnp.einsum("kthp,khnp->ktn", scaled_x, carried, precision=highest)
    length = grad_z_out.shape[0]
    grad_x_out = grad_x.reshape(length, grad_z_out.shape[1]).astype(jnp.bfloat16)
    grad_bc = jnp.concatenate([grad_b.reshape(length, -1), grad_c.reshape(length, -1)], axis=1)
    return (grad_z_out, grad_x_out, grad_bc)


def times_rows(left, weights):
    return lax.dot_general(
        left, weights, (((1,), (1,)), ((), ())), preferred_element_type=jnp.float32
    )


def row_term(events, projected, norm_scale):
    return (
        lax.dot_general(
            events, projected, (((0,), (0,)), ((), ())), preferred_element_type=jnp.float32
        )
        * norm_scale
    )


def per_device(
    events,
    ssm_input,
    gate_input,
    grad_out,
    shared_b,
    shared_c,
    log_decay,
    entry_state,
    w_gate,
    w_value,
    w_shared,
):
    partials = ssd_partials(
        ssm_input, gate_input, grad_out, shared_b, shared_c, log_decay, entry_state[0], SPAN
    )
    grad_z = partials[0]
    block_sum = partials[9]
    block_log = partials[10]

    def combine(earlier_part, later_part):
        return (
            earlier_part[0] * later_part[0],
            later_part[1] + later_part[0][:, None, None] * earlier_part[1],
        )

    identity = (jnp.ones_like(block_log), jnp.zeros_like(block_sum))
    _, incoming = entering((jnp.exp(block_log), block_sum), "ctx", combine, identity)
    grad_z, grad_x, grad_bc_part = finish_block(partials, incoming)
    grad_bc = lax.psum_scatter(grad_bc_part, "head", scatter_dimension=1, tiled=True).astype(
        jnp.bfloat16
    )
    input_part = (
        times_rows(grad_z, w_gate) + times_rows(grad_x, w_value) + times_rows(grad_bc, w_shared)
    )
    grad_input = lax.psum_scatter(
        input_part.astype(jnp.bfloat16), "head", scatter_dimension=1, tiled=True
    )
    norm_scale = 1.0 / math.sqrt(events.shape[0] * lax.axis_size("ctx"))
    head_cols = grad_z.shape[1]
    projected = jnp.concatenate([grad_z, grad_x, grad_bc], axis=1)
    reduced = lax.psum_scatter(
        row_term(events, projected, norm_scale), "ctx", scatter_dimension=0, tiled=True
    )
    grad_w_gate = reduced[:, :head_cols]
    grad_w_value = reduced[:, head_cols : 2 * head_cols]
    grad_w_shared = reduced[:, 2 * head_cols :]
    return (grad_input, grad_w_gate, grad_w_value, grad_w_shared)


def solution(mesh):
    placed = (
        P("ctx", None),
        P("ctx", "head"),
        P("ctx", "head"),
        P("ctx", "head"),
        P("ctx", None),
        P("ctx", None),
        P("head", "ctx"),
        P("ctx", "head", None, None),
        P(None, "head"),
        P(None, "head"),
        P(None, "head"),
    )
    return jax.shard_map(
        per_device,
        mesh=mesh,
        in_specs=placed,
        out_specs=(P("ctx", "head"), P("ctx", "head"), P("ctx", "head"), P("ctx", "head")),
        check_vma=False,
    )
```

profile of v0, /device:TPU:4, one launch (start us, length us, event | category | flops | bytes accessed | tf_op | source)
XLA Modules:
  0.0 637.8 jit_solution(115971449128456271)
XLA Ops:
  8.0 1.2 reduce-window.6
  9.8 1.0 copy.54
  10.8 1.0 copy.61
  12.0 0.9 fusion.12
  13.0 1.3 dynamic-slice.2
  15.0 115.5 %all-reduce = f32[256]{0:T(256)S(1)} all-reduce(f32[256]{0:T(256)S(1)} %get-tuple-element.163), channel_id=2, replica_groups=mesh['ctx'=64,'head'=8] {'ctx'}, use_global_device_ids=true, to_apply=%add | all-reduce | flops 256 | bytes 2048
  132.8 0.9 convolution_add_fusion.2
  133.7 1.0 fusion.9
  135.1 10.8 %all-gather.3.cloned.1.call-done = f32[64,4,128,64]{2,3,1,0:T(8,128)} async-done(((f32[1,4,128,64]{2,3,1,0:T(8,128)}), f32[64,4,128,64]{2,3,1,0:T(8,128)}) %all-gather.3.cloned.1.call-update) | async-done | bytes 8388624 | tf_op jit(solution)/shard_map/all_gather | solution.py:18
  145.9 76.3 %while.9 = (s32[]{:T(128)}, f32[4,128,64]{2,1,0:T(8,128)S(1)}, s32[]{:T(128)}, f32[64,4,128,64]{2,3,1,0:T(8,128)}, f32[64,4]{1,0:T(8,128)S(1)}, /*index=5*/s32[]{:T(128)}, s32[]{:T(128)}, s32[]{:T(128)}, s32[]{:T(128)}) while((s32[]{:T(128)}, f32[4,128,64]{2,1,0:T(8,128)S(1)}, s32[]{:T(128)}, f32[64,4,128,64]{2,3,1,0:T(8,128)}, ...), condition=%wide.region_3.4_spmd, body=%wide.region_2.3_spmd.sunk | while | flops 65542 | bytes 917699 | solution.py:27
  145.9 0.9 constant_dynamic-slice_fusion.2
  147.1 0.9 constant_dynamic-slice_fusion.2
  148.3 0.9 constant_dynamic-slice_fusion.2
  149.5 0.9 constant_dynamic-slice_fusion.2
  150.7 0.9 constant_dynamic-slice_fusion.2
  152.0 0.9 constant_dynamic-slice_fusion.2
  153.2 0.9 constant_dynamic-slice_fusion.2
  154.4 0.9 constant_dynamic-slice_fusion.2
  155.6 0.9 constant_dynamic-slice_fusion.2
  156.8 0.9 constant_dynamic-slice_fusion.2
  158.0 0.9 constant_dynamic-slice_fusion.2
  159.2 0.9 constant_dynamic-slice_fusion.2
  160.4 0.9 constant_dynamic-slice_fusion.2
  161.6 0.9 constant_dynamic-slice_fusion.2
  162.9 0.9 constant_dynamic-slice_fusion.2
  164.1 0.9 constant_dynamic-slice_fusion.2
  165.3 0.9 constant_dynamic-slice_fusion.2
  166.5 0.9 constant_dynamic-slice_fusion.2
  167.7 0.9 constant_dynamic-slice_fusion.2
  168.9 0.9 constant_dynamic-slice_fusion.2
  170.1 0.9 constant_dynamic-slice_fusion.2
  171.3 0.9 constant_dynamic-slice_fusion.2
  172.6 0.9 constant_dynamic-slice_fusion.2
  173.8 0.9 constant_dynamic-slice_fusion.2
  175.0 0.9 constant_dynamic-slice_fusion.2
  176.2 0.9 constant_dynamic-slice_fusion.2
  177.4 0.9 constant_dynamic-slice_fusion.2
  178.6 0.9 constant_dynamic-slice_fusion.2
  179.8 0.9 constant_dynamic-slice_fusion.2
  181.0 0.9 constant_dynamic-slice_fusion.2
  182.2 0.9 constant_dynamic-slice_fusion.2
  183.5 0.9 constant_dynamic-slice_fusion.2
  184.7 0.9 constant_dynamic-slice_fusion.2
  185.9 0.9 constant_dynamic-slice_fusion.2
  187.1 0.9 constant_dynamic-slice_fusion.2
  188.3 0.9 constant_dynamic-slice_fusion.2
  189.5 0.9 constant_dynamic-slice_fusion.2
  190.7 0.9 constant_dynamic-slice_fusion.2
  191.9 0.9 constant_dynamic-slice_fusion.2
  193.1 0.9 constant_dynamic-slice_fusion.2
  194.4 0.9 constant_dynamic-slice_fusion.2
  198.0 0.9 constant_dynamic-slice_fusion.2
  221.0 0.9 constant_dynamic-slice_fusion.2
  222.2 1.2 fusion.3
  224.2 1.6 pad_maximum_fusion
  225.9 2.1 fusion.10
  228.4 73.1 %reduce-scatter.8.cloned.1.call-done = f32[256,32]{0,1:T(8,128)} async-done(((f32[256,256]{0,1:T(8,128)}), f32[256,32]{0,1:T(8,128)}) %reduce-scatter.8.cloned.1.call-update) | async-done | bytes 32784 | tf_op jit(solution)/shard_map/reduce_scatter | solution.py:170
  302.5 1.0 copy.74
  304.1 2.1 copy.76
  306.2 85.7 %reduce-scatter.10.cloned.1.call-done = bf16[128,256]{1,0:T(8,128)(2,1)} async-done(((bf16[1024,256]{1,0:T(8,128)(2,1)}), bf16[128,256]{1,0:T(8,128)(2,1)}) %reduce-scatter.10.cloned.1.call-update) | async-done | bytes 65552
  391.9 1.6 copy.75
  393.5 235.1 %reduce-scatter.12.cloned.1.call-done = f32[16,544]{1,0:T(8,128)} async-done(((f32[1024,544]{1,0:T(8,128)}), f32[16,544]{1,0:T(8,128)}) %reduce-scatter.12.cloned.1.call-update) | async-done | bytes 34832
  628.6 1.3 fusion.41
  630.0 1.3 slice.28
  (274 shorter events, 40.7 us)
Async XLA Ops:
  7.2 296.4 %copy-start = (bf16[256,1024]{1,0:T(8,128)(2,1)S(1)}, bf16[256,1024]{1,0:T(8,128)(2,1)}, u32[]{:S(2)}) copy-start(bf16[256,1024]{1,0:T(8,128)(2,1)} %param.13) | copy-start | bytes 1572868
  7.2 4.8 copy-start.1
  7.2 123.5 %copy-start.9 = (bf16[256,256]{1,0:T(8,128)(2,1)S(1)}, bf16[256,256]{1,0:T(8,128)(2,1)}, u32[]{:S(2)}) copy-start(bf16[256,256]{1,0:T(8,128)(2,1)} %param.14) | copy-start | bytes 393220
  7.2 123.8 %copy-start.4 = (f32[1,4,128,64]{2,3,1,0:T(8,128)S(1)}, f32[1,4,128,64]{2,3,1,0:T(8,128)}, u32[]{:S(2)}) copy-start(f32[1,4,128,64]{2,3,1,0:T(8,128)} %param.20) | copy-start | bytes 393220
  7.2 138.6 %all-gather.3.cloned.1.call-start = ((), (), s32[]{:S(2)}) async-start(), calls=%async_computation.3 | async-start | bytes 8519680 | tf_op jit(solution)/shard_map/all_gather | solution.py:18
  11.9 120.5 %copy-start.6 = (f32[256,256]{0,1:T(8,128)}, f32[256,256]{0,1:T(8,128)S(1)}, u32[]{:S(2)}) copy-start(f32[256,256]{0,1:T(8,128)S(1)} %get-tuple-element.156) | copy-start | bytes 786436
  11.9 120.3 %copy-start.2 = (bf16[256,128]{1,0:T(8,128)(2,1)S(1)}, bf16[256,128]{1,0:T(8,128)(2,1)}, u32[]{:S(2)}) copy-start(bf16[256,128]{1,0:T(8,128)(2,1)} %param.17) | copy-start | bytes 196612
  12.9 288.5 %reduce-scatter.8.cloned.1.call-start = ((), (), s32[]{:S(2)}) async-start(), calls=%async_computation.4 | async-start | bytes 294912 | tf_op jit(solution)/shard_map/reduce_scatter | solution.py:170
  131.0 3.7 copy-start.11
  132.5 2.3 copy-start.8
  132.7 2.0 copy-start.3
  222.2 3.7 copy-start.7
  222.2 5.8 copy-start.5
  225.8 76.4 %copy-start.10 = (bf16[1024,32]{0,1:T(8,128)(2,1)S(1)}, bf16[1024,32]{0,1:T(8,128)(2,1)}, u32[]{:S(2)}) copy-start(bf16[1024,32]{0,1:T(8,128)(2,1)} %param.23) | copy-start | bytes 196612
  225.8 166.1 %reduce-scatter.10.cloned.1.call-start = ((), (), s32[]{:S(2)}) async-start(), calls=%async_computation.5 | async-start | bytes 589824
  303.6 325.1 %reduce-scatter.12.cloned.1.call-start = ((), (), s32[]{:S(2)}) async-start(), calls=%async_computation.6 | async-start | bytes 2662400
Sparse Core Ops, SparseCore 0:
  13.0 132.7 all-gather.2
  225.9 75.4 reduce-scatter.7
  305.9 85.9 reduce-scatter.9
  394.6 234.0 reduce-scatter.11
where the time goes:
time: 639 us; the launch traced here: 638 us
  waiting for transfers between devices  405 us (63%)
  blocking collectives  116 us (18%)
  local copies, waits for them, and re-layouts  78.9 us (12%)
  between operations  14.8 us (2%)
  other arithmetic  10.6 us (2%)
  matrix products  10 us (2%)
    unnamed x6, waiting for transfers between devices  321 us
    unnamed x1, blocking collectives  116 us
    reduce_scatter x1, waiting for transfers between devices, per_device(): lax.psum_scatter(grad_bc_part, 'head', scatter_dimension=1, tiled=True)  73.1 us
    dynamic_slice x126, local copies, waits for them, and re-layouts, one(): lax.dynamic_index_in_dim(a, source, 0, False)  66 us
  transfers between devices with their start and end apart: 4, of which 4 were waited for; matrix products, arithmetic and copies ran while one was open for 2% of the time, Pallas kernels for 0%

commit v1 on v0

--- a/solution.py
+++ b/solution.py
@@ -11,20 +11,31 @@
 highest = lax.Precision.HIGHEST
 
 
-def entering(part, axis, combine, identity):
+def suffix_scan(part, axis):
     count = lax.axis_size(axis)
     place = lax.axis_index(axis)
-    ahead = count - 1 - place
-    gathered = jax.tree.map(lambda a: lax.all_gather(a, axis), part)
-    state = jax.tree.map(lambda a, e: jnp.zeros_like(a) + jnp.asarray(e, a.dtype), part, identity)
-
-    def one(lap, state):
-        source = count - 1 - lap
-        return combine(
-            state, jax.tree.map(lambda a: lax.dynamic_index_in_dim(a, source, 0, False), gathered)
+
+    def shifted(tree, step):
+        pairs = [(source, source - step) for source in range(step, count)]
+        return jax.tree.map(lambda a: lax.ppermute(a, axis, pairs), tree)
+
+    def combine(near, far):
+        return (near[0] * far[0], near[1] + near[0][:, None, None] * far[1])
+
+    state = shifted(part, 1)
+    valid = place + 1 < count
+    state = (jnp.where(valid, state[0], 1.0), jnp.where(valid, state[1], 0.0))
+    step = 1
+    while step < count:
+        far = shifted(state, step)
+        joined = combine(state, far)
+        inside = place + step < count
+        state = (
+            jnp.where(inside, joined[0], state[0]),
+            jnp.where(inside, joined[1], state[1]),
         )
-
-    return lax.fori_loop(0, ahead, one, state)
+        step *= 2
+    return state
 
 
 def ssd_partials(ssm_input, gate_input, grad_out, shared_b, shared_c, log_decay, entry, block_len):
@@ -138,6 +149,13 @@
     )
 
 
+def summed_over(part, axis, split):
+    gathered = lax.all_to_all(part, axis, split, split, tiled=True)
+    shape = gathered.shape
+    pieces = shape[:split] + (lax.axis_size(axis), shape[split] // lax.axis_size(axis)) + shape[split + 1 :]
+    return jnp.sum(gathered.astype(jnp.float32).reshape(pieces), axis=split)
+
+
 def per_device(
     events,
     ssm_input,
@@ -154,58 +172,60 @@
     partials = ssd_partials(
         ssm_input, gate_input, grad_out, shared_b, shared_c, log_decay, entry_state[0], SPAN
     )
-    grad_z = partials[0]
     block_sum = partials[9]
     block_log = partials[10]
-
-    def combine(earlier_part, later_part):
-        return (
-            earlier_part[0] * later_part[0],
-            later_part[1] + later_part[0][:, None, None] * earlier_part[1],
-        )
-
-    identity = (jnp.ones_like(block_log), jnp.zeros_like(block_sum))
-    _, incoming = entering((jnp.exp(block_log), block_sum), "ctx", combine, identity)
+    _, incoming = suffix_scan((jnp.exp(block_log), block_sum), CTX)
     grad_z, grad_x, grad_bc_part = finish_block(partials, incoming)
-    grad_bc = lax.psum_scatter(grad_bc_part, "head", scatter_dimension=1, tiled=True).astype(
-        jnp.bfloat16
-    )
+    grad_bc = summed_over(grad_bc_part, HEAD, 1).astype(jnp.bfloat16)
     input_part = (
         times_rows(grad_z, w_gate) + times_rows(grad_x, w_value) + times_rows(grad_bc, w_shared)
     )
-    grad_input = lax.psum_scatter(
-        input_part.astype(jnp.bfloat16), "head", scatter_dimension=1, tiled=True
-    )
-    norm_scale = 1.0 / math.sqrt(events.shape[0] * lax.axis_size("ctx"))
+    grad_input = summed_over(input_part.astype(jnp.bfloat16), HEAD, 1).astype(jnp.bfloat16)
+    norm_scale = 1.0 / math.sqrt(events.shape[0] * lax.axis_size(CTX))
     head_cols = grad_z.shape[1]
     projected = jnp.concatenate([grad_z, grad_x, grad_bc], axis=1)
-    reduced = lax.psum_scatter(
-        row_term(events, projected, norm_scale), "ctx", scatter_dimension=0, tiled=True
-    )
+    rows = row_term(events, projected, norm_scale)
+    sizes = [lax.axis_size(name) for name in CTX]
+    rows = rows.reshape(*sizes, rows.shape[0] // math.prod(sizes), rows.shape[1])
+    for level in reversed(range(len(CTX))):
+        rows = summed_over(rows, CTX[level], level)
+    reduced = rows.reshape(rows.shape[-2], rows.shape[-1])
     grad_w_gate = reduced[:, :head_cols]
     grad_w_value = reduced[:, head_cols : 2 * head_cols]
     grad_w_shared = reduced[:, 2 * head_cols :]
     return (grad_input, grad_w_gate, grad_w_value, grad_w_shared)
 
 
+CTX = ("z", "y_lo", "core")
+HEAD = ("y_hi", "x")
+
+
 def solution(mesh):
+    ctx_size, head_size = mesh.devices.shape
+    z_size = ctx_size // 4
+    fine = jax.sharding.Mesh(
+        mesh.devices.reshape(z_size, 2, 2, 2, head_size // 2),
+        CTX + HEAD,
+    )
+    rows = P(CTX, None)
+    both = P(CTX, HEAD)
     placed = (
-        P("ctx", None),
-        P("ctx", "head"),
-        P("ctx", "head"),
-        P("ctx", "head"),
-        P("ctx", None),
-        P("ctx", None),
-        P("head", "ctx"),
-        P("ctx", "head", None, None),
-        P(None, "head"),
-        P(None, "head"),
-        P(None, "head"),
+        rows,
+        both,
+        both,
+        both,
+        rows,
+        rows,
+        P(HEAD, CTX),
+        P(CTX, HEAD, None, None),
+        P(None, HEAD),
+        P(None, HEAD),
+        P(None, HEAD),
     )
     return jax.shard_map(
         per_device,
-        mesh=mesh,
+        mesh=fine,
         in_specs=placed,
-        out_specs=(P("ctx", "head"), P("ctx", "head"), P("ctx", "head"), P("ctx", "head")),
+        out_specs=(both, both, both, both),
         check_vma=False,
     )

time: 639 us -> 198 us (0.31)
  the two profiles are of different devices: /device:TPU:4 before, /device:TPU:32 now
where the time goes in v1:
time: 198 us; the launch traced here: 197 us
  waiting for transfers between devices  109 us (55%)
  starting transfers between devices  56.3 us (28%)
  local copies, waits for them, and re-layouts  10.7 us (5%)
  matrix products  8.18 us (4%)
  blocking collectives  5.84 us (3%)
  other arithmetic  5.83 us (3%)
    all_to_all x4, waiting for transfers between devices, summed_over(): gathered = lax.all_to_all(part, axis, split, split, tiled=True)  66.5 us
    ppermute x13, waiting for transfers between devices, shifted(): return jax.tree.map(lambda a: lax.ppermute(a, axis, pairs), tree)  42.7 us
    ppermute x13, starting transfers between devices, shifted(): return jax.tree.map(lambda a: lax.ppermute(a, axis, pairs), tree)  29.4 us
    all_to_all x4, starting transfers between devices, summed_over(): gathered = lax.all_to_all(part, axis, split, split, tiled=True)  27 us
    all_to_all x1, blocking collectives, summed_over(): gathered = lax.all_to_all(part, axis, split, split, tiled=True)  5.84 us
  transfers between devices with their start and end apart: 17, of which 9 were waited for; matrix products, arithmetic and copies ran while one was open for 6% of the time, Pallas kernels for 0%

profile of v1, /device:TPU:32, one launch (start us, length us, event | category | flops | bytes accessed | tf_op | source)
XLA Modules:
  0.0 197.3 jit_solution(14237723721161363292)
XLA Ops:
  0.7 0.8 reshape.383
  1.5 1.2 reduce-window.6
  2.7 0.1 copy.71
  2.9 0.1 copy.58
  3.1 2.5 %collective-permute-start.1 = (f32[4]{0:T(128)S(1)}, f32[4]{0:T(128)S(1)}, u32[]{:S(2)}, u32[]{:S(2)}) collective-permute-start(f32[4]{0:T(128)S(1)} %get-tuple-element.34), channel_id=1, source_target_pairs={{8,0},{16,8},{24,16},{32,24},{40,32},{48,40},{56,48},{64,56},{72,6... | collective-permute-start | bytes 56 | tf_op jit(solution)/shard_map/ppermute | solution.py:20
  5.7 1.0 copy.63
  6.7 1.0 copy.56
  7.7 0.1 bitcast_multiply_fusion.1
  7.8 0.3 fusion.12
  8.1 2.6 %collective-permute-start = (f32[4,128,64]{1,2,0:T(8,128)S(1)}, f32[4,128,64]{1,2,0:T(8,128)S(1)}, u32[]{:S(2)}, u32[]{:S(2)}) collective-permute-start(f32[4,128,64]{1,2,0:T(8,128)S(1)} %fusion.12), channel_id=1, source_target_pairs={{8,0},{16,8},{24,16},{32,24},{40,32},{48,40},{56,48},{64,56},{72,6... | collective-permute-start | bytes 393224 | tf_op jit(solution)/shard_map/ppermute | solution.py:20
  10.9 0.1 copy.60
  11.1 0.2 fusion.43
  11.3 0.4 convolution_bitcast_fusion.3
  11.7 0.3 fusion.44
  12.0 0.8 fusion.1
  12.8 0.3 fusion.46
  13.1 0.3 convolution_add_fusion.2
  13.4 1.0 fusion.11
  14.4 1.1 convolution_bitcast_fusion.1
  15.5 2.4 %collective-permute-start.2 = (f32[4,128,64]{1,2,0:T(8,128)S(1)}, f32[4,128,64]{1,2,0:T(8,128)S(1)}, u32[]{:S(2)}, u32[]{:S(2)}) collective-permute-start(f32[4,128,64]{1,2,0:T(8,128)S(1)} %broadcast_select_fusion), channel_id=1, source_target_pairs={{8,0},{16,8},{24,16},{32,24},{40,32},{48,40},{56,48},{64,56},{72,6... | collective-permute-start | bytes 393224 | tf_op jit(solution)/shard_map/ppermute | solution.py:20
  17.9 7.3 %collective-permute-start.3 = (f32[4]{0:T(128)S(1)}, f32[4]{0:T(128)S(1)}, u32[]{:S(2)}, u32[]{:S(2)}) collective-permute-start(f32[4]{0:T(128)S(1)} %broadcast_select_fusion.6), channel_id=1, source_target_pairs={{8,0},{16,8},{24,16},{32,24},{40,32},{48,40},{56,48},{64,56},{72,6... | collective-permute-start | bytes 56 | tf_op jit(solution)/shard_map/ppermute | solution.py:20
  25.4 2.4 %collective-permute-start.4 = (f32[4,128,64]{1,2,0:T(8,128)S(1)}, f32[4,128,64]{1,2,0:T(8,128)S(1)}, u32[]{:S(2)}, u32[]{:S(2)}) collective-permute-start(f32[4,128,64]{1,2,0:T(8,128)S(1)} %add_select_fusion.5), channel_id=1, source_target_pairs={{16,0},{24,8},{32,16},{40,24},{48,32},{56,40},{64,48},{72,56},{80,... | collective-permute-start | bytes 393224 | tf_op jit(solution)/shard_map/ppermute | solution.py:20
  27.7 1.9 collective-permute-start.5
  29.7 2.5 %collective-permute-done.4 = f32[4,128,64]{1,2,0:T(8,128)S(1)} collective-permute-done((f32[4,128,64]{1,2,0:T(8,128)S(1)}, f32[4,128,64]{1,2,0:T(8,128)S(1)}, u32[]{:S(2)}, u32[]{:S(2)}) %collective-permute-start.4) | collective-permute-done | bytes 131104 | tf_op jit(solution)/shard_map/ppermute | solution.py:20
  32.2 0.1 add_select_fusion.4
  32.3 1.9 collective-permute-start.6
  34.3 1.9 collective-permute-start.7
  36.2 3.0 %collective-permute-done.6 = f32[4,128,64]{1,2,0:T(8,128)S(1)} collective-permute-done((f32[4,128,64]{1,2,0:T(8,128)S(1)}, f32[4,128,64]{1,2,0:T(8,128)S(1)}, u32[]{:S(2)}, u32[]{:S(2)}) %collective-permute-start.6) | collective-permute-done | bytes 131104 | tf_op jit(solution)/shard_map/ppermute | solution.py:20
  39.2 0.1 add_select_fusion.3
  39.3 1.3 collective-permute-start.8
  40.6 1.3 collective-permute-start.9
  41.9 8.9 %collective-permute-done.8 = f32[4,128,64]{1,2,0:T(8,128)S(1)} collective-permute-done((f32[4,128,64]{1,2,0:T(8,128)S(1)}, f32[4,128,64]{1,2,0:T(8,128)S(1)}, u32[]{:S(2)}, u32[]{:S(2)}) %collective-permute-start.8) | collective-permute-done | bytes 131104 | tf_op jit(solution)/shard_map/ppermute | solution.py:20
  50.8 0.1 add_select_fusion.2
  50.9 1.3 collective-permute-start.10
  52.2 1.3 collective-permute-start.11
  53.5 13.5 %collective-permute-done.10 = f32[4,128,64]{1,2,0:T(8,128)S(1)} collective-permute-done((f32[4,128,64]{1,2,0:T(8,128)S(1)}, f32[4,128,64]{1,2,0:T(8,128)S(1)}, u32[]{:S(2)}, u32[]{:S(2)}) %collective-permute-start.10) | collective-permute-done | bytes 131104 | tf_op jit(solution)/shard_map/ppermute | solution.py:20
  67.1 1.3 collective-permute-start.12
  68.4 14.7 %collective-permute-done.12 = f32[4,128,64]{1,2,0:T(8,128)S(1)} collective-permute-done((f32[4,128,64]{1,2,0:T(8,128)S(1)}, f32[4,128,64]{1,2,0:T(8,128)S(1)}, u32[]{:S(2)}, u32[]{:S(2)}) %collective-permute-start.12) | collective-permute-done | bytes 131104 | tf_op jit(solution)/shard_map/ppermute | solution.py:20
  83.1 0.5 fusion.13
  83.6 0.7 pad_maximum_fusion
  84.3 6.6 %all-to-all-start = ((f32[256,8,32]{0,2,1:T(8,128)}), f32[256,8,32]{0,2,1:T(8,128)S(1)}, u32[]{:S(2)}, u32[]{:S(2)}) async-start(f32[256,8,32]{0,2,1:T(8,128)} %pad_maximum_fusion), calls=%async_computation | async-start | bytes 524288 | tf_op jit(solution)/shard_map/all_to_all | solution.py:153
  91.0 0.3 fusion.10
  91.3 8.5 %all-to-all-done = f32[256,8,32]{0,2,1:T(8,128)S(1)} async-done(((f32[256,8,32]{0,2,1:T(8,128)}), f32[256,8,32]{0,2,1:T(8,128)S(1)}, u32[]{:S(2)}, u32[]{:S(2)}) %all-to-all-start) | async-done | bytes 262176 | tf_op jit(solution)/shard_map/all_to_all | solution.py:153
  99.8 1.8 multiply_bitcast_fusion
  101.6 2.1 %copy.67 = f32[1024,544]{1,0:T(8,128)S(1)} copy(f32[1024,544]{0,1:T(8,128)} %multiply_bitcast_fusion) | data formatting | bytes 4456448 | tf_op jit(solution)/shard_map/mul | solution.py:145
  103.7 0.3 copy.68
  104.1 5.8 %all_to_all.30 = f32[16,2,2,16,544]{4,3,1,0,2:T(8,128)S(1)} all-to-all(f32[16,2,2,16,544]{4,3,1,0,2:T(8,128)S(1)} %copy.68), channel_id=1, replica_groups=mesh['z'=16,'y_lo'=2,'core'=2,'y_hi'=2,'x'=4] {'core'}, dimensions={2} | all-to-all | bytes 4456448 | tf_op jit(solution)/shard_map/all_to_all | solution.py:153
  109.9 1.4 reduce_sum.72
  111.3 2.6 %copy.69 = f32[16,2,1,16,544]{4,3,0,2,1:T(8,128)} copy(f32[16,2,1,16,544]{4,3,1,0,2:T(8,128)} %bitcast.154) | data formatting | bytes 2228224 | tf_op jit(solution)/shard_map/reduce_sum | solution.py:156
  113.9 3.8 %all-to-all-start.3 = ((f32[16,2,1,16,544]{4,3,0,2,1:T(8,128)}), f32[16,2,1,16,544]{4,3,0,2,1:T(8,128)S(1)}, u32[]{:S(2)}, u32[]{:S(2)}) async-start(f32[16,2,1,16,544]{4,3,0,2,1:T(8,128)} %copy.69), calls=%async_computation.3 | async-start | bytes 2621440 | tf_op jit(solution)/shard_map/all_to_all | solution.py:153
  117.6 0.3 fusion.45
  118.0 0.3 convolution_add_fusion.1
  118.4 0.1 copy-done.7
  118.5 0.3 fusion.2
  118.8 0.9 copy.76
  119.7 14.9 %all-to-all-done.3 = f32[16,2,1,16,544]{4,3,0,2,1:T(8,128)S(1)} async-done(((f32[16,2,1,16,544]{4,3,0,2,1:T(8,128)}), f32[16,2,1,16,544]{4,3,0,2,1:T(8,128)S(1)}, u32[]{:S(2)}, u32[]{:S(2)}) %all-to-all-start.3) | async-done | bytes 1114144 | tf_op jit(solution)/shard_map/all_to_all | solution.py:153
  134.6 3.5 %all-to-all-start.1 = ((bf16[256,8,128]{2,0,1:T(8,128)(2,1)}), bf16[256,8,128]{2,0,1:T(8,128)(2,1)S(1)}, u32[]{:S(2)}, u32[]{:S(2)}) async-start(bf16[256,8,128]{2,0,1:T(8,128)(2,1)} %bitcast.150), calls=%async_computation.1 | async-start | bytes 1048576 | tf_op jit(solution)/shard_map/all_to_all | solution.py:153
  138.1 1.0 reduce_sum.74
  139.1 10.3 %all-to-all-done.1 = bf16[256,8,128]{2,0,1:T(8,128)(2,1)S(1)} async-done(((bf16[256,8,128]{2,0,1:T(8,128)(2,1)}), bf16[256,8,128]{2,0,1:T(8,128)(2,1)S(1)}, u32[]{:S(2)}, u32[]{:S(2)}) %all-to-all-start.1) | async-done | bytes 524320 | tf_op jit(solution)/shard_map/all_to_all | solution.py:153
  149.3 13.1 %all-to-all-start.4 = ((f32[16,1,1,16,544]{4,3,2,1,0:T(8,128)}), f32[16,1,1,16,544]{4,3,2,1,0:T(8,128)S(1)}, u32[]{:S(2)}, u32[]{:S(2)}) async-start(f32[16,1,1,16,544]{4,3,2,1,0:T(8,128)} %bitcast.46), calls=%async_computation.4 | async-start | bytes 1310720 | tf_op jit(solution)/shard_map/all_to_all | solution.py:153
  162.4 0.7 reduce_sum.71
  163.1 32.9 %all-to-all-done.4 = f32[16,1,1,16,544]{4,3,2,1,0:T(8,128)S(1)} async-done(((f32[16,1,1,16,544]{4,3,2,1,0:T(8,128)}), f32[16,1,1,16,544]{4,3,2,1,0:T(8,128)S(1)}, u32[]{:S(2)}, u32[]{:S(2)}) %all-to-all-start.4) | async-done | bytes 557088 | tf_op jit(solution)/shard_map/all_to_all | solution.py:153
  196.1 0.6 slice.28
  196.7 0.6 fusion.42
  (48 shorter events, 0.8 us)
Async XLA Ops:
  0.6 99.2 %copy-start = (bf16[256,1024]{1,0:T(8,128)(2,1)S(1)}, bf16[256,1024]{1,0:T(8,128)(2,1)}, u32[]{:S(2)}) copy-start(bf16[256,1024]{1,0:T(8,128)(2,1)} %param.11) | copy-start | bytes 1572868
  0.6 7.2 %copy-start.1 = (bf16[256,128]{1,0:T(8,128)(2,1)S(1)}, bf16[256,128]{1,0:T(8,128)(2,1)}, u32[]{:S(2)}) copy-start(bf16[256,128]{1,0:T(8,128)(2,1)} %param.16) | copy-start | bytes 196612
  0.7 10.3 %copy-start.6 = (bf16[256,256]{1,0:T(8,128)(2,1)S(1)}, bf16[256,256]{1,0:T(8,128)(2,1)}, u32[]{:S(2)}) copy-start(bf16[256,256]{1,0:T(8,128)(2,1)} %param.12) | copy-start | bytes 393220
  0.7 10.4 %copy-start.2 = (bf16[256,128]{1,0:T(8,128)(2,1)S(1)}, bf16[256,128]{1,0:T(8,128)(2,1)}, u32[]{:S(2)}) copy-start(bf16[256,128]{1,0:T(8,128)(2,1)} %param.15) | copy-start | bytes 196612
  0.7 10.6 %copy-start.4 = (f32[1,4,128,64]{2,3,1,0:T(8,128)S(1)}, f32[1,4,128,64]{2,3,1,0:T(8,128)}, u32[]{:S(2)}) copy-start(f32[1,4,128,64]{2,3,1,0:T(8,128)} %param.18) | copy-start | bytes 393220
  3.1 14.8 %collective-permute-start.1 = (f32[4]{0:T(128)S(1)}, f32[4]{0:T(128)S(1)}, u32[]{:S(2)}, u32[]{:S(2)}) collective-permute-start(f32[4]{0:T(128)S(1)} %get-tuple-element.34), channel_id=1, source_target_pairs={{8,0},{16,8},{24,16},{32,24},{40,32},{48,40},{56,48},{64,56},{72,6... | collective-permute-start | bytes 56 | tf_op jit(solution)/shard_map/ppermute | solution.py:20
  8.1 7.3 %collective-permute-start = (f32[4,128,64]{1,2,0:T(8,128)S(1)}, f32[4,128,64]{1,2,0:T(8,128)S(1)}, u32[]{:S(2)}, u32[]{:S(2)}) collective-permute-start(f32[4,128,64]{1,2,0:T(8,128)S(1)} %fusion.12), channel_id=1, source_target_pairs={{8,0},{16,8},{24,16},{32,24},{40,32},{48,40},{56,48},{64,56},{72,6... | collective-permute-start | bytes 393224 | tf_op jit(solution)/shard_map/ppermute | solution.py:20
  15.5 9.8 %collective-permute-start.2 = (f32[4,128,64]{1,2,0:T(8,128)S(1)}, f32[4,128,64]{1,2,0:T(8,128)S(1)}, u32[]{:S(2)}, u32[]{:S(2)}) collective-permute-start(f32[4,128,64]{1,2,0:T(8,128)S(1)} %broadcast_select_fusion), channel_id=1, source_target_pairs={{8,0},{16,8},{24,16},{32,24},{40,32},{48,40},{56,48},{64,56},{72,6... | collective-permute-start | bytes 393224 | tf_op jit(solution)/shard_map/ppermute | solution.py:20
  17.9 9.8 %collective-permute-start.3 = (f32[4]{0:T(128)S(1)}, f32[4]{0:T(128)S(1)}, u32[]{:S(2)}, u32[]{:S(2)}) collective-permute-start(f32[4]{0:T(128)S(1)} %broadcast_select_fusion.6), channel_id=1, source_target_pairs={{8,0},{16,8},{24,16},{32,24},{40,32},{48,40},{56,48},{64,56},{72,6... | collective-permute-start | bytes 56 | tf_op jit(solution)/shard_map/ppermute | solution.py:20
  25.4 6.9 %collective-permute-start.4 = (f32[4,128,64]{1,2,0:T(8,128)S(1)}, f32[4,128,64]{1,2,0:T(8,128)S(1)}, u32[]{:S(2)}, u32[]{:S(2)}) collective-permute-start(f32[4,128,64]{1,2,0:T(8,128)S(1)} %add_select_fusion.5), channel_id=1, source_target_pairs={{16,0},{24,8},{32,16},{40,24},{48,32},{56,40},{64,48},{72,56},{80,... | collective-permute-start | bytes 393224 | tf_op jit(solution)/shard_map/ppermute | solution.py:20
  27.7 6.5 %collective-permute-start.5 = (f32[4]{0:T(128)S(1)}, f32[4]{0:T(128)S(1)}, u32[]{:S(2)}, u32[]{:S(2)}) collective-permute-start(f32[4]{0:T(128)S(1)} %broadcast_select_fusion.5), channel_id=1, source_target_pairs={{16,0},{24,8},{32,16},{40,24},{48,32},{56,40},{64,48},{72,56},{80,... | collective-permute-start | bytes 56 | tf_op jit(solution)/shard_map/ppermute | solution.py:20
  32.3 6.9 %collective-permute-start.6 = (f32[4,128,64]{1,2,0:T(8,128)S(1)}, f32[4,128,64]{1,2,0:T(8,128)S(1)}, u32[]{:S(2)}, u32[]{:S(2)}) collective-permute-start(f32[4,128,64]{1,2,0:T(8,128)S(1)} %add_select_fusion.4), channel_id=1, source_target_pairs={{32,0},{40,8},{48,16},{56,24},{64,32},{72,40},{80,48},{88,56},{96,... | collective-permute-start | bytes 393224 | tf_op jit(solution)/shard_map/ppermute | solution.py:20
  34.3 6.3 %collective-permute-start.7 = (f32[4]{0:T(128)S(1)}, f32[4]{0:T(128)S(1)}, u32[]{:S(2)}, u32[]{:S(2)}) collective-permute-start(f32[4]{0:T(128)S(1)} %broadcast_select_fusion.4), channel_id=1, source_target_pairs={{32,0},{40,8},{48,16},{56,24},{64,32},{72,40},{80,48},{88,56},{96,... | collective-permute-start | bytes 56 | tf_op jit(solution)/shard_map/ppermute | solution.py:20
  39.3 11.5 %collective-permute-start.8 = (f32[4,128,64]{1,2,0:T(8,128)S(1)}, f32[4,128,64]{1,2,0:T(8,128)S(1)}, u32[]{:S(2)}, u32[]{:S(2)}) collective-permute-start(f32[4,128,64]{1,2,0:T(8,128)S(1)} %add_select_fusion.3), channel_id=1, source_target_pairs={{64,0},{72,8},{80,16},{88,24},{96,32},{104,40},{112,48},{120,56},{... | collective-permute-start | bytes 393224 | tf_op jit(solution)/shard_map/ppermute | solution.py:20
  40.6 11.6 %collective-permute-start.9 = (f32[4]{0:T(128)S(1)}, f32[4]{0:T(128)S(1)}, u32[]{:S(2)}, u32[]{:S(2)}) collective-permute-start(f32[4]{0:T(128)S(1)} %broadcast_select_fusion.3), channel_id=1, source_target_pairs={{64,0},{72,8},{80,16},{88,24},{96,32},{104,40},{112,48},{120,56},{... | collective-permute-start | bytes 56 | tf_op jit(solution)/shard_map/ppermute | solution.py:20
  50.9 16.1 %collective-permute-start.10 = (f32[4,128,64]{1,2,0:T(8,128)S(1)}, f32[4,128,64]{1,2,0:T(8,128)S(1)}, u32[]{:S(2)}, u32[]{:S(2)}) collective-permute-start(f32[4,128,64]{1,2,0:T(8,128)S(1)} %add_select_fusion.2), channel_id=1, source_target_pairs={{128,0},{136,8},{144,16},{152,24},{160,32},{168,40},{176,48},{184,... | collective-permute-start | bytes 393224 | tf_op jit(solution)/shard_map/ppermute | solution.py:20
  52.2 16.1 %collective-permute-start.11 = (f32[4]{0:T(128)S(1)}, f32[4]{0:T(128)S(1)}, u32[]{:S(2)}, u32[]{:S(2)}) collective-permute-start(f32[4]{0:T(128)S(1)} %broadcast_select_fusion.2), channel_id=1, source_target_pairs={{128,0},{136,8},{144,16},{152,24},{160,32},{168,40},{176,48},{184,... | collective-permute-start | bytes 56 | tf_op jit(solution)/shard_map/ppermute | solution.py:20
  67.1 16.0 %collective-permute-start.12 = (f32[4,128,64]{1,2,0:T(8,128)S(1)}, f32[4,128,64]{1,2,0:T(8,128)S(1)}, u32[]{:S(2)}, u32[]{:S(2)}) collective-permute-start(f32[4,128,64]{1,2,0:T(8,128)S(1)} %add_select_fusion.1), channel_id=1, source_target_pairs={{256,0},{264,8},{272,16},{280,24},{288,32},{296,40},{304,48},{312,... | collective-permute-start | bytes 393224 | tf_op jit(solution)/shard_map/ppermute | solution.py:20
  84.3 15.4 %all-to-all-start = ((f32[256,8,32]{0,2,1:T(8,128)}), f32[256,8,32]{0,2,1:T(8,128)S(1)}, u32[]{:S(2)}, u32[]{:S(2)}) async-start(f32[256,8,32]{0,2,1:T(8,128)} %pad_maximum_fusion), calls=%async_computation | async-start | bytes 524288 | tf_op jit(solution)/shard_map/all_to_all | solution.py:153
  111.3 6.3 %copy-start.3 = (bf16[1024,256]{1,0:T(8,128)(2,1)S(1)}, bf16[1024,256]{1,0:T(8,128)(2,1)}, u32[]{:S(2)}) copy-start(bf16[1024,256]{1,0:T(8,128)(2,1)} %param.19) | copy-start | bytes 1572868
  113.9 4.1 %copy-start.5 = (bf16[1024,256]{1,0:T(8,128)(2,1)S(1)}, bf16[1024,256]{1,0:T(8,128)(2,1)}, u32[]{:S(2)}) copy-start(bf16[1024,256]{1,0:T(8,128)(2,1)} %param.20) | copy-start | bytes 1572868
  113.9 20.7 %all-to-all-start.3 = ((f32[16,2,1,16,544]{4,3,0,2,1:T(8,128)}), f32[16,2,1,16,544]{4,3,0,2,1:T(8,128)S(1)}, u32[]{:S(2)}, u32[]{:S(2)}) async-start(f32[16,2,1,16,544]{4,3,0,2,1:T(8,128)} %copy.69), calls=%async_computation.3 | async-start | bytes 2621440 | tf_op jit(solution)/shard_map/all_to_all | solution.py:153
  117.6 0.8 copy-start.7
  134.6 14.8 %all-to-all-start.1 = ((bf16[256,8,128]{2,0,1:T(8,128)(2,1)}), bf16[256,8,128]{2,0,1:T(8,128)(2,1)S(1)}, u32[]{:S(2)}, u32[]{:S(2)}) async-start(bf16[256,8,128]{2,0,1:T(8,128)(2,1)} %bitcast.150), calls=%async_computation.1 | async-start | bytes 1048576 | tf_op jit(solution)/shard_map/all_to_all | solution.py:153
  149.3 46.7 %all-to-all-start.4 = ((f32[16,1,1,16,544]{4,3,2,1,0:T(8,128)}), f32[16,1,1,16,544]{4,3,2,1,0:T(8,128)S(1)}, u32[]{:S(2)}, u32[]{:S(2)}) async-start(f32[16,1,1,16,544]{4,3,2,1,0:T(8,128)} %bitcast.46), calls=%async_computation.4 | async-start | bytes 1310720 | tf_op jit(solution)/shard_map/all_to_all | solution.py:153

commit v2 on v1

--- a/solution.py
+++ b/solution.py
@@ -188,7 +188,7 @@
     sizes = [lax.axis_size(name) for name in CTX]
     rows = rows.reshape(*sizes, rows.shape[0] // math.prod(sizes), rows.shape[1])
     for level in reversed(range(len(CTX))):
-        rows = summed_over(rows, CTX[level], level)
+        rows = summed_over(rows.astype(jnp.bfloat16), CTX[level], level)
     reduced = rows.reshape(rows.shape[-2], rows.shape[-1])
     grad_w_gate = reduced[:, :head_cols]
     grad_w_value = reduced[:, head_cols : 2 * head_cols]

time: 198 us -> 173 us (0.87)
  waiting for transfers between devices: 109 us -> 88.8 us
  local copies, waits for them, and re-layouts: 10.7 us -> 7.02 us
    all_to_all x4, waiting for transfers between devices: 66.5 us -> 46.5 us  [summed_over(): gathered = lax.all_to_all(part, axis, split, split, tiled=True)]
    convert_element_type x0 -> x3, local copies, waits for them, and re-layouts: none -> 2.69 us  [per_device(): rows = summed_over(rows.astype(jnp.bfloat16), CTX[level], level)]
    reduce_sum x1 -> x0, local copies, waits for them, and re-layouts: 2.56 us -> none  [summed_over(): return jnp.sum(gathered.astype(jnp.float32).reshape(pieces), axis=split)]
    mul x1 -> x0, local copies, waits for them, and re-layouts: 2.08 us -> none  [row_term(): lax.dot_general(events, projected, (((0,), (0,)), ((), ())), preferred_el...]
where the time goes in v2:
time: 173 us; the launch traced here: 172 us
  waiting for transfers between devices  88.8 us (51%)
  starting transfers between devices  56.8 us (33%)
  matrix products  7.81 us (5%)
  local copies, waits for them, and re-layouts  7.02 us (4%)
  other arithmetic  4.99 us (3%)
  blocking collectives  4.79 us (3%)
    all_to_all x4, waiting for transfers between devices, summed_over(): gathered = lax.all_to_all(part, axis, split, split, tiled=True)  46.5 us
    ppermute x13, waiting for transfers between devices, shifted(): return jax.tree.map(lambda a: lax.ppermute(a, axis, pairs), tree)  42.4 us
    ppermute x13, starting transfers between devices, shifted(): return jax.tree.map(lambda a: lax.ppermute(a, axis, pairs), tree)  29.4 us
    all_to_all x4, starting transfers between devices, summed_over(): gathered = lax.all_to_all(part, axis, split, split, tiled=True)  27.5 us
    all_to_all x1, blocking collectives, summed_over(): gathered = lax.all_to_all(part, axis, split, split, tiled=True)  4.79 us
  transfers between devices with their start and end apart: 17, of which 9 were waited for; matrix products, arithmetic and copies ran while one was open for 6% of the time, Pallas kernels for 0%

profile of v2, /device:TPU:32, one launch (start us, length us, event | category | flops | bytes accessed | tf_op | source)
XLA Modules:
  0.0 171.5 jit_solution(1050042046324910039)
XLA Ops:
  0.7 0.8 reshape.400
  1.4 1.2 reduce-window.6
  2.7 0.1 copy.71
  2.9 0.1 copy.58
  3.1 2.5 %collective-permute-start.1 = (f32[4]{0:T(128)S(1)}, f32[4]{0:T(128)S(1)}, u32[]{:S(2)}, u32[]{:S(2)}) collective-permute-start(f32[4]{0:T(128)S(1)} %get-tuple-element.34), channel_id=1, source_target_pairs={{8,0},{16,8},{24,16},{32,24},{40,32},{48,40},{56,48},{64,56},{72,6... | collective-permute-start | bytes 56 | tf_op jit(solution)/shard_map/ppermute | solution.py:20
  5.7 0.1 copy.63
  5.9 0.1 copy.56
  6.0 0.1 bitcast_multiply_fusion.1
  6.1 0.3 fusion.13
  6.3 2.6 %collective-permute-start = (f32[4,128,64]{1,2,0:T(8,128)S(1)}, f32[4,128,64]{1,2,0:T(8,128)S(1)}, u32[]{:S(2)}, u32[]{:S(2)}) collective-permute-start(f32[4,128,64]{1,2,0:T(8,128)S(1)} %fusion.13), channel_id=1, source_target_pairs={{8,0},{16,8},{24,16},{32,24},{40,32},{48,40},{56,48},{64,56},{72,6... | collective-permute-start | bytes 393224 | tf_op jit(solution)/shard_map/ppermute | solution.py:20
  9.1 0.1 copy.64
  9.2 0.1 copy.60
  9.3 0.2 fusion.44
  9.5 0.4 convolution_bitcast_fusion.3
  9.9 0.3 fusion.45
  10.2 0.8 fusion.2
  11.0 0.3 fusion.47
  11.3 0.3 convolution_add_fusion.2
  11.6 1.0 fusion.12
  12.7 0.3 fusion.46
  13.0 1.1 convolution_bitcast_fusion.1
  14.1 2.0 %collective-permute-start.2 = (f32[4,128,64]{1,2,0:T(8,128)S(1)}, f32[4,128,64]{1,2,0:T(8,128)S(1)}, u32[]{:S(2)}, u32[]{:S(2)}) collective-permute-start(f32[4,128,64]{1,2,0:T(8,128)S(1)} %broadcast_select_fusion), channel_id=1, source_target_pairs={{8,0},{16,8},{24,16},{32,24},{40,32},{48,40},{56,48},{64,56},{72,6... | collective-permute-start | bytes 393224 | tf_op jit(solution)/shard_map/ppermute | solution.py:20
  16.2 7.7 %collective-permute-start.3 = (f32[4]{0:T(128)S(1)}, f32[4]{0:T(128)S(1)}, u32[]{:S(2)}, u32[]{:S(2)}) collective-permute-start(f32[4]{0:T(128)S(1)} %broadcast_select_fusion.6), channel_id=1, source_target_pairs={{8,0},{16,8},{24,16},{32,24},{40,32},{48,40},{56,48},{64,56},{72,6... | collective-permute-start | bytes 56 | tf_op jit(solution)/shard_map/ppermute | solution.py:20
  23.9 0.1 add_select_fusion.5
  24.0 2.4 %collective-permute-start.4 = (f32[4,128,64]{1,2,0:T(8,128)S(1)}, f32[4,128,64]{1,2,0:T(8,128)S(1)}, u32[]{:S(2)}, u32[]{:S(2)}) collective-permute-start(f32[4,128,64]{1,2,0:T(8,128)S(1)} %add_select_fusion.5), channel_id=1, source_target_pairs={{16,0},{24,8},{32,16},{40,24},{48,32},{56,40},{64,48},{72,56},{80,... | collective-permute-start | bytes 393224 | tf_op jit(solution)/shard_map/ppermute | solution.py:20
  26.4 1.9 %collective-permute-start.5 = (f32[4]{0:T(128)S(1)}, f32[4]{0:T(128)S(1)}, u32[]{:S(2)}, u32[]{:S(2)}) collective-permute-start(f32[4]{0:T(128)S(1)} %broadcast_select_fusion.5), channel_id=1, source_target_pairs={{16,0},{24,8},{32,16},{40,24},{48,32},{56,40},{64,48},{72,56},{80,... | collective-permute-start | bytes 56 | tf_op jit(solution)/shard_map/ppermute | solution.py:20
  28.3 2.6 %collective-permute-done.4 = f32[4,128,64]{1,2,0:T(8,128)S(1)} collective-permute-done((f32[4,128,64]{1,2,0:T(8,128)S(1)}, f32[4,128,64]{1,2,0:T(8,128)S(1)}, u32[]{:S(2)}, u32[]{:S(2)}) %collective-permute-start.4) | collective-permute-done | bytes 131104 | tf_op jit(solution)/shard_map/ppermute | solution.py:20
  30.9 1.9 %collective-permute-start.6 = (f32[4,128,64]{1,2,0:T(8,128)S(1)}, f32[4,128,64]{1,2,0:T(8,128)S(1)}, u32[]{:S(2)}, u32[]{:S(2)}) collective-permute-start(f32[4,128,64]{1,2,0:T(8,128)S(1)} %add_select_fusion.4), channel_id=1, source_target_pairs={{32,0},{40,8},{48,16},{56,24},{64,32},{72,40},{80,48},{88,56},{96,... | collective-permute-start | bytes 393224 | tf_op jit(solution)/shard_map/ppermute | solution.py:20
  32.9 1.9 %collective-permute-start.7 = (f32[4]{0:T(128)S(1)}, f32[4]{0:T(128)S(1)}, u32[]{:S(2)}, u32[]{:S(2)}) collective-permute-start(f32[4]{0:T(128)S(1)} %broadcast_select_fusion.4), channel_id=1, source_target_pairs={{32,0},{40,8},{48,16},{56,24},{64,32},{72,40},{80,48},{88,56},{96,... | collective-permute-start | bytes 56 | tf_op jit(solution)/shard_map/ppermute | solution.py:20
  34.8 3.0 %collective-permute-done.6 = f32[4,128,64]{1,2,0:T(8,128)S(1)} collective-permute-done((f32[4,128,64]{1,2,0:T(8,128)S(1)}, f32[4,128,64]{1,2,0:T(8,128)S(1)}, u32[]{:S(2)}, u32[]{:S(2)}) %collective-permute-start.6) | collective-permute-done | bytes 131104 | tf_op jit(solution)/shard_map/ppermute | solution.py:20
  37.8 0.1 add_select_fusion.3
  37.9 1.3 collective-permute-start.8
  39.2 1.3 collective-permute-start.9
  40.5 8.2 %collective-permute-done.8 = f32[4,128,64]{1,2,0:T(8,128)S(1)} collective-permute-done((f32[4,128,64]{1,2,0:T(8,128)S(1)}, f32[4,128,64]{1,2,0:T(8,128)S(1)}, u32[]{:S(2)}, u32[]{:S(2)}) %collective-permute-start.8) | collective-permute-done | bytes 131104 | tf_op jit(solution)/shard_map/ppermute | solution.py:20
  48.8 1.3 collective-permute-start.10
  50.2 1.3 collective-permute-start.11
  51.5 13.8 %collective-permute-done.10 = f32[4,128,64]{1,2,0:T(8,128)S(1)} collective-permute-done((f32[4,128,64]{1,2,0:T(8,128)S(1)}, f32[4,128,64]{1,2,0:T(8,128)S(1)}, u32[]{:S(2)}, u32[]{:S(2)}) %collective-permute-start.10) | collective-permute-done | bytes 131104 | tf_op jit(solution)/shard_map/ppermute | solution.py:20
  65.4 1.3 collective-permute-start.12
  66.7 14.7 %collective-permute-done.12 = f32[4,128,64]{1,2,0:T(8,128)S(1)} collective-permute-done((f32[4,128,64]{1,2,0:T(8,128)S(1)}, f32[4,128,64]{1,2,0:T(8,128)S(1)}, u32[]{:S(2)}, u32[]{:S(2)}) %collective-permute-start.12) | collective-permute-done | bytes 131104 | tf_op jit(solution)/shard_map/ppermute | solution.py:20
  81.4 0.5 fusion.14
  81.9 0.7 pad_maximum_fusion
  82.6 6.4 %all-to-all-start = ((f32[256,8,32]{0,2,1:T(8,128)}), f32[256,8,32]{0,2,1:T(8,128)S(1)}, u32[]{:S(2)}, u32[]{:S(2)}) async-start(f32[256,8,32]{0,2,1:T(8,128)} %pad_maximum_fusion), calls=%async_computation | async-start | bytes 524288 | tf_op jit(solution)/shard_map/all_to_all | solution.py:153
  89.0 0.3 fusion.11
  89.4 8.5 %all-to-all-done = f32[256,8,32]{0,2,1:T(8,128)S(1)} async-done(((f32[256,8,32]{0,2,1:T(8,128)}), f32[256,8,32]{0,2,1:T(8,128)S(1)}, u32[]{:S(2)}, u32[]{:S(2)}) %all-to-all-start) | async-done | bytes 262176 | tf_op jit(solution)/shard_map/all_to_all | solution.py:153
  97.9 1.5 fusion
  99.3 1.7 copy.67
  101.0 0.1 copy.68
  101.1 4.8 %all_to_all.30 = bf16[16,2,2,16,544]{4,3,1,0,2:T(8,128)(2,1)S(1)} all-to-all(bf16[16,2,2,16,544]{4,3,1,0,2:T(8,128)(2,1)S(1)} %copy.68), channel_id=1, replica_groups=mesh['z'=16,'y_lo'=2,'core'=2,'y_hi'=2,'x'=4] {'core'}, dimensions={2} | all-to-all | bytes 2228224 | tf_op jit(solution)/shard_map/all_to_all | solution.py:153
  105.9 0.6 reduce_sum.74
  106.6 0.9 copy.69
  107.5 6.5 %all-to-all-start.3 = ((bf16[16,2,1,16,544]{4,3,0,2,1:T(8,128)(2,1)}), bf16[16,2,1,16,544]{4,3,0,2,1:T(8,128)(2,1)S(1)}, u32[]{:S(2)}, u32[]{:S(2)}) async-start(bf16[16,2,1,16,544]{4,3,0,2,1:T(8,128)(2,1)} %copy.69), calls=%async_computation.3 | async-start | bytes 1310720 | tf_op jit(solution)/shard_map/all_to_all | solution.py:153
  114.0 0.3 convolution_add_fusion.1
  114.3 0.5 copy-done.11
  114.8 0.3 fusion.3
  115.1 0.9 copy.76
  116.0 8.4 %all-to-all-done.3 = bf16[16,2,1,16,544]{4,3,0,2,1:T(8,128)(2,1)S(1)} async-done(((bf16[16,2,1,16,544]{4,3,0,2,1:T(8,128)(2,1)}), bf16[16,2,1,16,544]{4,3,0,2,1:T(8,128)(2,1)S(1)}, u32[]{:S(2)}, u32[]{:S(2)}) %all-to-all-start.3) | async-done | bytes 557088 | tf_op jit(solution)/shard_map/all_to_all | solution.py:153
  124.4 3.5 %all-to-all-start.1 = ((bf16[256,8,128]{2,0,1:T(8,128)(2,1)}), bf16[256,8,128]{2,0,1:T(8,128)(2,1)S(1)}, u32[]{:S(2)}, u32[]{:S(2)}) async-start(bf16[256,8,128]{2,0,1:T(8,128)(2,1)} %bitcast.150), calls=%async_computation.1 | async-start | bytes 1048576 | tf_op jit(solution)/shard_map/all_to_all | solution.py:153
  127.9 0.9 reduce_sum.75
  128.8 10.6 %all-to-all-done.1 = bf16[256,8,128]{2,0,1:T(8,128)(2,1)S(1)} async-done(((bf16[256,8,128]{2,0,1:T(8,128)(2,1)}), bf16[256,8,128]{2,0,1:T(8,128)(2,1)S(1)}, u32[]{:S(2)}, u32[]{:S(2)}) %all-to-all-start.1) | async-done | bytes 524320 | tf_op jit(solution)/shard_map/all_to_all | solution.py:153
  139.4 11.1 %all-to-all-start.4 = ((bf16[16,1,1,16,544]{4,3,2,1,0:T(8,128)(2,1)}), bf16[16,1,1,16,544]{4,3,2,1,0:T(8,128)(2,1)S(1)}, u32[]{:S(2)}, u32[]{:S(2)}) async-start(bf16[16,1,1,16,544]{4,3,2,1,0:T(8,128)(2,1)} %bitcast.46), calls=%async_computation.4 | async-start | bytes 655360 | tf_op jit(solution)/shard_map/all_to_all | solution.py:153
  150.5 0.7 reduce_sum.73
  151.2 19.0 %all-to-all-done.4 = bf16[16,1,1,16,544]{4,3,2,1,0:T(8,128)(2,1)S(1)} async-done(((bf16[16,1,1,16,544]{4,3,2,1,0:T(8,128)(2,1)}), bf16[16,1,1,16,544]{4,3,2,1,0:T(8,128)(2,1)S(1)}, u32[]{:S(2)}, u32[]{:S(2)}) %all-to-all-start.4) | async-done | bytes 278560 | tf_op jit(solution)/shard_map/all_to_all | solution.py:153
  170.3 0.6 slice.28
  170.9 0.6 fusion.43
  (56 shorter events, 0.9 us)
Async XLA Ops:
  0.6 97.2 %copy-start = (bf16[256,1024]{1,0:T(8,128)(2,1)S(1)}, bf16[256,1024]{1,0:T(8,128)(2,1)}, u32[]{:S(2)}) copy-start(bf16[256,1024]{1,0:T(8,128)(2,1)} %param.11) | copy-start | bytes 1572868
  0.6 5.1 %copy-start.8 = (bf16[256,256]{1,0:T(8,128)(2,1)S(1)}, bf16[256,256]{1,0:T(8,128)(2,1)}, u32[]{:S(2)}) copy-start(bf16[256,256]{1,0:T(8,128)(2,1)} %param.13) | copy-start | bytes 393220
  0.7 5.2 %copy-start.9 = (bf16[256,256]{1,0:T(8,128)(2,1)S(1)}, bf16[256,256]{1,0:T(8,128)(2,1)}, u32[]{:S(2)}) copy-start(bf16[256,256]{1,0:T(8,128)(2,1)} %param.14) | copy-start | bytes 393220
  2.7 3.3 %copy-start.1 = (bf16[256,128]{1,0:T(8,128)(2,1)S(1)}, bf16[256,128]{1,0:T(8,128)(2,1)}, u32[]{:S(2)}) copy-start(bf16[256,128]{1,0:T(8,128)(2,1)} %param.16) | copy-start | bytes 196612
  3.1 13.1 %collective-permute-start.1 = (f32[4]{0:T(128)S(1)}, f32[4]{0:T(128)S(1)}, u32[]{:S(2)}, u32[]{:S(2)}) collective-permute-start(f32[4]{0:T(128)S(1)} %get-tuple-element.34), channel_id=1, source_target_pairs={{8,0},{16,8},{24,16},{32,24},{40,32},{48,40},{56,48},{64,56},{72,6... | collective-permute-start | bytes 56 | tf_op jit(solution)/shard_map/ppermute | solution.py:20
  5.6 3.6 %copy-start.10 = (bf16[256,256]{1,0:T(8,128)(2,1)S(1)}, bf16[256,256]{1,0:T(8,128)(2,1)}, u32[]{:S(2)}) copy-start(bf16[256,256]{1,0:T(8,128)(2,1)} %param.12) | copy-start | bytes 393220
  5.6 3.7 %copy-start.2 = (bf16[256,128]{1,0:T(8,128)(2,1)S(1)}, bf16[256,128]{1,0:T(8,128)(2,1)}, u32[]{:S(2)}) copy-start(bf16[256,128]{1,0:T(8,128)(2,1)} %param.15) | copy-start | bytes 196612
  5.8 3.6 %copy-start.4 = (f32[1,4,128,64]{2,3,1,0:T(8,128)S(1)}, f32[1,4,128,64]{2,3,1,0:T(8,128)}, u32[]{:S(2)}) copy-start(f32[1,4,128,64]{2,3,1,0:T(8,128)} %param.18) | copy-start | bytes 393220
  6.3 7.7 %collective-permute-start = (f32[4,128,64]{1,2,0:T(8,128)S(1)}, f32[4,128,64]{1,2,0:T(8,128)S(1)}, u32[]{:S(2)}, u32[]{:S(2)}) collective-permute-start(f32[4,128,64]{1,2,0:T(8,128)S(1)} %fusion.13), channel_id=1, source_target_pairs={{8,0},{16,8},{24,16},{32,24},{40,32},{48,40},{56,48},{64,56},{72,6... | collective-permute-start | bytes 393224 | tf_op jit(solution)/shard_map/ppermute | solution.py:20
  11.6 1.0 copy-start.3
  14.1 9.8 %collective-permute-start.2 = (f32[4,128,64]{1,2,0:T(8,128)S(1)}, f32[4,128,64]{1,2,0:T(8,128)S(1)}, u32[]{:S(2)}, u32[]{:S(2)}) collective-permute-start(f32[4,128,64]{1,2,0:T(8,128)S(1)} %broadcast_select_fusion), channel_id=1, source_target_pairs={{8,0},{16,8},{24,16},{32,24},{40,32},{48,40},{56,48},{64,56},{72,6... | collective-permute-start | bytes 393224 | tf_op jit(solution)/shard_map/ppermute | solution.py:20
  16.2 10.2 %collective-permute-start.3 = (f32[4]{0:T(128)S(1)}, f32[4]{0:T(128)S(1)}, u32[]{:S(2)}, u32[]{:S(2)}) collective-permute-start(f32[4]{0:T(128)S(1)} %broadcast_select_fusion.6), channel_id=1, source_target_pairs={{8,0},{16,8},{24,16},{32,24},{40,32},{48,40},{56,48},{64,56},{72,6... | collective-permute-start | bytes 56 | tf_op jit(solution)/shard_map/ppermute | solution.py:20
  24.0 6.9 %collective-permute-start.4 = (f32[4,128,64]{1,2,0:T(8,128)S(1)}, f32[4,128,64]{1,2,0:T(8,128)S(1)}, u32[]{:S(2)}, u32[]{:S(2)}) collective-permute-start(f32[4,128,64]{1,2,0:T(8,128)S(1)} %add_select_fusion.5), channel_id=1, source_target_pairs={{16,0},{24,8},{32,16},{40,24},{48,32},{56,40},{64,48},{72,56},{80,... | collective-permute-start | bytes 393224 | tf_op jit(solution)/shard_map/ppermute | solution.py:20
  26.4 6.5 %collective-permute-start.5 = (f32[4]{0:T(128)S(1)}, f32[4]{0:T(128)S(1)}, u32[]{:S(2)}, u32[]{:S(2)}) collective-permute-start(f32[4]{0:T(128)S(1)} %broadcast_select_fusion.5), channel_id=1, source_target_pairs={{16,0},{24,8},{32,16},{40,24},{48,32},{56,40},{64,48},{72,56},{80,... | collective-permute-start | bytes 56 | tf_op jit(solution)/shard_map/ppermute | solution.py:20
  30.9 6.9 %collective-permute-start.6 = (f32[4,128,64]{1,2,0:T(8,128)S(1)}, f32[4,128,64]{1,2,0:T(8,128)S(1)}, u32[]{:S(2)}, u32[]{:S(2)}) collective-permute-start(f32[4,128,64]{1,2,0:T(8,128)S(1)} %add_select_fusion.4), channel_id=1, source_target_pairs={{32,0},{40,8},{48,16},{56,24},{64,32},{72,40},{80,48},{88,56},{96,... | collective-permute-start | bytes 393224 | tf_op jit(solution)/shard_map/ppermute | solution.py:20
  32.9 6.3 %collective-permute-start.7 = (f32[4]{0:T(128)S(1)}, f32[4]{0:T(128)S(1)}, u32[]{:S(2)}, u32[]{:S(2)}) collective-permute-start(f32[4]{0:T(128)S(1)} %broadcast_select_fusion.4), channel_id=1, source_target_pairs={{32,0},{40,8},{48,16},{56,24},{64,32},{72,40},{80,48},{88,56},{96,... | collective-permute-start | bytes 56 | tf_op jit(solution)/shard_map/ppermute | solution.py:20
  37.9 10.9 %collective-permute-start.8 = (f32[4,128,64]{1,2,0:T(8,128)S(1)}, f32[4,128,64]{1,2,0:T(8,128)S(1)}, u32[]{:S(2)}, u32[]{:S(2)}) collective-permute-start(f32[4,128,64]{1,2,0:T(8,128)S(1)} %add_select_fusion.3), channel_id=1, source_target_pairs={{64,0},{72,8},{80,16},{88,24},{96,32},{104,40},{112,48},{120,56},{... | collective-permute-start | bytes 393224 | tf_op jit(solution)/shard_map/ppermute | solution.py:20
  39.2 10.9 %collective-permute-start.9 = (f32[4]{0:T(128)S(1)}, f32[4]{0:T(128)S(1)}, u32[]{:S(2)}, u32[]{:S(2)}) collective-permute-start(f32[4]{0:T(128)S(1)} %broadcast_select_fusion.3), channel_id=1, source_target_pairs={{64,0},{72,8},{80,16},{88,24},{96,32},{104,40},{112,48},{120,56},{... | collective-permute-start | bytes 56 | tf_op jit(solution)/shard_map/ppermute | solution.py:20
  48.8 16.5 %collective-permute-start.10 = (f32[4,128,64]{1,2,0:T(8,128)S(1)}, f32[4,128,64]{1,2,0:T(8,128)S(1)}, u32[]{:S(2)}, u32[]{:S(2)}) collective-permute-start(f32[4,128,64]{1,2,0:T(8,128)S(1)} %add_select_fusion.2), channel_id=1, source_target_pairs={{128,0},{136,8},{144,16},{152,24},{160,32},{168,40},{176,48},{184,... | collective-permute-start | bytes 393224 | tf_op jit(solution)/shard_map/ppermute | solution.py:20
  50.2 16.5 %collective-permute-start.11 = (f32[4]{0:T(128)S(1)}, f32[4]{0:T(128)S(1)}, u32[]{:S(2)}, u32[]{:S(2)}) collective-permute-start(f32[4]{0:T(128)S(1)} %broadcast_select_fusion.2), channel_id=1, source_target_pairs={{128,0},{136,8},{144,16},{152,24},{160,32},{168,40},{176,48},{184,... | collective-permute-start | bytes 56 | tf_op jit(solution)/shard_map/ppermute | solution.py:20
  65.4 16.0 %collective-permute-start.12 = (f32[4,128,64]{1,2,0:T(8,128)S(1)}, f32[4,128,64]{1,2,0:T(8,128)S(1)}, u32[]{:S(2)}, u32[]{:S(2)}) collective-permute-start(f32[4,128,64]{1,2,0:T(8,128)S(1)} %add_select_fusion.1), channel_id=1, source_target_pairs={{256,0},{264,8},{272,16},{280,24},{288,32},{296,40},{304,48},{312,... | collective-permute-start | bytes 393224 | tf_op jit(solution)/shard_map/ppermute | solution.py:20
  82.6 15.2 %all-to-all-start = ((f32[256,8,32]{0,2,1:T(8,128)}), f32[256,8,32]{0,2,1:T(8,128)S(1)}, u32[]{:S(2)}, u32[]{:S(2)}) async-start(f32[256,8,32]{0,2,1:T(8,128)} %pad_maximum_fusion), calls=%async_computation | async-start | bytes 524288 | tf_op jit(solution)/shard_map/all_to_all | solution.py:153
  89.4 8.5 %copy-start.6 = (bf16[1,256,4,64]{1,3,2,0:T(8,128)(2,1)}, bf16[1,256,4,64]{1,3,2,0:T(8,128)(2,1)S(1)}, u32[]{:S(2)}) copy-start(bf16[1,256,4,64]{1,3,2,0:T(8,128)(2,1)S(1)} %fusion.11) | copy-start | bytes 393220
  106.5 7.4 %copy-start.5 = (bf16[1024,256]{1,0:T(8,128)(2,1)S(1)}, bf16[1024,256]{1,0:T(8,128)(2,1)}, u32[]{:S(2)}) copy-start(bf16[1024,256]{1,0:T(8,128)(2,1)} %param.20) | copy-start | bytes 1572868
  106.5 7.4 %copy-start.7 = (bf16[1,256,4,64]{1,3,2,0:T(8,128)(2,1)S(1)}, bf16[1,256,4,64]{1,3,2,0:T(8,128)(2,1)}, u32[]{:S(2)}) copy-start(bf16[1,256,4,64]{1,3,2,0:T(8,128)(2,1)} %copy-done.6) | copy-start | bytes 393220
  107.5 17.0 %all-to-all-start.3 = ((bf16[16,2,1,16,544]{4,3,0,2,1:T(8,128)(2,1)}), bf16[16,2,1,16,544]{4,3,0,2,1:T(8,128)(2,1)S(1)}, u32[]{:S(2)}, u32[]{:S(2)}) async-start(bf16[16,2,1,16,544]{4,3,0,2,1:T(8,128)(2,1)} %copy.69), calls=%async_computation.3 | async-start | bytes 1310720 | tf_op jit(solution)/shard_map/all_to_all | solution.py:153
  114.0 0.8 copy-start.11
  124.4 15.0 %all-to-all-start.1 = ((bf16[256,8,128]{2,0,1:T(8,128)(2,1)}), bf16[256,8,128]{2,0,1:T(8,128)(2,1)S(1)}, u32[]{:S(2)}, u32[]{:S(2)}) async-start(bf16[256,8,128]{2,0,1:T(8,128)(2,1)} %bitcast.150), calls=%async_computation.1 | async-start | bytes 1048576 | tf_op jit(solution)/shard_map/all_to_all | solution.py:153
  139.4 30.8 %all-to-all-start.4 = ((bf16[16,1,1,16,544]{4,3,2,1,0:T(8,128)(2,1)}), bf16[16,1,1,16,544]{4,3,2,1,0:T(8,128)(2,1)S(1)}, u32[]{:S(2)}, u32[]{:S(2)}) async-start(bf16[16,1,1,16,544]{4,3,2,1,0:T(8,128)(2,1)} %bitcast.46), calls=%async_computation.4 | async-start | bytes 655360 | tf_op jit(solution)/shard_map/all_to_all | solution.py:153

commit v3 on v2

--- a/solution.py
+++ b/solution.py
@@ -11,31 +11,54 @@
 highest = lax.Precision.HIGHEST
 
 
-def suffix_scan(part, axis):
-    count = lax.axis_size(axis)
-    place = lax.axis_index(axis)
-
-    def shifted(tree, step):
-        pairs = [(source, source - step) for source in range(step, count)]
-        return jax.tree.map(lambda a: lax.ppermute(a, axis, pairs), tree)
-
-    def combine(near, far):
-        return (near[0] * far[0], near[1] + near[0][:, None, None] * far[1])
-
-    state = shifted(part, 1)
-    valid = place + 1 < count
-    state = (jnp.where(valid, state[0], 1.0), jnp.where(valid, state[1], 0.0))
-    step = 1
+def join(near, far):
+    return (near[0] * far[0], near[1] + near[0][..., None, None] * far[1])
+
+
+def pick(flag, first, second):
+    return jax.tree.map(lambda a, b: jnp.where(flag, a, b), first, second)
+
+
+def swap(tree, axis):
+    return jax.tree.map(lambda a: lax.ppermute(a, axis, [(0, 1), (1, 0)]), tree)
+
+
+def shift(tree, axis, step):
+    pairs = [(source, source - step) for source in range(step, lax.axis_size(axis))]
+    return jax.tree.map(lambda a: lax.ppermute(a, axis, pairs), tree)
+
+
+def suffix_scan(part):
+    z_axis, pair_axis, core_axis = CTX
+    core = lax.axis_index(core_axis)
+    pair = lax.axis_index(pair_axis)
+    plane = pair * 2 + core
+    identity = jax.tree.map(lambda a: jnp.zeros_like(a) + jnp.asarray(1.0 if a.ndim == 1 else 0.0, a.dtype), part)
+    other = swap(part, core_axis)
+    pair_total = pick(core == 0, join(part, other), join(other, part))
+    other_pair = swap(pair_total, pair_axis)
+    total = pick(pair == 0, join(pair_total, other_pair), join(other_pair, pair_total))
+    within = join(pick(core == 0, other, identity), pick(pair == 0, other_pair, identity))
+    head = (
+        lax.dynamic_index_in_dim(total[0], plane, 0, False),
+        lax.dynamic_index_in_dim(total[1], plane, 0, False),
+    )
+    one = (jnp.ones_like(head[0]), jnp.zeros_like(head[1]))
+    z = lax.axis_index(z_axis)
+    count = lax.axis_size(z_axis)
+    near = pick(z + 1 < count, shift(head, z_axis, 1), one)
+    far = pick(z + 2 < count, shift(head, z_axis, 2), one)
+    later = join(near, far)
+    step = 2
     while step < count:
-        far = shifted(state, step)
-        joined = combine(state, far)
-        inside = place + step < count
-        state = (
-            jnp.where(inside, joined[0], state[0]),
-            jnp.where(inside, joined[1], state[1]),
-        )
+        later = pick(z + step < count, join(later, shift(later, z_axis, step)), later)
         step *= 2
-    return state
+    mine = later[1]
+    theirs = swap(mine, core_axis)
+    two = jnp.where(core == 0, jnp.stack([mine, theirs]), jnp.stack([theirs, mine]))
+    two_other = swap(two, pair_axis)
+    four = jnp.where(pair == 0, jnp.concatenate([two, two_other]), jnp.concatenate([two_other, two]))
+    return within[1] + within[0][:, None, None] * four
 
 
 def ssd_partials(ssm_input, gate_input, grad_out, shared_b, shared_c, log_decay, entry, block_len):
@@ -174,7 +197,7 @@
     )
     block_sum = partials[9]
     block_log = partials[10]
-    _, incoming = suffix_scan((jnp.exp(block_log), block_sum), CTX)
+    incoming = suffix_scan((jnp.exp(block_log), block_sum))
     grad_z, grad_x, grad_bc_part = finish_block(partials, incoming)
     grad_bc = summed_over(grad_bc_part, HEAD, 1).astype(jnp.bfloat16)
     input_part = (

time: 173 us -> 171 us (0.988)
  the two profiles are of different devices: /device:TPU:32 before, /device:TPU:64 now
where the time goes in v3:
time: 171 us; the launch traced here: 170 us
  waiting for transfers between devices  75.4 us (44%)
  starting transfers between devices  61 us (36%)
  local copies, waits for them, and re-layouts  8.81 us (5%)
  matrix products  8.69 us (5%)
  other arithmetic  7.26 us (4%)
  blocking collectives  4.79 us (3%)
  between operations  3.63 us (2%)
    all_to_all x4, waiting for transfers between devices, summed_over(): gathered = lax.all_to_all(part, axis, split, split, tiled=True)  46.4 us
    ppermute x9, waiting for transfers between devices, shift(): return jax.tree.map(lambda a: lax.ppermute(a, axis, pairs), tree)  25.3 us
    all_to_all x4, starting transfers between devices, summed_over(): gathered = lax.all_to_all(part, axis, split, split, tiled=True)  24.8 us
    ppermute x9, starting transfers between devices, shift(): return jax.tree.map(lambda a: lax.ppermute(a, axis, pairs), tree)  20.2 us
    ppermute x6, starting transfers between devices, swap(): return jax.tree.map(lambda a: lax.ppermute(a, axis, [(0, 1), (1, 0)]), tree)  16 us
    all_to_all x1, blocking collectives, summed_over(): gathered = lax.all_to_all(part, axis, split, split, tiled=True)  4.79 us
    ppermute x6, waiting for transfers between devices, swap(): return jax.tree.map(lambda a: lax.ppermute(a, axis, [(0, 1), (1, 0)]), tree)  3.65 us
  transfers between devices with their start and end apart: 19, of which 12 were waited for; matrix products, arithmetic and copies ran while one was open for 8% of the time, Pallas kernels for 0%

profile of v3, /device:TPU:64, one launch (start us, length us, event | category | flops | bytes accessed | tf_op | source)
XLA Modules:
  0.0 169.6 jit_solution(14624648777124041)
XLA Ops:
  0.7 0.8 reshape.401
  1.5 1.2 reduce-window.6
  3.1 1.9 %collective-permute-start.1 = (f32[4]{0:T(128)S(1)}, f32[4]{0:T(128)S(1)}, u32[]{:S(2)}, u32[]{:S(2)}) collective-permute-start(f32[4]{0:T(128)S(1)} %fusion.43), channel_id=1, source_target_pairs={{0,8},{8,0},{1,9},{9,1},{2,10},{10,2},{3,11},{11,3},{4,12},{12,4},... | collective-permute-start | bytes 56 | tf_op jit(solution)/shard_map/ppermute | solution.py:23
  5.7 0.2 fusion.45
  5.9 0.3 fusion.46
  6.3 0.3 fusion.13
  6.6 2.4 %collective-permute-start = (f32[4,128,64]{1,2,0:T(8,128)S(1)}, f32[4,128,64]{1,2,0:T(8,128)S(1)}, u32[]{:S(2)}, u32[]{:S(2)}) collective-permute-start(f32[4,128,64]{1,2,0:T(8,128)S(1)} %fusion.13), channel_id=1, source_target_pairs={{0,8},{8,0},{1,9},{9,1},{2,10},{10,2},{3,11},{11,3},{4,12},{12,4},... | collective-permute-start | bytes 393224 | tf_op jit(solution)/shard_map/ppermute | solution.py:23
  9.0 1.0 fusion.12
  10.2 3.5 %collective-permute-start.2 = (f32[4,128,64]{1,2,0:T(8,128)S(1)}, f32[4,128,64]{1,2,0:T(8,128)S(1)}, u32[]{:S(2)}, u32[]{:S(2)}) collective-permute-start(f32[4,128,64]{1,2,0:T(8,128)S(1)} %add_select_fusion), channel_id=1, source_target_pairs={{0,16},{16,0},{1,17},{17,1},{2,18},{18,2},{3,19},{19,3},{4,20},{20... | collective-permute-start | bytes 393224 | tf_op jit(solution)/shard_map/ppermute | solution.py:23
  13.7 0.3 fusion.47
  14.0 2.4 %collective-permute-start.3 = (f32[4]{0:T(128)S(1)}, f32[4]{0:T(128)S(1)}, u32[]{:S(2)}, u32[]{:S(2)}) collective-permute-start(f32[4]{0:T(128)S(1)} %get-tuple-element.43), channel_id=1, source_target_pairs={{0,16},{16,0},{1,17},{17,1},{2,18},{18,2},{3,19},{19,3},{4,20},{20... | collective-permute-start | bytes 56 | tf_op jit(solution)/shard_map/ppermute | solution.py:23
  16.4 0.6 dynamic-slice.2
  17.0 2.5 %collective-permute-done.3 = f32[4]{0:T(128)S(1)} collective-permute-done((f32[4]{0:T(128)S(1)}, f32[4]{0:T(128)S(1)}, u32[]{:S(2)}, u32[]{:S(2)}) %collective-permute-start.3) | collective-permute-done | bytes 48 | tf_op jit(solution)/shard_map/ppermute | solution.py:23
  19.5 0.6 dynamic-slice.3
  20.1 1.3 select_bitcast_fusion
  21.4 5.3 %collective-permute-start.6 = (f32[128,64]{0,1:T(8,128)S(1)}, f32[128,64]{0,1:T(8,128)S(1)}, u32[]{:S(2)}, u32[]{:S(2)}) collective-permute-start(f32[128,64]{0,1:T(8,128)S(1)} %select_bitcast_fusion), channel_id=1, source_target_pairs={{64,0},{96,32},{128,64},{160,96},{192,128},{224,160},{256,192},{28... | collective-permute-start | bytes 98312 | tf_op jit(solution)/shard_map/ppermute | solution.py:28
  26.8 1.9 %collective-permute-start.4 = (f32[128,64]{0,1:T(8,128)S(1)}, f32[128,64]{0,1:T(8,128)S(1)}, u32[]{:S(2)}, u32[]{:S(2)}) collective-permute-start(f32[128,64]{0,1:T(8,128)S(1)} %select_bitcast_fusion), channel_id=1, source_target_pairs={{32,0},{64,32},{96,64},{128,96},{160,128},{192,160},{224,192},{256... | collective-permute-start | bytes 98312 | tf_op jit(solution)/shard_map/ppermute | solution.py:28
  28.7 1.2 fusion.39
  29.9 0.6 dynamic_slice.22
  30.4 1.9 %collective-permute-start.5 = (f32[]{:T(128)}, f32[]{:T(128)}, u32[]{:S(2)}, u32[]{:S(2)}) collective-permute-start(f32[]{:T(128)} %bitcast.34), channel_id=1, source_target_pairs={{32,0},{64,32},{96,64},{128,96},{160,128},{192,160},{224,192},{256... | collective-permute-start | bytes 20 | tf_op jit(solution)/shard_map/ppermute | solution.py:28
  32.4 3.8 %collective-permute-done.5 = f32[]{:T(128)} collective-permute-done((f32[]{:T(128)}, f32[]{:T(128)}, u32[]{:S(2)}, u32[]{:S(2)}) %collective-permute-start.5) | collective-permute-done | bytes 36 | tf_op jit(solution)/shard_map/ppermute | solution.py:28
  36.7 1.9 %collective-permute-start.8 = (f32[128,64]{0,1:T(8,128)S(1)}, f32[128,64]{0,1:T(8,128)S(1)}, u32[]{:S(2)}, u32[]{:S(2)}) collective-permute-start(f32[128,64]{0,1:T(8,128)S(1)} %multiply_add_fusion), channel_id=1, source_target_pairs={{64,0},{96,32},{128,64},{160,96},{192,128},{224,160},{256,192},{28... | collective-permute-start | bytes 98312 | tf_op jit(solution)/shard_map/ppermute | solution.py:28
  38.7 0.8 fusion.2
  39.5 1.9 %collective-permute-start.7 = (f32[]{:T(128)}, f32[]{:T(128)}, u32[]{:S(2)}, u32[]{:S(2)}) collective-permute-start(f32[]{:T(128)} %bitcast.34), channel_id=1, source_target_pairs={{64,0},{96,32},{128,64},{160,96},{192,128},{224,160},{256,192},{28... | collective-permute-start | bytes 20 | tf_op jit(solution)/shard_map/ppermute | solution.py:28
  41.4 5.9 %collective-permute-done.7 = f32[]{:T(128)} collective-permute-done((f32[]{:T(128)}, f32[]{:T(128)}, u32[]{:S(2)}, u32[]{:S(2)}) %collective-permute-start.7) | collective-permute-done | bytes 36 | tf_op jit(solution)/shard_map/ppermute | solution.py:28
  48.0 1.3 collective-permute-start.10
  49.3 0.4 convolution_bitcast_fusion.3
  49.7 3.3 %collective-permute-start.9 = (f32[]{:T(128)}, f32[]{:T(128)}, u32[]{:S(2)}, u32[]{:S(2)}) collective-permute-start(f32[]{:T(128)} %mul.303), channel_id=1, source_target_pairs={{64,0},{96,32},{128,64},{160,96},{192,128},{224,160},{256,192},{28... | collective-permute-start | bytes 20 | tf_op jit(solution)/shard_map/ppermute | solution.py:28
  53.0 4.5 %collective-permute-done.9 = f32[]{:T(128)} collective-permute-done((f32[]{:T(128)}, f32[]{:T(128)}, u32[]{:S(2)}, u32[]{:S(2)}) %collective-permute-start.9) | collective-permute-done | bytes 36 | tf_op jit(solution)/shard_map/ppermute | solution.py:28
  58.1 1.3 collective-permute-start.12
  59.4 0.3 convolution_add_fusion.2
  59.7 1.3 collective-permute-start.11
  61.0 8.8 %collective-permute-done.11 = f32[]{:T(128)} collective-permute-done((f32[]{:T(128)}, f32[]{:T(128)}, u32[]{:S(2)}, u32[]{:S(2)}) %collective-permute-start.11) | collective-permute-done | bytes 36 | tf_op jit(solution)/shard_map/ppermute | solution.py:28
  70.4 2.3 %collective-permute-done.12 = f32[128,64]{0,1:T(8,128)S(1)} collective-permute-done((f32[128,64]{0,1:T(8,128)S(1)}, f32[128,64]{0,1:T(8,128)S(1)}, u32[]{:S(2)}, u32[]{:S(2)}) %collective-permute-start.12) | collective-permute-done | bytes 32800 | tf_op jit(solution)/shard_map/ppermute | solution.py:28
  72.7 1.9 %collective-permute-start.13 = (f32[128,64]{0,1:T(8,128)S(1)}, f32[128,64]{0,1:T(8,128)S(1)}, u32[]{:S(2)}, u32[]{:S(2)}) collective-permute-start(f32[128,64]{0,1:T(8,128)S(1)} %add_select_fusion.1), channel_id=1, source_target_pairs={{0,8},{8,0},{1,9},{9,1},{2,10},{10,2},{3,11},{11,3},{4,12},{12,4},... | collective-permute-start | bytes 98312 | tf_op jit(solution)/shard_map/ppermute | solution.py:23
  74.6 0.3 fusion.48
  74.9 0.9 collective-permute-done.13
  75.8 3.9 %collective-permute-start.14 = (f32[2,128,64]{1,2,0:T(8,128)S(1)}, f32[2,128,64]{1,2,0:T(8,128)S(1)}, u32[]{:S(2)}, u32[]{:S(2)}) collective-permute-start(f32[2,128,64]{1,2,0:T(8,128)S(1)} %maximum_select_fusion.1), channel_id=1, source_target_pairs={{0,16},{16,0},{1,17},{17,1},{2,18},{18,2},{3,19},{19,3},{4,20},{20... | collective-permute-start | bytes 196616 | tf_op jit(solution)/shard_map/ppermute | solution.py:23
  79.7 2.0 %convolution_bitcast_fusion.1 = f32[1,256,4,64]{1,3,2,0:T(8,128)S(1)} fusion(f32[256,4,64]{0,2,1:T(8,128)S(1)} %bitcast.182, f32[256,256]{1,0:T(8,128)} %copy-done.8, f32[4,256]{1,0:T(4,128)S(1)} %bitcast_add_fusion.1, pred[256,256]{1,0:T(8,128)(4,1)S(1)} %copy-done.16), kind=kOutput, calls=%fused_computation.11 | convolution fusion | flops 202375168 | bytes 856064 | tf_op jit(solution)/shard_map/hkst,kshp->kthp/dot_general | solution.py:107
  81.9 0.2 collective-permute-done.14
  82.2 0.4 fusion.14
  82.6 0.7 pad_maximum_fusion
  83.4 5.8 %all-to-all-start = ((f32[256,8,32]{0,2,1:T(8,128)}), f32[256,8,32]{0,2,1:T(8,128)S(1)}, u32[]{:S(2)}, u32[]{:S(2)}) async-start(f32[256,8,32]{0,2,1:T(8,128)} %pad_maximum_fusion), calls=%async_computation | async-start | bytes 524288 | tf_op jit(solution)/shard_map/all_to_all | solution.py:176
  89.2 0.3 fusion.11
  89.5 8.5 %all-to-all-done = f32[256,8,32]{0,2,1:T(8,128)S(1)} async-done(((f32[256,8,32]{0,2,1:T(8,128)}), f32[256,8,32]{0,2,1:T(8,128)S(1)}, u32[]{:S(2)}, u32[]{:S(2)}) %all-to-all-start) | async-done | bytes 262176 | tf_op jit(solution)/shard_map/all_to_all | solution.py:176
  98.0 1.5 fusion
  99.5 1.7 copy.67
  101.3 4.8 %all_to_all.30 = bf16[16,2,2,16,544]{4,3,1,0,2:T(8,128)(2,1)S(1)} all-to-all(bf16[16,2,2,16,544]{4,3,1,0,2:T(8,128)(2,1)S(1)} %copy.68), channel_id=1, replica_groups=mesh['z'=16,'y_lo'=2,'core'=2,'y_hi'=2,'x'=4] {'core'}, dimensions={2} | all-to-all | bytes 2228224 | tf_op jit(solution)/shard_map/all_to_all | solution.py:176
  106.1 0.6 reduce_sum.74
  106.7 0.9 copy.69
  107.6 3.5 %all-to-all-start.3 = ((bf16[16,2,1,16,544]{4,3,0,2,1:T(8,128)(2,1)}), bf16[16,2,1,16,544]{4,3,0,2,1:T(8,128)(2,1)S(1)}, u32[]{:S(2)}, u32[]{:S(2)}) async-start(bf16[16,2,1,16,544]{4,3,0,2,1:T(8,128)(2,1)} %copy.69), calls=%async_computation.3 | async-start | bytes 1310720 | tf_op jit(solution)/shard_map/all_to_all | solution.py:176
  111.2 0.4 convolution_add_fusion.1
  111.6 0.5 copy-done.14
  112.0 0.3 fusion.3
  112.3 0.9 copy.76
  113.3 7.8 %all-to-all-done.3 = bf16[16,2,1,16,544]{4,3,0,2,1:T(8,128)(2,1)S(1)} async-done(((bf16[16,2,1,16,544]{4,3,0,2,1:T(8,128)(2,1)}), bf16[16,2,1,16,544]{4,3,0,2,1:T(8,128)(2,1)S(1)}, u32[]{:S(2)}, u32[]{:S(2)}) %all-to-all-start.3) | async-done | bytes 557088 | tf_op jit(solution)/shard_map/all_to_all | solution.py:176
  121.1 3.5 %all-to-all-start.1 = ((bf16[256,8,128]{2,0,1:T(8,128)(2,1)}), bf16[256,8,128]{2,0,1:T(8,128)(2,1)S(1)}, u32[]{:S(2)}, u32[]{:S(2)}) async-start(bf16[256,8,128]{2,0,1:T(8,128)(2,1)} %bitcast.161), calls=%async_computation.1 | async-start | bytes 1048576 | tf_op jit(solution)/shard_map/all_to_all | solution.py:176
  124.6 0.9 reduce_sum.75
  125.5 10.3 %all-to-all-done.1 = bf16[256,8,128]{2,0,1:T(8,128)(2,1)S(1)} async-done(((bf16[256,8,128]{2,0,1:T(8,128)(2,1)}), bf16[256,8,128]{2,0,1:T(8,128)(2,1)S(1)}, u32[]{:S(2)}, u32[]{:S(2)}) %all-to-all-start.1) | async-done | bytes 524320 | tf_op jit(solution)/shard_map/all_to_all | solution.py:176
  135.9 12.0 %all-to-all-start.4 = ((bf16[16,1,1,16,544]{4,3,2,1,0:T(8,128)(2,1)}), bf16[16,1,1,16,544]{4,3,2,1,0:T(8,128)(2,1)S(1)}, u32[]{:S(2)}, u32[]{:S(2)}) async-start(bf16[16,1,1,16,544]{4,3,2,1,0:T(8,128)(2,1)} %bitcast.50), calls=%async_computation.4 | async-start | bytes 655360 | tf_op jit(solution)/shard_map/all_to_all | solution.py:176
  147.8 0.7 reduce_sum.73
  148.6 19.8 %all-to-all-done.4 = bf16[16,1,1,16,544]{4,3,2,1,0:T(8,128)(2,1)S(1)} async-done(((bf16[16,1,1,16,544]{4,3,2,1,0:T(8,128)(2,1)}), bf16[16,1,1,16,544]{4,3,2,1,0:T(8,128)(2,1)S(1)}, u32[]{:S(2)}, u32[]{:S(2)}) %all-to-all-start.4) | async-done | bytes 278560 | tf_op jit(solution)/shard_map/all_to_all | solution.py:176
  168.4 0.6 slice.28
  169.0 0.6 fusion.44
  (75 shorter events, 1.7 us)
Async XLA Ops:
  0.6 97.3 %copy-start = (bf16[256,1024]{1,0:T(8,128)(2,1)S(1)}, bf16[256,1024]{1,0:T(8,128)(2,1)}, u32[]{:S(2)}) copy-start(bf16[256,1024]{1,0:T(8,128)(2,1)} %param.11) | copy-start | bytes 1572868
  0.6 4.7 %copy-start.9 = (bf16[256,256]{1,0:T(8,128)(2,1)S(1)}, bf16[256,256]{1,0:T(8,128)(2,1)}, u32[]{:S(2)}) copy-start(bf16[256,256]{1,0:T(8,128)(2,1)} %param.12) | copy-start | bytes 393220
  0.7 4.8 %copy-start.10 = (bf16[256,256]{1,0:T(8,128)(2,1)S(1)}, bf16[256,256]{1,0:T(8,128)(2,1)}, u32[]{:S(2)}) copy-start(bf16[256,256]{1,0:T(8,128)(2,1)} %param.13) | copy-start | bytes 393220
  0.7 4.9 %copy-start.11 = (bf16[256,256]{1,0:T(8,128)(2,1)S(1)}, bf16[256,256]{1,0:T(8,128)(2,1)}, u32[]{:S(2)}) copy-start(bf16[256,256]{1,0:T(8,128)(2,1)} %param.14) | copy-start | bytes 393220
  0.7 5.0 %copy-start.1 = (bf16[256,128]{1,0:T(8,128)(2,1)S(1)}, bf16[256,128]{1,0:T(8,128)(2,1)}, u32[]{:S(2)}) copy-start(bf16[256,128]{1,0:T(8,128)(2,1)} %param.16) | copy-start | bytes 196612
  0.7 5.0 %copy-start.2 = (bf16[256,128]{1,0:T(8,128)(2,1)S(1)}, bf16[256,128]{1,0:T(8,128)(2,1)}, u32[]{:S(2)}) copy-start(bf16[256,128]{1,0:T(8,128)(2,1)} %param.15) | copy-start | bytes 196612
  2.9 3.0 %copy-start.4 = (f32[1,4,128,64]{2,3,1,0:T(8,128)S(1)}, f32[1,4,128,64]{2,3,1,0:T(8,128)}, u32[]{:S(2)}) copy-start(f32[1,4,128,64]{2,3,1,0:T(8,128)} %param.18) | copy-start | bytes 393220
  3.1 3.2 %collective-permute-start.1 = (f32[4]{0:T(128)S(1)}, f32[4]{0:T(128)S(1)}, u32[]{:S(2)}, u32[]{:S(2)}) collective-permute-start(f32[4]{0:T(128)S(1)} %fusion.43), channel_id=1, source_target_pairs={{0,8},{8,0},{1,9},{9,1},{2,10},{10,2},{3,11},{11,3},{4,12},{12,4},... | collective-permute-start | bytes 56 | tf_op jit(solution)/shard_map/ppermute | solution.py:23
  5.1 33.6 %copy-start.15 = (pred[256,256]{1,0:T(8,128)(4,1)}, pred[256,256]{1,0:T(8,128)(4,1)S(1)}, u32[]{:S(2)}) copy-start(pred[256,256]{1,0:T(8,128)(4,1)S(1)} %iota_compare_fusion) | copy-start | bytes 196612
  5.9 7.8 %copy-start.8 = (f32[256,256]{1,0:T(8,128)}, f32[256,256]{1,0:T(8,128)S(1)}, u32[]{:S(2)}) copy-start(f32[256,256]{1,0:T(8,128)S(1)} %fusion.45) | copy-start | bytes 786436
  6.3 13.8 %copy-start.18 = (f32[4]{0:T(128)}, f32[4]{0:T(128)S(1)}, u32[]{:S(2)}) copy-start(f32[4]{0:T(128)S(1)} %get-tuple-element.43) | copy-start | bytes 52
  6.6 3.4 %collective-permute-start = (f32[4,128,64]{1,2,0:T(8,128)S(1)}, f32[4,128,64]{1,2,0:T(8,128)S(1)}, u32[]{:S(2)}, u32[]{:S(2)}) collective-permute-start(f32[4,128,64]{1,2,0:T(8,128)S(1)} %fusion.13), channel_id=1, source_target_pairs={{0,8},{8,0},{1,9},{9,1},{2,10},{10,2},{3,11},{11,3},{4,12},{12,4},... | collective-permute-start | bytes 393224 | tf_op jit(solution)/shard_map/ppermute | solution.py:23
  9.0 4.6 %copy-start.3 = (bf16[1024,256]{1,0:T(8,128)(2,1)S(1)}, bf16[1024,256]{1,0:T(8,128)(2,1)}, u32[]{:S(2)}) copy-start(bf16[1024,256]{1,0:T(8,128)(2,1)} %param.19) | copy-start | bytes 1572868
  10.0 29.5 %copy-start.12 = (bf16[1,256,4,64]{1,3,2,0:T(8,128)(2,1)}, bf16[1,256,4,64]{1,3,2,0:T(8,128)(2,1)S(1)}, u32[]{:S(2)}) copy-start(bf16[1,256,4,64]{1,3,2,0:T(8,128)(2,1)S(1)} %fusion.12) | copy-start | bytes 393220
  10.2 9.9 %collective-permute-start.2 = (f32[4,128,64]{1,2,0:T(8,128)S(1)}, f32[4,128,64]{1,2,0:T(8,128)S(1)}, u32[]{:S(2)}, u32[]{:S(2)}) collective-permute-start(f32[4,128,64]{1,2,0:T(8,128)S(1)} %add_select_fusion), channel_id=1, source_target_pairs={{0,16},{16,0},{1,17},{17,1},{2,18},{18,2},{3,19},{19,3},{4,20},{20... | collective-permute-start | bytes 393224 | tf_op jit(solution)/shard_map/ppermute | solution.py:23
  14.0 5.5 %collective-permute-start.3 = (f32[4]{0:T(128)S(1)}, f32[4]{0:T(128)S(1)}, u32[]{:S(2)}, u32[]{:S(2)}) collective-permute-start(f32[4]{0:T(128)S(1)} %get-tuple-element.43), channel_id=1, source_target_pairs={{0,16},{16,0},{1,17},{17,1},{2,18},{18,2},{3,19},{19,3},{4,20},{20... | collective-permute-start | bytes 56 | tf_op jit(solution)/shard_map/ppermute | solution.py:23
  21.4 15.3 %collective-permute-start.6 = (f32[128,64]{0,1:T(8,128)S(1)}, f32[128,64]{0,1:T(8,128)S(1)}, u32[]{:S(2)}, u32[]{:S(2)}) collective-permute-start(f32[128,64]{0,1:T(8,128)S(1)} %select_bitcast_fusion), channel_id=1, source_target_pairs={{64,0},{96,32},{128,64},{160,96},{192,128},{224,160},{256,192},{28... | collective-permute-start | bytes 98312 | tf_op jit(solution)/shard_map/ppermute | solution.py:28
  26.8 9.9 %collective-permute-start.4 = (f32[128,64]{0,1:T(8,128)S(1)}, f32[128,64]{0,1:T(8,128)S(1)}, u32[]{:S(2)}, u32[]{:S(2)}) collective-permute-start(f32[128,64]{0,1:T(8,128)S(1)} %select_bitcast_fusion), channel_id=1, source_target_pairs={{32,0},{64,32},{96,64},{128,96},{160,128},{192,160},{224,192},{256... | collective-permute-start | bytes 98312 | tf_op jit(solution)/shard_map/ppermute | solution.py:28
  30.4 5.7 %collective-permute-start.5 = (f32[]{:T(128)}, f32[]{:T(128)}, u32[]{:S(2)}, u32[]{:S(2)}) collective-permute-start(f32[]{:T(128)} %bitcast.34), channel_id=1, source_target_pairs={{32,0},{64,32},{96,64},{128,96},{160,128},{192,160},{224,192},{256... | collective-permute-start | bytes 20 | tf_op jit(solution)/shard_map/ppermute | solution.py:28
  36.7 11.2 %collective-permute-start.8 = (f32[128,64]{0,1:T(8,128)S(1)}, f32[128,64]{0,1:T(8,128)S(1)}, u32[]{:S(2)}, u32[]{:S(2)}) collective-permute-start(f32[128,64]{0,1:T(8,128)S(1)} %multiply_add_fusion), channel_id=1, source_target_pairs={{64,0},{96,32},{128,64},{160,96},{192,128},{224,160},{256,192},{28... | collective-permute-start | bytes 98312 | tf_op jit(solution)/shard_map/ppermute | solution.py:28
  39.5 7.9 %collective-permute-start.7 = (f32[]{:T(128)}, f32[]{:T(128)}, u32[]{:S(2)}, u32[]{:S(2)}) collective-permute-start(f32[]{:T(128)} %bitcast.34), channel_id=1, source_target_pairs={{64,0},{96,32},{128,64},{160,96},{192,128},{224,160},{256,192},{28... | collective-permute-start | bytes 20 | tf_op jit(solution)/shard_map/ppermute | solution.py:28
  48.0 10.1 %collective-permute-start.10 = (f32[128,64]{0,1:T(8,128)S(1)}, f32[128,64]{0,1:T(8,128)S(1)}, u32[]{:S(2)}, u32[]{:S(2)}) collective-permute-start(f32[128,64]{0,1:T(8,128)S(1)} %add_select_fusion.3), channel_id=1, source_target_pairs={{128,0},{160,32},{192,64},{224,96},{256,128},{288,160},{320,192},{... | collective-permute-start | bytes 98312 | tf_op jit(solution)/shard_map/ppermute | solution.py:28
  49.7 30.1 %copy-start.16 = (pred[256,256]{1,0:T(8,128)(4,1)S(1)}, pred[256,256]{1,0:T(8,128)(4,1)}, u32[]{:S(2)}) copy-start(pred[256,256]{1,0:T(8,128)(4,1)} %copy-done.15) | copy-start | bytes 196612
  49.7 7.8 %collective-permute-start.9 = (f32[]{:T(128)}, f32[]{:T(128)}, u32[]{:S(2)}, u32[]{:S(2)}) collective-permute-start(f32[]{:T(128)} %mul.303), channel_id=1, source_target_pairs={{64,0},{96,32},{128,64},{160,96},{192,128},{224,160},{256,192},{28... | collective-permute-start | bytes 20 | tf_op jit(solution)/shard_map/ppermute | solution.py:28
  58.1 14.5 %collective-permute-start.12 = (f32[128,64]{0,1:T(8,128)S(1)}, f32[128,64]{0,1:T(8,128)S(1)}, u32[]{:S(2)}, u32[]{:S(2)}) collective-permute-start(f32[128,64]{0,1:T(8,128)S(1)} %add_select_fusion.2), channel_id=1, source_target_pairs={{256,0},{288,32},{320,64},{352,96},{384,128},{416,160},{448,192},{... | collective-permute-start | bytes 98312 | tf_op jit(solution)/shard_map/ppermute | solution.py:28
  59.7 10.1 %collective-permute-start.11 = (f32[]{:T(128)}, f32[]{:T(128)}, u32[]{:S(2)}, u32[]{:S(2)}) collective-permute-start(f32[]{:T(128)} %select_n.131), channel_id=1, source_target_pairs={{128,0},{160,32},{192,64},{224,96},{256,128},{288,160},{320,192},{... | collective-permute-start | bytes 20 | tf_op jit(solution)/shard_map/ppermute | solution.py:28
  72.7 3.1 %collective-permute-start.13 = (f32[128,64]{0,1:T(8,128)S(1)}, f32[128,64]{0,1:T(8,128)S(1)}, u32[]{:S(2)}, u32[]{:S(2)}) collective-permute-start(f32[128,64]{0,1:T(8,128)S(1)} %add_select_fusion.1), channel_id=1, source_target_pairs={{0,8},{8,0},{1,9},{9,1},{2,10},{10,2},{3,11},{11,3},{4,12},{12,4},... | collective-permute-start | bytes 98312 | tf_op jit(solution)/shard_map/ppermute | solution.py:23
  74.9 7.3 %copy-start.17 = (f32[4]{0:T(128)S(1)}, f32[4]{0:T(128)}, u32[]{:S(2)}) copy-start(f32[4]{0:T(128)} %get-tuple-element.30) | copy-start | bytes 52
  75.8 6.3 %collective-permute-start.14 = (f32[2,128,64]{1,2,0:T(8,128)S(1)}, f32[2,128,64]{1,2,0:T(8,128)S(1)}, u32[]{:S(2)}, u32[]{:S(2)}) collective-permute-start(f32[2,128,64]{1,2,0:T(8,128)S(1)} %maximum_select_fusion.1), channel_id=1, source_target_pairs={{0,16},{16,0},{1,17},{17,1},{2,18},{18,2},{3,19},{19,3},{4,20},{20... | collective-permute-start | bytes 196616 | tf_op jit(solution)/shard_map/ppermute | solution.py:23
  82.2 15.8 %copy-start.13 = (bf16[1,256,4,64]{1,3,2,0:T(8,128)(2,1)S(1)}, bf16[1,256,4,64]{1,3,2,0:T(8,128)(2,1)}, u32[]{:S(2)}) copy-start(bf16[1,256,4,64]{1,3,2,0:T(8,128)(2,1)} %copy-done.12) | copy-start | bytes 393220
  83.4 14.6 %all-to-all-start = ((f32[256,8,32]{0,2,1:T(8,128)}), f32[256,8,32]{0,2,1:T(8,128)S(1)}, u32[]{:S(2)}, u32[]{:S(2)}) async-start(f32[256,8,32]{0,2,1:T(8,128)} %pad_maximum_fusion), calls=%async_computation | async-start | bytes 524288 | tf_op jit(solution)/shard_map/all_to_all | solution.py:176
  89.4 8.5 %copy-start.6 = (bf16[1,256,4,64]{1,3,2,0:T(8,128)(2,1)}, bf16[1,256,4,64]{1,3,2,0:T(8,128)(2,1)S(1)}, u32[]{:S(2)}) copy-start(bf16[1,256,4,64]{1,3,2,0:T(8,128)(2,1)S(1)} %fusion.11) | copy-start | bytes 393220
  106.7 4.5 %copy-start.5 = (bf16[1024,256]{1,0:T(8,128)(2,1)S(1)}, bf16[1024,256]{1,0:T(8,128)(2,1)}, u32[]{:S(2)}) copy-start(bf16[1024,256]{1,0:T(8,128)(2,1)} %param.20) | copy-start | bytes 1572868
  106.7 4.5 %copy-start.7 = (bf16[1,256,4,64]{1,3,2,0:T(8,128)(2,1)S(1)}, bf16[1,256,4,64]{1,3,2,0:T(8,128)(2,1)}, u32[]{:S(2)}) copy-start(bf16[1,256,4,64]{1,3,2,0:T(8,128)(2,1)} %copy-done.6) | copy-start | bytes 393220
  107.6 13.5 %all-to-all-start.3 = ((bf16[16,2,1,16,544]{4,3,0,2,1:T(8,128)(2,1)}), bf16[16,2,1,16,544]{4,3,0,2,1:T(8,128)(2,1)S(1)}, u32[]{:S(2)}, u32[]{:S(2)}) async-start(bf16[16,2,1,16,544]{4,3,0,2,1:T(8,128)(2,1)} %copy.69), calls=%async_computation.3 | async-start | bytes 1310720 | tf_op jit(solution)/shard_map/all_to_all | solution.py:176
  111.2 0.8 copy-start.14
  121.1 14.8 %all-to-all-start.1 = ((bf16[256,8,128]{2,0,1:T(8,128)(2,1)}), bf16[256,8,128]{2,0,1:T(8,128)(2,1)S(1)}, u32[]{:S(2)}, u32[]{:S(2)}) async-start(bf16[256,8,128]{2,0,1:T(8,128)(2,1)} %bitcast.161), calls=%async_computation.1 | async-start | bytes 1048576 | tf_op jit(solution)/shard_map/all_to_all | solution.py:176
  135.9 32.5 %all-to-all-start.4 = ((bf16[16,1,1,16,544]{4,3,2,1,0:T(8,128)(2,1)}), bf16[16,1,1,16,544]{4,3,2,1,0:T(8,128)(2,1)S(1)}, u32[]{:S(2)}, u32[]{:S(2)}) async-start(bf16[16,1,1,16,544]{4,3,2,1,0:T(8,128)(2,1)} %bitcast.50), calls=%async_computation.4 | async-start | bytes 655360 | tf_op jit(solution)/shard_map/all_to_all | solution.py:176

commit v4 on v3

--- a/solution.py
+++ b/solution.py
@@ -19,45 +19,67 @@
     return jax.tree.map(lambda a, b: jnp.where(flag, a, b), first, second)
 
 
-def swap(tree, axis):
-    return jax.tree.map(lambda a: lax.ppermute(a, axis, [(0, 1), (1, 0)]), tree)
-
-
-def shift(tree, axis, step):
-    pairs = [(source, source - step) for source in range(step, lax.axis_size(axis))]
-    return jax.tree.map(lambda a: lax.ppermute(a, axis, pairs), tree)
+def packed(pair):
+    rows = jnp.broadcast_to(pair[0][..., None, None], pair[0].shape + (8, pair[1].shape[-1]))
+    return jnp.concatenate([pair[1], rows], axis=-2)
+
+
+def unpacked(block):
+    return (block[..., -8, 0], block[..., :-8, :])
+
+
+def rolled(block, axis, step):
+    count = lax.axis_size(axis)
+    return lax.ppermute(block, axis, [(source, (source - step) % count) for source in range(count)])
+
+
+def fold(parts):
+    total = parts[0]
+    for part in parts[1:]:
+        total = join(total, part)
+    return total
 
 
 def suffix_scan(part):
-    z_axis, pair_axis, core_axis = CTX
-    core = lax.axis_index(core_axis)
-    pair = lax.axis_index(pair_axis)
-    plane = pair * 2 + core
-    identity = jax.tree.map(lambda a: jnp.zeros_like(a) + jnp.asarray(1.0 if a.ndim == 1 else 0.0, a.dtype), part)
-    other = swap(part, core_axis)
-    pair_total = pick(core == 0, join(part, other), join(other, part))
-    other_pair = swap(pair_total, pair_axis)
-    total = pick(pair == 0, join(pair_total, other_pair), join(other_pair, pair_total))
-    within = join(pick(core == 0, other, identity), pick(pair == 0, other_pair, identity))
-    head = (
-        lax.dynamic_index_in_dim(total[0], plane, 0, False),
-        lax.dynamic_index_in_dim(total[1], plane, 0, False),
-    )
-    one = (jnp.ones_like(head[0]), jnp.zeros_like(head[1]))
+    z_axis = CTX[0]
+    plane_axis = CTX[1:]
+    plane = lax.axis_index(plane_axis)
+    width = lax.axis_size(plane_axis)
+    own = packed(part)
+    got = [own] + [rolled(own, plane_axis, step) for step in range(1, width)]
+    pairs = [unpacked(block) for block in got]
+    identity = (jnp.ones_like(part[0]), jnp.zeros_like(part[1]))
+    within = fold([pick(plane + step < width, pairs[step], identity) for step in range(1, width)])
+    stacked = jnp.stack([lax.dynamic_index_in_dim(block, plane, 0, False) for block in got])
+    by_place = [
+        unpacked(lax.dynamic_index_in_dim(stacked, (place - plane) % width, 0, False))
+        for place in range(width)
+    ]
+    total = fold(by_place)
+    one = (jnp.ones_like(total[0]), jnp.zeros_like(total[1]))
     z = lax.axis_index(z_axis)
     count = lax.axis_size(z_axis)
-    near = pick(z + 1 < count, shift(head, z_axis, 1), one)
-    far = pick(z + 2 < count, shift(head, z_axis, 2), one)
-    later = join(near, far)
-    step = 2
-    while step < count:
-        later = pick(z + step < count, join(later, shift(later, z_axis, step)), later)
-        step *= 2
+    radix = 4
+    span = 1
+    later = None
+    while span < count:
+        source = packed(total) if later is None else packed(later)
+        base = one if later is None else later
+        parts = [base] if later is not None else []
+        for k in range(1, radix + (1 if later is None else 0)):
+            step = k * span
+            if step >= count:
+                break
+            pairs_k = [(s, s - step) for s in range(step, count)]
+            parts.append(pick(z + step < count, unpacked(lax.ppermute(source, z_axis, pairs_k)), one))
+        later = fold(parts)
+        span *= radix
     mine = later[1]
-    theirs = swap(mine, core_axis)
-    two = jnp.where(core == 0, jnp.stack([mine, theirs]), jnp.stack([theirs, mine]))
-    two_other = swap(two, pair_axis)
-    four = jnp.where(pair == 0, jnp.concatenate([two, two_other]), jnp.concatenate([two_other, two]))
+    gathered = [mine] + [rolled(mine, plane_axis, step) for step in range(1, width)]
+    block = jnp.stack(gathered)
+    four = jnp.stack(
+        [lax.dynamic_index_in_dim(block, (place - plane) % width, 0, False) for place in range(width)]
+    )
     return within[1] + within[0][:, None, None] * four
 
 

time: 171 us -> 175 us (1.023)
  local copies, waits for them, and re-layouts: 8.81 us -> 17.5 us
  waiting for transfers between devices: 75.4 us -> 68.4 us
  between operations: 3.63 us -> 7.93 us
  starting transfers between devices: 61 us -> 57.8 us
  other arithmetic: 7.26 us -> 9.61 us
    ppermute x15 -> x13, waiting for transfers between devices: 28.9 us -> 21.6 us  [the longest x7 20 us: suffix_scan(): lax.ppermute(source, z_axis, pairs_k)]
    slice x2 -> x12, local copies, waits for them, and re-layouts: 0.17 us -> 7.32 us  [the longest x10 7.14 us: unpacked(): return (block[..., -8, 0], block[..., :-8, :])]
    ppermute x15 -> x13, starting transfers between devices: 36.3 us -> 31 us  [the longest x6 17.1 us: rolled(): lax.ppermute(block, axis, [(source, (source - step) % count) for source i...]
    all_to_all x4, starting transfers between devices: 24.8 us -> 26.8 us  [summed_over(): gathered = lax.all_to_all(part, axis, split, split, tiled=True)]
  transfers between devices with their start and end apart: 19 -> 17, of which waited for: 12 -> 11; matrix products, arithmetic and copies ran while one was open for 8% -> 9% of each run, Pallas kernels for 0% -> 0%
where the time goes in v4:
time: 175 us; the launch traced here: 174 us
  waiting for transfers between devices  68.4 us (39%)
  starting transfers between devices  57.8 us (33%)
  local copies, waits for them, and re-layouts  17.5 us (10%)
  other arithmetic  9.61 us (5%)
  between operations  7.93 us (5%)
  matrix products  7.71 us (4%)
  blocking collectives  4.79 us (3%)
    all_to_all x4, waiting for transfers between devices, summed_over(): gathered = lax.all_to_all(part, axis, split, split, tiled=True)  46.7 us
    all_to_all x4, starting transfers between devices, summed_over(): gathered = lax.all_to_all(part, axis, split, split, tiled=True)  26.8 us
    ppermute x7, waiting for transfers between devices, suffix_scan(): lax.ppermute(source, z_axis, pairs_k)  20 us
    ppermute x6, starting transfers between devices, rolled(): lax.ppermute(block, axis, [(source, (source - step) % count) for source i...  17.1 us
    ppermute x7, starting transfers between devices, suffix_scan(): lax.ppermute(source, z_axis, pairs_k)  13.9 us
    slice x10, local copies, waits for them, and re-layouts, unpacked(): return (block[..., -8, 0], block[..., :-8, :])  7.14 us
    all_to_all x1, blocking collectives, summed_over(): gathered = lax.all_to_all(part, axis, split, split, tiled=True)  4.79 us
  transfers between devices with their start and end apart: 17, of which 11 were waited for; matrix products, arithmetic and copies ran while one was open for 9% of the time, Pallas kernels for 0%

profile of v4, /device:TPU:64, one launch (start us, length us, event | category | flops | bytes accessed | tf_op | source)
XLA Modules:
  0.0 173.7 jit_solution(16076469988383680398)
XLA Ops:
  0.7 0.8 reshape.414
  1.4 1.2 reduce-window.6
  3.9 0.7 pad_maximum_fusion
  4.7 1.9 %collective-permute-start.2 = (f32[4,136,64]{1,2,0:T(8,128)}, f32[4,136,64]{1,2,0:T(8,128)}, u32[]{:S(2)}, u32[]{:S(2)}) collective-permute-start(f32[4,136,64]{1,2,0:T(8,128)} %pad_maximum_fusion), channel_id=1, source_target_pairs={{0,8},{8,16},{16,24},{24,0},{1,9},{9,17},{17,25},{25,1},{2,10},{10... | collective-permute-start | bytes 417800 | tf_op jit(solution)/shard_map/ppermute | solution.py:33
  6.6 3.5 %collective-permute-start.1 = (f32[4,136,64]{1,2,0:T(8,128)}, f32[4,136,64]{1,2,0:T(8,128)}, u32[]{:S(2)}, u32[]{:S(2)}) collective-permute-start(f32[4,136,64]{1,2,0:T(8,128)} %pad_maximum_fusion), channel_id=1, source_target_pairs={{0,16},{8,24},{16,0},{24,8},{1,17},{9,25},{17,1},{25,9},{2,18},{10... | collective-permute-start | bytes 417800 | tf_op jit(solution)/shard_map/ppermute | solution.py:33
  10.1 3.4 %collective-permute-start = (f32[4,136,64]{1,2,0:T(8,128)}, f32[4,136,64]{1,2,0:T(8,128)}, u32[]{:S(2)}, u32[]{:S(2)}) collective-permute-start(f32[4,136,64]{1,2,0:T(8,128)} %pad_maximum_fusion), channel_id=1, source_target_pairs={{0,24},{8,0},{16,8},{24,16},{1,25},{9,1},{17,9},{25,17},{2,26},{10... | collective-permute-start | bytes 417800 | tf_op jit(solution)/shard_map/ppermute | solution.py:33
  14.2 0.8 fusion.2
  15.0 1.0 fusion.11
  16.1 0.6 copy-done.9
  17.6 0.9 constant_dynamic-slice_fusion.4
  18.4 0.8 constant_dynamic-slice_fusion.5
  19.3 0.9 collective-permute-done
  20.2 0.8 constant_dynamic-slice_fusion.6
  21.1 0.5 slice.144
  21.6 0.5 slice.145
  22.1 0.5 slice.146
  24.6 0.7 fusion.55
  25.3 0.5 slice.147
  26.4 1.3 collective-permute-start.6
  27.7 1.3 collective-permute-start.5
  29.0 5.5 %collective-permute-start.4 = (f32[136,64]{0,1:T(8,128)S(1)}, f32[136,64]{0,1:T(8,128)}, u32[]{:S(2)}, u32[]{:S(2)}) collective-permute-start(f32[136,64]{0,1:T(8,128)S(1)} %concatenate.21), channel_id=1, source_target_pairs={{64,0},{96,32},{128,64},{160,96},{192,128},{224,160},{256,192},{28... | collective-permute-start | bytes 104456 | tf_op jit(solution)/shard_map/ppermute | solution.py:74
  34.6 1.9 %collective-permute-start.3 = (f32[136,64]{0,1:T(8,128)S(1)}, f32[136,64]{0,1:T(8,128)}, u32[]{:S(2)}, u32[]{:S(2)}) collective-permute-start(f32[136,64]{0,1:T(8,128)S(1)} %concatenate.21), channel_id=1, source_target_pairs={{32,0},{64,32},{96,64},{128,96},{160,128},{192,160},{224,192},{256... | collective-permute-start | bytes 104456 | tf_op jit(solution)/shard_map/ppermute | solution.py:74
  37.0 1.8 %collective-permute-done.6 = f32[136,64]{0,1:T(8,128)S(1)} collective-permute-done((f32[136,64]{0,1:T(8,128)S(1)}, f32[136,64]{0,1:T(8,128)S(1)}, u32[]{:S(2)}, u32[]{:S(2)}) %collective-permute-start.6) | collective-permute-done | bytes 34848 | tf_op jit(solution)/shard_map/ppermute | solution.py:74
  38.7 0.5 slice.155
  39.9 5.5 %collective-permute-done.5 = f32[136,64]{0,1:T(8,128)} collective-permute-done((f32[136,64]{0,1:T(8,128)S(1)}, f32[136,64]{0,1:T(8,128)}, u32[]{:S(2)}, u32[]{:S(2)}) %collective-permute-start.5) | collective-permute-done | bytes 34848 | tf_op jit(solution)/shard_map/ppermute | solution.py:74
  45.4 1.2 slice.153
  47.3 1.1 collective-permute-done.4
  48.4 1.2 slice.151
  50.2 1.2 slice.149
  52.1 0.8 fusion.49
  52.9 1.3 collective-permute-start.9
  54.2 1.3 collective-permute-start.8
  55.5 1.3 collective-permute-start.7
  56.8 0.9 fusion.64
  57.6 9.0 %collective-permute-done.7 = f32[136,64]{0,1:T(8,128)S(1)} collective-permute-done((f32[136,64]{0,1:T(8,128)S(1)}, f32[136,64]{0,1:T(8,128)S(1)}, u32[]{:S(2)}, u32[]{:S(2)}) %collective-permute-start.7) | collective-permute-done | bytes 34848 | tf_op jit(solution)/shard_map/ppermute | solution.py:74
  66.6 0.5 slice.157
  67.8 2.6 %collective-permute-done.8 = f32[136,64]{0,1:T(8,128)S(1)} collective-permute-done((f32[136,64]{0,1:T(8,128)S(1)}, f32[136,64]{0,1:T(8,128)S(1)}, u32[]{:S(2)}, u32[]{:S(2)}) %collective-permute-start.8) | collective-permute-done | bytes 34848 | tf_op jit(solution)/shard_map/ppermute | solution.py:74
  70.4 0.5 slice.159
  71.6 1.9 %collective-permute-start.12 = (f32[128,64]{0,1:T(8,128)S(1)}, f32[128,64]{0,1:T(8,128)S(1)}, u32[]{:S(2)}, u32[]{:S(2)}) collective-permute-start(f32[128,64]{0,1:T(8,128)S(1)} %fusion.43), channel_id=1, source_target_pairs={{0,8},{8,16},{16,24},{24,0},{1,9},{9,17},{17,25},{25,1},{2,10},{10... | collective-permute-start | bytes 98312 | tf_op jit(solution)/shard_map/ppermute | solution.py:33
  73.5 3.1 %collective-permute-start.11 = (f32[128,64]{0,1:T(8,128)S(1)}, f32[128,64]{0,1:T(8,128)S(1)}, u32[]{:S(2)}, u32[]{:S(2)}) collective-permute-start(f32[128,64]{0,1:T(8,128)S(1)} %fusion.43), channel_id=1, source_target_pairs={{0,16},{8,24},{16,0},{24,8},{1,17},{9,25},{17,1},{25,9},{2,18},{10... | collective-permute-start | bytes 98312 | tf_op jit(solution)/shard_map/ppermute | solution.py:33
  76.6 3.4 %collective-permute-start.10 = (f32[128,64]{0,1:T(8,128)S(1)}, f32[128,64]{0,1:T(8,128)S(1)}, u32[]{:S(2)}, u32[]{:S(2)}) collective-permute-start(f32[128,64]{0,1:T(8,128)S(1)} %fusion.43), channel_id=1, source_target_pairs={{0,24},{8,0},{16,8},{24,16},{1,25},{9,1},{17,9},{25,17},{2,26},{10... | collective-permute-start | bytes 98312 | tf_op jit(solution)/shard_map/ppermute | solution.py:33
  80.0 0.8 fusion.65
  80.8 0.7 collective-permute-done.10
  81.6 1.1 fusion.35
  83.7 0.7 pad_maximum_fusion.2
  84.5 6.9 %all-to-all-start = ((f32[256,8,32]{0,2,1:T(8,128)}), f32[256,8,32]{0,2,1:T(8,128)S(1)}, u32[]{:S(2)}, u32[]{:S(2)}) async-start(f32[256,8,32]{0,2,1:T(8,128)} %pad_maximum_fusion.2), calls=%async_computation | async-start | bytes 524288 | tf_op jit(solution)/shard_map/all_to_all | solution.py:198
  91.3 1.1 fusion.12
  92.4 8.7 %all-to-all-done = f32[256,8,32]{0,2,1:T(8,128)S(1)} async-done(((f32[256,8,32]{0,2,1:T(8,128)}), f32[256,8,32]{0,2,1:T(8,128)S(1)}, u32[]{:S(2)}, u32[]{:S(2)}) %all-to-all-start) | async-done | bytes 262176 | tf_op jit(solution)/shard_map/all_to_all | solution.py:198
  101.2 1.5 fusion
  102.6 1.7 copy.67
  104.4 4.8 %all_to_all.30 = bf16[16,2,2,16,544]{4,3,1,0,2:T(8,128)(2,1)S(1)} all-to-all(bf16[16,2,2,16,544]{4,3,1,0,2:T(8,128)(2,1)S(1)} %copy.68), channel_id=1, replica_groups=mesh['z'=16,'y_lo'=2,'core'=2,'y_hi'=2,'x'=4] {'core'}, dimensions={2} | all-to-all | bytes 2228224 | tf_op jit(solution)/shard_map/all_to_all | solution.py:198
  109.2 0.6 reduce_sum.74
  109.9 0.9 copy.69
  110.8 3.5 %all-to-all-start.3 = ((bf16[16,2,1,16,544]{4,3,0,2,1:T(8,128)(2,1)}), bf16[16,2,1,16,544]{4,3,0,2,1:T(8,128)(2,1)S(1)}, u32[]{:S(2)}, u32[]{:S(2)}) async-start(bf16[16,2,1,16,544]{4,3,0,2,1:T(8,128)(2,1)} %copy.69), calls=%async_computation.3 | async-start | bytes 1310720 | tf_op jit(solution)/shard_map/all_to_all | solution.py:198
  115.5 0.9 copy.76
  116.4 7.9 %all-to-all-done.3 = bf16[16,2,1,16,544]{4,3,0,2,1:T(8,128)(2,1)S(1)} async-done(((bf16[16,2,1,16,544]{4,3,0,2,1:T(8,128)(2,1)}), bf16[16,2,1,16,544]{4,3,0,2,1:T(8,128)(2,1)S(1)}, u32[]{:S(2)}, u32[]{:S(2)}) %all-to-all-start.3) | async-done | bytes 557088 | tf_op jit(solution)/shard_map/all_to_all | solution.py:198
  124.2 3.5 %all-to-all-start.1 = ((bf16[256,8,128]{2,0,1:T(8,128)(2,1)}), bf16[256,8,128]{2,0,1:T(8,128)(2,1)S(1)}, u32[]{:S(2)}, u32[]{:S(2)}) async-start(bf16[256,8,128]{2,0,1:T(8,128)(2,1)} %bitcast.170), calls=%async_computation.1 | async-start | bytes 1048576 | tf_op jit(solution)/shard_map/all_to_all | solution.py:198
  127.7 0.9 reduce_sum.75
  128.7 10.3 %all-to-all-done.1 = bf16[256,8,128]{2,0,1:T(8,128)(2,1)S(1)} async-done(((bf16[256,8,128]{2,0,1:T(8,128)(2,1)}), bf16[256,8,128]{2,0,1:T(8,128)(2,1)S(1)}, u32[]{:S(2)}, u32[]{:S(2)}) %all-to-all-start.1) | async-done | bytes 524320 | tf_op jit(solution)/shard_map/all_to_all | solution.py:198
  139.0 12.9 %all-to-all-start.4 = ((bf16[16,1,1,16,544]{4,3,2,1,0:T(8,128)(2,1)}), bf16[16,1,1,16,544]{4,3,2,1,0:T(8,128)(2,1)S(1)}, u32[]{:S(2)}, u32[]{:S(2)}) async-start(bf16[16,1,1,16,544]{4,3,2,1,0:T(8,128)(2,1)} %bitcast.65), calls=%async_computation.4 | async-start | bytes 655360 | tf_op jit(solution)/shard_map/all_to_all | solution.py:198
  151.9 0.7 reduce_sum.73
  152.6 19.8 %all-to-all-done.4 = bf16[16,1,1,16,544]{4,3,2,1,0:T(8,128)(2,1)S(1)} async-done(((bf16[16,1,1,16,544]{4,3,2,1,0:T(8,128)(2,1)}), bf16[16,1,1,16,544]{4,3,2,1,0:T(8,128)(2,1)S(1)}, u32[]{:S(2)}, u32[]{:S(2)}) %all-to-all-start.4) | async-done | bytes 278560 | tf_op jit(solution)/shard_map/all_to_all | solution.py:198
  172.5 0.6 slice.163
  173.1 0.6 fusion.66
  (80 shorter events, 5.5 us)
Async XLA Ops:
  0.6 100.5 %copy-start = (bf16[256,1024]{1,0:T(8,128)(2,1)S(1)}, bf16[256,1024]{1,0:T(8,128)(2,1)}, u32[]{:S(2)}) copy-start(bf16[256,1024]{1,0:T(8,128)(2,1)} %param.11) | copy-start | bytes 1572868
  0.6 2.6 %copy-start.6 = (bf16[256,256]{1,0:T(8,128)(2,1)S(1)}, bf16[256,256]{1,0:T(8,128)(2,1)}, u32[]{:S(2)}) copy-start(bf16[256,256]{1,0:T(8,128)(2,1)} %param.13) | copy-start | bytes 393220
  0.7 2.7 %copy-start.7 = (bf16[256,256]{1,0:T(8,128)(2,1)S(1)}, bf16[256,256]{1,0:T(8,128)(2,1)}, u32[]{:S(2)}) copy-start(bf16[256,256]{1,0:T(8,128)(2,1)} %param.14) | copy-start | bytes 393220
  2.7 0.9 copy-start.1
  3.2 10.4 %copy-start.8 = (bf16[256,256]{1,0:T(8,128)(2,1)S(1)}, bf16[256,256]{1,0:T(8,128)(2,1)}, u32[]{:S(2)}) copy-start(bf16[256,256]{1,0:T(8,128)(2,1)} %param.12) | copy-start | bytes 393220
  3.3 10.4 %copy-start.2 = (bf16[256,128]{1,0:T(8,128)(2,1)S(1)}, bf16[256,128]{1,0:T(8,128)(2,1)}, u32[]{:S(2)}) copy-start(bf16[256,128]{1,0:T(8,128)(2,1)} %param.15) | copy-start | bytes 196612
  3.5 10.4 %copy-start.4 = (f32[1,4,128,64]{2,3,1,0:T(8,128)S(1)}, f32[1,4,128,64]{2,3,1,0:T(8,128)}, u32[]{:S(2)}) copy-start(f32[1,4,128,64]{2,3,1,0:T(8,128)} %param.18) | copy-start | bytes 393220
  4.7 12.9 %collective-permute-start.2 = (f32[4,136,64]{1,2,0:T(8,128)}, f32[4,136,64]{1,2,0:T(8,128)}, u32[]{:S(2)}, u32[]{:S(2)}) collective-permute-start(f32[4,136,64]{1,2,0:T(8,128)} %pad_maximum_fusion), channel_id=1, source_target_pairs={{0,8},{8,16},{16,24},{24,0},{1,9},{9,17},{17,25},{25,1},{2,10},{10... | collective-permute-start | bytes 417800 | tf_op jit(solution)/shard_map/ppermute | solution.py:33
  6.6 11.8 %collective-permute-start.1 = (f32[4,136,64]{1,2,0:T(8,128)}, f32[4,136,64]{1,2,0:T(8,128)}, u32[]{:S(2)}, u32[]{:S(2)}) collective-permute-start(f32[4,136,64]{1,2,0:T(8,128)} %pad_maximum_fusion), channel_id=1, source_target_pairs={{0,16},{8,24},{16,0},{24,8},{1,17},{9,25},{17,1},{25,9},{2,18},{10... | collective-permute-start | bytes 417800 | tf_op jit(solution)/shard_map/ppermute | solution.py:33
  10.1 10.1 %collective-permute-start = (f32[4,136,64]{1,2,0:T(8,128)}, f32[4,136,64]{1,2,0:T(8,128)}, u32[]{:S(2)}, u32[]{:S(2)}) collective-permute-start(f32[4,136,64]{1,2,0:T(8,128)} %pad_maximum_fusion), channel_id=1, source_target_pairs={{0,24},{8,0},{16,8},{24,16},{1,25},{9,1},{17,9},{25,17},{2,26},{10... | collective-permute-start | bytes 417800 | tf_op jit(solution)/shard_map/ppermute | solution.py:33
  13.5 1.5 copy-start.14
  15.0 1.7 copy-start.3
  16.0 0.6 copy-start.9
  26.4 12.3 %collective-permute-start.6 = (f32[136,64]{0,1:T(8,128)S(1)}, f32[136,64]{0,1:T(8,128)S(1)}, u32[]{:S(2)}, u32[]{:S(2)}) collective-permute-start(f32[136,64]{0,1:T(8,128)S(1)} %concatenate.21), channel_id=1, source_target_pairs={{128,0},{160,32},{192,64},{224,96},{256,128},{288,160},{320,192},{... | collective-permute-start | bytes 104456 | tf_op jit(solution)/shard_map/ppermute | solution.py:74
  27.7 17.7 %collective-permute-start.5 = (f32[136,64]{0,1:T(8,128)S(1)}, f32[136,64]{0,1:T(8,128)}, u32[]{:S(2)}, u32[]{:S(2)}) collective-permute-start(f32[136,64]{0,1:T(8,128)S(1)} %concatenate.21), channel_id=1, source_target_pairs={{96,0},{128,32},{160,64},{192,96},{224,128},{256,160},{288,192},{3... | collective-permute-start | bytes 104456 | tf_op jit(solution)/shard_map/ppermute | solution.py:74
  29.0 19.3 %collective-permute-start.4 = (f32[136,64]{0,1:T(8,128)S(1)}, f32[136,64]{0,1:T(8,128)}, u32[]{:S(2)}, u32[]{:S(2)}) collective-permute-start(f32[136,64]{0,1:T(8,128)S(1)} %concatenate.21), channel_id=1, source_target_pairs={{64,0},{96,32},{128,64},{160,96},{192,128},{224,160},{256,192},{28... | collective-permute-start | bytes 104456 | tf_op jit(solution)/shard_map/ppermute | solution.py:74
  34.6 15.6 %collective-permute-start.3 = (f32[136,64]{0,1:T(8,128)S(1)}, f32[136,64]{0,1:T(8,128)}, u32[]{:S(2)}, u32[]{:S(2)}) collective-permute-start(f32[136,64]{0,1:T(8,128)S(1)} %concatenate.21), channel_id=1, source_target_pairs={{32,0},{64,32},{96,64},{128,96},{160,128},{192,160},{224,192},{256... | collective-permute-start | bytes 104456 | tf_op jit(solution)/shard_map/ppermute | solution.py:74
  52.9 18.7 %collective-permute-start.9 = (f32[136,64]{0,1:T(8,128)S(1)}, f32[136,64]{0,1:T(8,128)S(1)}, u32[]{:S(2)}, u32[]{:S(2)}) collective-permute-start(f32[136,64]{0,1:T(8,128)S(1)} %concatenate.22), channel_id=1, source_target_pairs={{384,0},{416,32},{448,64},{480,96},{385,1},{417,33},{449,65},{481,... | collective-permute-start | bytes 104456 | tf_op jit(solution)/shard_map/ppermute | solution.py:74
  54.2 16.2 %collective-permute-start.8 = (f32[136,64]{0,1:T(8,128)S(1)}, f32[136,64]{0,1:T(8,128)S(1)}, u32[]{:S(2)}, u32[]{:S(2)}) collective-permute-start(f32[136,64]{0,1:T(8,128)S(1)} %concatenate.22), channel_id=1, source_target_pairs={{256,0},{288,32},{320,64},{352,96},{384,128},{416,160},{448,192},{... | collective-permute-start | bytes 104456 | tf_op jit(solution)/shard_map/ppermute | solution.py:74
  55.5 11.1 %collective-permute-start.7 = (f32[136,64]{0,1:T(8,128)S(1)}, f32[136,64]{0,1:T(8,128)S(1)}, u32[]{:S(2)}, u32[]{:S(2)}) collective-permute-start(f32[136,64]{0,1:T(8,128)S(1)} %concatenate.22), channel_id=1, source_target_pairs={{128,0},{160,32},{192,64},{224,96},{256,128},{288,160},{320,192},{... | collective-permute-start | bytes 104456 | tf_op jit(solution)/shard_map/ppermute | solution.py:74
  71.6 9.2 %collective-permute-start.12 = (f32[128,64]{0,1:T(8,128)S(1)}, f32[128,64]{0,1:T(8,128)S(1)}, u32[]{:S(2)}, u32[]{:S(2)}) collective-permute-start(f32[128,64]{0,1:T(8,128)S(1)} %fusion.43), channel_id=1, source_target_pairs={{0,8},{8,16},{16,24},{24,0},{1,9},{9,17},{17,25},{25,1},{2,10},{10... | collective-permute-start | bytes 98312 | tf_op jit(solution)/shard_map/ppermute | solution.py:33
  73.5 7.3 %collective-permute-start.11 = (f32[128,64]{0,1:T(8,128)S(1)}, f32[128,64]{0,1:T(8,128)S(1)}, u32[]{:S(2)}, u32[]{:S(2)}) collective-permute-start(f32[128,64]{0,1:T(8,128)S(1)} %fusion.43), channel_id=1, source_target_pairs={{0,16},{8,24},{16,0},{24,8},{1,17},{9,25},{17,1},{25,9},{2,18},{10... | collective-permute-start | bytes 98312 | tf_op jit(solution)/shard_map/ppermute | solution.py:33
  76.6 4.9 %collective-permute-start.10 = (f32[128,64]{0,1:T(8,128)S(1)}, f32[128,64]{0,1:T(8,128)S(1)}, u32[]{:S(2)}, u32[]{:S(2)}) collective-permute-start(f32[128,64]{0,1:T(8,128)S(1)} %fusion.43), channel_id=1, source_target_pairs={{0,24},{8,0},{16,8},{24,16},{1,25},{9,1},{17,9},{25,17},{2,26},{10... | collective-permute-start | bytes 98312 | tf_op jit(solution)/shard_map/ppermute | solution.py:33
  83.0 8.3 %copy-start.15 = (pred[256,256]{1,0:T(8,128)(4,1)S(1)}, pred[256,256]{1,0:T(8,128)(4,1)}, u32[]{:S(2)}) copy-start(pred[256,256]{1,0:T(8,128)(4,1)} %copy-done.14) | copy-start | bytes 196612
  84.5 16.7 %copy-start.10 = (bf16[1,256,4,64]{1,3,2,0:T(8,128)(2,1)S(1)}, bf16[1,256,4,64]{1,3,2,0:T(8,128)(2,1)}, u32[]{:S(2)}) copy-start(bf16[1,256,4,64]{1,3,2,0:T(8,128)(2,1)} %copy-done.9) | copy-start | bytes 393220
  84.5 16.7 %all-to-all-start = ((f32[256,8,32]{0,2,1:T(8,128)}), f32[256,8,32]{0,2,1:T(8,128)S(1)}, u32[]{:S(2)}, u32[]{:S(2)}) async-start(f32[256,8,32]{0,2,1:T(8,128)} %pad_maximum_fusion.2), calls=%async_computation | async-start | bytes 524288 | tf_op jit(solution)/shard_map/all_to_all | solution.py:198
  92.4 11.9 %copy-start.11 = (bf16[1,256,4,64]{1,3,2,0:T(8,128)(2,1)}, bf16[1,256,4,64]{1,3,2,0:T(8,128)(2,1)S(1)}, u32[]{:S(2)}) copy-start(bf16[1,256,4,64]{1,3,2,0:T(8,128)(2,1)S(1)} %fusion.12) | copy-start | bytes 393220
  109.8 4.5 %copy-start.5 = (bf16[1024,256]{1,0:T(8,128)(2,1)S(1)}, bf16[1024,256]{1,0:T(8,128)(2,1)}, u32[]{:S(2)}) copy-start(bf16[1024,256]{1,0:T(8,128)(2,1)} %param.20) | copy-start | bytes 1572868
  109.9 4.4 %copy-start.12 = (bf16[1,256,4,64]{1,3,2,0:T(8,128)(2,1)S(1)}, bf16[1,256,4,64]{1,3,2,0:T(8,128)(2,1)}, u32[]{:S(2)}) copy-start(bf16[1,256,4,64]{1,3,2,0:T(8,128)(2,1)} %copy-done.11) | copy-start | bytes 393220
  110.8 13.5 %all-to-all-start.3 = ((bf16[16,2,1,16,544]{4,3,0,2,1:T(8,128)(2,1)}), bf16[16,2,1,16,544]{4,3,0,2,1:T(8,128)(2,1)S(1)}, u32[]{:S(2)}, u32[]{:S(2)}) async-start(bf16[16,2,1,16,544]{4,3,0,2,1:T(8,128)(2,1)} %copy.69), calls=%async_computation.3 | async-start | bytes 1310720 | tf_op jit(solution)/shard_map/all_to_all | solution.py:198
  114.3 0.8 copy-start.13
  124.2 14.8 %all-to-all-start.1 = ((bf16[256,8,128]{2,0,1:T(8,128)(2,1)}), bf16[256,8,128]{2,0,1:T(8,128)(2,1)S(1)}, u32[]{:S(2)}, u32[]{:S(2)}) async-start(bf16[256,8,128]{2,0,1:T(8,128)(2,1)} %bitcast.170), calls=%async_computation.1 | async-start | bytes 1048576 | tf_op jit(solution)/shard_map/all_to_all | solution.py:198
  139.0 33.4 %all-to-all-start.4 = ((bf16[16,1,1,16,544]{4,3,2,1,0:T(8,128)(2,1)}), bf16[16,1,1,16,544]{4,3,2,1,0:T(8,128)(2,1)S(1)}, u32[]{:S(2)}, u32[]{:S(2)}) async-start(bf16[16,1,1,16,544]{4,3,2,1,0:T(8,128)(2,1)} %bitcast.65), calls=%async_computation.4 | async-start | bytes 655360 | tf_op jit(solution)/shard_map/all_to_all | solution.py:198

commit v5 on v3

--- a/solution.py
+++ b/solution.py
@@ -179,6 +179,18 @@
     return jnp.sum(gathered.astype(jnp.float32).reshape(pieces), axis=split)
 
 
+def spread_sum(part, axis):
+    count = lax.axis_size(axis)
+    place = lax.axis_index(axis)
+    chunks = part.reshape(part.shape[0], count, part.shape[1] // count).transpose(1, 0, 2)
+    total = lax.dynamic_index_in_dim(chunks, place, 0, False).astype(jnp.float32)
+    for step in range(1, count):
+        piece = lax.dynamic_index_in_dim(chunks, (place - step) % count, 0, False)
+        pairs = [(source, (source - step) % count) for source in range(count)]
+        total = total + lax.ppermute(piece, axis, pairs).astype(jnp.float32)
+    return total
+
+
 def per_device(
     events,
     ssm_input,
@@ -203,7 +215,7 @@
     input_part = (
         times_rows(grad_z, w_gate) + times_rows(grad_x, w_value) + times_rows(grad_bc, w_shared)
     )
-    grad_input = summed_over(input_part.astype(jnp.bfloat16), HEAD, 1).astype(jnp.bfloat16)
+    grad_input = spread_sum(input_part.astype(jnp.bfloat16), HEAD).astype(jnp.bfloat16)
     norm_scale = 1.0 / math.sqrt(events.shape[0] * lax.axis_size(CTX))
     head_cols = grad_z.shape[1]
     projected = jnp.concatenate([grad_z, grad_x, grad_bc], axis=1)

time: 171 us -> 168 us (0.982)
  the two profiles are of different devices: /device:TPU:64 before, /device:TPU:32 now
where the time goes in v5:
time: 168 us; the launch traced here: 167 us
  starting transfers between devices  77.8 us (46%)
  waiting for transfers between devices  47.4 us (28%)
  blocking collectives  17.3 us (10%)
  local copies, waits for them, and re-layouts  7.44 us (4%)
  matrix products  6.71 us (4%)
  other arithmetic  6.06 us (4%)
  between operations  4.11 us (2%)
    ppermute x9, waiting for transfers between devices, shift(): return jax.tree.map(lambda a: lax.ppermute(a, axis, pairs), tree)  28.8 us
    ppermute x7, starting transfers between devices, spread_sum(): total = total + lax.ppermute(piece, axis, pairs).astype(jnp.float32)  27.5 us
    all_to_all x2, blocking collectives, summed_over(): gathered = lax.all_to_all(part, axis, split, split, tiled=True)  17.3 us
    all_to_all x2, starting transfers between devices, summed_over(): gathered = lax.all_to_all(part, axis, split, split, tiled=True)  17.2 us
    ppermute x9, starting transfers between devices, shift(): return jax.tree.map(lambda a: lax.ppermute(a, axis, pairs), tree)  16.8 us
    ppermute x6, starting transfers between devices, swap(): return jax.tree.map(lambda a: lax.ppermute(a, axis, [(0, 1), (1, 0)]), tree)  16.3 us
    all_to_all x2, waiting for transfers between devices, summed_over(): gathered = lax.all_to_all(part, axis, split, split, tiled=True)  8.51 us
    ppermute x6, waiting for transfers between devices, swap(): return jax.tree.map(lambda a: lax.ppermute(a, axis, [(0, 1), (1, 0)]), tree)  5.47 us
  transfers between devices with their start and end apart: 24, of which 13 were waited for; matrix products, arithmetic and copies ran while one was open for 6% of the time, Pallas kernels for 0%

profile of v5, /device:TPU:32, one launch (start us, length us, event | category | flops | bytes accessed | tf_op | source)
XLA Modules:
  0.0 166.9 jit_solution(10126388034680843386)
XLA Ops:
  0.7 0.8 reshape.419
  1.5 1.2 reduce-window.6
  3.1 1.9 %collective-permute-start.1 = (f32[4]{0:T(128)S(1)}, f32[4]{0:T(128)S(1)}, u32[]{:S(2)}, u32[]{:S(2)}) collective-permute-start(f32[4]{0:T(128)S(1)} %fusion.50), channel_id=1, source_target_pairs={{0,8},{8,0},{1,9},{9,1},{2,10},{10,2},{3,11},{11,3},{4,12},{12,4},... | collective-permute-start | bytes 56 | tf_op jit(solution)/shard_map/ppermute | solution.py:23
  6.4 2.4 %collective-permute-start = (f32[4,128,64]{1,2,0:T(8,128)S(1)}, f32[4,128,64]{1,2,0:T(8,128)S(1)}, u32[]{:S(2)}, u32[]{:S(2)}) collective-permute-start(f32[4,128,64]{1,2,0:T(8,128)S(1)} %fusion.13), channel_id=1, source_target_pairs={{0,8},{8,0},{1,9},{9,1},{2,10},{10,2},{3,11},{11,3},{4,12},{12,4},... | collective-permute-start | bytes 393224 | tf_op jit(solution)/shard_map/ppermute | solution.py:23
  9.0 0.8 collective-permute-done
  9.9 3.5 %collective-permute-start.2 = (f32[4,128,64]{1,2,0:T(8,128)S(1)}, f32[4,128,64]{1,2,0:T(8,128)S(1)}, u32[]{:S(2)}, u32[]{:S(2)}) collective-permute-start(f32[4,128,64]{1,2,0:T(8,128)S(1)} %add_select_fusion), channel_id=1, source_target_pairs={{0,16},{16,0},{1,17},{17,1},{2,18},{18,2},{3,19},{19,3},{4,20},{20... | collective-permute-start | bytes 393224 | tf_op jit(solution)/shard_map/ppermute | solution.py:23
  13.4 1.0 fusion.12
  14.4 2.4 %collective-permute-start.3 = (f32[4]{0:T(128)S(1)}, f32[4]{0:T(128)S(1)}, u32[]{:S(2)}, u32[]{:S(2)}) collective-permute-start(f32[4]{0:T(128)S(1)} %get-tuple-element.51), channel_id=1, source_target_pairs={{0,16},{16,0},{1,17},{17,1},{2,18},{18,2},{3,19},{19,3},{4,20},{20... | collective-permute-start | bytes 56 | tf_op jit(solution)/shard_map/ppermute | solution.py:23
  16.7 0.6 dynamic-slice.34
  17.3 2.5 %collective-permute-done.3 = f32[4]{0:T(128)S(1)} collective-permute-done((f32[4]{0:T(128)S(1)}, f32[4]{0:T(128)S(1)}, u32[]{:S(2)}, u32[]{:S(2)}) %collective-permute-start.3) | collective-permute-done | bytes 48 | tf_op jit(solution)/shard_map/ppermute | solution.py:23
  19.8 0.6 dynamic-slice.35
  20.4 1.3 select_bitcast_fusion
  21.7 1.3 collective-permute-start.6
  23.0 5.8 %collective-permute-start.4 = (f32[128,64]{0,1:T(8,128)S(1)}, f32[128,64]{0,1:T(8,128)S(1)}, u32[]{:S(2)}, u32[]{:S(2)}) collective-permute-start(f32[128,64]{0,1:T(8,128)S(1)} %select_bitcast_fusion), channel_id=1, source_target_pairs={{32,0},{64,32},{96,64},{128,96},{160,128},{192,160},{224,192},{256... | collective-permute-start | bytes 98312 | tf_op jit(solution)/shard_map/ppermute | solution.py:28
  28.8 0.6 dynamic_slice.31
  29.4 1.9 %collective-permute-start.5 = (f32[]{:T(128)}, f32[]{:T(128)}, u32[]{:S(2)}, u32[]{:S(2)}) collective-permute-start(f32[]{:T(128)} %bitcast.34), channel_id=1, source_target_pairs={{32,0},{64,32},{96,64},{128,96},{160,128},{192,160},{224,192},{256... | collective-permute-start | bytes 20 | tf_op jit(solution)/shard_map/ppermute | solution.py:28
  31.4 3.7 %collective-permute-done.5 = f32[]{:T(128)} collective-permute-done((f32[]{:T(128)}, f32[]{:T(128)}, u32[]{:S(2)}, u32[]{:S(2)}) %collective-permute-start.5) | collective-permute-done | bytes 36 | tf_op jit(solution)/shard_map/ppermute | solution.py:28
  35.7 1.3 collective-permute-start.8
  37.0 0.8 fusion.2
  37.9 1.3 collective-permute-start.7
  39.2 7.5 %collective-permute-done.7 = f32[]{:T(128)} collective-permute-done((f32[]{:T(128)}, f32[]{:T(128)}, u32[]{:S(2)}, u32[]{:S(2)}) %collective-permute-start.7) | collective-permute-done | bytes 36 | tf_op jit(solution)/shard_map/ppermute | solution.py:28
  47.4 1.3 collective-permute-start.10
  48.7 0.4 convolution_bitcast_fusion.3
  49.1 1.3 collective-permute-start.9
  50.4 6.2 %collective-permute-done.9 = f32[]{:T(128)} collective-permute-done((f32[]{:T(128)}, f32[]{:T(128)}, u32[]{:S(2)}, u32[]{:S(2)}) %collective-permute-start.9) | collective-permute-done | bytes 36 | tf_op jit(solution)/shard_map/ppermute | solution.py:28
  57.2 0.4 collective-permute-done.10
  57.6 1.3 collective-permute-start.12
  58.9 0.3 convolution_add_fusion.2
  59.2 1.3 collective-permute-start.11
  60.5 8.3 %collective-permute-done.11 = f32[]{:T(128)} collective-permute-done((f32[]{:T(128)}, f32[]{:T(128)}, u32[]{:S(2)}, u32[]{:S(2)}) %collective-permute-start.11) | collective-permute-done | bytes 36 | tf_op jit(solution)/shard_map/ppermute | solution.py:28
  69.5 2.7 %collective-permute-done.12 = f32[128,64]{0,1:T(8,128)S(1)} collective-permute-done((f32[128,64]{0,1:T(8,128)S(1)}, f32[128,64]{0,1:T(8,128)S(1)}, u32[]{:S(2)}, u32[]{:S(2)}) %collective-permute-start.12) | collective-permute-done | bytes 32800 | tf_op jit(solution)/shard_map/ppermute | solution.py:28
  72.2 1.9 %collective-permute-start.13 = (f32[128,64]{0,1:T(8,128)S(1)}, f32[128,64]{0,1:T(8,128)S(1)}, u32[]{:S(2)}, u32[]{:S(2)}) collective-permute-start(f32[128,64]{0,1:T(8,128)S(1)} %add_select_fusion.1), channel_id=1, source_target_pairs={{0,8},{8,0},{1,9},{9,1},{2,10},{10,2},{3,11},{11,3},{4,12},{12,4},... | collective-permute-start | bytes 98312 | tf_op jit(solution)/shard_map/ppermute | solution.py:23
  74.4 0.9 collective-permute-done.13
  75.3 4.3 %collective-permute-start.14 = (f32[2,128,64]{1,2,0:T(8,128)S(1)}, f32[2,128,64]{1,2,0:T(8,128)S(1)}, u32[]{:S(2)}, u32[]{:S(2)}) collective-permute-start(f32[2,128,64]{1,2,0:T(8,128)S(1)} %maximum_select_fusion.1), channel_id=1, source_target_pairs={{0,16},{16,0},{1,17},{17,1},{2,18},{18,2},{3,19},{19,3},{4,20},{20... | collective-permute-start | bytes 196616 | tf_op jit(solution)/shard_map/ppermute | solution.py:23
  79.6 1.1 convolution_bitcast_fusion.1
  80.8 1.2 collective-permute-done.14
  82.1 0.4 fusion.14
  82.5 0.7 pad_maximum_fusion
  83.2 5.3 %all-to-all-start = ((f32[256,8,32]{0,2,1:T(8,128)}), f32[256,8,32]{0,2,1:T(8,128)S(1)}, u32[]{:S(2)}, u32[]{:S(2)}) async-start(f32[256,8,32]{0,2,1:T(8,128)} %pad_maximum_fusion), calls=%async_computation | async-start | bytes 524288 | tf_op jit(solution)/shard_map/all_to_all | solution.py:176
  88.5 0.3 fusion.11
  88.8 8.5 %all-to-all-done = f32[256,8,32]{0,2,1:T(8,128)S(1)} async-done(((f32[256,8,32]{0,2,1:T(8,128)}), f32[256,8,32]{0,2,1:T(8,128)S(1)}, u32[]{:S(2)}, u32[]{:S(2)}) %all-to-all-start) | async-done | bytes 262176 | tf_op jit(solution)/shard_map/all_to_all | solution.py:176
  97.3 0.5 fusion
  97.8 0.7 copy.90
  98.6 4.8 %all_to_all.21 = bf16[16,2,2,16,544]{4,3,1,0,2:T(8,128)(2,1)S(1)} all-to-all(bf16[16,2,2,16,544]{4,3,1,0,2:T(8,128)(2,1)S(1)} %copy.91), channel_id=1, replica_groups=mesh['z'=16,'y_lo'=2,'core'=2,'y_hi'=2,'x'=4] {'core'}, dimensions={2} | all-to-all | bytes 2228224 | tf_op jit(solution)/shard_map/all_to_all | solution.py:176
  103.4 0.6 reduce_sum.61
  104.1 12.5 %all_to_all.22 = bf16[16,2,1,16,544]{4,3,0,2,1:T(8,128)(2,1)S(1)} all-to-all(bf16[16,2,1,16,544]{4,3,0,2,1:T(8,128)(2,1)S(1)} %copy.92), channel_id=1, replica_groups=mesh['z'=16,'y_lo'=2,'core'=2,'y_hi'=2,'x'=4] {'y_lo'}, dimensions={1} | all-to-all | bytes 1114112 | tf_op jit(solution)/shard_map/all_to_all | solution.py:176
  116.6 0.9 reduce_sum.62
  117.5 11.9 %all-to-all-start.3 = ((bf16[16,1,1,16,544]{4,3,2,1,0:T(8,128)(2,1)}), bf16[16,1,1,16,544]{4,3,2,1,0:T(8,128)(2,1)S(1)}, u32[]{:S(2)}, u32[]{:S(2)}) async-start(bf16[16,1,1,16,544]{4,3,2,1,0:T(8,128)(2,1)} %bitcast.58), calls=%async_computation.3 | async-start | bytes 655360 | tf_op jit(solution)/shard_map/all_to_all | solution.py:176
  129.5 0.3 fusion.54
  130.0 0.4 convolution_add_fusion.1
  130.4 0.5 copy-done.9
  130.9 0.3 fusion.3
  131.3 1.2 constant_dynamic-slice_fusion.7
  132.5 2.8 %collective-permute-start.21 = (bf16[256,128]{1,0:T(8,128)(2,1)S(1)}, bf16[256,128]{1,0:T(8,128)(2,1)S(1)}, u32[]{:S(2)}, u32[]{:S(2)}) collective-permute-start(bf16[256,128]{1,0:T(8,128)(2,1)S(1)} %bitcast.217), channel_id=1, source_target_pairs={{0,1},{1,2},{2,3},{3,4},{4,5},{5,6},{6,7},{7,0},{8,9},{9,10},{10,1... | collective-permute-start | bytes 196616 | tf_op jit(solution)/shard_map/ppermute | solution.py:190
  135.3 6.7 %collective-permute-start.15 = (bf16[256,128]{1,0:T(8,128)(2,1)S(1)}, bf16[256,128]{1,0:T(8,128)(2,1)S(1)}, u32[]{:S(2)}, u32[]{:S(2)}) collective-permute-start(bf16[256,128]{1,0:T(8,128)(2,1)S(1)} %bitcast.215), channel_id=1, source_target_pairs={{0,7},{1,0},{2,1},{3,2},{4,3},{5,4},{6,5},{7,6},{8,15},{9,8},{10,9... | collective-permute-start | bytes 196616 | tf_op jit(solution)/shard_map/ppermute | solution.py:190
  142.1 1.9 %collective-permute-start.16 = (bf16[256,128]{1,0:T(8,128)(2,1)S(1)}, bf16[256,128]{1,0:T(8,128)(2,1)S(1)}, u32[]{:S(2)}, u32[]{:S(2)}) collective-permute-start(bf16[256,128]{1,0:T(8,128)(2,1)S(1)} %bitcast.218), channel_id=1, source_target_pairs={{0,6},{1,7},{2,0},{3,1},{4,2},{5,3},{6,4},{7,5},{8,14},{9,15},{10,... | collective-permute-start | bytes 196616 | tf_op jit(solution)/shard_map/ppermute | solution.py:190
  144.1 2.8 %collective-permute-start.17 = (bf16[256,128]{1,0:T(8,128)(2,1)S(1)}, bf16[256,128]{1,0:T(8,128)(2,1)S(1)}, u32[]{:S(2)}, u32[]{:S(2)}) collective-permute-start(bf16[256,128]{1,0:T(8,128)(2,1)S(1)} %bitcast.216), channel_id=1, source_target_pairs={{0,5},{1,6},{2,7},{3,0},{4,1},{5,2},{6,3},{7,4},{8,13},{9,14},{10,... | collective-permute-start | bytes 196616 | tf_op jit(solution)/shard_map/ppermute | solution.py:190
  146.8 4.9 %collective-permute-start.18 = (bf16[256,128]{1,0:T(8,128)(2,1)S(1)}, bf16[256,128]{1,0:T(8,128)(2,1)S(1)}, u32[]{:S(2)}, u32[]{:S(2)}) collective-permute-start(bf16[256,128]{1,0:T(8,128)(2,1)S(1)} %bitcast.214), channel_id=1, source_target_pairs={{0,4},{1,5},{2,6},{3,7},{4,0},{5,1},{6,2},{7,3},{8,12},{9,13},{10,... | collective-permute-start | bytes 196616 | tf_op jit(solution)/shard_map/ppermute | solution.py:190
  151.7 1.9 %collective-permute-start.19 = (bf16[256,128]{1,0:T(8,128)(2,1)S(1)}, bf16[256,128]{1,0:T(8,128)(2,1)S(1)}, u32[]{:S(2)}, u32[]{:S(2)}) collective-permute-start(bf16[256,128]{1,0:T(8,128)(2,1)S(1)} %bitcast.213), channel_id=1, source_target_pairs={{0,3},{1,4},{2,5},{3,6},{4,7},{5,0},{6,1},{7,2},{8,11},{9,12},{10,... | collective-permute-start | bytes 196616 | tf_op jit(solution)/shard_map/ppermute | solution.py:190
  153.7 6.6 %collective-permute-start.20 = (bf16[256,128]{1,0:T(8,128)(2,1)S(1)}, bf16[256,128]{1,0:T(8,128)(2,1)S(1)}, u32[]{:S(2)}, u32[]{:S(2)}) collective-permute-start(bf16[256,128]{1,0:T(8,128)(2,1)S(1)} %bitcast.212), channel_id=1, source_target_pairs={{0,2},{1,3},{2,4},{3,5},{4,6},{5,7},{6,0},{7,1},{8,10},{9,11},{10,... | collective-permute-start | bytes 196616 | tf_op jit(solution)/shard_map/ppermute | solution.py:190
  160.3 4.6 %collective-permute-done.20 = bf16[256,128]{1,0:T(8,128)(2,1)S(1)} collective-permute-done((bf16[256,128]{1,0:T(8,128)(2,1)S(1)}, bf16[256,128]{1,0:T(8,128)(2,1)S(1)}, u32[]{:S(2)}, u32[]{:S(2)}) %collective-permute-start.20) | collective-permute-done | bytes 65568 | tf_op jit(solution)/shard_map/ppermute | solution.py:190
  164.9 0.7 fusion.42
  165.6 0.6 slice.28
  166.2 0.6 fusion.51
  (76 shorter events, 2.9 us)
Async XLA Ops:
  0.6 96.7 %copy-start = (bf16[256,1024]{1,0:T(8,128)(2,1)S(1)}, bf16[256,1024]{1,0:T(8,128)(2,1)}, u32[]{:S(2)}) copy-start(bf16[256,1024]{1,0:T(8,128)(2,1)} %param.11) | copy-start | bytes 1572868
  0.6 4.6 %copy-start.6 = (bf16[256,256]{1,0:T(8,128)(2,1)S(1)}, bf16[256,256]{1,0:T(8,128)(2,1)}, u32[]{:S(2)}) copy-start(bf16[256,256]{1,0:T(8,128)(2,1)} %param.13) | copy-start | bytes 393220
  0.7 4.7 %copy-start.7 = (bf16[256,256]{1,0:T(8,128)(2,1)S(1)}, bf16[256,256]{1,0:T(8,128)(2,1)}, u32[]{:S(2)}) copy-start(bf16[256,256]{1,0:T(8,128)(2,1)} %param.14) | copy-start | bytes 393220
  0.7 4.8 %copy-start.1 = (bf16[256,128]{1,0:T(8,128)(2,1)S(1)}, bf16[256,128]{1,0:T(8,128)(2,1)}, u32[]{:S(2)}) copy-start(bf16[256,128]{1,0:T(8,128)(2,1)} %param.16) | copy-start | bytes 196612
  0.7 4.8 %copy-start.2 = (bf16[256,128]{1,0:T(8,128)(2,1)S(1)}, bf16[256,128]{1,0:T(8,128)(2,1)}, u32[]{:S(2)}) copy-start(bf16[256,128]{1,0:T(8,128)(2,1)} %param.15) | copy-start | bytes 196612
  0.7 5.0 %copy-start.4 = (f32[1,4,128,64]{2,3,1,0:T(8,128)S(1)}, f32[1,4,128,64]{2,3,1,0:T(8,128)}, u32[]{:S(2)}) copy-start(f32[1,4,128,64]{2,3,1,0:T(8,128)} %param.18) | copy-start | bytes 393220
  3.1 3.1 %collective-permute-start.1 = (f32[4]{0:T(128)S(1)}, f32[4]{0:T(128)S(1)}, u32[]{:S(2)}, u32[]{:S(2)}) collective-permute-start(f32[4]{0:T(128)S(1)} %fusion.50), channel_id=1, source_target_pairs={{0,8},{8,0},{1,9},{9,1},{2,10},{10,2},{3,11},{11,3},{4,12},{12,4},... | collective-permute-start | bytes 56 | tf_op jit(solution)/shard_map/ppermute | solution.py:23
  5.3 3.6 %copy-start.8 = (bf16[256,256]{1,0:T(8,128)(2,1)S(1)}, bf16[256,256]{1,0:T(8,128)(2,1)}, u32[]{:S(2)}) copy-start(bf16[256,256]{1,0:T(8,128)(2,1)} %param.12) | copy-start | bytes 393220
  6.4 3.3 %collective-permute-start = (f32[4,128,64]{1,2,0:T(8,128)S(1)}, f32[4,128,64]{1,2,0:T(8,128)S(1)}, u32[]{:S(2)}, u32[]{:S(2)}) collective-permute-start(f32[4,128,64]{1,2,0:T(8,128)S(1)} %fusion.13), channel_id=1, source_target_pairs={{0,8},{8,0},{1,9},{9,1},{2,10},{10,2},{3,11},{11,3},{4,12},{12,4},... | collective-permute-start | bytes 393224 | tf_op jit(solution)/shard_map/ppermute | solution.py:23
  9.9 10.5 %collective-permute-start.2 = (f32[4,128,64]{1,2,0:T(8,128)S(1)}, f32[4,128,64]{1,2,0:T(8,128)S(1)}, u32[]{:S(2)}, u32[]{:S(2)}) collective-permute-start(f32[4,128,64]{1,2,0:T(8,128)S(1)} %add_select_fusion), channel_id=1, source_target_pairs={{0,16},{16,0},{1,17},{17,1},{2,18},{18,2},{3,19},{19,3},{4,20},{20... | collective-permute-start | bytes 393224 | tf_op jit(solution)/shard_map/ppermute | solution.py:23
  14.4 5.5 %collective-permute-start.3 = (f32[4]{0:T(128)S(1)}, f32[4]{0:T(128)S(1)}, u32[]{:S(2)}, u32[]{:S(2)}) collective-permute-start(f32[4]{0:T(128)S(1)} %get-tuple-element.51), channel_id=1, source_target_pairs={{0,16},{16,0},{1,17},{17,1},{2,18},{18,2},{3,19},{19,3},{4,20},{20... | collective-permute-start | bytes 56 | tf_op jit(solution)/shard_map/ppermute | solution.py:23
  21.7 14.0 %collective-permute-start.6 = (f32[128,64]{0,1:T(8,128)S(1)}, f32[128,64]{0,1:T(8,128)S(1)}, u32[]{:S(2)}, u32[]{:S(2)}) collective-permute-start(f32[128,64]{0,1:T(8,128)S(1)} %select_bitcast_fusion), channel_id=1, source_target_pairs={{64,0},{96,32},{128,64},{160,96},{192,128},{224,160},{256,192},{28... | collective-permute-start | bytes 98312 | tf_op jit(solution)/shard_map/ppermute | solution.py:28
  23.0 12.7 %collective-permute-start.4 = (f32[128,64]{0,1:T(8,128)S(1)}, f32[128,64]{0,1:T(8,128)S(1)}, u32[]{:S(2)}, u32[]{:S(2)}) collective-permute-start(f32[128,64]{0,1:T(8,128)S(1)} %select_bitcast_fusion), channel_id=1, source_target_pairs={{32,0},{64,32},{96,64},{128,96},{160,128},{192,160},{224,192},{256... | collective-permute-start | bytes 98312 | tf_op jit(solution)/shard_map/ppermute | solution.py:28
  29.4 5.6 %collective-permute-start.5 = (f32[]{:T(128)}, f32[]{:T(128)}, u32[]{:S(2)}, u32[]{:S(2)}) collective-permute-start(f32[]{:T(128)} %bitcast.34), channel_id=1, source_target_pairs={{32,0},{64,32},{96,64},{128,96},{160,128},{192,160},{224,192},{256... | collective-permute-start | bytes 20 | tf_op jit(solution)/shard_map/ppermute | solution.py:28
  35.7 11.6 %collective-permute-start.8 = (f32[128,64]{0,1:T(8,128)S(1)}, f32[128,64]{0,1:T(8,128)S(1)}, u32[]{:S(2)}, u32[]{:S(2)}) collective-permute-start(f32[128,64]{0,1:T(8,128)S(1)} %multiply_add_fusion), channel_id=1, source_target_pairs={{64,0},{96,32},{128,64},{160,96},{192,128},{224,160},{256,192},{28... | collective-permute-start | bytes 98312 | tf_op jit(solution)/shard_map/ppermute | solution.py:28
  37.9 8.8 %collective-permute-start.7 = (f32[]{:T(128)}, f32[]{:T(128)}, u32[]{:S(2)}, u32[]{:S(2)}) collective-permute-start(f32[]{:T(128)} %bitcast.34), channel_id=1, source_target_pairs={{64,0},{96,32},{128,64},{160,96},{192,128},{224,160},{256,192},{28... | collective-permute-start | bytes 20 | tf_op jit(solution)/shard_map/ppermute | solution.py:28
  47.4 10.3 %collective-permute-start.10 = (f32[128,64]{0,1:T(8,128)S(1)}, f32[128,64]{0,1:T(8,128)S(1)}, u32[]{:S(2)}, u32[]{:S(2)}) collective-permute-start(f32[128,64]{0,1:T(8,128)S(1)} %add_select_fusion.3), channel_id=1, source_target_pairs={{128,0},{160,32},{192,64},{224,96},{256,128},{288,160},{320,192},{... | collective-permute-start | bytes 98312 | tf_op jit(solution)/shard_map/ppermute | solution.py:28
  49.1 7.5 %collective-permute-start.9 = (f32[]{:T(128)}, f32[]{:T(128)}, u32[]{:S(2)}, u32[]{:S(2)}) collective-permute-start(f32[]{:T(128)} %mul.306), channel_id=1, source_target_pairs={{64,0},{96,32},{128,64},{160,96},{192,128},{224,160},{256,192},{28... | collective-permute-start | bytes 20 | tf_op jit(solution)/shard_map/ppermute | solution.py:28
  57.6 14.5 %collective-permute-start.12 = (f32[128,64]{0,1:T(8,128)S(1)}, f32[128,64]{0,1:T(8,128)S(1)}, u32[]{:S(2)}, u32[]{:S(2)}) collective-permute-start(f32[128,64]{0,1:T(8,128)S(1)} %add_select_fusion.2), channel_id=1, source_target_pairs={{256,0},{288,32},{320,64},{352,96},{384,128},{416,160},{448,192},{... | collective-permute-start | bytes 98312 | tf_op jit(solution)/shard_map/ppermute | solution.py:28
  59.2 9.6 %collective-permute-start.11 = (f32[]{:T(128)}, f32[]{:T(128)}, u32[]{:S(2)}, u32[]{:S(2)}) collective-permute-start(f32[]{:T(128)} %select_n.187), channel_id=1, source_target_pairs={{128,0},{160,32},{192,64},{224,96},{256,128},{288,160},{320,192},{... | collective-permute-start | bytes 20 | tf_op jit(solution)/shard_map/ppermute | solution.py:28
  72.2 3.1 %collective-permute-start.13 = (f32[128,64]{0,1:T(8,128)S(1)}, f32[128,64]{0,1:T(8,128)S(1)}, u32[]{:S(2)}, u32[]{:S(2)}) collective-permute-start(f32[128,64]{0,1:T(8,128)S(1)} %add_select_fusion.1), channel_id=1, source_target_pairs={{0,8},{8,0},{1,9},{9,1},{2,10},{10,2},{3,11},{11,3},{4,12},{12,4},... | collective-permute-start | bytes 98312 | tf_op jit(solution)/shard_map/ppermute | solution.py:23
  75.3 6.7 %collective-permute-start.14 = (f32[2,128,64]{1,2,0:T(8,128)S(1)}, f32[2,128,64]{1,2,0:T(8,128)S(1)}, u32[]{:S(2)}, u32[]{:S(2)}) collective-permute-start(f32[2,128,64]{1,2,0:T(8,128)S(1)} %maximum_select_fusion.1), channel_id=1, source_target_pairs={{0,16},{16,0},{1,17},{17,1},{2,18},{18,2},{3,19},{19,3},{4,20},{20... | collective-permute-start | bytes 196616 | tf_op jit(solution)/shard_map/ppermute | solution.py:23
  83.2 14.1 %all-to-all-start = ((f32[256,8,32]{0,2,1:T(8,128)}), f32[256,8,32]{0,2,1:T(8,128)S(1)}, u32[]{:S(2)}, u32[]{:S(2)}) async-start(f32[256,8,32]{0,2,1:T(8,128)} %pad_maximum_fusion), calls=%async_computation | async-start | bytes 524288 | tf_op jit(solution)/shard_map/all_to_all | solution.py:176
  104.1 25.4 %copy-start.3 = (bf16[1024,256]{1,0:T(8,128)(2,1)S(1)}, bf16[1024,256]{1,0:T(8,128)(2,1)}, u32[]{:S(2)}) copy-start(bf16[1024,256]{1,0:T(8,128)(2,1)} %param.19) | copy-start | bytes 1572868
  117.5 12.5 %copy-start.5 = (bf16[1024,256]{1,0:T(8,128)(2,1)S(1)}, bf16[1024,256]{1,0:T(8,128)(2,1)}, u32[]{:S(2)}) copy-start(bf16[1024,256]{1,0:T(8,128)(2,1)} %param.20) | copy-start | bytes 1572868
  117.5 48.0 %all-to-all-start.3 = ((bf16[16,1,1,16,544]{4,3,2,1,0:T(8,128)(2,1)}), bf16[16,1,1,16,544]{4,3,2,1,0:T(8,128)(2,1)S(1)}, u32[]{:S(2)}, u32[]{:S(2)}) async-start(bf16[16,1,1,16,544]{4,3,2,1,0:T(8,128)(2,1)} %bitcast.58), calls=%async_computation.3 | async-start | bytes 655360 | tf_op jit(solution)/shard_map/all_to_all | solution.py:176
  130.0 0.8 copy-start.9
  132.5 19.2 %collective-permute-start.21 = (bf16[256,128]{1,0:T(8,128)(2,1)S(1)}, bf16[256,128]{1,0:T(8,128)(2,1)S(1)}, u32[]{:S(2)}, u32[]{:S(2)}) collective-permute-start(bf16[256,128]{1,0:T(8,128)(2,1)S(1)} %bitcast.217), channel_id=1, source_target_pairs={{0,1},{1,2},{2,3},{3,4},{4,5},{5,6},{6,7},{7,0},{8,9},{9,10},{10,1... | collective-permute-start | bytes 196616 | tf_op jit(solution)/shard_map/ppermute | solution.py:190
  135.3 18.3 %collective-permute-start.15 = (bf16[256,128]{1,0:T(8,128)(2,1)S(1)}, bf16[256,128]{1,0:T(8,128)(2,1)S(1)}, u32[]{:S(2)}, u32[]{:S(2)}) collective-permute-start(bf16[256,128]{1,0:T(8,128)(2,1)S(1)} %bitcast.215), channel_id=1, source_target_pairs={{0,7},{1,0},{2,1},{3,2},{4,3},{5,4},{6,5},{7,6},{8,15},{9,8},{10,9... | collective-permute-start | bytes 196616 | tf_op jit(solution)/shard_map/ppermute | solution.py:190
  142.1 18.1 %collective-permute-start.16 = (bf16[256,128]{1,0:T(8,128)(2,1)S(1)}, bf16[256,128]{1,0:T(8,128)(2,1)S(1)}, u32[]{:S(2)}, u32[]{:S(2)}) collective-permute-start(bf16[256,128]{1,0:T(8,128)(2,1)S(1)} %bitcast.218), channel_id=1, source_target_pairs={{0,6},{1,7},{2,0},{3,1},{4,2},{5,3},{6,4},{7,5},{8,14},{9,15},{10,... | collective-permute-start | bytes 196616 | tf_op jit(solution)/shard_map/ppermute | solution.py:190
  144.1 16.2 %collective-permute-start.17 = (bf16[256,128]{1,0:T(8,128)(2,1)S(1)}, bf16[256,128]{1,0:T(8,128)(2,1)S(1)}, u32[]{:S(2)}, u32[]{:S(2)}) collective-permute-start(bf16[256,128]{1,0:T(8,128)(2,1)S(1)} %bitcast.216), channel_id=1, source_target_pairs={{0,5},{1,6},{2,7},{3,0},{4,1},{5,2},{6,3},{7,4},{8,13},{9,14},{10,... | collective-permute-start | bytes 196616 | tf_op jit(solution)/shard_map/ppermute | solution.py:190
  146.8 13.4 %collective-permute-start.18 = (bf16[256,128]{1,0:T(8,128)(2,1)S(1)}, bf16[256,128]{1,0:T(8,128)(2,1)S(1)}, u32[]{:S(2)}, u32[]{:S(2)}) collective-permute-start(bf16[256,128]{1,0:T(8,128)(2,1)S(1)} %bitcast.214), channel_id=1, source_target_pairs={{0,4},{1,5},{2,6},{3,7},{4,0},{5,1},{6,2},{7,3},{8,12},{9,13},{10,... | collective-permute-start | bytes 196616 | tf_op jit(solution)/shard_map/ppermute | solution.py:190
  151.7 8.6 %collective-permute-start.19 = (bf16[256,128]{1,0:T(8,128)(2,1)S(1)}, bf16[256,128]{1,0:T(8,128)(2,1)S(1)}, u32[]{:S(2)}, u32[]{:S(2)}) collective-permute-start(bf16[256,128]{1,0:T(8,128)(2,1)S(1)} %bitcast.213), channel_id=1, source_target_pairs={{0,3},{1,4},{2,5},{3,6},{4,7},{5,0},{6,1},{7,2},{8,11},{9,12},{10,... | collective-permute-start | bytes 196616 | tf_op jit(solution)/shard_map/ppermute | solution.py:190
  153.7 11.2 %collective-permute-start.20 = (bf16[256,128]{1,0:T(8,128)(2,1)S(1)}, bf16[256,128]{1,0:T(8,128)(2,1)S(1)}, u32[]{:S(2)}, u32[]{:S(2)}) collective-permute-start(bf16[256,128]{1,0:T(8,128)(2,1)S(1)} %bitcast.212), channel_id=1, source_target_pairs={{0,2},{1,3},{2,4},{3,5},{4,6},{5,7},{6,0},{7,1},{8,10},{9,11},{10,... | collective-permute-start | bytes 196616 | tf_op jit(solution)/shard_map/ppermute | solution.py:190

commit v6 on v5

--- a/solution.py
+++ b/solution.py
@@ -19,13 +19,27 @@
     return jax.tree.map(lambda a, b: jnp.where(flag, a, b), first, second)
 
 
+def packed(pair):
+    rows = jnp.broadcast_to(pair[0][..., None, None], pair[0].shape + (8, pair[1].shape[-1]))
+    return jnp.concatenate([pair[1], rows], axis=-2)
+
+
+def unpacked(block):
+    return (block[..., -8, 0], block[..., :-8, :])
+
+
+def moved(tree, axis, pairs):
+    if isinstance(tree, tuple):
+        return unpacked(lax.ppermute(packed(tree), axis, pairs))
+    return lax.ppermute(tree, axis, pairs)
+
+
 def swap(tree, axis):
-    return jax.tree.map(lambda a: lax.ppermute(a, axis, [(0, 1), (1, 0)]), tree)
+    return moved(tree, axis, [(0, 1), (1, 0)])
 
 
 def shift(tree, axis, step):
-    pairs = [(source, source - step) for source in range(step, lax.axis_size(axis))]
-    return jax.tree.map(lambda a: lax.ppermute(a, axis, pairs), tree)
+    return moved(tree, axis, [(source, source - step) for source in range(step, lax.axis_size(axis))])
 
 
 def suffix_scan(part):

time: 168 us -> 172 us (1.024)
  starting transfers between devices: 77.8 us -> 68.6 us
  waiting for transfers between devices: 47.4 us -> 55 us
  local copies, waits for them, and re-layouts: 7.44 us -> 12.2 us
    ppermute x15 -> x9, starting transfers between devices: 33.1 us -> 23.1 us  [the longest x7 17.9 us: moved(): return unpacked(lax.ppermute(packed(tree), axis, pairs))]
    ppermute x15 -> x9, waiting for transfers between devices: 34.3 us -> 42.7 us  [the longest x7 37.6 us: moved(): return unpacked(lax.ppermute(packed(tree), axis, pairs))]
    slice x2 -> x7, local copies, waits for them, and re-layouts: 0.17 us -> 2.24 us  [the longest x5 2.07 us: unpacked(): return (block[..., -8, 0], block[..., :-8, :])]
    unnamed x31 -> x27, local copies, waits for them, and re-layouts: 1 us -> 2.8 us
    select_n x4 -> x6, other arithmetic: 0.12 us -> 1.85 us  [pick(): return jax.tree.map(lambda a, b: jnp.where(flag, a, b), first, second)]
  transfers between devices with their start and end apart: 24 -> 18, of which waited for: 13 -> 10; matrix products, arithmetic and copies ran while one was open for 6% -> 5% of each run, Pallas kernels for 0% -> 0%
where the time goes in v6:
time: 172 us
  starting transfers between devices  68.6 us (40%)
  waiting for transfers between devices  55 us (32%)
  blocking collectives  17.3 us (10%)
  local copies, waits for them, and re-layouts  12.2 us (7%)
  other arithmetic  7.56 us (4%)
  matrix products  6.71 us (4%)
  between operations  4.12 us (2%)
    ppermute x7, waiting for transfers between devices, moved(): return unpacked(lax.ppermute(packed(tree), axis, pairs))  37.6 us
    ppermute x7, starting transfers between devices, spread_sum(): total = total + lax.ppermute(piece, axis, pairs).astype(jnp.float32)  27.5 us
    all_to_all x2, starting transfers between devices, summed_over(): gathered = lax.all_to_all(part, axis, split, split, tiled=True)  18 us
    ppermute x7, starting transfers between devices, moved(): return unpacked(lax.ppermute(packed(tree), axis, pairs))  17.9 us
    all_to_all x2, blocking collectives, summed_over(): gathered = lax.all_to_all(part, axis, split, split, tiled=True)  17.3 us
    all_to_all x2, waiting for transfers between devices, summed_over(): gathered = lax.all_to_all(part, axis, split, split, tiled=True)  7.73 us
    ppermute x2, starting transfers between devices, moved(): return lax.ppermute(tree, axis, pairs)  5.14 us
    ppermute x2, waiting for transfers between devices, moved(): return lax.ppermute(tree, axis, pairs)  5.03 us
  transfers between devices with their start and end apart: 18, of which 10 were waited for; matrix products, arithmetic and copies ran while one was open for 5% of the time, Pallas kernels for 0%

profile of v6, /device:TPU:32, one launch (start us, length us, event | category | flops | bytes accessed | tf_op | source)
XLA Modules:
  0.0 171.5 jit_solution(11456520522366563278)
XLA Ops:
  0.7 0.8 reshape.416
  1.4 1.2 reduce-window.6
  3.2 1.0 copy.88
  4.2 1.0 copy.84
  6.0 1.9 %collective-permute-start = (f32[4,136,64]{2,0,1:T(4,128)S(1)}, f32[4,136,64]{2,0,1:T(4,128)S(1)}, u32[]{:S(2)}, u32[]{:S(2)}) collective-permute-start(f32[4,136,64]{2,0,1:T(4,128)S(1)} %pad_maximum_fusion), channel_id=1, source_target_pairs={{0,8},{8,0},{1,9},{9,1},{2,10},{10,2},{3,11},{11,3},{4,12},{12,4},... | collective-permute-start | bytes 417800 | tf_op jit(solution)/shard_map/ppermute | solution.py:33
  8.5 1.0 collective-permute-done
  10.0 3.5 %collective-permute-start.1 = (f32[4,136,64]{2,0,1:T(4,128)S(1)}, f32[4,136,64]{2,0,1:T(4,128)S(1)}, u32[]{:S(2)}, u32[]{:S(2)}) collective-permute-start(f32[4,136,64]{2,0,1:T(4,128)S(1)} %pad_maximum_fusion.1), channel_id=1, source_target_pairs={{0,16},{16,0},{1,17},{17,1},{2,18},{18,2},{3,19},{19,3},{4,20},{20... | collective-permute-start | bytes 417800 | tf_op jit(solution)/shard_map/ppermute | solution.py:33
  13.5 0.6 dynamic-slice.34
  14.1 6.4 %collective-permute-done.1 = f32[4,136,64]{2,0,1:T(4,128)S(1)} collective-permute-done((f32[4,136,64]{2,0,1:T(4,128)S(1)}, f32[4,136,64]{2,0,1:T(4,128)S(1)}, u32[]{:S(2)}, u32[]{:S(2)}) %collective-permute-start.1) | collective-permute-done | bytes 139296 | tf_op jit(solution)/shard_map/ppermute | solution.py:33
  20.7 0.6 dynamic-slice.35
  21.3 0.6 dynamic_slice.31
  21.9 1.5 broadcast_select_fusion
  23.4 0.7 concatenate.38
  24.1 1.3 collective-permute-start.3
  25.4 7.4 %collective-permute-start.2 = (f32[136,64]{1,0:T(8,128)S(1)}, f32[136,64]{1,0:T(8,128)S(1)}, u32[]{:S(2)}, u32[]{:S(2)}) collective-permute-start(f32[136,64]{1,0:T(8,128)S(1)} %concatenate.38), channel_id=1, source_target_pairs={{32,0},{64,32},{96,64},{128,96},{160,128},{192,160},{224,192},{256... | collective-permute-start | bytes 104456 | tf_op jit(solution)/shard_map/ppermute | solution.py:33
  32.9 0.5 slice.85
  34.1 3.0 %collective-permute-done.2 = f32[136,64]{1,0:T(8,128)S(1)} collective-permute-done((f32[136,64]{1,0:T(8,128)S(1)}, f32[136,64]{1,0:T(8,128)S(1)}, u32[]{:S(2)}, u32[]{:S(2)}) %collective-permute-start.2) | collective-permute-done | bytes 34848 | tf_op jit(solution)/shard_map/ppermute | solution.py:33
  37.1 0.5 slice.83
  38.3 1.3 collective-permute-start.4
  39.6 1.0 fusion.11
  40.6 5.4 %collective-permute-done.4 = f32[136,64]{1,0:T(8,128)S(1)} collective-permute-done((f32[136,64]{1,0:T(8,128)S(1)}, f32[136,64]{1,0:T(8,128)S(1)}, u32[]{:S(2)}, u32[]{:S(2)}) %collective-permute-start.4) | collective-permute-done | bytes 34848 | tf_op jit(solution)/shard_map/ppermute | solution.py:33
  45.9 0.5 slice.87
  47.2 1.3 collective-permute-start.5
  48.5 0.8 fusion.2
  49.3 8.6 %collective-permute-done.5 = f32[136,64]{1,0:T(8,128)S(1)} collective-permute-done((f32[136,64]{1,0:T(8,128)S(1)}, f32[136,64]{1,0:T(8,128)S(1)}, u32[]{:S(2)}, u32[]{:S(2)}) %collective-permute-start.5) | collective-permute-done | bytes 34848 | tf_op jit(solution)/shard_map/ppermute | solution.py:33
  57.9 0.5 slice.89
  59.1 1.3 collective-permute-start.6
  60.4 0.4 convolution_bitcast_fusion.3
  60.8 13.2 %collective-permute-done.6 = f32[136,64]{1,0:T(8,128)S(1)} collective-permute-done((f32[136,64]{1,0:T(8,128)S(1)}, f32[136,64]{1,0:T(8,128)S(1)}, u32[]{:S(2)}, u32[]{:S(2)}) %collective-permute-start.6) | collective-permute-done | bytes 34848 | tf_op jit(solution)/shard_map/ppermute | solution.py:33
  74.0 1.9 %collective-permute-start.7 = (f32[128,64]{1,0:T(8,128)S(1)}, f32[128,64]{1,0:T(8,128)S(1)}, u32[]{:S(2)}, u32[]{:S(2)}) collective-permute-start(f32[128,64]{1,0:T(8,128)S(1)} %add_select_fusion.1), channel_id=1, source_target_pairs={{0,8},{8,0},{1,9},{9,1},{2,10},{10,2},{3,11},{11,3},{4,12},{12,4},... | collective-permute-start | bytes 98312 | tf_op jit(solution)/shard_map/ppermute | solution.py:34
  76.0 0.3 convolution_add_fusion.2
  76.3 0.9 collective-permute-done.7
  77.4 3.2 %collective-permute-start.8 = (f32[2,128,64]{2,0,1:T(2,128)S(1)}, f32[2,128,64]{2,0,1:T(2,128)S(1)}, u32[]{:S(2)}, u32[]{:S(2)}) collective-permute-start(f32[2,128,64]{2,0,1:T(2,128)S(1)} %maximum_select_fusion.1), channel_id=1, source_target_pairs={{0,16},{16,0},{1,17},{17,1},{2,18},{18,2},{3,19},{19,3},{4,20},{20... | collective-permute-start | bytes 196616 | tf_op jit(solution)/shard_map/ppermute | solution.py:34
  80.8 4.1 %collective-permute-done.8 = f32[2,128,64]{2,0,1:T(2,128)S(1)} collective-permute-done((f32[2,128,64]{2,0,1:T(2,128)S(1)}, f32[2,128,64]{2,0,1:T(2,128)S(1)}, u32[]{:S(2)}, u32[]{:S(2)}) %collective-permute-start.8) | collective-permute-done | bytes 65568 | tf_op jit(solution)/shard_map/ppermute | solution.py:34
  84.9 0.4 fusion.33
  85.4 0.3 fusion.5
  85.7 0.4 convolution_bitcast_fusion.4
  86.4 0.7 pad_maximum_fusion.2
  87.1 6.7 %all-to-all-start = ((f32[256,8,32]{0,2,1:T(8,128)}), f32[256,8,32]{0,2,1:T(8,128)S(1)}, u32[]{:S(2)}, u32[]{:S(2)}) async-start(f32[256,8,32]{0,2,1:T(8,128)} %pad_maximum_fusion.2), calls=%async_computation | async-start | bytes 524288 | tf_op jit(solution)/shard_map/all_to_all | solution.py:190
  93.7 1.1 fusion.12
  94.8 7.7 %all-to-all-done = f32[256,8,32]{0,2,1:T(8,128)S(1)} async-done(((f32[256,8,32]{0,2,1:T(8,128)}), f32[256,8,32]{0,2,1:T(8,128)S(1)}, u32[]{:S(2)}, u32[]{:S(2)}) %all-to-all-start) | async-done | bytes 262176 | tf_op jit(solution)/shard_map/all_to_all | solution.py:190
  102.6 0.5 fusion
  103.0 0.7 copy.101
  103.9 4.8 %all_to_all.21 = bf16[16,2,2,16,544]{4,3,1,0,2:T(8,128)(2,1)S(1)} all-to-all(bf16[16,2,2,16,544]{4,3,1,0,2:T(8,128)(2,1)S(1)} %copy.102), channel_id=1, replica_groups=mesh['z'=16,'y_lo'=2,'core'=2,'y_hi'=2,'x'=4] {'core'}, dimensions={2} | all-to-all | bytes 2228224 | tf_op jit(solution)/shard_map/all_to_all | solution.py:190
  108.7 0.6 reduce_sum.61
  109.4 12.5 %all_to_all.22 = bf16[16,2,1,16,544]{4,3,0,2,1:T(8,128)(2,1)S(1)} all-to-all(bf16[16,2,1,16,544]{4,3,0,2,1:T(8,128)(2,1)S(1)} %copy.103), channel_id=1, replica_groups=mesh['z'=16,'y_lo'=2,'core'=2,'y_hi'=2,'x'=4] {'y_lo'}, dimensions={1} | all-to-all | bytes 1114112 | tf_op jit(solution)/shard_map/all_to_all | solution.py:190
  121.9 0.9 reduce_sum.62
  122.8 11.4 %all-to-all-start.3 = ((bf16[16,1,1,16,544]{4,3,2,1,0:T(8,128)(2,1)}), bf16[16,1,1,16,544]{4,3,2,1,0:T(8,128)(2,1)S(1)}, u32[]{:S(2)}, u32[]{:S(2)}) async-start(bf16[16,1,1,16,544]{4,3,2,1,0:T(8,128)(2,1)} %bitcast.59), calls=%async_computation.3 | async-start | bytes 655360 | tf_op jit(solution)/shard_map/all_to_all | solution.py:190
  134.2 0.3 fusion.54
  134.7 0.4 convolution_add_fusion.1
  135.1 0.5 copy-done.7
  135.5 0.3 fusion.3
  135.9 1.2 constant_dynamic-slice_fusion.7
  137.2 2.8 %collective-permute-start.15 = (bf16[256,128]{1,0:T(8,128)(2,1)S(1)}, bf16[256,128]{1,0:T(8,128)(2,1)S(1)}, u32[]{:S(2)}, u32[]{:S(2)}) collective-permute-start(bf16[256,128]{1,0:T(8,128)(2,1)S(1)} %bitcast.190), channel_id=1, source_target_pairs={{0,1},{1,2},{2,3},{3,4},{4,5},{5,6},{6,7},{7,0},{8,9},{9,10},{10,1... | collective-permute-start | bytes 196616 | tf_op jit(solution)/shard_map/ppermute | solution.py:204
  140.0 6.7 %collective-permute-start.9 = (bf16[256,128]{1,0:T(8,128)(2,1)S(1)}, bf16[256,128]{1,0:T(8,128)(2,1)S(1)}, u32[]{:S(2)}, u32[]{:S(2)}) collective-permute-start(bf16[256,128]{1,0:T(8,128)(2,1)S(1)} %bitcast.188), channel_id=1, source_target_pairs={{0,7},{1,0},{2,1},{3,2},{4,3},{5,4},{6,5},{7,6},{8,15},{9,8},{10,9... | collective-permute-start | bytes 196616 | tf_op jit(solution)/shard_map/ppermute | solution.py:204
  146.8 1.9 %collective-permute-start.10 = (bf16[256,128]{1,0:T(8,128)(2,1)S(1)}, bf16[256,128]{1,0:T(8,128)(2,1)S(1)}, u32[]{:S(2)}, u32[]{:S(2)}) collective-permute-start(bf16[256,128]{1,0:T(8,128)(2,1)S(1)} %bitcast.191), channel_id=1, source_target_pairs={{0,6},{1,7},{2,0},{3,1},{4,2},{5,3},{6,4},{7,5},{8,14},{9,15},{10,... | collective-permute-start | bytes 196616 | tf_op jit(solution)/shard_map/ppermute | solution.py:204
  148.7 2.8 %collective-permute-start.11 = (bf16[256,128]{1,0:T(8,128)(2,1)S(1)}, bf16[256,128]{1,0:T(8,128)(2,1)S(1)}, u32[]{:S(2)}, u32[]{:S(2)}) collective-permute-start(bf16[256,128]{1,0:T(8,128)(2,1)S(1)} %bitcast.189), channel_id=1, source_target_pairs={{0,5},{1,6},{2,7},{3,0},{4,1},{5,2},{6,3},{7,4},{8,13},{9,14},{10,... | collective-permute-start | bytes 196616 | tf_op jit(solution)/shard_map/ppermute | solution.py:204
  151.5 4.9 %collective-permute-start.12 = (bf16[256,128]{1,0:T(8,128)(2,1)S(1)}, bf16[256,128]{1,0:T(8,128)(2,1)S(1)}, u32[]{:S(2)}, u32[]{:S(2)}) collective-permute-start(bf16[256,128]{1,0:T(8,128)(2,1)S(1)} %bitcast.187), channel_id=1, source_target_pairs={{0,4},{1,5},{2,6},{3,7},{4,0},{5,1},{6,2},{7,3},{8,12},{9,13},{10,... | collective-permute-start | bytes 196616 | tf_op jit(solution)/shard_map/ppermute | solution.py:204
  156.4 1.9 %collective-permute-start.13 = (bf16[256,128]{1,0:T(8,128)(2,1)S(1)}, bf16[256,128]{1,0:T(8,128)(2,1)S(1)}, u32[]{:S(2)}, u32[]{:S(2)}) collective-permute-start(bf16[256,128]{1,0:T(8,128)(2,1)S(1)} %bitcast.186), channel_id=1, source_target_pairs={{0,3},{1,4},{2,5},{3,6},{4,7},{5,0},{6,1},{7,2},{8,11},{9,12},{10,... | collective-permute-start | bytes 196616 | tf_op jit(solution)/shard_map/ppermute | solution.py:204
  158.3 6.6 %collective-permute-start.14 = (bf16[256,128]{1,0:T(8,128)(2,1)S(1)}, bf16[256,128]{1,0:T(8,128)(2,1)S(1)}, u32[]{:S(2)}, u32[]{:S(2)}) collective-permute-start(bf16[256,128]{1,0:T(8,128)(2,1)S(1)} %bitcast.185), channel_id=1, source_target_pairs={{0,2},{1,3},{2,4},{3,5},{4,6},{5,7},{6,0},{7,1},{8,10},{9,11},{10,... | collective-permute-start | bytes 196616 | tf_op jit(solution)/shard_map/ppermute | solution.py:204
  165.0 4.6 %collective-permute-done.14 = bf16[256,128]{1,0:T(8,128)(2,1)S(1)} collective-permute-done((bf16[256,128]{1,0:T(8,128)(2,1)S(1)}, bf16[256,128]{1,0:T(8,128)(2,1)S(1)}, u32[]{:S(2)}, u32[]{:S(2)}) %collective-permute-start.14) | collective-permute-done | bytes 65568 | tf_op jit(solution)/shard_map/ppermute | solution.py:204
  169.6 0.7 fusion.40
  170.3 0.6 slice.93
  170.9 0.6 fusion.51
  (73 shorter events, 3.9 us)
Async XLA Ops:
  0.6 101.9 %copy-start = (bf16[256,1024]{1,0:T(8,128)(2,1)S(1)}, bf16[256,1024]{1,0:T(8,128)(2,1)}, u32[]{:S(2)}) copy-start(bf16[256,1024]{1,0:T(8,128)(2,1)} %param.11) | copy-start | bytes 1572868
  0.6 4.7 %copy-start.1 = (bf16[256,128]{1,0:T(8,128)(2,1)S(1)}, bf16[256,128]{1,0:T(8,128)(2,1)}, u32[]{:S(2)}) copy-start(bf16[256,128]{1,0:T(8,128)(2,1)} %param.16) | copy-start | bytes 196612
  5.2 2.8 %copy-start.4 = (f32[1,4,128,64]{2,3,1,0:T(8,128)S(1)}, f32[1,4,128,64]{2,3,1,0:T(8,128)}, u32[]{:S(2)}) copy-start(f32[1,4,128,64]{2,3,1,0:T(8,128)} %param.18) | copy-start | bytes 393220
  5.3 3.0 %copy-start.2 = (bf16[256,128]{1,0:T(8,128)(2,1)S(1)}, bf16[256,128]{1,0:T(8,128)(2,1)}, u32[]{:S(2)}) copy-start(bf16[256,128]{1,0:T(8,128)(2,1)} %param.15) | copy-start | bytes 196612
  6.0 3.5 %collective-permute-start = (f32[4,136,64]{2,0,1:T(4,128)S(1)}, f32[4,136,64]{2,0,1:T(4,128)S(1)}, u32[]{:S(2)}, u32[]{:S(2)}) collective-permute-start(f32[4,136,64]{2,0,1:T(4,128)S(1)} %pad_maximum_fusion), channel_id=1, source_target_pairs={{0,8},{8,0},{1,9},{9,1},{2,10},{10,2},{3,11},{11,3},{4,12},{12,4},... | collective-permute-start | bytes 417800 | tf_op jit(solution)/shard_map/ppermute | solution.py:33
  8.2 24.5 %copy-start.6 = (bf16[256,256]{1,0:T(8,128)(2,1)S(1)}, bf16[256,256]{1,0:T(8,128)(2,1)}, u32[]{:S(2)}) copy-start(bf16[256,256]{1,0:T(8,128)(2,1)} %param.12) | copy-start | bytes 393220
  10.0 10.6 %collective-permute-start.1 = (f32[4,136,64]{2,0,1:T(4,128)S(1)}, f32[4,136,64]{2,0,1:T(4,128)S(1)}, u32[]{:S(2)}, u32[]{:S(2)}) collective-permute-start(f32[4,136,64]{2,0,1:T(4,128)S(1)} %pad_maximum_fusion.1), channel_id=1, source_target_pairs={{0,16},{16,0},{1,17},{17,1},{2,18},{18,2},{3,19},{19,3},{4,20},{20... | collective-permute-start | bytes 417800 | tf_op jit(solution)/shard_map/ppermute | solution.py:33
  24.1 8.8 %collective-permute-start.3 = (f32[136,64]{1,0:T(8,128)S(1)}, f32[136,64]{1,0:T(8,128)S(1)}, u32[]{:S(2)}, u32[]{:S(2)}) collective-permute-start(f32[136,64]{1,0:T(8,128)S(1)} %concatenate.38), channel_id=1, source_target_pairs={{64,0},{96,32},{128,64},{160,96},{192,128},{224,160},{256,192},{28... | collective-permute-start | bytes 104456 | tf_op jit(solution)/shard_map/ppermute | solution.py:33
  25.4 11.7 %collective-permute-start.2 = (f32[136,64]{1,0:T(8,128)S(1)}, f32[136,64]{1,0:T(8,128)S(1)}, u32[]{:S(2)}, u32[]{:S(2)}) collective-permute-start(f32[136,64]{1,0:T(8,128)S(1)} %concatenate.38), channel_id=1, source_target_pairs={{32,0},{64,32},{96,64},{128,96},{160,128},{192,160},{224,192},{256... | collective-permute-start | bytes 104456 | tf_op jit(solution)/shard_map/ppermute | solution.py:33
  38.3 7.7 %collective-permute-start.4 = (f32[136,64]{1,0:T(8,128)S(1)}, f32[136,64]{1,0:T(8,128)S(1)}, u32[]{:S(2)}, u32[]{:S(2)}) collective-permute-start(f32[136,64]{1,0:T(8,128)S(1)} %concatenate.39), channel_id=1, source_target_pairs={{64,0},{96,32},{128,64},{160,96},{192,128},{224,160},{256,192},{28... | collective-permute-start | bytes 104456 | tf_op jit(solution)/shard_map/ppermute | solution.py:33
  47.2 10.7 %collective-permute-start.5 = (f32[136,64]{1,0:T(8,128)S(1)}, f32[136,64]{1,0:T(8,128)S(1)}, u32[]{:S(2)}, u32[]{:S(2)}) collective-permute-start(f32[136,64]{1,0:T(8,128)S(1)} %concatenate.40), channel_id=1, source_target_pairs={{128,0},{160,32},{192,64},{224,96},{256,128},{288,160},{320,192},{... | collective-permute-start | bytes 104456 | tf_op jit(solution)/shard_map/ppermute | solution.py:33
  59.1 14.9 %collective-permute-start.6 = (f32[136,64]{1,0:T(8,128)S(1)}, f32[136,64]{1,0:T(8,128)S(1)}, u32[]{:S(2)}, u32[]{:S(2)}) collective-permute-start(f32[136,64]{1,0:T(8,128)S(1)} %concatenate.41), channel_id=1, source_target_pairs={{256,0},{288,32},{320,64},{352,96},{384,128},{416,160},{448,192},{... | collective-permute-start | bytes 104456 | tf_op jit(solution)/shard_map/ppermute | solution.py:33
  74.0 3.1 %collective-permute-start.7 = (f32[128,64]{1,0:T(8,128)S(1)}, f32[128,64]{1,0:T(8,128)S(1)}, u32[]{:S(2)}, u32[]{:S(2)}) collective-permute-start(f32[128,64]{1,0:T(8,128)S(1)} %add_select_fusion.1), channel_id=1, source_target_pairs={{0,8},{8,0},{1,9},{9,1},{2,10},{10,2},{3,11},{11,3},{4,12},{12,4},... | collective-permute-start | bytes 98312 | tf_op jit(solution)/shard_map/ppermute | solution.py:34
  77.4 7.5 %collective-permute-start.8 = (f32[2,128,64]{2,0,1:T(2,128)S(1)}, f32[2,128,64]{2,0,1:T(2,128)S(1)}, u32[]{:S(2)}, u32[]{:S(2)}) collective-permute-start(f32[2,128,64]{2,0,1:T(2,128)S(1)} %maximum_select_fusion.1), channel_id=1, source_target_pairs={{0,16},{16,0},{1,17},{17,1},{2,18},{18,2},{3,19},{19,3},{4,20},{20... | collective-permute-start | bytes 196616 | tf_op jit(solution)/shard_map/ppermute | solution.py:34
  87.1 15.4 %all-to-all-start = ((f32[256,8,32]{0,2,1:T(8,128)}), f32[256,8,32]{0,2,1:T(8,128)S(1)}, u32[]{:S(2)}, u32[]{:S(2)}) async-start(f32[256,8,32]{0,2,1:T(8,128)} %pad_maximum_fusion.2), calls=%async_computation | async-start | bytes 524288 | tf_op jit(solution)/shard_map/all_to_all | solution.py:190
  109.3 24.8 %copy-start.3 = (bf16[1024,256]{1,0:T(8,128)(2,1)S(1)}, bf16[1024,256]{1,0:T(8,128)(2,1)}, u32[]{:S(2)}) copy-start(bf16[1024,256]{1,0:T(8,128)(2,1)} %param.19) | copy-start | bytes 1572868
  122.8 11.9 %copy-start.5 = (bf16[1024,256]{1,0:T(8,128)(2,1)S(1)}, bf16[1024,256]{1,0:T(8,128)(2,1)}, u32[]{:S(2)}) copy-start(bf16[1024,256]{1,0:T(8,128)(2,1)} %param.20) | copy-start | bytes 1572868
  122.8 47.5 %all-to-all-start.3 = ((bf16[16,1,1,16,544]{4,3,2,1,0:T(8,128)(2,1)}), bf16[16,1,1,16,544]{4,3,2,1,0:T(8,128)(2,1)S(1)}, u32[]{:S(2)}, u32[]{:S(2)}) async-start(bf16[16,1,1,16,544]{4,3,2,1,0:T(8,128)(2,1)} %bitcast.59), calls=%async_computation.3 | async-start | bytes 655360 | tf_op jit(solution)/shard_map/all_to_all | solution.py:190
  134.7 0.8 copy-start.7
  137.2 19.2 %collective-permute-start.15 = (bf16[256,128]{1,0:T(8,128)(2,1)S(1)}, bf16[256,128]{1,0:T(8,128)(2,1)S(1)}, u32[]{:S(2)}, u32[]{:S(2)}) collective-permute-start(bf16[256,128]{1,0:T(8,128)(2,1)S(1)} %bitcast.190), channel_id=1, source_target_pairs={{0,1},{1,2},{2,3},{3,4},{4,5},{5,6},{6,7},{7,0},{8,9},{9,10},{10,1... | collective-permute-start | bytes 196616 | tf_op jit(solution)/shard_map/ppermute | solution.py:204
  140.0 18.3 %collective-permute-start.9 = (bf16[256,128]{1,0:T(8,128)(2,1)S(1)}, bf16[256,128]{1,0:T(8,128)(2,1)S(1)}, u32[]{:S(2)}, u32[]{:S(2)}) collective-permute-start(bf16[256,128]{1,0:T(8,128)(2,1)S(1)} %bitcast.188), channel_id=1, source_target_pairs={{0,7},{1,0},{2,1},{3,2},{4,3},{5,4},{6,5},{7,6},{8,15},{9,8},{10,9... | collective-permute-start | bytes 196616 | tf_op jit(solution)/shard_map/ppermute | solution.py:204
  146.8 18.1 %collective-permute-start.10 = (bf16[256,128]{1,0:T(8,128)(2,1)S(1)}, bf16[256,128]{1,0:T(8,128)(2,1)S(1)}, u32[]{:S(2)}, u32[]{:S(2)}) collective-permute-start(bf16[256,128]{1,0:T(8,128)(2,1)S(1)} %bitcast.191), channel_id=1, source_target_pairs={{0,6},{1,7},{2,0},{3,1},{4,2},{5,3},{6,4},{7,5},{8,14},{9,15},{10,... | collective-permute-start | bytes 196616 | tf_op jit(solution)/shard_map/ppermute | solution.py:204
  148.7 16.2 %collective-permute-start.11 = (bf16[256,128]{1,0:T(8,128)(2,1)S(1)}, bf16[256,128]{1,0:T(8,128)(2,1)S(1)}, u32[]{:S(2)}, u32[]{:S(2)}) collective-permute-start(bf16[256,128]{1,0:T(8,128)(2,1)S(1)} %bitcast.189), channel_id=1, source_target_pairs={{0,5},{1,6},{2,7},{3,0},{4,1},{5,2},{6,3},{7,4},{8,13},{9,14},{10,... | collective-permute-start | bytes 196616 | tf_op jit(solution)/shard_map/ppermute | solution.py:204
  151.5 13.4 %collective-permute-start.12 = (bf16[256,128]{1,0:T(8,128)(2,1)S(1)}, bf16[256,128]{1,0:T(8,128)(2,1)S(1)}, u32[]{:S(2)}, u32[]{:S(2)}) collective-permute-start(bf16[256,128]{1,0:T(8,128)(2,1)S(1)} %bitcast.187), channel_id=1, source_target_pairs={{0,4},{1,5},{2,6},{3,7},{4,0},{5,1},{6,2},{7,3},{8,12},{9,13},{10,... | collective-permute-start | bytes 196616 | tf_op jit(solution)/shard_map/ppermute | solution.py:204
  156.4 8.6 %collective-permute-start.13 = (bf16[256,128]{1,0:T(8,128)(2,1)S(1)}, bf16[256,128]{1,0:T(8,128)(2,1)S(1)}, u32[]{:S(2)}, u32[]{:S(2)}) collective-permute-start(bf16[256,128]{1,0:T(8,128)(2,1)S(1)} %bitcast.186), channel_id=1, source_target_pairs={{0,3},{1,4},{2,5},{3,6},{4,7},{5,0},{6,1},{7,2},{8,11},{9,12},{10,... | collective-permute-start | bytes 196616 | tf_op jit(solution)/shard_map/ppermute | solution.py:204
  158.3 11.2 %collective-permute-start.14 = (bf16[256,128]{1,0:T(8,128)(2,1)S(1)}, bf16[256,128]{1,0:T(8,128)(2,1)S(1)}, u32[]{:S(2)}, u32[]{:S(2)}) collective-permute-start(bf16[256,128]{1,0:T(8,128)(2,1)S(1)} %bitcast.185), channel_id=1, source_target_pairs={{0,2},{1,3},{2,4},{3,5},{4,6},{5,7},{6,0},{7,1},{8,10},{9,11},{10,... | collective-permute-start | bytes 196616 | tf_op jit(solution)/shard_map/ppermute | solution.py:204

commit v7 on v6

--- a/solution.py
+++ b/solution.py
@@ -60,13 +60,10 @@
     one = (jnp.ones_like(head[0]), jnp.zeros_like(head[1]))
     z = lax.axis_index(z_axis)
     count = lax.axis_size(z_axis)
-    near = pick(z + 1 < count, shift(head, z_axis, 1), one)
-    far = pick(z + 2 < count, shift(head, z_axis, 2), one)
-    later = join(near, far)
-    step = 2
-    while step < count:
-        later = pick(z + step < count, join(later, shift(later, z_axis, step)), later)
-        step *= 2
+    planes = unpacked(lax.all_gather(packed(head), z_axis))
+    later = one
+    for source in reversed(range(count)):
+        later = pick(source > z, join((planes[0][source], planes[1][source]), later), later)
     mine = later[1]
     theirs = swap(mine, core_axis)
     two = jnp.where(core == 0, jnp.stack([mine, theirs]), jnp.stack([theirs, mine]))

time: 172 us -> 185 us (1.076)
  blocking collectives: 17.3 us -> 56.7 us
  waiting for transfers between devices: 55 us -> 24 us
  other arithmetic: 7.56 us -> 27.5 us
  starting transfers between devices: 68.6 us -> 54.3 us
  between operations: 4.12 us -> 2.24 us
    all_gather x0 -> x1, blocking collectives: none -> 39.4 us  [suffix_scan(): planes = unpacked(lax.all_gather(packed(head), z_axis))]
    ppermute x7 -> x2, waiting for transfers between devices: 37.6 us -> 6.58 us  [moved(): return unpacked(lax.ppermute(packed(tree), axis, pairs))]
    ppermute x7 -> x2, starting transfers between devices: 17.9 us -> 5.4 us  [moved(): return unpacked(lax.ppermute(packed(tree), axis, pairs))]
    select_n x6 -> x5, other arithmetic: 1.85 us -> 11.8 us  [pick(): return jax.tree.map(lambda a, b: jnp.where(flag, a, b), first, second)]
    add x1, other arithmetic: 0.02 us -> 9.52 us  [join(): return (near[0] * far[0], near[1] + near[0][..., None, None] * far[1])]
    unnamed x27 -> x52, local copies, waits for them, and re-layouts: 2.8 us -> 4.95 us
    all_to_all x2, starting transfers between devices: 18 us -> 15.9 us  [summed_over(): gathered = lax.all_to_all(part, axis, split, split, tiled=True)]
    slice x5 -> x1, local copies, waits for them, and re-layouts: 2.07 us -> 0.02 us  [unpacked(): return (block[..., -8, 0], block[..., :-8, :])]
  transfers between devices with their start and end apart: 18 -> 13, of which waited for: 10 -> 5; matrix products, arithmetic and copies ran while one was open for 5% -> 4% of each run, Pallas kernels for 0% -> 0%
where the time goes in v7:
time: 185 us; the launch traced here: 184 us
  blocking collectives  56.7 us (31%)
  starting transfers between devices  54.3 us (29%)
  other arithmetic  27.5 us (15%)
  waiting for transfers between devices  24 us (13%)
  local copies, waits for them, and re-layouts  12.4 us (7%)
  matrix products  6.71 us (4%)
  between operations  2.24 us (1%)
    all_gather x1, blocking collectives, suffix_scan(): planes = unpacked(lax.all_gather(packed(head), z_axis))  39.4 us
    ppermute x7, starting transfers between devices, spread_sum(): total = total + lax.ppermute(piece, axis, pairs).astype(jnp.float32)  27.5 us
    all_to_all x2, blocking collectives, summed_over(): gathered = lax.all_to_all(part, axis, split, split, tiled=True)  17.3 us
    all_to_all x2, starting transfers between devices, summed_over(): gathered = lax.all_to_all(part, axis, split, split, tiled=True)  15.9 us
    select_n x5, other arithmetic, pick(): return jax.tree.map(lambda a, b: jnp.where(flag, a, b), first, second)  11.8 us
    add x1, other arithmetic, join(): return (near[0] * far[0], near[1] + near[0][..., None, None] * far[1])  9.52 us
    all_to_all x2, waiting for transfers between devices, summed_over(): gathered = lax.all_to_all(part, axis, split, split, tiled=True)  7.72 us
    ppermute x2, waiting for transfers between devices, moved(): return unpacked(lax.ppermute(packed(tree), axis, pairs))  6.58 us
  transfers between devices with their start and end apart: 13, of which 5 were waited for; matrix products, arithmetic and copies ran while one was open for 4% of the time, Pallas kernels for 0%

profile of v7, /device:TPU:32, one launch (start us, length us, event | category | flops | bytes accessed | tf_op | source)
XLA Modules:
  0.0 183.8 jit_solution(6783726977128843686)
XLA Ops:
  0.7 0.8 reshape.467
  1.4 1.2 reduce-window.6
  2.9 1.0 copy.122
  3.9 1.0 copy.126
  5.1 0.3 fusion.58
  5.4 0.1 copy.127
  5.5 0.2 fusion.60
  6.0 1.9 %collective-permute-start = (f32[4,136,64]{2,0,1:T(4,128)S(1)}, f32[4,136,64]{2,0,1:T(4,128)S(1)}, u32[]{:S(2)}, u32[]{:S(2)}) collective-permute-start(f32[4,136,64]{2,0,1:T(4,128)S(1)} %pad_maximum_fusion), channel_id=1, source_target_pairs={{0,8},{8,0},{1,9},{9,1},{2,10},{10,2},{3,11},{11,3},{4,12},{12,4},... | collective-permute-start | bytes 417800 | tf_op jit(solution)/shard_map/ppermute | solution.py:33
  8.2 0.2 fusion.67
  8.4 0.3 fusion.68
  8.6 1.0 fusion.11
  9.6 0.8 fusion.2
  10.5 0.4 convolution_bitcast_fusion.3
  10.9 0.6 select_reduce_fusion
  11.6 0.2 add_select_fusion
  11.9 3.5 %collective-permute-start.1 = (f32[4,136,64]{2,0,1:T(4,128)S(1)}, f32[4,136,64]{2,0,1:T(4,128)S(1)}, u32[]{:S(2)}, u32[]{:S(2)}) collective-permute-start(f32[4,136,64]{2,0,1:T(4,128)S(1)} %pad_maximum_fusion.1), channel_id=1, source_target_pairs={{0,16},{16,0},{1,17},{17,1},{2,18},{18,2},{3,19},{19,3},{4,20},{20... | collective-permute-start | bytes 417800 | tf_op jit(solution)/shard_map/ppermute | solution.py:33
  15.4 0.3 convolution_add_fusion.2
  15.7 0.6 dynamic-slice.34
  16.3 6.6 %collective-permute-done.1 = f32[4,136,64]{2,0,1:T(4,128)S(1)} collective-permute-done((f32[4,136,64]{2,0,1:T(4,128)S(1)}, f32[4,136,64]{2,0,1:T(4,128)S(1)}, u32[]{:S(2)}, u32[]{:S(2)}) %collective-permute-start.1) | collective-permute-done | bytes 139296 | tf_op jit(solution)/shard_map/ppermute | solution.py:33
  23.0 0.6 dynamic-slice.35
  23.6 1.5 broadcast_select_fusion
  25.1 0.5 subtract_exponential_fusion
  25.7 0.6 dynamic_slice.31
  26.3 0.6 pad_bitcast_fusion
  26.9 39.4 %all-gather.1 = f32[16,136,64]{1,2,0:T(8,128)S(1)} all-gather(f32[1,136,64]{1,2,0:T(8,128)S(1)} %pad_bitcast_fusion), channel_id=2, replica_groups=mesh['z'=16,'y_lo'=2,'core'=2,'y_hi'=2,'x'=4] {'z'}, dimensions={0}, use_global_device_ids=true | all-gather | bytes 591872 | tf_op jit(solution)/shard_map/all_gather | solution.py:63
  66.4 0.6 fusion.64
  69.3 9.5 %multiply_add_fusion = (f32[1,128,64]{2,1,0:T(8,128)S(1)}, f32[1,128,64]{2,1,0:T(8,128)S(1)}) fusion(f32[1,128,64]{2,1,0:T(8,128)S(1)} %copy.161, f32[]{:T(128)} %bitcast.33, f32[1,128,64]{2,1,0:T(8,128)S(1)} %copy.162, f32[1,128,64]{2,1,0:T(8,128)S(1)} %copy.163, f32[1,128,64]{2,1,0:T(8,128)S(1)} %copy.164, f32[1,128,64]{2,1,0:T(8,128)S(1)} %copy.165, ...), kind=kLoop, calls=%fused_computation.109 | loop fusion | flops 376832 | bytes 589903 | tf_op jit(solution)/shard_map/add | solution.py:15
  78.8 9.5 %fusion.57 = f32[128,64]{1,0:T(8,128)S(1)} fusion(f32[1,128,64]{2,1,0:T(8,128)S(1)} %copy.161, f32[1,128,64]{2,1,0:T(8,128)S(1)} %copy.162, f32[1,128,64]{2,1,0:T(8,128)S(1)} %copy.163, f32[1,128,64]{2,1,0:T(8,128)S(1)} %copy.164, f32[1,128,64]{2,1,0:T(8,128)S(1)} %copy.165, f32[1,128,64]{2,1,0:T(8,128)S(1)} %copy.166, f32[1,128,64]{2,1,0:T(8,128)S(1)} %copy.167, ...), kind=kLoop, calls=%fused_computation.106 | loop fusion | flops 385024 | bytes 557136 | tf_op jit(solution)/shard_map/jit(_where)/select_n | solution.py:19
  88.3 1.9 %collective-permute-start.2 = (f32[128,64]{1,0:T(8,128)S(1)}, f32[128,64]{1,0:T(8,128)S(1)}, u32[]{:S(2)}, u32[]{:S(2)}) collective-permute-start(f32[128,64]{1,0:T(8,128)S(1)} %fusion.57), channel_id=1, source_target_pairs={{0,8},{8,0},{1,9},{9,1},{2,10},{10,2},{3,11},{11,3},{4,12},{12,4},... | collective-permute-start | bytes 98312 | tf_op jit(solution)/shard_map/ppermute | solution.py:34
  90.3 1.2 collective-permute-done.2
  91.5 0.3 maximum_select_fusion.1
  91.8 3.5 %collective-permute-start.3 = (f32[2,128,64]{2,0,1:T(2,128)S(1)}, f32[2,128,64]{2,0,1:T(2,128)S(1)}, u32[]{:S(2)}, u32[]{:S(2)}) collective-permute-start(f32[2,128,64]{2,0,1:T(2,128)S(1)} %maximum_select_fusion.1), channel_id=1, source_target_pairs={{0,16},{16,0},{1,17},{17,1},{2,18},{18,2},{3,19},{19,3},{4,20},{20... | collective-permute-start | bytes 196616 | tf_op jit(solution)/shard_map/ppermute | solution.py:34
  95.4 3.8 %collective-permute-done.3 = f32[2,128,64]{2,0,1:T(2,128)S(1)} collective-permute-done((f32[2,128,64]{2,0,1:T(2,128)S(1)}, f32[2,128,64]{2,0,1:T(2,128)S(1)}, u32[]{:S(2)}, u32[]{:S(2)}) %collective-permute-start.3) | collective-permute-done | bytes 65568 | tf_op jit(solution)/shard_map/ppermute | solution.py:34
  99.2 0.4 fusion.33
  99.7 0.3 fusion.5
  100.0 0.4 convolution_bitcast_fusion.4
  100.4 0.3 convolution_add_fusion.3
  100.7 0.7 pad_maximum_fusion.2
  101.4 6.9 %all-to-all-start = ((f32[256,8,32]{0,2,1:T(8,128)}), f32[256,8,32]{0,2,1:T(8,128)S(1)}, u32[]{:S(2)}, u32[]{:S(2)}) async-start(f32[256,8,32]{0,2,1:T(8,128)} %pad_maximum_fusion.2), calls=%async_computation | async-start | bytes 524288 | tf_op jit(solution)/shard_map/all_to_all | solution.py:187
  108.3 1.1 fusion.12
  109.4 7.7 %all-to-all-done = f32[256,8,32]{0,2,1:T(8,128)S(1)} async-done(((f32[256,8,32]{0,2,1:T(8,128)}), f32[256,8,32]{0,2,1:T(8,128)S(1)}, u32[]{:S(2)}, u32[]{:S(2)}) %all-to-all-start) | async-done | bytes 262176 | tf_op jit(solution)/shard_map/all_to_all | solution.py:187
  117.2 0.5 fusion
  117.6 0.7 copy.158
  118.5 4.8 %all_to_all.21 = bf16[16,2,2,16,544]{4,3,1,0,2:T(8,128)(2,1)S(1)} all-to-all(bf16[16,2,2,16,544]{4,3,1,0,2:T(8,128)(2,1)S(1)} %copy.159), channel_id=1, replica_groups=mesh['z'=16,'y_lo'=2,'core'=2,'y_hi'=2,'x'=4] {'core'}, dimensions={2} | all-to-all | bytes 2228224 | tf_op jit(solution)/shard_map/all_to_all | solution.py:187
  123.3 0.6 reduce_sum.61
  124.0 12.5 %all_to_all.22 = bf16[16,2,1,16,544]{4,3,0,2,1:T(8,128)(2,1)S(1)} all-to-all(bf16[16,2,1,16,544]{4,3,0,2,1:T(8,128)(2,1)S(1)} %copy.160), channel_id=1, replica_groups=mesh['z'=16,'y_lo'=2,'core'=2,'y_hi'=2,'x'=4] {'y_lo'}, dimensions={1} | all-to-all | bytes 1114112 | tf_op jit(solution)/shard_map/all_to_all | solution.py:187
  136.5 0.9 reduce_sum.62
  137.4 9.0 %all-to-all-start.3 = ((bf16[16,1,1,16,544]{4,3,2,1,0:T(8,128)(2,1)}), bf16[16,1,1,16,544]{4,3,2,1,0:T(8,128)(2,1)S(1)}, u32[]{:S(2)}, u32[]{:S(2)}) async-start(bf16[16,1,1,16,544]{4,3,2,1,0:T(8,128)(2,1)} %bitcast.89), calls=%async_computation.3 | async-start | bytes 655360 | tf_op jit(solution)/shard_map/all_to_all | solution.py:187
  146.4 0.4 fusion.69
  147.0 0.4 convolution_add_fusion.1
  147.3 0.5 copy-done.9
  147.8 0.3 fusion.3
  148.2 1.2 constant_dynamic-slice_fusion.7
  149.5 2.8 %collective-permute-start.10 = (bf16[256,128]{1,0:T(8,128)(2,1)S(1)}, bf16[256,128]{1,0:T(8,128)(2,1)S(1)}, u32[]{:S(2)}, u32[]{:S(2)}) collective-permute-start(bf16[256,128]{1,0:T(8,128)(2,1)S(1)} %bitcast.303), channel_id=1, source_target_pairs={{0,1},{1,2},{2,3},{3,4},{4,5},{5,6},{6,7},{7,0},{8,9},{9,10},{10,1... | collective-permute-start | bytes 196616 | tf_op jit(solution)/shard_map/ppermute | solution.py:201
  152.2 6.7 %collective-permute-start.4 = (bf16[256,128]{1,0:T(8,128)(2,1)S(1)}, bf16[256,128]{1,0:T(8,128)(2,1)S(1)}, u32[]{:S(2)}, u32[]{:S(2)}) collective-permute-start(bf16[256,128]{1,0:T(8,128)(2,1)S(1)} %bitcast.301), channel_id=1, source_target_pairs={{0,7},{1,0},{2,1},{3,2},{4,3},{5,4},{6,5},{7,6},{8,15},{9,8},{10,9... | collective-permute-start | bytes 196616 | tf_op jit(solution)/shard_map/ppermute | solution.py:201
  159.0 1.9 %collective-permute-start.5 = (bf16[256,128]{1,0:T(8,128)(2,1)S(1)}, bf16[256,128]{1,0:T(8,128)(2,1)S(1)}, u32[]{:S(2)}, u32[]{:S(2)}) collective-permute-start(bf16[256,128]{1,0:T(8,128)(2,1)S(1)} %bitcast.300), channel_id=1, source_target_pairs={{0,6},{1,7},{2,0},{3,1},{4,2},{5,3},{6,4},{7,5},{8,14},{9,15},{10,... | collective-permute-start | bytes 196616 | tf_op jit(solution)/shard_map/ppermute | solution.py:201
  160.9 2.8 %collective-permute-start.6 = (bf16[256,128]{1,0:T(8,128)(2,1)S(1)}, bf16[256,128]{1,0:T(8,128)(2,1)S(1)}, u32[]{:S(2)}, u32[]{:S(2)}) collective-permute-start(bf16[256,128]{1,0:T(8,128)(2,1)S(1)} %bitcast.302), channel_id=1, source_target_pairs={{0,5},{1,6},{2,7},{3,0},{4,1},{5,2},{6,3},{7,4},{8,13},{9,14},{10,... | collective-permute-start | bytes 196616 | tf_op jit(solution)/shard_map/ppermute | solution.py:201
  163.7 4.9 %collective-permute-start.7 = (bf16[256,128]{1,0:T(8,128)(2,1)S(1)}, bf16[256,128]{1,0:T(8,128)(2,1)S(1)}, u32[]{:S(2)}, u32[]{:S(2)}) collective-permute-start(bf16[256,128]{1,0:T(8,128)(2,1)S(1)} %bitcast.304), channel_id=1, source_target_pairs={{0,4},{1,5},{2,6},{3,7},{4,0},{5,1},{6,2},{7,3},{8,12},{9,13},{10,... | collective-permute-start | bytes 196616 | tf_op jit(solution)/shard_map/ppermute | solution.py:201
  168.6 1.9 %collective-permute-start.8 = (bf16[256,128]{1,0:T(8,128)(2,1)S(1)}, bf16[256,128]{1,0:T(8,128)(2,1)S(1)}, u32[]{:S(2)}, u32[]{:S(2)}) collective-permute-start(bf16[256,128]{1,0:T(8,128)(2,1)S(1)} %bitcast.306), channel_id=1, source_target_pairs={{0,3},{1,4},{2,5},{3,6},{4,7},{5,0},{6,1},{7,2},{8,11},{9,12},{10,... | collective-permute-start | bytes 196616 | tf_op jit(solution)/shard_map/ppermute | solution.py:201
  170.6 6.6 %collective-permute-start.9 = (bf16[256,128]{1,0:T(8,128)(2,1)S(1)}, bf16[256,128]{1,0:T(8,128)(2,1)S(1)}, u32[]{:S(2)}, u32[]{:S(2)}) collective-permute-start(bf16[256,128]{1,0:T(8,128)(2,1)S(1)} %bitcast.305), channel_id=1, source_target_pairs={{0,2},{1,3},{2,4},{3,5},{4,6},{5,7},{6,0},{7,1},{8,10},{9,11},{10,... | collective-permute-start | bytes 196616 | tf_op jit(solution)/shard_map/ppermute | solution.py:201
  177.2 4.6 %collective-permute-done.9 = bf16[256,128]{1,0:T(8,128)(2,1)S(1)} collective-permute-done((bf16[256,128]{1,0:T(8,128)(2,1)S(1)}, bf16[256,128]{1,0:T(8,128)(2,1)S(1)}, u32[]{:S(2)}, u32[]{:S(2)}) %collective-permute-start.9) | collective-permute-done | bytes 65568 | tf_op jit(solution)/shard_map/ppermute | solution.py:201
  181.8 0.7 fusion.40
  182.6 0.6 fusion.66
  183.2 0.6 slice.258
  (83 shorter events, 3.5 us)
Async XLA Ops:
  0.6 116.5 %copy-start = (bf16[256,1024]{1,0:T(8,128)(2,1)S(1)}, bf16[256,1024]{1,0:T(8,128)(2,1)}, u32[]{:S(2)}) copy-start(bf16[256,1024]{1,0:T(8,128)(2,1)} %param.11) | copy-start | bytes 1572868
  0.6 4.4 %copy-start.1 = (bf16[256,128]{1,0:T(8,128)(2,1)S(1)}, bf16[256,128]{1,0:T(8,128)(2,1)}, u32[]{:S(2)}) copy-start(bf16[256,128]{1,0:T(8,128)(2,1)} %param.16) | copy-start | bytes 196612
  5.0 3.0 %copy-start.6 = (bf16[256,256]{1,0:T(8,128)(2,1)S(1)}, bf16[256,256]{1,0:T(8,128)(2,1)}, u32[]{:S(2)}) copy-start(bf16[256,256]{1,0:T(8,128)(2,1)} %param.12) | copy-start | bytes 393220
  5.1 3.1 %copy-start.2 = (bf16[256,128]{1,0:T(8,128)(2,1)S(1)}, bf16[256,128]{1,0:T(8,128)(2,1)}, u32[]{:S(2)}) copy-start(bf16[256,128]{1,0:T(8,128)(2,1)} %param.15) | copy-start | bytes 196612
  5.1 3.3 %copy-start.4 = (f32[1,4,128,64]{2,3,1,0:T(8,128)S(1)}, f32[1,4,128,64]{2,3,1,0:T(8,128)}, u32[]{:S(2)}) copy-start(f32[1,4,128,64]{2,3,1,0:T(8,128)} %param.18) | copy-start | bytes 393220
  6.0 4.9 %collective-permute-start = (f32[4,136,64]{2,0,1:T(4,128)S(1)}, f32[4,136,64]{2,0,1:T(4,128)S(1)}, u32[]{:S(2)}, u32[]{:S(2)}) collective-permute-start(f32[4,136,64]{2,0,1:T(4,128)S(1)} %pad_maximum_fusion), channel_id=1, source_target_pairs={{0,8},{8,0},{1,9},{9,1},{2,10},{10,2},{3,11},{11,3},{4,12},{12,4},... | collective-permute-start | bytes 417800 | tf_op jit(solution)/shard_map/ppermute | solution.py:33
  11.9 11.0 %collective-permute-start.1 = (f32[4,136,64]{2,0,1:T(4,128)S(1)}, f32[4,136,64]{2,0,1:T(4,128)S(1)}, u32[]{:S(2)}, u32[]{:S(2)}) collective-permute-start(f32[4,136,64]{2,0,1:T(4,128)S(1)} %pad_maximum_fusion.1), channel_id=1, source_target_pairs={{0,16},{16,0},{1,17},{17,1},{2,18},{18,2},{3,19},{19,3},{4,20},{20... | collective-permute-start | bytes 417800 | tf_op jit(solution)/shard_map/ppermute | solution.py:33
  69.3 29.9 %copy-start.10 = (f32[4]{0:T(128)S(1)}, f32[4]{0:T(128)}, u32[]{:S(2)}) copy-start(f32[4]{0:T(128)} %get-tuple-element.88) | copy-start | bytes 52
  69.3 29.9 %copy-start.11 = (f32[4]{0:T(128)S(1)}, f32[4]{0:T(128)}, u32[]{:S(2)}) copy-start(f32[4]{0:T(128)} %get-tuple-element.24) | copy-start | bytes 52
  88.3 3.1 %collective-permute-start.2 = (f32[128,64]{1,0:T(8,128)S(1)}, f32[128,64]{1,0:T(8,128)S(1)}, u32[]{:S(2)}, u32[]{:S(2)}) collective-permute-start(f32[128,64]{1,0:T(8,128)S(1)} %fusion.57), channel_id=1, source_target_pairs={{0,8},{8,0},{1,9},{9,1},{2,10},{10,2},{3,11},{11,3},{4,12},{12,4},... | collective-permute-start | bytes 98312 | tf_op jit(solution)/shard_map/ppermute | solution.py:34
  91.8 7.5 %collective-permute-start.3 = (f32[2,128,64]{2,0,1:T(2,128)S(1)}, f32[2,128,64]{2,0,1:T(2,128)S(1)}, u32[]{:S(2)}, u32[]{:S(2)}) collective-permute-start(f32[2,128,64]{2,0,1:T(2,128)S(1)} %maximum_select_fusion.1), channel_id=1, source_target_pairs={{0,16},{16,0},{1,17},{17,1},{2,18},{18,2},{3,19},{19,3},{4,20},{20... | collective-permute-start | bytes 196616 | tf_op jit(solution)/shard_map/ppermute | solution.py:34
  101.4 15.7 %all-to-all-start = ((f32[256,8,32]{0,2,1:T(8,128)}), f32[256,8,32]{0,2,1:T(8,128)S(1)}, u32[]{:S(2)}, u32[]{:S(2)}) async-start(f32[256,8,32]{0,2,1:T(8,128)} %pad_maximum_fusion.2), calls=%async_computation | async-start | bytes 524288 | tf_op jit(solution)/shard_map/all_to_all | solution.py:187
  109.4 7.8 %copy-start.7 = (bf16[1,256,4,64]{1,3,2,0:T(8,128)(2,1)}, bf16[1,256,4,64]{1,3,2,0:T(8,128)(2,1)S(1)}, u32[]{:S(2)}) copy-start(bf16[1,256,4,64]{1,3,2,0:T(8,128)(2,1)S(1)} %fusion.12) | copy-start | bytes 393220
  124.0 22.4 %copy-start.3 = (bf16[1024,256]{1,0:T(8,128)(2,1)S(1)}, bf16[1024,256]{1,0:T(8,128)(2,1)}, u32[]{:S(2)}) copy-start(bf16[1024,256]{1,0:T(8,128)(2,1)} %param.19) | copy-start | bytes 1572868
  137.4 9.5 %copy-start.5 = (bf16[1024,256]{1,0:T(8,128)(2,1)S(1)}, bf16[1024,256]{1,0:T(8,128)(2,1)}, u32[]{:S(2)}) copy-start(bf16[1024,256]{1,0:T(8,128)(2,1)} %param.20) | copy-start | bytes 1572868
  137.4 9.5 %copy-start.8 = (bf16[1,256,4,64]{1,3,2,0:T(8,128)(2,1)S(1)}, bf16[1,256,4,64]{1,3,2,0:T(8,128)(2,1)}, u32[]{:S(2)}) copy-start(bf16[1,256,4,64]{1,3,2,0:T(8,128)(2,1)} %copy-done.7) | copy-start | bytes 393220
  137.4 45.1 %all-to-all-start.3 = ((bf16[16,1,1,16,544]{4,3,2,1,0:T(8,128)(2,1)}), bf16[16,1,1,16,544]{4,3,2,1,0:T(8,128)(2,1)S(1)}, u32[]{:S(2)}, u32[]{:S(2)}) async-start(bf16[16,1,1,16,544]{4,3,2,1,0:T(8,128)(2,1)} %bitcast.89), calls=%async_computation.3 | async-start | bytes 655360 | tf_op jit(solution)/shard_map/all_to_all | solution.py:187
  146.9 0.8 copy-start.9
  149.5 19.2 %collective-permute-start.10 = (bf16[256,128]{1,0:T(8,128)(2,1)S(1)}, bf16[256,128]{1,0:T(8,128)(2,1)S(1)}, u32[]{:S(2)}, u32[]{:S(2)}) collective-permute-start(bf16[256,128]{1,0:T(8,128)(2,1)S(1)} %bitcast.303), channel_id=1, source_target_pairs={{0,1},{1,2},{2,3},{3,4},{4,5},{5,6},{6,7},{7,0},{8,9},{9,10},{10,1... | collective-permute-start | bytes 196616 | tf_op jit(solution)/shard_map/ppermute | solution.py:201
  152.2 18.3 %collective-permute-start.4 = (bf16[256,128]{1,0:T(8,128)(2,1)S(1)}, bf16[256,128]{1,0:T(8,128)(2,1)S(1)}, u32[]{:S(2)}, u32[]{:S(2)}) collective-permute-start(bf16[256,128]{1,0:T(8,128)(2,1)S(1)} %bitcast.301), channel_id=1, source_target_pairs={{0,7},{1,0},{2,1},{3,2},{4,3},{5,4},{6,5},{7,6},{8,15},{9,8},{10,9... | collective-permute-start | bytes 196616 | tf_op jit(solution)/shard_map/ppermute | solution.py:201
  159.0 18.2 %collective-permute-start.5 = (bf16[256,128]{1,0:T(8,128)(2,1)S(1)}, bf16[256,128]{1,0:T(8,128)(2,1)S(1)}, u32[]{:S(2)}, u32[]{:S(2)}) collective-permute-start(bf16[256,128]{1,0:T(8,128)(2,1)S(1)} %bitcast.300), channel_id=1, source_target_pairs={{0,6},{1,7},{2,0},{3,1},{4,2},{5,3},{6,4},{7,5},{8,14},{9,15},{10,... | collective-permute-start | bytes 196616 | tf_op jit(solution)/shard_map/ppermute | solution.py:201
  160.9 16.3 %collective-permute-start.6 = (bf16[256,128]{1,0:T(8,128)(2,1)S(1)}, bf16[256,128]{1,0:T(8,128)(2,1)S(1)}, u32[]{:S(2)}, u32[]{:S(2)}) collective-permute-start(bf16[256,128]{1,0:T(8,128)(2,1)S(1)} %bitcast.302), channel_id=1, source_target_pairs={{0,5},{1,6},{2,7},{3,0},{4,1},{5,2},{6,3},{7,4},{8,13},{9,14},{10,... | collective-permute-start | bytes 196616 | tf_op jit(solution)/shard_map/ppermute | solution.py:201
  163.7 13.5 %collective-permute-start.7 = (bf16[256,128]{1,0:T(8,128)(2,1)S(1)}, bf16[256,128]{1,0:T(8,128)(2,1)S(1)}, u32[]{:S(2)}, u32[]{:S(2)}) collective-permute-start(bf16[256,128]{1,0:T(8,128)(2,1)S(1)} %bitcast.304), channel_id=1, source_target_pairs={{0,4},{1,5},{2,6},{3,7},{4,0},{5,1},{6,2},{7,3},{8,12},{9,13},{10,... | collective-permute-start | bytes 196616 | tf_op jit(solution)/shard_map/ppermute | solution.py:201
  168.6 8.6 %collective-permute-start.8 = (bf16[256,128]{1,0:T(8,128)(2,1)S(1)}, bf16[256,128]{1,0:T(8,128)(2,1)S(1)}, u32[]{:S(2)}, u32[]{:S(2)}) collective-permute-start(bf16[256,128]{1,0:T(8,128)(2,1)S(1)} %bitcast.306), channel_id=1, source_target_pairs={{0,3},{1,4},{2,5},{3,6},{4,7},{5,0},{6,1},{7,2},{8,11},{9,12},{10,... | collective-permute-start | bytes 196616 | tf_op jit(solution)/shard_map/ppermute | solution.py:201
  170.6 11.2 %collective-permute-start.9 = (bf16[256,128]{1,0:T(8,128)(2,1)S(1)}, bf16[256,128]{1,0:T(8,128)(2,1)S(1)}, u32[]{:S(2)}, u32[]{:S(2)}) collective-permute-start(bf16[256,128]{1,0:T(8,128)(2,1)S(1)} %bitcast.305), channel_id=1, source_target_pairs={{0,2},{1,3},{2,4},{3,5},{4,6},{5,7},{6,0},{7,1},{8,10},{9,11},{10,... | collective-permute-start | bytes 196616 | tf_op jit(solution)/shard_map/ppermute | solution.py:201

commit v8 on v5

--- a/solution.py
+++ b/solution.py
@@ -28,7 +28,7 @@
     return jax.tree.map(lambda a: lax.ppermute(a, axis, pairs), tree)
 
 
-def suffix_scan(part):
+def suffix_scan(part, tied):
     z_axis, pair_axis, core_axis = CTX
     core = lax.axis_index(core_axis)
     pair = lax.axis_index(pair_axis)
@@ -53,12 +53,12 @@
     while step < count:
         later = pick(z + step < count, join(later, shift(later, z_axis, step)), later)
         step *= 2
-    mine = later[1]
+    mine, tied = lax.optimization_barrier((later[1], tied))
     theirs = swap(mine, core_axis)
     two = jnp.where(core == 0, jnp.stack([mine, theirs]), jnp.stack([theirs, mine]))
     two_other = swap(two, pair_axis)
     four = jnp.where(pair == 0, jnp.concatenate([two, two_other]), jnp.concatenate([two_other, two]))
-    return within[1] + within[0][:, None, None] * four
+    return within[1] + within[0][:, None, None] * four, tied
 
 
 def ssd_partials(ssm_input, gate_input, grad_out, shared_b, shared_c, log_decay, entry, block_len):
@@ -191,6 +191,24 @@
     return total
 
 
+def swap_sum(rows, axis, dim):
+    place = lax.axis_index(axis)
+    own = lax.dynamic_index_in_dim(rows, place, dim, True)
+    other = lax.dynamic_index_in_dim(rows, 1 - place, dim, True)
+    return own + swap(other.astype(jnp.bfloat16), axis).astype(jnp.float32)
+
+
+def reduce_rows(rows, paired):
+    sizes = [lax.axis_size(name) for name in CTX]
+    rows = rows.reshape(*sizes, rows.shape[0] // math.prod(sizes), rows.shape[1])
+    for level in reversed(range(len(CTX))):
+        if paired and level > 0:
+            rows = swap_sum(rows, CTX[level], level)
+        else:
+            rows = summed_over(rows.astype(jnp.bfloat16), CTX[level], level)
+    return rows.reshape(rows.shape[-2], rows.shape[-1])
+
+
 def per_device(
     events,
     ssm_input,
@@ -209,25 +227,21 @@
     )
     block_sum = partials[9]
     block_log = partials[10]
-    incoming = suffix_scan((jnp.exp(block_log), block_sum))
+    norm_scale = 1.0 / math.sqrt(events.shape[0] * lax.axis_size(CTX))
+    gate_rows = reduce_rows(row_term(events, partials[0], norm_scale), True)
+    incoming, gate_rows = suffix_scan((jnp.exp(block_log), block_sum), gate_rows)
     grad_z, grad_x, grad_bc_part = finish_block(partials, incoming)
     grad_bc = summed_over(grad_bc_part, HEAD, 1).astype(jnp.bfloat16)
     input_part = (
         times_rows(grad_z, w_gate) + times_rows(grad_x, w_value) + times_rows(grad_bc, w_shared)
     )
     grad_input = spread_sum(input_part.astype(jnp.bfloat16), HEAD).astype(jnp.bfloat16)
-    norm_scale = 1.0 / math.sqrt(events.shape[0] * lax.axis_size(CTX))
     head_cols = grad_z.shape[1]
-    projected = jnp.concatenate([grad_z, grad_x, grad_bc], axis=1)
-    rows = row_term(events, projected, norm_scale)
-    sizes = [lax.axis_size(name) for name in CTX]
-    rows = rows.reshape(*sizes, rows.shape[0] // math.prod(sizes), rows.shape[1])
-    for level in reversed(range(len(CTX))):
-        rows = summed_over(rows.astype(jnp.bfloat16), CTX[level], level)
-    reduced = rows.reshape(rows.shape[-2], rows.shape[-1])
-    grad_w_gate = reduced[:, :head_cols]
-    grad_w_value = reduced[:, head_cols : 2 * head_cols]
-    grad_w_shared = reduced[:, 2 * head_cols :]
+    rest = jnp.concatenate([grad_x, grad_bc], axis=1)
+    rest_rows = reduce_rows(row_term(events, rest, norm_scale), False)
+    grad_w_gate = gate_rows
+    grad_w_value = rest_rows[:, :head_cols]
+    grad_w_shared = rest_rows[:, head_cols:]
     return (grad_input, grad_w_gate, grad_w_value, grad_w_shared)
 
 

time: 168 us -> 191 us (1.14)
  starting transfers between devices: 77.8 us -> 101 us
  blocking collectives: 17.3 us -> 4.37 us
  other arithmetic: 6.06 us -> 11.7 us
  matrix products: 6.71 us -> 10.2 us
  local copies, waits for them, and re-layouts: 7.44 us -> 9.63 us
    all_to_all x2 -> x4, starting transfers between devices: 17.2 us -> 34.5 us  [summed_over(): gathered = lax.all_to_all(part, axis, split, split, tiled=True)]
    all_to_all x2 -> x1, blocking collectives: 17.3 us -> 4.37 us  [summed_over(): gathered = lax.all_to_all(part, axis, split, split, tiled=True)]
    all_to_all x2 -> x4, waiting for transfers between devices: 8.51 us -> 14.2 us  [summed_over(): gathered = lax.all_to_all(part, axis, split, split, tiled=True)]
    ppermute x6 -> x8, starting transfers between devices: 16.3 us -> 19.6 us  [swap(): return jax.tree.map(lambda a: lax.ppermute(a, axis, [(0, 1), (1, 0)]), tree)]
    ppermute x6 -> x8, waiting for transfers between devices: 5.47 us -> 2.2 us  [swap(): return jax.tree.map(lambda a: lax.ppermute(a, axis, [(0, 1), (1, 0)]), tree)]
    ppermute x9, starting transfers between devices: 16.8 us -> 19.1 us  [shift(): return jax.tree.map(lambda a: lax.ppermute(a, axis, pairs), tree)]
  transfers between devices with their start and end apart: 24 -> 28, of which waited for: 13 -> 12; matrix products, arithmetic and copies ran while one was open for 6% -> 11% of each run, Pallas kernels for 0% -> 0%
where the time goes in v8:
time: 191 us; the launch traced here: 190 us
  starting transfers between devices  101 us (53%)
  waiting for transfers between devices  49 us (26%)
  other arithmetic  11.7 us (6%)
  matrix products  10.2 us (5%)
  local copies, waits for them, and re-layouts  9.63 us (5%)
  blocking collectives  4.37 us (2%)
  between operations  4.24 us (2%)
    all_to_all x4, starting transfers between devices, summed_over(): gathered = lax.all_to_all(part, axis, split, split, tiled=True)  34.5 us
    ppermute x9, waiting for transfers between devices, shift(): return jax.tree.map(lambda a: lax.ppermute(a, axis, pairs), tree)  28 us
    ppermute x7, starting transfers between devices, spread_sum(): total = total + lax.ppermute(piece, axis, pairs).astype(jnp.float32)  27.5 us
    ppermute x8, starting transfers between devices, swap(): return jax.tree.map(lambda a: lax.ppermute(a, axis, [(0, 1), (1, 0)]), tree)  19.6 us
    ppermute x9, starting transfers between devices, shift(): return jax.tree.map(lambda a: lax.ppermute(a, axis, pairs), tree)  19.1 us
    all_to_all x4, waiting for transfers between devices, summed_over(): gathered = lax.all_to_all(part, axis, split, split, tiled=True)  14.2 us
    ppermute x7, waiting for transfers between devices, spread_sum(): total = total + lax.ppermute(piece, axis, pairs).astype(jnp.float32)  4.61 us
    all_to_all x1, blocking collectives, summed_over(): gathered = lax.all_to_all(part, axis, split, split, tiled=True)  4.37 us
  transfers between devices with their start and end apart: 28, of which 12 were waited for; matrix products, arithmetic and copies ran while one was open for 11% of the time, Pallas kernels for 0%

profile of v8, /device:TPU:32, one launch (start us, length us, event | category | flops | bytes accessed | tf_op | source)
XLA Modules:
  0.0 190.0 jit_solution(4695732121076941738)
XLA Ops:
  0.7 0.8 reshape.426
  1.4 1.2 reduce-window.6
  3.1 2.1 %collective-permute-start.1 = (f32[4]{0:T(128)S(1)}, f32[4]{0:T(128)S(1)}, u32[]{:S(2)}, u32[]{:S(2)}) collective-permute-start(f32[4]{0:T(128)S(1)} %fusion.50), channel_id=1, source_target_pairs={{0,8},{8,0},{1,9},{9,1},{2,10},{10,2},{3,11},{11,3},{4,12},{12,4},... | collective-permute-start | bytes 56 | tf_op jit(solution)/shard_map/ppermute | solution.py:23
  6.8 1.0 fusion.14
  7.9 0.6 copy-done.8
  9.2 0.7 dynamic-slice_convert_fusion
  9.9 2.4 %collective-permute-start.13 = (bf16[16,2,1,16,256]{4,3,2,1,0:T(8,128)(2,1)}, bf16[16,2,1,16,256]{4,3,2,1,0:T(8,128)(2,1)}, u32[]{:S(2)}, u32[]{:S(2)}) collective-permute-start(bf16[16,2,1,16,256]{4,3,2,1,0:T(8,128)(2,1)} %dynamic-slice_convert_fusion), channel_id=1, source_target_pairs={{0,8},{8,0},{1,9},{9,1},{2,10},{10,2},{3,11},{11,3},{4,12},{12,4},... | collective-permute-start | bytes 786440 | tf_op jit(solution)/shard_map/ppermute | solution.py:23
  12.8 0.7 subtract_exponential_fusion
  13.5 0.9 fusion.15
  14.5 1.9 %collective-permute-start = (f32[4,128,64]{1,2,0:T(8,128)}, f32[4,128,64]{1,2,0:T(8,128)}, u32[]{:S(2)}, u32[]{:S(2)}) collective-permute-start(f32[4,128,64]{1,2,0:T(8,128)} %fusion.15), channel_id=1, source_target_pairs={{0,8},{8,0},{1,9},{9,1},{2,10},{10,2},{3,11},{11,3},{4,12},{12,4},... | collective-permute-start | bytes 393224 | tf_op jit(solution)/shard_map/ppermute | solution.py:23
  16.4 0.8 fusion.3
  17.3 2.0 %convolution_bitcast_fusion.3 = f32[256,128]{0,1:T(8,128)} fusion(f32[256,4,64]{0,2,1:T(8,128)S(1)} %bitcast.198, f32[1,4,128,64]{2,3,1,0:T(8,128)} %param.18), kind=kOutput, calls=%fused_computation.23 | convolution fusion | flops 100663296 | bytes 524288 | tf_op jit(solution)/shard_map/kthp,khnp->ktn/dot_general | solution.py:105
  19.3 3.5 %collective-permute-start.3 = (f32[4]{0:T(128)S(1)}, f32[4]{0:T(128)S(1)}, u32[]{:S(2)}, u32[]{:S(2)}) collective-permute-start(f32[4]{0:T(128)S(1)} %get-tuple-element.55), channel_id=1, source_target_pairs={{0,16},{16,0},{1,17},{17,1},{2,18},{18,2},{3,19},{19,3},{4,20},{20... | collective-permute-start | bytes 56 | tf_op jit(solution)/shard_map/ppermute | solution.py:23
  23.4 1.1 add_select_fusion
  24.5 2.4 %collective-permute-start.2 = (f32[4,128,64]{1,2,0:T(8,128)S(1)}, f32[4,128,64]{1,2,0:T(8,128)S(1)}, u32[]{:S(2)}, u32[]{:S(2)}) collective-permute-start(f32[4,128,64]{1,2,0:T(8,128)S(1)} %add_select_fusion), channel_id=1, source_target_pairs={{0,16},{16,0},{1,17},{17,1},{2,18},{18,2},{3,19},{19,3},{4,20},{20... | collective-permute-start | bytes 393224 | tf_op jit(solution)/shard_map/ppermute | solution.py:23
  26.8 1.2 fusion.46
  28.6 1.3 collective-permute-start.7
  29.9 7.4 %collective-permute-start.5 = (f32[]{:T(128)}, f32[]{:T(128)}, u32[]{:S(2)}, u32[]{:S(2)}) collective-permute-start(f32[]{:T(128)} %bitcast.34), channel_id=1, source_target_pairs={{32,0},{64,32},{96,64},{128,96},{160,128},{192,160},{224,192},{256... | collective-permute-start | bytes 20 | tf_op jit(solution)/shard_map/ppermute | solution.py:28
  38.4 2.7 %collective-permute-done.5 = f32[]{:T(128)} collective-permute-done((f32[]{:T(128)}, f32[]{:T(128)}, u32[]{:S(2)}, u32[]{:S(2)}) %collective-permute-start.5) | collective-permute-done | bytes 36 | tf_op jit(solution)/shard_map/ppermute | solution.py:28
  41.7 1.3 collective-permute-start.9
  43.0 5.2 %collective-permute-done.9 = f32[]{:T(128)} collective-permute-done((f32[]{:T(128)}, f32[]{:T(128)}, u32[]{:S(2)}, u32[]{:S(2)}) %collective-permute-start.9) | collective-permute-done | bytes 36 | tf_op jit(solution)/shard_map/ppermute | solution.py:28
  48.9 1.3 select_bitcast_fusion
  50.2 1.4 collective-permute-start.6
  51.7 2.5 %collective-permute-start.4 = (f32[128,64]{0,1:T(8,128)S(1)}, f32[128,64]{0,1:T(8,128)S(1)}, u32[]{:S(2)}, u32[]{:S(2)}) collective-permute-start(f32[128,64]{0,1:T(8,128)S(1)} %select_bitcast_fusion), channel_id=1, source_target_pairs={{32,0},{64,32},{96,64},{128,96},{160,128},{192,160},{224,192},{256... | collective-permute-start | bytes 98312 | tf_op jit(solution)/shard_map/ppermute | solution.py:28
  54.2 1.0 convert_add_fusion
  55.2 2.4 %collective-permute-done.6 = f32[128,64]{0,1:T(8,128)S(1)} collective-permute-done((f32[128,64]{0,1:T(8,128)S(1)}, f32[128,64]{0,1:T(8,128)S(1)}, u32[]{:S(2)}, u32[]{:S(2)}) %collective-permute-start.6) | collective-permute-done | bytes 32800 | tf_op jit(solution)/shard_map/ppermute | solution.py:28
  57.6 1.7 collective-permute-done.4
  59.3 1.3 collective-permute-start.8
  60.6 1.9 %collective-permute-start.14 = (bf16[16,1,1,16,256]{4,3,2,1,0:T(8,128)(2,1)S(1)}, bf16[16,1,1,16,256]{4,3,2,1,0:T(8,128)(2,1)S(1)}, u32[]{:S(2)}, u32[]{:S(2)}) collective-permute-start(bf16[16,1,1,16,256]{4,3,2,1,0:T(8,128)(2,1)S(1)} %dynamic-slice_convert_fusion.1), channel_id=1, source_target_pairs={{0,16},{16,0},{1,17},{17,1},{2,18},{18,2},{3,19},{19,3},{4,20},{20... | collective-permute-start | bytes 393224 | tf_op jit(solution)/shard_map/ppermute | solution.py:23
  62.6 4.7 %collective-permute-done.8 = f32[128,64]{0,1:T(8,128)S(1)} collective-permute-done((f32[128,64]{0,1:T(8,128)S(1)}, f32[128,64]{0,1:T(8,128)S(1)}, u32[]{:S(2)}, u32[]{:S(2)}) %collective-permute-start.8) | collective-permute-done | bytes 32800 | tf_op jit(solution)/shard_map/ppermute | solution.py:28
  67.3 1.4 collective-permute-start.10
  68.7 0.7 add_convert_fusion
  69.4 14.1 %all-to-all-start = ((bf16[16,1,1,16,256]{4,3,2,1,0:T(8,128)(2,1)}), bf16[16,1,1,16,256]{4,3,2,1,0:T(8,128)(2,1)S(1)}, u32[]{:S(2)}, u32[]{:S(2)}) async-start(bf16[16,1,1,16,256]{4,3,2,1,0:T(8,128)(2,1)} %add_convert_fusion), calls=%async_computation | async-start | bytes 262144 | tf_op jit(solution)/shard_map/all_to_all | solution.py:176
  83.5 1.3 collective-permute-start.12
  85.1 1.3 collective-permute-start.11
  86.4 8.2 %collective-permute-done.11 = f32[]{:T(128)} collective-permute-done((f32[]{:T(128)}, f32[]{:T(128)}, u32[]{:S(2)}, u32[]{:S(2)}) %collective-permute-start.11) | collective-permute-done | bytes 36 | tf_op jit(solution)/shard_map/ppermute | solution.py:28
  95.2 3.2 %collective-permute-done.12 = f32[128,64]{0,1:T(8,128)S(1)} collective-permute-done((f32[128,64]{0,1:T(8,128)S(1)}, f32[128,64]{0,1:T(8,128)S(1)}, u32[]{:S(2)}, u32[]{:S(2)}) %collective-permute-start.12) | collective-permute-done | bytes 32800 | tf_op jit(solution)/shard_map/ppermute | solution.py:28
  98.4 0.6 convert_reduce_fusion.1
  99.0 1.9 %collective-permute-start.15 = (f32[128,64]{0,1:T(8,128)S(1)}, f32[128,64]{0,1:T(8,128)S(1)}, u32[]{:S(2)}, u32[]{:S(2)}) collective-permute-start(f32[128,64]{0,1:T(8,128)S(1)} %add_select_fusion.1), channel_id=1, source_target_pairs={{0,8},{8,0},{1,9},{9,1},{2,10},{10,2},{3,11},{11,3},{4,12},{12,4},... | collective-permute-start | bytes 98312 | tf_op jit(solution)/shard_map/ppermute | solution.py:23
  101.2 0.9 collective-permute-done.15
  102.1 3.6 %collective-permute-start.16 = (f32[2,128,64]{1,2,0:T(8,128)S(1)}, f32[2,128,64]{1,2,0:T(8,128)S(1)}, u32[]{:S(2)}, u32[]{:S(2)}) collective-permute-start(f32[2,128,64]{1,2,0:T(8,128)S(1)} %maximum_select_fusion.1), channel_id=1, source_target_pairs={{0,16},{16,0},{1,17},{17,1},{2,18},{18,2},{3,19},{19,3},{4,20},{20... | collective-permute-start | bytes 196616 | tf_op jit(solution)/shard_map/ppermute | solution.py:23
  105.8 1.1 convolution_bitcast_fusion.1
  107.2 1.3 collective-permute-done.16
  108.4 1.0 fusion.35
  109.8 0.7 pad_maximum_fusion
  110.6 6.9 %all-to-all-start.1 = ((f32[256,8,32]{0,2,1:T(8,128)}), f32[256,8,32]{0,2,1:T(8,128)S(1)}, u32[]{:S(2)}, u32[]{:S(2)}) async-start(f32[256,8,32]{0,2,1:T(8,128)} %pad_maximum_fusion), calls=%async_computation.1 | async-start | bytes 524288 | tf_op jit(solution)/shard_map/all_to_all | solution.py:176
  117.8 8.5 %all-to-all-done.1 = f32[256,8,32]{0,2,1:T(8,128)S(1)} async-done(((f32[256,8,32]{0,2,1:T(8,128)}), f32[256,8,32]{0,2,1:T(8,128)S(1)}, u32[]{:S(2)}, u32[]{:S(2)}) %all-to-all-start.1) | async-done | bytes 262176 | tf_op jit(solution)/shard_map/all_to_all | solution.py:176
  127.1 4.4 %all_to_all.26 = bf16[16,2,2,16,288]{4,3,1,0,2:T(8,128)(2,1)S(1)} all-to-all(bf16[16,2,2,16,288]{4,3,1,0,2:T(8,128)(2,1)S(1)} %copy.94), channel_id=1, replica_groups=mesh['z'=16,'y_lo'=2,'core'=2,'y_hi'=2,'x'=4] {'core'}, dimensions={2} | all-to-all | bytes 1179648 | tf_op jit(solution)/shard_map/all_to_all | solution.py:176
  131.8 0.8 copy.95
  132.6 3.5 %all-to-all-start.3 = ((bf16[16,2,1,16,288]{4,3,0,2,1:T(8,128)(2,1)}), bf16[16,2,1,16,288]{4,3,0,2,1:T(8,128)(2,1)S(1)}, u32[]{:S(2)}, u32[]{:S(2)}) async-start(bf16[16,2,1,16,288]{4,3,0,2,1:T(8,128)(2,1)} %copy.95), calls=%async_computation.3 | async-start | bytes 786432 | tf_op jit(solution)/shard_map/all_to_all | solution.py:176
  136.1 1.4 convolution_add_fusion.1
  137.5 5.7 %all-to-all-done.3 = bf16[16,2,1,16,288]{4,3,0,2,1:T(8,128)(2,1)S(1)} async-done(((bf16[16,2,1,16,288]{4,3,0,2,1:T(8,128)(2,1)}), bf16[16,2,1,16,288]{4,3,0,2,1:T(8,128)(2,1)S(1)}, u32[]{:S(2)}, u32[]{:S(2)}) %all-to-all-start.3) | async-done | bytes 294944 | tf_op jit(solution)/shard_map/all_to_all | solution.py:176
  143.2 0.8 reduce_sum.72
  144.0 10.0 %all-to-all-start.4 = ((bf16[16,1,1,16,288]{4,3,2,1,0:T(8,128)(2,1)}), bf16[16,1,1,16,288]{4,3,2,1,0:T(8,128)(2,1)S(1)}, u32[]{:S(2)}, u32[]{:S(2)}) async-start(bf16[16,1,1,16,288]{4,3,2,1,0:T(8,128)(2,1)} %bitcast.60), calls=%async_computation.4 | async-start | bytes 393216 | tf_op jit(solution)/shard_map/all_to_all | solution.py:176
  154.4 1.2 constant_dynamic-slice_fusion.7
  155.7 2.8 %collective-permute-start.23 = (bf16[256,128]{1,0:T(8,128)(2,1)S(1)}, bf16[256,128]{1,0:T(8,128)(2,1)S(1)}, u32[]{:S(2)}, u32[]{:S(2)}) collective-permute-start(bf16[256,128]{1,0:T(8,128)(2,1)S(1)} %bitcast.224), channel_id=1, source_target_pairs={{0,1},{1,2},{2,3},{3,4},{4,5},{5,6},{6,7},{7,0},{8,9},{9,10},{10,1... | collective-permute-start | bytes 196616 | tf_op jit(solution)/shard_map/ppermute | solution.py:190
  158.5 6.7 %collective-permute-start.17 = (bf16[256,128]{1,0:T(8,128)(2,1)S(1)}, bf16[256,128]{1,0:T(8,128)(2,1)S(1)}, u32[]{:S(2)}, u32[]{:S(2)}) collective-permute-start(bf16[256,128]{1,0:T(8,128)(2,1)S(1)} %bitcast.222), channel_id=1, source_target_pairs={{0,7},{1,0},{2,1},{3,2},{4,3},{5,4},{6,5},{7,6},{8,15},{9,8},{10,9... | collective-permute-start | bytes 196616 | tf_op jit(solution)/shard_map/ppermute | solution.py:190
  165.3 1.9 %collective-permute-start.18 = (bf16[256,128]{1,0:T(8,128)(2,1)S(1)}, bf16[256,128]{1,0:T(8,128)(2,1)S(1)}, u32[]{:S(2)}, u32[]{:S(2)}) collective-permute-start(bf16[256,128]{1,0:T(8,128)(2,1)S(1)} %bitcast.225), channel_id=1, source_target_pairs={{0,6},{1,7},{2,0},{3,1},{4,2},{5,3},{6,4},{7,5},{8,14},{9,15},{10,... | collective-permute-start | bytes 196616 | tf_op jit(solution)/shard_map/ppermute | solution.py:190
  167.2 2.8 %collective-permute-start.19 = (bf16[256,128]{1,0:T(8,128)(2,1)S(1)}, bf16[256,128]{1,0:T(8,128)(2,1)S(1)}, u32[]{:S(2)}, u32[]{:S(2)}) collective-permute-start(bf16[256,128]{1,0:T(8,128)(2,1)S(1)} %bitcast.223), channel_id=1, source_target_pairs={{0,5},{1,6},{2,7},{3,0},{4,1},{5,2},{6,3},{7,4},{8,13},{9,14},{10,... | collective-permute-start | bytes 196616 | tf_op jit(solution)/shard_map/ppermute | solution.py:190
  170.0 4.9 %collective-permute-start.20 = (bf16[256,128]{1,0:T(8,128)(2,1)S(1)}, bf16[256,128]{1,0:T(8,128)(2,1)S(1)}, u32[]{:S(2)}, u32[]{:S(2)}) collective-permute-start(bf16[256,128]{1,0:T(8,128)(2,1)S(1)} %bitcast.221), channel_id=1, source_target_pairs={{0,4},{1,5},{2,6},{3,7},{4,0},{5,1},{6,2},{7,3},{8,12},{9,13},{10,... | collective-permute-start | bytes 196616 | tf_op jit(solution)/shard_map/ppermute | solution.py:190
  174.9 1.9 %collective-permute-start.21 = (bf16[256,128]{1,0:T(8,128)(2,1)S(1)}, bf16[256,128]{1,0:T(8,128)(2,1)S(1)}, u32[]{:S(2)}, u32[]{:S(2)}) collective-permute-start(bf16[256,128]{1,0:T(8,128)(2,1)S(1)} %bitcast.220), channel_id=1, source_target_pairs={{0,3},{1,4},{2,5},{3,6},{4,7},{5,0},{6,1},{7,2},{8,11},{9,12},{10,... | collective-permute-start | bytes 196616 | tf_op jit(solution)/shard_map/ppermute | solution.py:190
  176.8 6.6 %collective-permute-start.22 = (bf16[256,128]{1,0:T(8,128)(2,1)S(1)}, bf16[256,128]{1,0:T(8,128)(2,1)S(1)}, u32[]{:S(2)}, u32[]{:S(2)}) collective-permute-start(bf16[256,128]{1,0:T(8,128)(2,1)S(1)} %bitcast.219), channel_id=1, source_target_pairs={{0,2},{1,3},{2,4},{3,5},{4,6},{5,7},{6,0},{7,1},{8,10},{9,11},{10,... | collective-permute-start | bytes 196616 | tf_op jit(solution)/shard_map/ppermute | solution.py:190
  183.4 4.6 %collective-permute-done.22 = bf16[256,128]{1,0:T(8,128)(2,1)S(1)} collective-permute-done((bf16[256,128]{1,0:T(8,128)(2,1)S(1)}, bf16[256,128]{1,0:T(8,128)(2,1)S(1)}, u32[]{:S(2)}, u32[]{:S(2)}) %collective-permute-start.22) | collective-permute-done | bytes 65568 | tf_op jit(solution)/shard_map/ppermute | solution.py:190
  188.0 0.7 fusion.42
  (122 shorter events, 9.1 us)
Async XLA Ops:
  0.6 7.9 %copy-start = (bf16[256,1024]{1,0:T(8,128)(2,1)S(1)}, bf16[256,1024]{1,0:T(8,128)(2,1)}, u32[]{:S(2)}) copy-start(bf16[256,1024]{1,0:T(8,128)(2,1)} %param.11) | copy-start | bytes 1572868
  0.6 5.3 %copy-start.17 = (bf16[256,256]{1,0:T(8,128)(2,1)S(1)}, bf16[256,256]{1,0:T(8,128)(2,1)}, u32[]{:S(2)}) copy-start(bf16[256,256]{1,0:T(8,128)(2,1)} %param.12) | copy-start | bytes 393220
  0.7 5.4 %copy-start.18 = (bf16[256,256]{1,0:T(8,128)(2,1)S(1)}, bf16[256,256]{1,0:T(8,128)(2,1)}, u32[]{:S(2)}) copy-start(bf16[256,256]{1,0:T(8,128)(2,1)} %param.13) | copy-start | bytes 393220
  1.4 4.8 %copy-start.19 = (bf16[256,256]{1,0:T(8,128)(2,1)S(1)}, bf16[256,256]{1,0:T(8,128)(2,1)}, u32[]{:S(2)}) copy-start(bf16[256,256]{1,0:T(8,128)(2,1)} %param.14) | copy-start | bytes 393220
  3.0 3.3 %copy-start.3 = (bf16[256,128]{1,0:T(8,128)(2,1)S(1)}, bf16[256,128]{1,0:T(8,128)(2,1)}, u32[]{:S(2)}) copy-start(bf16[256,128]{1,0:T(8,128)(2,1)} %param.16) | copy-start | bytes 196612
  3.0 3.3 %copy-start.4 = (bf16[256,128]{1,0:T(8,128)(2,1)S(1)}, bf16[256,128]{1,0:T(8,128)(2,1)}, u32[]{:S(2)}) copy-start(bf16[256,128]{1,0:T(8,128)(2,1)} %param.15) | copy-start | bytes 196612
  3.1 2.7 %copy-start.16 = (f32[4,1,256]{0,2,1:T(8,128)}, f32[4,1,256]{0,2,1:T(8,128)S(1)}, u32[]{:S(2)}) copy-start(f32[4,1,256]{0,2,1:T(8,128)S(1)} %bitcast_add_fusion) | copy-start | bytes 12292
  3.1 3.4 %copy-start.6 = (f32[1,4,128,64]{2,3,1,0:T(8,128)S(1)}, f32[1,4,128,64]{2,3,1,0:T(8,128)}, u32[]{:S(2)}) copy-start(f32[1,4,128,64]{2,3,1,0:T(8,128)} %param.18) | copy-start | bytes 393220
  3.1 9.7 %collective-permute-start.1 = (f32[4]{0:T(128)S(1)}, f32[4]{0:T(128)S(1)}, u32[]{:S(2)}, u32[]{:S(2)}) collective-permute-start(f32[4]{0:T(128)S(1)} %fusion.50), channel_id=1, source_target_pairs={{0,8},{8,0},{1,9},{9,1},{2,10},{10,2},{3,11},{11,3},{4,12},{12,4},... | collective-permute-start | bytes 56 | tf_op jit(solution)/shard_map/ppermute | solution.py:23
  5.2 1.6 copy-start.21
  6.5 1.3 copy-start.12
  7.8 0.7 copy-start.8
  9.2 3.2 %copy-start.1 = (f32[1024,256]{1,0:T(8,128)}, f32[1024,256]{1,0:T(8,128)S(1)}, u32[]{:S(2)}) copy-start(f32[1024,256]{1,0:T(8,128)S(1)} %copy.83) | copy-start | bytes 3145732
  9.2 3.3 %copy-start.5 = (bf16[1024,256]{1,0:T(8,128)(2,1)S(1)}, bf16[1024,256]{1,0:T(8,128)(2,1)}, u32[]{:S(2)}) copy-start(bf16[1024,256]{1,0:T(8,128)(2,1)} %param.19) | copy-start | bytes 1572868
  9.2 3.3 %copy-start.9 = (bf16[1,256,4,64]{1,3,2,0:T(8,128)(2,1)S(1)}, bf16[1,256,4,64]{1,3,2,0:T(8,128)(2,1)}, u32[]{:S(2)}) copy-start(bf16[1,256,4,64]{1,3,2,0:T(8,128)(2,1)} %copy-done.8) | copy-start | bytes 393220
  9.9 44.2 %collective-permute-start.13 = (bf16[16,2,1,16,256]{4,3,2,1,0:T(8,128)(2,1)}, bf16[16,2,1,16,256]{4,3,2,1,0:T(8,128)(2,1)}, u32[]{:S(2)}, u32[]{:S(2)}) collective-permute-start(bf16[16,2,1,16,256]{4,3,2,1,0:T(8,128)(2,1)} %dynamic-slice_convert_fusion), channel_id=1, source_target_pairs={{0,8},{8,0},{1,9},{9,1},{2,10},{10,2},{3,11},{11,3},{4,12},{12,4},... | collective-permute-start | bytes 786440 | tf_op jit(solution)/shard_map/ppermute | solution.py:23
  12.5 4.0 %copy-start.10 = (f32[256,256]{0,1:T(8,128)}, f32[256,256]{0,1:T(8,128)S(1)}, u32[]{:S(2)}) copy-start(f32[256,256]{0,1:T(8,128)S(1)} %get-tuple-element.51) | copy-start | bytes 786436
  12.5 4.0 %copy-start.22 = (pred[256,256]{1,0:T(8,128)(4,1)S(1)}, pred[256,256]{1,0:T(8,128)(4,1)}, u32[]{:S(2)}) copy-start(pred[256,256]{1,0:T(8,128)(4,1)} %copy-done.21) | copy-start | bytes 196612
  13.5 13.3 %copy-start.25 = (f32[4]{0:T(128)}, f32[4]{0:T(128)S(1)}, u32[]{:S(2)}) copy-start(f32[4]{0:T(128)S(1)} %get-tuple-element.55) | copy-start | bytes 52
  14.5 8.9 %collective-permute-start = (f32[4,128,64]{1,2,0:T(8,128)}, f32[4,128,64]{1,2,0:T(8,128)}, u32[]{:S(2)}, u32[]{:S(2)}) collective-permute-start(f32[4,128,64]{1,2,0:T(8,128)} %fusion.15), channel_id=1, source_target_pairs={{0,8},{8,0},{1,9},{9,1},{2,10},{10,2},{3,11},{11,3},{4,12},{12,4},... | collective-permute-start | bytes 393224 | tf_op jit(solution)/shard_map/ppermute | solution.py:23
  17.3 36.9 %copy-start.2 = (f32[1024,256]{1,0:T(8,128)S(1)}, f32[1024,256]{1,0:T(8,128)}, u32[]{:S(2)}) copy-start(f32[1024,256]{1,0:T(8,128)} %copy-done.1) | copy-start | bytes 3145732
  19.3 7.5 %collective-permute-start.3 = (f32[4]{0:T(128)S(1)}, f32[4]{0:T(128)S(1)}, u32[]{:S(2)}, u32[]{:S(2)}) collective-permute-start(f32[4]{0:T(128)S(1)} %get-tuple-element.55), channel_id=1, source_target_pairs={{0,16},{16,0},{1,17},{17,1},{2,18},{18,2},{3,19},{19,3},{4,20},{20... | collective-permute-start | bytes 56 | tf_op jit(solution)/shard_map/ppermute | solution.py:23
  24.5 24.4 %collective-permute-start.2 = (f32[4,128,64]{1,2,0:T(8,128)S(1)}, f32[4,128,64]{1,2,0:T(8,128)S(1)}, u32[]{:S(2)}, u32[]{:S(2)}) collective-permute-start(f32[4,128,64]{1,2,0:T(8,128)S(1)} %add_select_fusion), channel_id=1, source_target_pairs={{0,16},{16,0},{1,17},{17,1},{2,18},{18,2},{3,19},{19,3},{4,20},{20... | collective-permute-start | bytes 393224 | tf_op jit(solution)/shard_map/ppermute | solution.py:23
  28.6 9.2 %collective-permute-start.7 = (f32[]{:T(128)}, f32[]{:T(128)}, u32[]{:S(2)}, u32[]{:S(2)}) collective-permute-start(f32[]{:T(128)} %bitcast.34), channel_id=1, source_target_pairs={{64,0},{96,32},{128,64},{160,96},{192,128},{224,160},{256,192},{28... | collective-permute-start | bytes 20 | tf_op jit(solution)/shard_map/ppermute | solution.py:28
  29.9 11.2 %collective-permute-start.5 = (f32[]{:T(128)}, f32[]{:T(128)}, u32[]{:S(2)}, u32[]{:S(2)}) collective-permute-start(f32[]{:T(128)} %bitcast.34), channel_id=1, source_target_pairs={{32,0},{64,32},{96,64},{128,96},{160,128},{192,160},{224,192},{256... | collective-permute-start | bytes 20 | tf_op jit(solution)/shard_map/ppermute | solution.py:28
  41.7 6.5 %collective-permute-start.9 = (f32[]{:T(128)}, f32[]{:T(128)}, u32[]{:S(2)}, u32[]{:S(2)}) collective-permute-start(f32[]{:T(128)} %mul.315), channel_id=1, source_target_pairs={{64,0},{96,32},{128,64},{160,96},{192,128},{224,160},{256,192},{28... | collective-permute-start | bytes 20 | tf_op jit(solution)/shard_map/ppermute | solution.py:28
  48.9 20.5 %copy-start.14 = (f32[4,128,64]{1,2,0:T(8,128)}, f32[4,128,64]{1,2,0:T(8,128)S(1)}, u32[]{:S(2)}) copy-start(f32[4,128,64]{1,2,0:T(8,128)S(1)} %collective-permute-done.2) | copy-start | bytes 393220
  50.2 34.6 %copy-start.7 = (f32[256,128]{0,1:T(8,128)S(1)}, f32[256,128]{0,1:T(8,128)}, u32[]{:S(2)}) copy-start(f32[256,128]{0,1:T(8,128)} %convolution_bitcast_fusion.3) | copy-start | bytes 393220
  50.2 7.4 %collective-permute-start.6 = (f32[128,64]{0,1:T(8,128)S(1)}, f32[128,64]{0,1:T(8,128)S(1)}, u32[]{:S(2)}, u32[]{:S(2)}) collective-permute-start(f32[128,64]{0,1:T(8,128)S(1)} %select_bitcast_fusion), channel_id=1, source_target_pairs={{64,0},{96,32},{128,64},{160,96},{192,128},{224,160},{256,192},{28... | collective-permute-start | bytes 98312 | tf_op jit(solution)/shard_map/ppermute | solution.py:28
  51.7 7.6 %collective-permute-start.4 = (f32[128,64]{0,1:T(8,128)S(1)}, f32[128,64]{0,1:T(8,128)S(1)}, u32[]{:S(2)}, u32[]{:S(2)}) collective-permute-start(f32[128,64]{0,1:T(8,128)S(1)} %select_bitcast_fusion), channel_id=1, source_target_pairs={{32,0},{64,32},{96,64},{128,96},{160,128},{192,160},{224,192},{256... | collective-permute-start | bytes 98312 | tf_op jit(solution)/shard_map/ppermute | solution.py:28
  59.3 7.9 %collective-permute-start.8 = (f32[128,64]{0,1:T(8,128)S(1)}, f32[128,64]{0,1:T(8,128)S(1)}, u32[]{:S(2)}, u32[]{:S(2)}) collective-permute-start(f32[128,64]{0,1:T(8,128)S(1)} %multiply_add_fusion), channel_id=1, source_target_pairs={{64,0},{96,32},{128,64},{160,96},{192,128},{224,160},{256,192},{28... | collective-permute-start | bytes 98312 | tf_op jit(solution)/shard_map/ppermute | solution.py:28
  60.6 8.1 %collective-permute-start.14 = (bf16[16,1,1,16,256]{4,3,2,1,0:T(8,128)(2,1)S(1)}, bf16[16,1,1,16,256]{4,3,2,1,0:T(8,128)(2,1)S(1)}, u32[]{:S(2)}, u32[]{:S(2)}) collective-permute-start(bf16[16,1,1,16,256]{4,3,2,1,0:T(8,128)(2,1)S(1)} %dynamic-slice_convert_fusion.1), channel_id=1, source_target_pairs={{0,16},{16,0},{1,17},{17,1},{2,18},{18,2},{3,19},{19,3},{4,20},{20... | collective-permute-start | bytes 393224 | tf_op jit(solution)/shard_map/ppermute | solution.py:23
  67.2 38.5 %copy-start.11 = (f32[256,256]{0,1:T(8,128)S(1)}, f32[256,256]{0,1:T(8,128)}, u32[]{:S(2)}) copy-start(f32[256,256]{0,1:T(8,128)} %copy-done.10) | copy-start | bytes 786436
  67.3 38.5 %copy-start.13 = (f32[256,256]{1,0:T(8,128)S(1)}, f32[256,256]{1,0:T(8,128)}, u32[]{:S(2)}) copy-start(f32[256,256]{1,0:T(8,128)} %copy-done.12) | copy-start | bytes 786436
  67.3 38.5 %copy-start.23 = (pred[256,256]{1,0:T(8,128)(4,1)S(1)}, pred[256,256]{1,0:T(8,128)(4,1)}, u32[]{:S(2)}) copy-start(pred[256,256]{1,0:T(8,128)(4,1)} %copy-done.21) | copy-start | bytes 196612
  67.3 16.2 %collective-permute-start.10 = (f32[128,64]{0,1:T(8,128)S(1)}, f32[128,64]{0,1:T(8,128)S(1)}, u32[]{:S(2)}, u32[]{:S(2)}) collective-permute-start(f32[128,64]{0,1:T(8,128)S(1)} %add_select_fusion.3), channel_id=1, source_target_pairs={{128,0},{160,32},{192,64},{224,96},{256,128},{288,160},{320,192},{... | collective-permute-start | bytes 98312 | tf_op jit(solution)/shard_map/ppermute | solution.py:28
  69.4 29.0 %all-to-all-start = ((bf16[16,1,1,16,256]{4,3,2,1,0:T(8,128)(2,1)}), bf16[16,1,1,16,256]{4,3,2,1,0:T(8,128)(2,1)S(1)}, u32[]{:S(2)}, u32[]{:S(2)}) async-start(bf16[16,1,1,16,256]{4,3,2,1,0:T(8,128)(2,1)} %add_convert_fusion), calls=%async_computation | async-start | bytes 262144 | tf_op jit(solution)/shard_map/all_to_all | solution.py:176
  83.5 14.9 %collective-permute-start.12 = (f32[128,64]{0,1:T(8,128)S(1)}, f32[128,64]{0,1:T(8,128)S(1)}, u32[]{:S(2)}, u32[]{:S(2)}) collective-permute-start(f32[128,64]{0,1:T(8,128)S(1)} %add_select_fusion.2), channel_id=1, source_target_pairs={{256,0},{288,32},{320,64},{352,96},{384,128},{416,160},{448,192},{... | collective-permute-start | bytes 98312 | tf_op jit(solution)/shard_map/ppermute | solution.py:28
  85.1 9.5 %collective-permute-start.11 = (f32[]{:T(128)}, f32[]{:T(128)}, u32[]{:S(2)}, u32[]{:S(2)}) collective-permute-start(f32[]{:T(128)} %select_n.201), channel_id=1, source_target_pairs={{128,0},{160,32},{192,64},{224,96},{256,128},{288,160},{320,192},{... | collective-permute-start | bytes 20 | tf_op jit(solution)/shard_map/ppermute | solution.py:28
  99.0 3.1 %collective-permute-start.15 = (f32[128,64]{0,1:T(8,128)S(1)}, f32[128,64]{0,1:T(8,128)S(1)}, u32[]{:S(2)}, u32[]{:S(2)}) collective-permute-start(f32[128,64]{0,1:T(8,128)S(1)} %add_select_fusion.1), channel_id=1, source_target_pairs={{0,8},{8,0},{1,9},{9,1},{2,10},{10,2},{3,11},{11,3},{4,12},{12,4},... | collective-permute-start | bytes 98312 | tf_op jit(solution)/shard_map/ppermute | solution.py:23
  102.1 6.3 %copy-start.15 = (f32[4,128,64]{1,2,0:T(8,128)S(1)}, f32[4,128,64]{1,2,0:T(8,128)}, u32[]{:S(2)}) copy-start(f32[4,128,64]{1,2,0:T(8,128)} %copy-done.14) | copy-start | bytes 393220
  102.1 6.3 %copy-start.24 = (f32[4]{0:T(128)S(1)}, f32[4]{0:T(128)}, u32[]{:S(2)}) copy-start(f32[4]{0:T(128)} %get-tuple-element.34) | copy-start | bytes 52
  102.1 6.3 %collective-permute-start.16 = (f32[2,128,64]{1,2,0:T(8,128)S(1)}, f32[2,128,64]{1,2,0:T(8,128)S(1)}, u32[]{:S(2)}, u32[]{:S(2)}) collective-permute-start(f32[2,128,64]{1,2,0:T(8,128)S(1)} %maximum_select_fusion.1), channel_id=1, source_target_pairs={{0,16},{16,0},{1,17},{17,1},{2,18},{18,2},{3,19},{19,3},{4,20},{20... | collective-permute-start | bytes 196616 | tf_op jit(solution)/shard_map/ppermute | solution.py:23
  110.6 15.7 %all-to-all-start.1 = ((f32[256,8,32]{0,2,1:T(8,128)}), f32[256,8,32]{0,2,1:T(8,128)S(1)}, u32[]{:S(2)}, u32[]{:S(2)}) async-start(f32[256,8,32]{0,2,1:T(8,128)} %pad_maximum_fusion), calls=%async_computation.1 | async-start | bytes 524288 | tf_op jit(solution)/shard_map/all_to_all | solution.py:176
  132.6 10.6 %all-to-all-start.3 = ((bf16[16,2,1,16,288]{4,3,0,2,1:T(8,128)(2,1)}), bf16[16,2,1,16,288]{4,3,0,2,1:T(8,128)(2,1)S(1)}, u32[]{:S(2)}, u32[]{:S(2)}) async-start(bf16[16,2,1,16,288]{4,3,0,2,1:T(8,128)(2,1)} %copy.95), calls=%async_computation.3 | async-start | bytes 786432 | tf_op jit(solution)/shard_map/all_to_all | solution.py:176
  136.1 17.9 %copy-start.20 = (bf16[1024,32]{0,1:T(8,128)(2,1)S(1)}, bf16[1024,32]{0,1:T(8,128)(2,1)}, u32[]{:S(2)}) copy-start(bf16[1024,32]{0,1:T(8,128)(2,1)} %param.21) | copy-start | bytes 196612
  144.0 44.7 %all-to-all-start.4 = ((bf16[16,1,1,16,288]{4,3,2,1,0:T(8,128)(2,1)}), bf16[16,1,1,16,288]{4,3,2,1,0:T(8,128)(2,1)S(1)}, u32[]{:S(2)}, u32[]{:S(2)}) async-start(bf16[16,1,1,16,288]{4,3,2,1,0:T(8,128)(2,1)} %bitcast.60), calls=%async_computation.4 | async-start | bytes 393216 | tf_op jit(solution)/shard_map/all_to_all | solution.py:176
  155.7 19.2 %collective-permute-start.23 = (bf16[256,128]{1,0:T(8,128)(2,1)S(1)}, bf16[256,128]{1,0:T(8,128)(2,1)S(1)}, u32[]{:S(2)}, u32[]{:S(2)}) collective-permute-start(bf16[256,128]{1,0:T(8,128)(2,1)S(1)} %bitcast.224), channel_id=1, source_target_pairs={{0,1},{1,2},{2,3},{3,4},{4,5},{5,6},{6,7},{7,0},{8,9},{9,10},{10,1... | collective-permute-start | bytes 196616 | tf_op jit(solution)/shard_map/ppermute | solution.py:190
  158.5 18.3 %collective-permute-start.17 = (bf16[256,128]{1,0:T(8,128)(2,1)S(1)}, bf16[256,128]{1,0:T(8,128)(2,1)S(1)}, u32[]{:S(2)}, u32[]{:S(2)}) collective-permute-start(bf16[256,128]{1,0:T(8,128)(2,1)S(1)} %bitcast.222), channel_id=1, source_target_pairs={{0,7},{1,0},{2,1},{3,2},{4,3},{5,4},{6,5},{7,6},{8,15},{9,8},{10,9... | collective-permute-start | bytes 196616 | tf_op jit(solution)/shard_map/ppermute | solution.py:190
  165.3 18.1 %collective-permute-start.18 = (bf16[256,128]{1,0:T(8,128)(2,1)S(1)}, bf16[256,128]{1,0:T(8,128)(2,1)S(1)}, u32[]{:S(2)}, u32[]{:S(2)}) collective-permute-start(bf16[256,128]{1,0:T(8,128)(2,1)S(1)} %bitcast.225), channel_id=1, source_target_pairs={{0,6},{1,7},{2,0},{3,1},{4,2},{5,3},{6,4},{7,5},{8,14},{9,15},{10,... | collective-permute-start | bytes 196616 | tf_op jit(solution)/shard_map/ppermute | solution.py:190
  167.2 16.2 %collective-permute-start.19 = (bf16[256,128]{1,0:T(8,128)(2,1)S(1)}, bf16[256,128]{1,0:T(8,128)(2,1)S(1)}, u32[]{:S(2)}, u32[]{:S(2)}) collective-permute-start(bf16[256,128]{1,0:T(8,128)(2,1)S(1)} %bitcast.223), channel_id=1, source_target_pairs={{0,5},{1,6},{2,7},{3,0},{4,1},{5,2},{6,3},{7,4},{8,13},{9,14},{10,... | collective-permute-start | bytes 196616 | tf_op jit(solution)/shard_map/ppermute | solution.py:190
  170.0 13.4 %collective-permute-start.20 = (bf16[256,128]{1,0:T(8,128)(2,1)S(1)}, bf16[256,128]{1,0:T(8,128)(2,1)S(1)}, u32[]{:S(2)}, u32[]{:S(2)}) collective-permute-start(bf16[256,128]{1,0:T(8,128)(2,1)S(1)} %bitcast.221), channel_id=1, source_target_pairs={{0,4},{1,5},{2,6},{3,7},{4,0},{5,1},{6,2},{7,3},{8,12},{9,13},{10,... | collective-permute-start | bytes 196616 | tf_op jit(solution)/shard_map/ppermute | solution.py:190
  174.9 8.6 %collective-permute-start.21 = (bf16[256,128]{1,0:T(8,128)(2,1)S(1)}, bf16[256,128]{1,0:T(8,128)(2,1)S(1)}, u32[]{:S(2)}, u32[]{:S(2)}) collective-permute-start(bf16[256,128]{1,0:T(8,128)(2,1)S(1)} %bitcast.220), channel_id=1, source_target_pairs={{0,3},{1,4},{2,5},{3,6},{4,7},{5,0},{6,1},{7,2},{8,11},{9,12},{10,... | collective-permute-start | bytes 196616 | tf_op jit(solution)/shard_map/ppermute | solution.py:190
  176.8 11.2 %collective-permute-start.22 = (bf16[256,128]{1,0:T(8,128)(2,1)S(1)}, bf16[256,128]{1,0:T(8,128)(2,1)S(1)}, u32[]{:S(2)}, u32[]{:S(2)}) collective-permute-start(bf16[256,128]{1,0:T(8,128)(2,1)S(1)} %bitcast.219), channel_id=1, source_target_pairs={{0,2},{1,3},{2,4},{3,5},{4,6},{5,7},{6,0},{7,1},{8,10},{9,11},{10,... | collective-permute-start | bytes 196616 | tf_op jit(solution)/shard_map/ppermute | solution.py:190

commit v9 on v5

--- a/solution.py
+++ b/solution.py
@@ -191,6 +191,13 @@
     return total
 
 
+def swap_sum(rows, axis, dim):
+    place = lax.axis_index(axis)
+    own = lax.dynamic_index_in_dim(rows, place, dim, True)
+    other = lax.dynamic_index_in_dim(rows, 1 - place, dim, True)
+    return own + swap(other.astype(jnp.bfloat16), axis).astype(jnp.float32)
+
+
 def per_device(
     events,
     ssm_input,
@@ -223,7 +230,10 @@
     sizes = [lax.axis_size(name) for name in CTX]
     rows = rows.reshape(*sizes, rows.shape[0] // math.prod(sizes), rows.shape[1])
     for level in reversed(range(len(CTX))):
-        rows = summed_over(rows.astype(jnp.bfloat16), CTX[level], level)
+        if level > 0:
+            rows = swap_sum(rows, CTX[level], level)
+        else:
+            rows = summed_over(rows.astype(jnp.bfloat16), CTX[level], level)
     reduced = rows.reshape(rows.shape[-2], rows.shape[-1])
     grad_w_gate = reduced[:, :head_cols]
     grad_w_value = reduced[:, head_cols : 2 * head_cols]

time: 168 us -> 173 us (1.030)
  the two profiles are of different devices: /device:TPU:32 before, /device:TPU:38 now
where the time goes in v9:
time: 173 us; the launch traced here: 171 us
  starting transfers between devices  76.9 us (44%)
  waiting for transfers between devices  64.6 us (37%)
  local copies, waits for them, and re-layouts  9.61 us (6%)
  matrix products  8.53 us (5%)
  other arithmetic  7.75 us (4%)
  between operations  4.08 us (2%)
    ppermute x9, waiting for transfers between devices, shift(): return jax.tree.map(lambda a: lax.ppermute(a, axis, pairs), tree)  31.8 us
    ppermute x7, starting transfers between devices, spread_sum(): total = total + lax.ppermute(piece, axis, pairs).astype(jnp.float32)  26.4 us
    all_to_all x2, starting transfers between devices, summed_over(): gathered = lax.all_to_all(part, axis, split, split, tiled=True)  18.9 us
    ppermute x8, starting transfers between devices, swap(): return jax.tree.map(lambda a: lax.ppermute(a, axis, [(0, 1), (1, 0)]), tree)  18.7 us
    ppermute x8, waiting for transfers between devices, swap(): return jax.tree.map(lambda a: lax.ppermute(a, axis, [(0, 1), (1, 0)]), tree)  18.5 us
    ppermute x9, starting transfers between devices, shift(): return jax.tree.map(lambda a: lax.ppermute(a, axis, pairs), tree)  13 us
    ppermute x7, waiting for transfers between devices, spread_sum(): total = total + lax.ppermute(piece, axis, pairs).astype(jnp.float32)  7.83 us
    all_to_all x2, waiting for transfers between devices, summed_over(): gathered = lax.all_to_all(part, axis, split, split, tiled=True)  6.38 us
  transfers between devices with their start and end apart: 26, of which 15 were waited for; matrix products, arithmetic and copies ran while one was open for 7% of the time, Pallas kernels for 0%

profile of v9, /device:TPU:38, one launch (start us, length us, event | category | flops | bytes accessed | tf_op | source)
XLA Modules:
  0.0 171.5 jit_solution(14644586648032152368)
XLA Ops:
  0.7 0.8 reshape.398
  1.5 1.2 reduce-window.6
  3.1 1.9 %collective-permute-start.1 = (f32[4]{0:T(128)S(1)}, f32[4]{0:T(128)S(1)}, u32[]{:S(2)}, u32[]{:S(2)}) collective-permute-start(f32[4]{0:T(128)S(1)} %fusion.49), channel_id=1, source_target_pairs={{0,8},{8,0},{1,9},{9,1},{2,10},{10,2},{3,11},{11,3},{4,12},{12,4},... | collective-permute-start | bytes 56 | tf_op jit(solution)/shard_map/ppermute | solution.py:23
  5.1 1.1 fusion.51
  6.2 1.2 fusion.52
  8.2 2.4 %collective-permute-start = (f32[4,128,64]{1,2,0:T(8,128)S(1)}, f32[4,128,64]{1,2,0:T(8,128)S(1)}, u32[]{:S(2)}, u32[]{:S(2)}) collective-permute-start(f32[4,128,64]{1,2,0:T(8,128)S(1)} %fusion.12), channel_id=1, source_target_pairs={{0,8},{8,0},{1,9},{9,1},{2,10},{10,2},{3,11},{11,3},{4,12},{12,4},... | collective-permute-start | bytes 393224 | tf_op jit(solution)/shard_map/ppermute | solution.py:23
  10.8 0.8 collective-permute-done
  11.7 3.5 %collective-permute-start.2 = (f32[4,128,64]{1,2,0:T(8,128)S(1)}, f32[4,128,64]{1,2,0:T(8,128)S(1)}, u32[]{:S(2)}, u32[]{:S(2)}) collective-permute-start(f32[4,128,64]{1,2,0:T(8,128)S(1)} %add_select_fusion), channel_id=1, source_target_pairs={{0,16},{16,0},{1,17},{17,1},{2,18},{18,2},{3,19},{19,3},{4,20},{20... | collective-permute-start | bytes 393224 | tf_op jit(solution)/shard_map/ppermute | solution.py:23
  15.2 1.0 fusion.11
  16.2 2.5 %collective-permute-start.3 = (f32[4]{0:T(128)S(1)}, f32[4]{0:T(128)S(1)}, u32[]{:S(2)}, u32[]{:S(2)}) collective-permute-start(f32[4]{0:T(128)S(1)} %get-tuple-element.51), channel_id=1, source_target_pairs={{0,16},{16,0},{1,17},{17,1},{2,18},{18,2},{3,19},{19,3},{4,20},{20... | collective-permute-start | bytes 56 | tf_op jit(solution)/shard_map/ppermute | solution.py:23
  18.7 0.6 dynamic-slice.34
  19.3 2.5 %collective-permute-done.3 = f32[4]{0:T(128)S(1)} collective-permute-done((f32[4]{0:T(128)S(1)}, f32[4]{0:T(128)S(1)}, u32[]{:S(2)}, u32[]{:S(2)}) %collective-permute-start.3) | collective-permute-done | bytes 48 | tf_op jit(solution)/shard_map/ppermute | solution.py:23
  21.8 0.6 dynamic-slice.35
  22.4 1.3 select_bitcast_fusion
  23.7 1.3 collective-permute-start.6
  25.0 2.0 %collective-permute-start.4 = (f32[128,64]{0,1:T(8,128)S(1)}, f32[128,64]{0,1:T(8,128)S(1)}, u32[]{:S(2)}, u32[]{:S(2)}) collective-permute-start(f32[128,64]{0,1:T(8,128)S(1)} %select_bitcast_fusion), channel_id=1, source_target_pairs={{32,0},{64,32},{96,64},{128,96},{160,128},{192,160},{224,192},{256... | collective-permute-start | bytes 98312 | tf_op jit(solution)/shard_map/ppermute | solution.py:28
  27.0 0.6 dynamic_slice.45
  27.6 1.9 %collective-permute-start.5 = (f32[]{:T(128)}, f32[]{:T(128)}, u32[]{:S(2)}, u32[]{:S(2)}) collective-permute-start(f32[]{:T(128)} %bitcast.34), channel_id=1, source_target_pairs={{32,0},{64,32},{96,64},{128,96},{160,128},{192,160},{224,192},{256... | collective-permute-start | bytes 20 | tf_op jit(solution)/shard_map/ppermute | solution.py:28
  29.5 4.0 %collective-permute-done.5 = f32[]{:T(128)} collective-permute-done((f32[]{:T(128)}, f32[]{:T(128)}, u32[]{:S(2)}, u32[]{:S(2)}) %collective-permute-start.5) | collective-permute-done | bytes 36 | tf_op jit(solution)/shard_map/ppermute | solution.py:28
  34.2 1.3 collective-permute-start.8
  35.5 0.8 fusion.1
  36.3 1.3 collective-permute-start.7
  37.6 7.5 %collective-permute-done.7 = f32[]{:T(128)} collective-permute-done((f32[]{:T(128)}, f32[]{:T(128)}, u32[]{:S(2)}, u32[]{:S(2)}) %collective-permute-start.7) | collective-permute-done | bytes 36 | tf_op jit(solution)/shard_map/ppermute | solution.py:28
  45.8 1.3 collective-permute-start.10
  47.1 0.4 convolution_bitcast_fusion.3
  47.6 1.3 collective-permute-start.9
  48.9 6.2 %collective-permute-done.9 = f32[]{:T(128)} collective-permute-done((f32[]{:T(128)}, f32[]{:T(128)}, u32[]{:S(2)}, u32[]{:S(2)}) %collective-permute-start.9) | collective-permute-done | bytes 36 | tf_op jit(solution)/shard_map/ppermute | solution.py:28
  55.7 1.7 %collective-permute-done.10 = f32[128,64]{0,1:T(8,128)S(1)} collective-permute-done((f32[128,64]{0,1:T(8,128)S(1)}, f32[128,64]{0,1:T(8,128)S(1)}, u32[]{:S(2)}, u32[]{:S(2)}) %collective-permute-start.10) | collective-permute-done | bytes 32800 | tf_op jit(solution)/shard_map/ppermute | solution.py:28
  57.4 1.3 collective-permute-start.12
  59.1 1.3 collective-permute-start.11
  60.4 8.3 %collective-permute-done.11 = f32[]{:T(128)} collective-permute-done((f32[]{:T(128)}, f32[]{:T(128)}, u32[]{:S(2)}, u32[]{:S(2)}) %collective-permute-start.11) | collective-permute-done | bytes 36 | tf_op jit(solution)/shard_map/ppermute | solution.py:28
  69.3 4.0 %collective-permute-done.12 = f32[128,64]{0,1:T(8,128)S(1)} collective-permute-done((f32[128,64]{0,1:T(8,128)S(1)}, f32[128,64]{0,1:T(8,128)S(1)}, u32[]{:S(2)}, u32[]{:S(2)}) %collective-permute-start.12) | collective-permute-done | bytes 32800 | tf_op jit(solution)/shard_map/ppermute | solution.py:28
  73.3 1.9 %collective-permute-start.13 = (f32[128,64]{0,1:T(8,128)S(1)}, f32[128,64]{0,1:T(8,128)S(1)}, u32[]{:S(2)}, u32[]{:S(2)}) collective-permute-start(f32[128,64]{0,1:T(8,128)S(1)} %add_select_fusion.1), channel_id=1, source_target_pairs={{0,8},{8,0},{1,9},{9,1},{2,10},{10,2},{3,11},{11,3},{4,12},{12,4},... | collective-permute-start | bytes 98312 | tf_op jit(solution)/shard_map/ppermute | solution.py:23
  75.5 0.9 collective-permute-done.13
  76.4 2.4 %collective-permute-start.14 = (f32[2,128,64]{1,2,0:T(8,128)S(1)}, f32[2,128,64]{1,2,0:T(8,128)S(1)}, u32[]{:S(2)}, u32[]{:S(2)}) collective-permute-start(f32[2,128,64]{1,2,0:T(8,128)S(1)} %maximum_select_fusion.1), channel_id=1, source_target_pairs={{0,16},{16,0},{1,17},{17,1},{2,18},{18,2},{3,19},{19,3},{4,20},{20... | collective-permute-start | bytes 196616 | tf_op jit(solution)/shard_map/ppermute | solution.py:23
  78.8 1.1 convolution_bitcast_fusion.1
  79.9 2.6 %collective-permute-done.14 = f32[2,128,64]{1,2,0:T(8,128)S(1)} collective-permute-done((f32[2,128,64]{1,2,0:T(8,128)S(1)}, f32[2,128,64]{1,2,0:T(8,128)S(1)}, u32[]{:S(2)}, u32[]{:S(2)}) %collective-permute-start.14) | collective-permute-done | bytes 65568 | tf_op jit(solution)/shard_map/ppermute | solution.py:23
  82.6 0.4 fusion.13
  83.1 0.7 pad_maximum_fusion
  83.8 7.1 %all-to-all-start = ((f32[256,8,32]{0,2,1:T(8,128)}), f32[256,8,32]{0,2,1:T(8,128)S(1)}, u32[]{:S(2)}, u32[]{:S(2)}) async-start(f32[256,8,32]{0,2,1:T(8,128)} %pad_maximum_fusion), calls=%async_computation | async-start | bytes 524288 | tf_op jit(solution)/shard_map/all_to_all | solution.py:176
  91.2 6.4 %all-to-all-done = f32[256,8,32]{0,2,1:T(8,128)S(1)} async-done(((f32[256,8,32]{0,2,1:T(8,128)}), f32[256,8,32]{0,2,1:T(8,128)S(1)}, u32[]{:S(2)}, u32[]{:S(2)}) %all-to-all-start) | async-done | bytes 262176 | tf_op jit(solution)/shard_map/all_to_all | solution.py:176
  97.6 0.5 multiply_bitcast_fusion
  98.1 2.1 %copy.51 = f32[1024,544]{1,0:T(8,128)} copy(f32[1024,544]{0,1:T(8,128)S(1)} %multiply_bitcast_fusion) | data formatting | bytes 4456448 | tf_op jit(solution)/shard_map/mul | solution.py:168
  100.2 1.4 dynamic-slice_convert_fusion
  101.5 1.9 %collective-permute-start.22 = (bf16[16,2,1,16,544]{4,3,2,1,0:T(8,128)(2,1)S(1)}, bf16[16,2,1,16,544]{4,3,2,1,0:T(8,128)(2,1)S(1)}, u32[]{:S(2)}, u32[]{:S(2)}) collective-permute-start(bf16[16,2,1,16,544]{4,3,2,1,0:T(8,128)(2,1)S(1)} %dynamic-slice_convert_fusion), channel_id=1, source_target_pairs={{0,8},{8,0},{1,9},{9,1},{2,10},{10,2},{3,11},{11,3},{4,12},{12,4},... | collective-permute-start | bytes 1671176 | tf_op jit(solution)/shard_map/ppermute | solution.py:23
  103.5 2.1 %collective-permute-done.22 = bf16[16,2,1,16,544]{4,3,2,1,0:T(8,128)(2,1)S(1)} collective-permute-done((bf16[16,2,1,16,544]{4,3,2,1,0:T(8,128)(2,1)S(1)}, bf16[16,2,1,16,544]{4,3,2,1,0:T(8,128)(2,1)S(1)}, u32[]{:S(2)}, u32[]{:S(2)}) %collective-permute-start.22) | collective-permute-done | bytes 557088 | tf_op jit(solution)/shard_map/ppermute | solution.py:23
  105.5 1.4 convert_add_fusion
  107.1 2.2 %collective-permute-start.23 = (bf16[16,1,1,16,544]{4,3,2,1,0:T(8,128)(2,1)S(1)}, bf16[16,1,1,16,544]{4,3,2,1,0:T(8,128)(2,1)}, u32[]{:S(2)}, u32[]{:S(2)}) collective-permute-start(bf16[16,1,1,16,544]{4,3,2,1,0:T(8,128)(2,1)S(1)} %dynamic-slice_convert_fusion.1), channel_id=1, source_target_pairs={{0,16},{16,0},{1,17},{17,1},{2,18},{18,2},{3,19},{19,3},{4,20},{20... | collective-permute-start | bytes 835592 | tf_op jit(solution)/shard_map/ppermute | solution.py:23
  109.2 9.7 %collective-permute-done.23 = bf16[16,1,1,16,544]{4,3,2,1,0:T(8,128)(2,1)} collective-permute-done((bf16[16,1,1,16,544]{4,3,2,1,0:T(8,128)(2,1)S(1)}, bf16[16,1,1,16,544]{4,3,2,1,0:T(8,128)(2,1)}, u32[]{:S(2)}, u32[]{:S(2)}) %collective-permute-start.23) | collective-permute-done | bytes 278560 | tf_op jit(solution)/shard_map/ppermute | solution.py:23
  118.9 1.8 %add_convert_fusion = bf16[16,1,1,16,544]{4,3,2,1,0:T(8,128)(2,1)} fusion(bf16[16,1,1,16,544]{4,3,2,1,0:T(8,128)(2,1)} %collective-permute-done.23, f32[16,2,1,16,544]{4,3,2,1,0:T(8,128)S(1)} %convert_add_fusion, s32[]{:T(128)S(6)} %select_n.224), kind=kLoop, calls=%fused_computation.30 | loop fusion | flops 417792 | bytes 1114116 | tf_op jit(solution)/shard_map/convert_element_type | solution.py:236
  120.7 11.7 %all-to-all-start.1 = ((bf16[16,1,1,16,544]{4,3,2,1,0:T(8,128)(2,1)}), bf16[16,1,1,16,544]{4,3,2,1,0:T(8,128)(2,1)S(1)}, u32[]{:S(2)}, u32[]{:S(2)}) async-start(bf16[16,1,1,16,544]{4,3,2,1,0:T(8,128)(2,1)} %add_convert_fusion), calls=%async_computation.1 | async-start | bytes 655360 | tf_op jit(solution)/shard_map/all_to_all | solution.py:176
  133.8 1.2 constant_dynamic-slice_fusion.7
  135.1 4.0 %collective-permute-start.21 = (bf16[256,128]{1,0:T(8,128)(2,1)S(1)}, bf16[256,128]{1,0:T(8,128)(2,1)S(1)}, u32[]{:S(2)}, u32[]{:S(2)}) collective-permute-start(bf16[256,128]{1,0:T(8,128)(2,1)S(1)} %bitcast.213), channel_id=1, source_target_pairs={{0,1},{1,2},{2,3},{3,4},{4,5},{5,6},{6,7},{7,0},{8,9},{9,10},{10,1... | collective-permute-start | bytes 196616 | tf_op jit(solution)/shard_map/ppermute | solution.py:190
  139.1 2.2 %collective-permute-start.20 = (bf16[256,128]{1,0:T(8,128)(2,1)S(1)}, bf16[256,128]{1,0:T(8,128)(2,1)S(1)}, u32[]{:S(2)}, u32[]{:S(2)}) collective-permute-start(bf16[256,128]{1,0:T(8,128)(2,1)S(1)} %bitcast.211), channel_id=1, source_target_pairs={{0,2},{1,3},{2,4},{3,5},{4,6},{5,7},{6,0},{7,1},{8,10},{9,11},{10,... | collective-permute-start | bytes 196616 | tf_op jit(solution)/shard_map/ppermute | solution.py:190
  141.4 5.7 %collective-permute-start.19 = (bf16[256,128]{1,0:T(8,128)(2,1)S(1)}, bf16[256,128]{1,0:T(8,128)(2,1)S(1)}, u32[]{:S(2)}, u32[]{:S(2)}) collective-permute-start(bf16[256,128]{1,0:T(8,128)(2,1)S(1)} %bitcast.210), channel_id=1, source_target_pairs={{0,3},{1,4},{2,5},{3,6},{4,7},{5,0},{6,1},{7,2},{8,11},{9,12},{10,... | collective-permute-start | bytes 196616 | tf_op jit(solution)/shard_map/ppermute | solution.py:190
  147.1 2.5 %collective-permute-start.18 = (bf16[256,128]{1,0:T(8,128)(2,1)S(1)}, bf16[256,128]{1,0:T(8,128)(2,1)S(1)}, u32[]{:S(2)}, u32[]{:S(2)}) collective-permute-start(bf16[256,128]{1,0:T(8,128)(2,1)S(1)} %bitcast.212), channel_id=1, source_target_pairs={{0,4},{1,5},{2,6},{3,7},{4,0},{5,1},{6,2},{7,3},{8,12},{9,13},{10,... | collective-permute-start | bytes 196616 | tf_op jit(solution)/shard_map/ppermute | solution.py:190
  149.6 3.7 %collective-permute-start.17 = (bf16[256,128]{1,0:T(8,128)(2,1)S(1)}, bf16[256,128]{1,0:T(8,128)(2,1)S(1)}, u32[]{:S(2)}, u32[]{:S(2)}) collective-permute-start(bf16[256,128]{1,0:T(8,128)(2,1)S(1)} %bitcast.214), channel_id=1, source_target_pairs={{0,5},{1,6},{2,7},{3,0},{4,1},{5,2},{6,3},{7,4},{8,13},{9,14},{10,... | collective-permute-start | bytes 196616 | tf_op jit(solution)/shard_map/ppermute | solution.py:190
  153.4 6.3 %collective-permute-start.16 = (bf16[256,128]{1,0:T(8,128)(2,1)S(1)}, bf16[256,128]{1,0:T(8,128)(2,1)S(1)}, u32[]{:S(2)}, u32[]{:S(2)}) collective-permute-start(bf16[256,128]{1,0:T(8,128)(2,1)S(1)} %bitcast.216), channel_id=1, source_target_pairs={{0,6},{1,7},{2,0},{3,1},{4,2},{5,3},{6,4},{7,5},{8,14},{9,15},{10,... | collective-permute-start | bytes 196616 | tf_op jit(solution)/shard_map/ppermute | solution.py:190
  159.7 1.9 %collective-permute-start.15 = (bf16[256,128]{1,0:T(8,128)(2,1)S(1)}, bf16[256,128]{1,0:T(8,128)(2,1)S(1)}, u32[]{:S(2)}, u32[]{:S(2)}) collective-permute-start(bf16[256,128]{1,0:T(8,128)(2,1)S(1)} %bitcast.215), channel_id=1, source_target_pairs={{0,7},{1,0},{2,1},{3,2},{4,3},{5,4},{6,5},{7,6},{8,15},{9,8},{10,9... | collective-permute-start | bytes 196616 | tf_op jit(solution)/shard_map/ppermute | solution.py:190
  161.7 1.8 %collective-permute-done.16 = bf16[256,128]{1,0:T(8,128)(2,1)S(1)} collective-permute-done((bf16[256,128]{1,0:T(8,128)(2,1)S(1)}, bf16[256,128]{1,0:T(8,128)(2,1)S(1)}, u32[]{:S(2)}, u32[]{:S(2)}) %collective-permute-start.16) | collective-permute-done | bytes 65568 | tf_op jit(solution)/shard_map/ppermute | solution.py:190
  163.5 6.1 %collective-permute-done.15 = bf16[256,128]{1,0:T(8,128)(2,1)S(1)} collective-permute-done((bf16[256,128]{1,0:T(8,128)(2,1)S(1)}, bf16[256,128]{1,0:T(8,128)(2,1)S(1)}, u32[]{:S(2)}, u32[]{:S(2)}) %collective-permute-start.15) | collective-permute-done | bytes 65568 | tf_op jit(solution)/shard_map/ppermute | solution.py:190
  169.5 0.7 fusion.41
  170.3 0.6 fusion.50
  170.9 0.6 slice.28
  (78 shorter events, 3.9 us)
Async XLA Ops:
  0.6 97.0 %copy-start = (bf16[256,1024]{1,0:T(8,128)(2,1)S(1)}, bf16[256,1024]{1,0:T(8,128)(2,1)}, u32[]{:S(2)}) copy-start(bf16[256,1024]{1,0:T(8,128)(2,1)} %param.11) | copy-start | bytes 1572868
  0.6 7.3 %copy-start.1 = (bf16[256,128]{1,0:T(8,128)(2,1)S(1)}, bf16[256,128]{1,0:T(8,128)(2,1)}, u32[]{:S(2)}) copy-start(bf16[256,128]{1,0:T(8,128)(2,1)} %param.16) | copy-start | bytes 196612
  0.7 6.9 %copy-start.6 = (bf16[256,256]{1,0:T(8,128)(2,1)S(1)}, bf16[256,256]{1,0:T(8,128)(2,1)}, u32[]{:S(2)}) copy-start(bf16[256,256]{1,0:T(8,128)(2,1)} %param.13) | copy-start | bytes 393220
  0.7 7.0 %copy-start.7 = (bf16[256,256]{1,0:T(8,128)(2,1)S(1)}, bf16[256,256]{1,0:T(8,128)(2,1)}, u32[]{:S(2)}) copy-start(bf16[256,256]{1,0:T(8,128)(2,1)} %param.14) | copy-start | bytes 393220
  0.7 9.9 %copy-start.8 = (bf16[256,256]{1,0:T(8,128)(2,1)S(1)}, bf16[256,256]{1,0:T(8,128)(2,1)}, u32[]{:S(2)}) copy-start(bf16[256,256]{1,0:T(8,128)(2,1)} %param.12) | copy-start | bytes 393220
  3.1 4.8 %collective-permute-start.1 = (f32[4]{0:T(128)S(1)}, f32[4]{0:T(128)S(1)}, u32[]{:S(2)}, u32[]{:S(2)}) collective-permute-start(f32[4]{0:T(128)S(1)} %fusion.49), channel_id=1, source_target_pairs={{0,8},{8,0},{1,9},{9,1},{2,10},{10,2},{3,11},{11,3},{4,12},{12,4},... | collective-permute-start | bytes 56 | tf_op jit(solution)/shard_map/ppermute | solution.py:23
  8.2 3.4 %collective-permute-start = (f32[4,128,64]{1,2,0:T(8,128)S(1)}, f32[4,128,64]{1,2,0:T(8,128)S(1)}, u32[]{:S(2)}, u32[]{:S(2)}) collective-permute-start(f32[4,128,64]{1,2,0:T(8,128)S(1)} %fusion.12), channel_id=1, source_target_pairs={{0,8},{8,0},{1,9},{9,1},{2,10},{10,2},{3,11},{11,3},{4,12},{12,4},... | collective-permute-start | bytes 393224 | tf_op jit(solution)/shard_map/ppermute | solution.py:23
  11.7 10.7 %collective-permute-start.2 = (f32[4,128,64]{1,2,0:T(8,128)S(1)}, f32[4,128,64]{1,2,0:T(8,128)S(1)}, u32[]{:S(2)}, u32[]{:S(2)}) collective-permute-start(f32[4,128,64]{1,2,0:T(8,128)S(1)} %add_select_fusion), channel_id=1, source_target_pairs={{0,16},{16,0},{1,17},{17,1},{2,18},{18,2},{3,19},{19,3},{4,20},{20... | collective-permute-start | bytes 393224 | tf_op jit(solution)/shard_map/ppermute | solution.py:23
  15.1 32.0 %copy-start.4 = (f32[1,4,128,64]{2,3,1,0:T(8,128)S(1)}, f32[1,4,128,64]{2,3,1,0:T(8,128)}, u32[]{:S(2)}) copy-start(f32[1,4,128,64]{2,3,1,0:T(8,128)} %param.18) | copy-start | bytes 393220
  16.2 42.6 %copy-start.2 = (bf16[256,128]{1,0:T(8,128)(2,1)S(1)}, bf16[256,128]{1,0:T(8,128)(2,1)}, u32[]{:S(2)}) copy-start(bf16[256,128]{1,0:T(8,128)(2,1)} %param.15) | copy-start | bytes 196612
  16.2 5.6 %collective-permute-start.3 = (f32[4]{0:T(128)S(1)}, f32[4]{0:T(128)S(1)}, u32[]{:S(2)}, u32[]{:S(2)}) collective-permute-start(f32[4]{0:T(128)S(1)} %get-tuple-element.51), channel_id=1, source_target_pairs={{0,16},{16,0},{1,17},{17,1},{2,18},{18,2},{3,19},{19,3},{4,20},{20... | collective-permute-start | bytes 56 | tf_op jit(solution)/shard_map/ppermute | solution.py:23
  23.7 10.5 %collective-permute-start.6 = (f32[128,64]{0,1:T(8,128)S(1)}, f32[128,64]{0,1:T(8,128)S(1)}, u32[]{:S(2)}, u32[]{:S(2)}) collective-permute-start(f32[128,64]{0,1:T(8,128)S(1)} %select_bitcast_fusion), channel_id=1, source_target_pairs={{64,0},{96,32},{128,64},{160,96},{192,128},{224,160},{256,192},{28... | collective-permute-start | bytes 98312 | tf_op jit(solution)/shard_map/ppermute | solution.py:28
  25.0 9.2 %collective-permute-start.4 = (f32[128,64]{0,1:T(8,128)S(1)}, f32[128,64]{0,1:T(8,128)S(1)}, u32[]{:S(2)}, u32[]{:S(2)}) collective-permute-start(f32[128,64]{0,1:T(8,128)S(1)} %select_bitcast_fusion), channel_id=1, source_target_pairs={{32,0},{64,32},{96,64},{128,96},{160,128},{192,160},{224,192},{256... | collective-permute-start | bytes 98312 | tf_op jit(solution)/shard_map/ppermute | solution.py:28
  27.6 6.0 %collective-permute-start.5 = (f32[]{:T(128)}, f32[]{:T(128)}, u32[]{:S(2)}, u32[]{:S(2)}) collective-permute-start(f32[]{:T(128)} %bitcast.34), channel_id=1, source_target_pairs={{32,0},{64,32},{96,64},{128,96},{160,128},{192,160},{224,192},{256... | collective-permute-start | bytes 20 | tf_op jit(solution)/shard_map/ppermute | solution.py:28
  34.2 11.6 %collective-permute-start.8 = (f32[128,64]{0,1:T(8,128)S(1)}, f32[128,64]{0,1:T(8,128)S(1)}, u32[]{:S(2)}, u32[]{:S(2)}) collective-permute-start(f32[128,64]{0,1:T(8,128)S(1)} %multiply_add_fusion), channel_id=1, source_target_pairs={{64,0},{96,32},{128,64},{160,96},{192,128},{224,160},{256,192},{28... | collective-permute-start | bytes 98312 | tf_op jit(solution)/shard_map/ppermute | solution.py:28
  36.3 8.8 %collective-permute-start.7 = (f32[]{:T(128)}, f32[]{:T(128)}, u32[]{:S(2)}, u32[]{:S(2)}) collective-permute-start(f32[]{:T(128)} %bitcast.34), channel_id=1, source_target_pairs={{64,0},{96,32},{128,64},{160,96},{192,128},{224,160},{256,192},{28... | collective-permute-start | bytes 20 | tf_op jit(solution)/shard_map/ppermute | solution.py:28
  45.8 11.6 %collective-permute-start.10 = (f32[128,64]{0,1:T(8,128)S(1)}, f32[128,64]{0,1:T(8,128)S(1)}, u32[]{:S(2)}, u32[]{:S(2)}) collective-permute-start(f32[128,64]{0,1:T(8,128)S(1)} %add_select_fusion.3), channel_id=1, source_target_pairs={{128,0},{160,32},{192,64},{224,96},{256,128},{288,160},{320,192},{... | collective-permute-start | bytes 98312 | tf_op jit(solution)/shard_map/ppermute | solution.py:28
  47.6 7.5 %collective-permute-start.9 = (f32[]{:T(128)}, f32[]{:T(128)}, u32[]{:S(2)}, u32[]{:S(2)}) collective-permute-start(f32[]{:T(128)} %mul.308), channel_id=1, source_target_pairs={{64,0},{96,32},{128,64},{160,96},{192,128},{224,160},{256,192},{28... | collective-permute-start | bytes 20 | tf_op jit(solution)/shard_map/ppermute | solution.py:28
  57.4 15.8 %collective-permute-start.12 = (f32[128,64]{0,1:T(8,128)S(1)}, f32[128,64]{0,1:T(8,128)S(1)}, u32[]{:S(2)}, u32[]{:S(2)}) collective-permute-start(f32[128,64]{0,1:T(8,128)S(1)} %add_select_fusion.2), channel_id=1, source_target_pairs={{256,0},{288,32},{320,64},{352,96},{384,128},{416,160},{448,192},{... | collective-permute-start | bytes 98312 | tf_op jit(solution)/shard_map/ppermute | solution.py:28
  59.1 9.6 %collective-permute-start.11 = (f32[]{:T(128)}, f32[]{:T(128)}, u32[]{:S(2)}, u32[]{:S(2)}) collective-permute-start(f32[]{:T(128)} %select_n.201), channel_id=1, source_target_pairs={{128,0},{160,32},{192,64},{224,96},{256,128},{288,160},{320,192},{... | collective-permute-start | bytes 20 | tf_op jit(solution)/shard_map/ppermute | solution.py:28
  73.3 3.1 %collective-permute-start.13 = (f32[128,64]{0,1:T(8,128)S(1)}, f32[128,64]{0,1:T(8,128)S(1)}, u32[]{:S(2)}, u32[]{:S(2)}) collective-permute-start(f32[128,64]{0,1:T(8,128)S(1)} %add_select_fusion.1), channel_id=1, source_target_pairs={{0,8},{8,0},{1,9},{9,1},{2,10},{10,2},{3,11},{11,3},{4,12},{12,4},... | collective-permute-start | bytes 98312 | tf_op jit(solution)/shard_map/ppermute | solution.py:23
  76.4 6.2 %collective-permute-start.14 = (f32[2,128,64]{1,2,0:T(8,128)S(1)}, f32[2,128,64]{1,2,0:T(8,128)S(1)}, u32[]{:S(2)}, u32[]{:S(2)}) collective-permute-start(f32[2,128,64]{1,2,0:T(8,128)S(1)} %maximum_select_fusion.1), channel_id=1, source_target_pairs={{0,16},{16,0},{1,17},{17,1},{2,18},{18,2},{3,19},{19,3},{4,20},{20... | collective-permute-start | bytes 196616 | tf_op jit(solution)/shard_map/ppermute | solution.py:23
  83.8 13.8 %all-to-all-start = ((f32[256,8,32]{0,2,1:T(8,128)}), f32[256,8,32]{0,2,1:T(8,128)S(1)}, u32[]{:S(2)}, u32[]{:S(2)}) async-start(f32[256,8,32]{0,2,1:T(8,128)} %pad_maximum_fusion), calls=%async_computation | async-start | bytes 524288 | tf_op jit(solution)/shard_map/all_to_all | solution.py:176
  101.5 4.0 %collective-permute-start.22 = (bf16[16,2,1,16,544]{4,3,2,1,0:T(8,128)(2,1)S(1)}, bf16[16,2,1,16,544]{4,3,2,1,0:T(8,128)(2,1)S(1)}, u32[]{:S(2)}, u32[]{:S(2)}) collective-permute-start(bf16[16,2,1,16,544]{4,3,2,1,0:T(8,128)(2,1)S(1)} %dynamic-slice_convert_fusion), channel_id=1, source_target_pairs={{0,8},{8,0},{1,9},{9,1},{2,10},{10,2},{3,11},{11,3},{4,12},{12,4},... | collective-permute-start | bytes 1671176 | tf_op jit(solution)/shard_map/ppermute | solution.py:23
  103.5 29.0 %copy-start.3 = (bf16[1024,256]{1,0:T(8,128)(2,1)S(1)}, bf16[1024,256]{1,0:T(8,128)(2,1)}, u32[]{:S(2)}) copy-start(bf16[1024,256]{1,0:T(8,128)(2,1)} %param.19) | copy-start | bytes 1572868
  107.0 26.0 %copy-start.5 = (bf16[1024,256]{1,0:T(8,128)(2,1)S(1)}, bf16[1024,256]{1,0:T(8,128)(2,1)}, u32[]{:S(2)}) copy-start(bf16[1024,256]{1,0:T(8,128)(2,1)} %param.20) | copy-start | bytes 1572868
  107.1 11.9 %collective-permute-start.23 = (bf16[16,1,1,16,544]{4,3,2,1,0:T(8,128)(2,1)S(1)}, bf16[16,1,1,16,544]{4,3,2,1,0:T(8,128)(2,1)}, u32[]{:S(2)}, u32[]{:S(2)}) collective-permute-start(bf16[16,1,1,16,544]{4,3,2,1,0:T(8,128)(2,1)S(1)} %dynamic-slice_convert_fusion.1), channel_id=1, source_target_pairs={{0,16},{16,0},{1,17},{17,1},{2,18},{18,2},{3,19},{19,3},{4,20},{20... | collective-permute-start | bytes 835592 | tf_op jit(solution)/shard_map/ppermute | solution.py:23
  120.7 49.5 %all-to-all-start.1 = ((bf16[16,1,1,16,544]{4,3,2,1,0:T(8,128)(2,1)}), bf16[16,1,1,16,544]{4,3,2,1,0:T(8,128)(2,1)S(1)}, u32[]{:S(2)}, u32[]{:S(2)}) async-start(bf16[16,1,1,16,544]{4,3,2,1,0:T(8,128)(2,1)} %add_convert_fusion), calls=%async_computation.1 | async-start | bytes 655360 | tf_op jit(solution)/shard_map/all_to_all | solution.py:176
  132.5 0.9 copy-start.9
  135.1 18.3 %collective-permute-start.21 = (bf16[256,128]{1,0:T(8,128)(2,1)S(1)}, bf16[256,128]{1,0:T(8,128)(2,1)S(1)}, u32[]{:S(2)}, u32[]{:S(2)}) collective-permute-start(bf16[256,128]{1,0:T(8,128)(2,1)S(1)} %bitcast.213), channel_id=1, source_target_pairs={{0,1},{1,2},{2,3},{3,4},{4,5},{5,6},{6,7},{7,0},{8,9},{9,10},{10,1... | collective-permute-start | bytes 196616 | tf_op jit(solution)/shard_map/ppermute | solution.py:190
  139.1 20.6 %collective-permute-start.20 = (bf16[256,128]{1,0:T(8,128)(2,1)S(1)}, bf16[256,128]{1,0:T(8,128)(2,1)S(1)}, u32[]{:S(2)}, u32[]{:S(2)}) collective-permute-start(bf16[256,128]{1,0:T(8,128)(2,1)S(1)} %bitcast.211), channel_id=1, source_target_pairs={{0,2},{1,3},{2,4},{3,5},{4,6},{5,7},{6,0},{7,1},{8,10},{9,11},{10,... | collective-permute-start | bytes 196616 | tf_op jit(solution)/shard_map/ppermute | solution.py:190
  141.4 20.3 %collective-permute-start.19 = (bf16[256,128]{1,0:T(8,128)(2,1)S(1)}, bf16[256,128]{1,0:T(8,128)(2,1)S(1)}, u32[]{:S(2)}, u32[]{:S(2)}) collective-permute-start(bf16[256,128]{1,0:T(8,128)(2,1)S(1)} %bitcast.210), channel_id=1, source_target_pairs={{0,3},{1,4},{2,5},{3,6},{4,7},{5,0},{6,1},{7,2},{8,11},{9,12},{10,... | collective-permute-start | bytes 196616 | tf_op jit(solution)/shard_map/ppermute | solution.py:190
  147.1 14.6 %collective-permute-start.18 = (bf16[256,128]{1,0:T(8,128)(2,1)S(1)}, bf16[256,128]{1,0:T(8,128)(2,1)S(1)}, u32[]{:S(2)}, u32[]{:S(2)}) collective-permute-start(bf16[256,128]{1,0:T(8,128)(2,1)S(1)} %bitcast.212), channel_id=1, source_target_pairs={{0,4},{1,5},{2,6},{3,7},{4,0},{5,1},{6,2},{7,3},{8,12},{9,13},{10,... | collective-permute-start | bytes 196616 | tf_op jit(solution)/shard_map/ppermute | solution.py:190
  149.6 12.1 %collective-permute-start.17 = (bf16[256,128]{1,0:T(8,128)(2,1)S(1)}, bf16[256,128]{1,0:T(8,128)(2,1)S(1)}, u32[]{:S(2)}, u32[]{:S(2)}) collective-permute-start(bf16[256,128]{1,0:T(8,128)(2,1)S(1)} %bitcast.214), channel_id=1, source_target_pairs={{0,5},{1,6},{2,7},{3,0},{4,1},{5,2},{6,3},{7,4},{8,13},{9,14},{10,... | collective-permute-start | bytes 196616 | tf_op jit(solution)/shard_map/ppermute | solution.py:190
  153.4 10.1 %collective-permute-start.16 = (bf16[256,128]{1,0:T(8,128)(2,1)S(1)}, bf16[256,128]{1,0:T(8,128)(2,1)S(1)}, u32[]{:S(2)}, u32[]{:S(2)}) collective-permute-start(bf16[256,128]{1,0:T(8,128)(2,1)S(1)} %bitcast.216), channel_id=1, source_target_pairs={{0,6},{1,7},{2,0},{3,1},{4,2},{5,3},{6,4},{7,5},{8,14},{9,15},{10,... | collective-permute-start | bytes 196616 | tf_op jit(solution)/shard_map/ppermute | solution.py:190
  159.7 9.8 %collective-permute-start.15 = (bf16[256,128]{1,0:T(8,128)(2,1)S(1)}, bf16[256,128]{1,0:T(8,128)(2,1)S(1)}, u32[]{:S(2)}, u32[]{:S(2)}) collective-permute-start(bf16[256,128]{1,0:T(8,128)(2,1)S(1)} %bitcast.215), channel_id=1, source_target_pairs={{0,7},{1,0},{2,1},{3,2},{4,3},{5,4},{6,5},{7,6},{8,15},{9,8},{10,9... | collective-permute-start | bytes 196616 | tf_op jit(solution)/shard_map/ppermute | solution.py:190

commit v10 on v5

--- a/solution.py
+++ b/solution.py
@@ -223,6 +223,8 @@
     sizes = [lax.axis_size(name) for name in CTX]
     rows = rows.reshape(*sizes, rows.shape[0] // math.prod(sizes), rows.shape[1])
     for level in reversed(range(len(CTX))):
+        if level == 0:
+            rows, grad_input = lax.optimization_barrier((rows, grad_input))
         rows = summed_over(rows.astype(jnp.bfloat16), CTX[level], level)
     reduced = rows.reshape(rows.shape[-2], rows.shape[-1])
     grad_w_gate = reduced[:, :head_cols]

time: 168 us -> 190 us (1.13)
  the two profiles are of different devices: /device:TPU:32 before, /device:TPU:16 now
where the time goes in v10:
time: 190 us; the launch traced here: 188 us
  starting transfers between devices  67.2 us (35%)
  waiting for transfers between devices  49.3 us (26%)
  blocking collectives  38.3 us (20%)
  local copies, waits for them, and re-layouts  10.9 us (6%)
  matrix products  10.1 us (5%)
  other arithmetic  8.32 us (4%)
  between operations  4.31 us (2%)
    all_to_all x2, blocking collectives, summed_over(): gathered = lax.all_to_all(part, axis, split, split, tiled=True)  38.3 us
    ppermute x9, waiting for transfers between devices, shift(): return jax.tree.map(lambda a: lax.ppermute(a, axis, pairs), tree)  31.7 us
    ppermute x7, starting transfers between devices, spread_sum(): total = total + lax.ppermute(piece, axis, pairs).astype(jnp.float32)  29.9 us
    ppermute x6, starting transfers between devices, swap(): return jax.tree.map(lambda a: lax.ppermute(a, axis, [(0, 1), (1, 0)]), tree)  14.9 us
    all_to_all x2, waiting for transfers between devices, summed_over(): gathered = lax.all_to_all(part, axis, split, split, tiled=True)  13.7 us
    ppermute x9, starting transfers between devices, shift(): return jax.tree.map(lambda a: lax.ppermute(a, axis, pairs), tree)  11.6 us
    all_to_all x2, starting transfers between devices, summed_over(): gathered = lax.all_to_all(part, axis, split, split, tiled=True)  10.8 us
    ppermute x6, waiting for transfers between devices, swap(): return jax.tree.map(lambda a: lax.ppermute(a, axis, [(0, 1), (1, 0)]), tree)  3.93 us
  transfers between devices with their start and end apart: 24, of which 11 were waited for; matrix products, arithmetic and copies ran while one was open for 9% of the time, Pallas kernels for 0%

profile of v10, /device:TPU:16, one launch (start us, length us, event | category | flops | bytes accessed | tf_op | source)
XLA Modules:
  0.0 188.4 jit_solution(3760121092185924077)
XLA Ops:
  0.7 0.8 reshape.410
  1.5 1.2 reduce-window.6
  3.1 1.9 %collective-permute-start.1 = (f32[4]{0:T(128)S(1)}, f32[4]{0:T(128)S(1)}, u32[]{:S(2)}, u32[]{:S(2)}) collective-permute-start(f32[4]{0:T(128)S(1)} %fusion.50), channel_id=1, source_target_pairs={{0,8},{8,0},{1,9},{9,1},{2,10},{10,2},{3,11},{11,3},{4,12},{12,4},... | collective-permute-start | bytes 56 | tf_op jit(solution)/shard_map/ppermute | solution.py:23
  6.6 2.4 %collective-permute-start = (f32[4,128,64]{1,2,0:T(8,128)S(1)}, f32[4,128,64]{1,2,0:T(8,128)S(1)}, u32[]{:S(2)}, u32[]{:S(2)}) collective-permute-start(f32[4,128,64]{1,2,0:T(8,128)S(1)} %fusion.13), channel_id=1, source_target_pairs={{0,8},{8,0},{1,9},{9,1},{2,10},{10,2},{3,11},{11,3},{4,12},{12,4},... | collective-permute-start | bytes 393224 | tf_op jit(solution)/shard_map/ppermute | solution.py:23
  9.0 1.0 fusion.12
  10.1 3.2 %collective-permute-start.2 = (f32[4,128,64]{1,2,0:T(8,128)S(1)}, f32[4,128,64]{1,2,0:T(8,128)S(1)}, u32[]{:S(2)}, u32[]{:S(2)}) collective-permute-start(f32[4,128,64]{1,2,0:T(8,128)S(1)} %add_select_fusion), channel_id=1, source_target_pairs={{0,16},{16,0},{1,17},{17,1},{2,18},{18,2},{3,19},{19,3},{4,20},{20... | collective-permute-start | bytes 393224 | tf_op jit(solution)/shard_map/ppermute | solution.py:23
  13.8 2.7 %collective-permute-start.3 = (f32[4]{0:T(128)S(1)}, f32[4]{0:T(128)S(1)}, u32[]{:S(2)}, u32[]{:S(2)}) collective-permute-start(f32[4]{0:T(128)S(1)} %get-tuple-element.53), channel_id=1, source_target_pairs={{0,16},{16,0},{1,17},{17,1},{2,18},{18,2},{3,19},{19,3},{4,20},{20... | collective-permute-start | bytes 56 | tf_op jit(solution)/shard_map/ppermute | solution.py:23
  16.4 0.6 dynamic-slice.34
  17.0 2.2 %collective-permute-done.3 = f32[4]{0:T(128)S(1)} collective-permute-done((f32[4]{0:T(128)S(1)}, f32[4]{0:T(128)S(1)}, u32[]{:S(2)}, u32[]{:S(2)}) %collective-permute-start.3) | collective-permute-done | bytes 48 | tf_op jit(solution)/shard_map/ppermute | solution.py:23
  19.2 0.6 dynamic-slice.35
  19.8 1.3 select_bitcast_fusion
  21.1 1.3 collective-permute-start.6
  22.4 1.3 collective-permute-start.4
  23.7 1.2 fusion.46
  24.9 0.6 dynamic_slice.31
  25.5 1.3 collective-permute-start.5
  26.8 4.9 %collective-permute-done.5 = f32[]{:T(128)} collective-permute-done((f32[]{:T(128)}, f32[]{:T(128)}, u32[]{:S(2)}, u32[]{:S(2)}) %collective-permute-start.5) | collective-permute-done | bytes 36 | tf_op jit(solution)/shard_map/ppermute | solution.py:28
  32.4 1.3 collective-permute-start.8
  33.7 0.8 fusion.2
  34.5 1.3 collective-permute-start.7
  35.8 6.8 %collective-permute-done.7 = f32[]{:T(128)} collective-permute-done((f32[]{:T(128)}, f32[]{:T(128)}, u32[]{:S(2)}, u32[]{:S(2)}) %collective-permute-start.7) | collective-permute-done | bytes 36 | tf_op jit(solution)/shard_map/ppermute | solution.py:28
  43.4 1.3 collective-permute-start.10
  45.1 1.3 collective-permute-start.9
  46.4 6.6 %collective-permute-done.9 = f32[]{:T(128)} collective-permute-done((f32[]{:T(128)}, f32[]{:T(128)}, u32[]{:S(2)}, u32[]{:S(2)}) %collective-permute-start.9) | collective-permute-done | bytes 36 | tf_op jit(solution)/shard_map/ppermute | solution.py:28
  53.7 0.7 collective-permute-done.10
  54.4 1.3 collective-permute-start.12
  56.0 1.3 collective-permute-start.11
  57.3 9.3 %collective-permute-done.11 = f32[]{:T(128)} collective-permute-done((f32[]{:T(128)}, f32[]{:T(128)}, u32[]{:S(2)}, u32[]{:S(2)}) %collective-permute-start.11) | collective-permute-done | bytes 36 | tf_op jit(solution)/shard_map/ppermute | solution.py:28
  67.3 3.3 %collective-permute-done.12 = f32[128,64]{0,1:T(8,128)S(1)} collective-permute-done((f32[128,64]{0,1:T(8,128)S(1)}, f32[128,64]{0,1:T(8,128)S(1)}, u32[]{:S(2)}, u32[]{:S(2)}) %collective-permute-start.12) | collective-permute-done | bytes 32800 | tf_op jit(solution)/shard_map/ppermute | solution.py:28
  70.7 1.9 %collective-permute-start.13 = (f32[128,64]{0,1:T(8,128)S(1)}, f32[128,64]{0,1:T(8,128)S(1)}, u32[]{:S(2)}, u32[]{:S(2)}) collective-permute-start(f32[128,64]{0,1:T(8,128)S(1)} %add_select_fusion.1), channel_id=1, source_target_pairs={{0,8},{8,0},{1,9},{9,1},{2,10},{10,2},{3,11},{11,3},{4,12},{12,4},... | collective-permute-start | bytes 98312 | tf_op jit(solution)/shard_map/ppermute | solution.py:23
  72.9 0.9 collective-permute-done.13
  73.8 2.8 %collective-permute-start.14 = (f32[2,128,64]{1,2,0:T(8,128)S(1)}, f32[2,128,64]{1,2,0:T(8,128)}, u32[]{:S(2)}, u32[]{:S(2)}) collective-permute-start(f32[2,128,64]{1,2,0:T(8,128)S(1)} %maximum_select_fusion.1), channel_id=1, source_target_pairs={{0,16},{16,0},{1,17},{17,1},{2,18},{18,2},{3,19},{19,3},{4,20},{20... | collective-permute-start | bytes 196616 | tf_op jit(solution)/shard_map/ppermute | solution.py:23
  76.6 2.6 %convolution_bitcast_fusion.1 = f32[1,256,4,64]{1,3,2,0:T(8,128)} fusion(f32[256,4,64]{0,2,1:T(8,128)S(1)} %bitcast.208, f32[256,256]{1,0:T(8,128)S(1)} %fusion.52, f32[4,256]{1,0:T(4,128)S(1)} %bitcast_add_fusion.1, pred[256,256]{1,0:T(8,128)(4,1)} %copy-done.13), kind=kOutput, calls=%fused_computation.12 | convolution fusion | flops 202375168 | bytes 856064 | tf_op jit(solution)/shard_map/hkst,kshp->kthp/dot_general | solution.py:107
  79.4 0.8 collective-permute-done.14
  80.2 1.0 fusion.35
  81.2 1.2 fusion.11
  82.9 0.7 pad_maximum_fusion
  83.6 7.3 %all-to-all-start = ((f32[256,8,32]{0,2,1:T(8,128)}), f32[256,8,32]{0,2,1:T(8,128)S(1)}, u32[]{:S(2)}, u32[]{:S(2)}) async-start(f32[256,8,32]{0,2,1:T(8,128)} %pad_maximum_fusion), calls=%async_computation | async-start | bytes 524288 | tf_op jit(solution)/shard_map/all_to_all | solution.py:176
  91.2 5.5 %all-to-all-done = f32[256,8,32]{0,2,1:T(8,128)S(1)} async-done(((f32[256,8,32]{0,2,1:T(8,128)}), f32[256,8,32]{0,2,1:T(8,128)S(1)}, u32[]{:S(2)}, u32[]{:S(2)}) %all-to-all-start) | async-done | bytes 262176 | tf_op jit(solution)/shard_map/all_to_all | solution.py:176
  96.7 1.2 fusion.3
  98.0 1.2 constant_dynamic-slice_fusion.7
  99.2 2.8 %collective-permute-start.21 = (bf16[256,128]{1,0:T(8,128)(2,1)S(1)}, bf16[256,128]{1,0:T(8,128)(2,1)S(1)}, u32[]{:S(2)}, u32[]{:S(2)}) collective-permute-start(bf16[256,128]{1,0:T(8,128)(2,1)S(1)} %bitcast.214), channel_id=1, source_target_pairs={{0,1},{1,2},{2,3},{3,4},{4,5},{5,6},{6,7},{7,0},{8,9},{9,10},{10,1... | collective-permute-start | bytes 196616 | tf_op jit(solution)/shard_map/ppermute | solution.py:190
  102.0 6.7 %collective-permute-start.15 = (bf16[256,128]{1,0:T(8,128)(2,1)S(1)}, bf16[256,128]{1,0:T(8,128)(2,1)S(1)}, u32[]{:S(2)}, u32[]{:S(2)}) collective-permute-start(bf16[256,128]{1,0:T(8,128)(2,1)S(1)} %bitcast.213), channel_id=1, source_target_pairs={{0,7},{1,0},{2,1},{3,2},{4,3},{5,4},{6,5},{7,6},{8,15},{9,8},{10,9... | collective-permute-start | bytes 196616 | tf_op jit(solution)/shard_map/ppermute | solution.py:190
  108.7 0.6 copy.117
  109.4 0.6 copy.118
  110.0 0.6 copy.119
  110.6 0.6 copy.120
  111.3 0.6 copy.121
  111.9 1.9 %collective-permute-start.16 = (bf16[256,128]{1,0:T(8,128)(2,1)}, bf16[256,128]{1,0:T(8,128)(2,1)}, u32[]{:S(2)}, u32[]{:S(2)}) collective-permute-start(bf16[256,128]{1,0:T(8,128)(2,1)} %bitcast.184), channel_id=1, source_target_pairs={{0,6},{1,7},{2,0},{3,1},{4,2},{5,3},{6,4},{7,5},{8,14},{9,15},{10,... | collective-permute-start | bytes 196616 | tf_op jit(solution)/shard_map/ppermute | solution.py:190
  113.8 5.2 %collective-permute-start.17 = (bf16[256,128]{1,0:T(8,128)(2,1)}, bf16[256,128]{1,0:T(8,128)(2,1)}, u32[]{:S(2)}, u32[]{:S(2)}) collective-permute-start(bf16[256,128]{1,0:T(8,128)(2,1)} %bitcast.183), channel_id=1, source_target_pairs={{0,5},{1,6},{2,7},{3,0},{4,1},{5,2},{6,3},{7,4},{8,13},{9,14},{10,... | collective-permute-start | bytes 196616 | tf_op jit(solution)/shard_map/ppermute | solution.py:190
  119.0 2.5 %collective-permute-start.18 = (bf16[256,128]{1,0:T(8,128)(2,1)}, bf16[256,128]{1,0:T(8,128)(2,1)}, u32[]{:S(2)}, u32[]{:S(2)}) collective-permute-start(bf16[256,128]{1,0:T(8,128)(2,1)} %bitcast.182), channel_id=1, source_target_pairs={{0,4},{1,5},{2,6},{3,7},{4,0},{5,1},{6,2},{7,3},{8,12},{9,13},{10,... | collective-permute-start | bytes 196616 | tf_op jit(solution)/shard_map/ppermute | solution.py:190
  121.5 4.3 %collective-permute-start.19 = (bf16[256,128]{1,0:T(8,128)(2,1)}, bf16[256,128]{1,0:T(8,128)(2,1)}, u32[]{:S(2)}, u32[]{:S(2)}) collective-permute-start(bf16[256,128]{1,0:T(8,128)(2,1)} %bitcast.181), channel_id=1, source_target_pairs={{0,3},{1,4},{2,5},{3,6},{4,7},{5,0},{6,1},{7,2},{8,11},{9,12},{10,... | collective-permute-start | bytes 196616 | tf_op jit(solution)/shard_map/ppermute | solution.py:190
  125.8 6.6 %collective-permute-start.20 = (bf16[256,128]{1,0:T(8,128)(2,1)}, bf16[256,128]{1,0:T(8,128)(2,1)}, u32[]{:S(2)}, u32[]{:S(2)}) collective-permute-start(bf16[256,128]{1,0:T(8,128)(2,1)} %bitcast.180), channel_id=1, source_target_pairs={{0,2},{1,3},{2,4},{3,5},{4,6},{5,7},{6,0},{7,1},{8,10},{9,11},{10,... | collective-permute-start | bytes 196616 | tf_op jit(solution)/shard_map/ppermute | solution.py:190
  132.4 0.5 fusion
  132.9 0.7 copy.82
  133.8 4.8 %all_to_all.21 = bf16[16,2,2,16,544]{4,3,1,0,2:T(8,128)(2,1)S(1)} all-to-all(bf16[16,2,2,16,544]{4,3,1,0,2:T(8,128)(2,1)S(1)} %copy.83), channel_id=1, replica_groups=mesh['z'=16,'y_lo'=2,'core'=2,'y_hi'=2,'x'=4] {'core'}, dimensions={2} | all-to-all | bytes 2228224 | tf_op jit(solution)/shard_map/all_to_all | solution.py:176
  138.5 0.6 reduce_sum.60
  139.2 0.9 copy.84
  140.1 3.5 %all-to-all-start.2 = ((bf16[16,2,1,16,544]{4,3,0,2,1:T(8,128)(2,1)}), bf16[16,2,1,16,544]{4,3,0,2,1:T(8,128)(2,1)S(1)}, u32[]{:S(2)}, u32[]{:S(2)}) async-start(bf16[16,2,1,16,544]{4,3,0,2,1:T(8,128)(2,1)} %copy.84), calls=%async_computation.2 | async-start | bytes 1310720 | tf_op jit(solution)/shard_map/all_to_all | solution.py:176
  143.6 1.7 fusion.42
  145.3 8.2 %all-to-all-done.2 = bf16[16,2,1,16,544]{4,3,0,2,1:T(8,128)(2,1)S(1)} async-done(((bf16[16,2,1,16,544]{4,3,0,2,1:T(8,128)(2,1)}), bf16[16,2,1,16,544]{4,3,0,2,1:T(8,128)(2,1)S(1)}, u32[]{:S(2)}, u32[]{:S(2)}) %all-to-all-start.2) | async-done | bytes 557088 | tf_op jit(solution)/shard_map/all_to_all | solution.py:176
  153.6 33.5 %all_to_all.22 = bf16[16,1,1,16,544]{4,3,2,1,0:T(8,128)(2,1)S(1)} all-to-all(bf16[16,1,1,16,544]{4,3,2,1,0:T(8,128)(2,1)S(1)} %bitcast.196), channel_id=1, replica_groups=mesh['z'=16,'y_lo'=2,'core'=2,'y_hi'=2,'x'=4] {'z'}, dimensions={0} | all-to-all | bytes 557056 | tf_op jit(solution)/shard_map/all_to_all | solution.py:176
  187.2 0.6 slice.28
  187.8 0.6 fusion.51
  (88 shorter events, 4.6 us)
Async XLA Ops:
  0.6 131.8 %copy-start = (bf16[256,1024]{1,0:T(8,128)(2,1)S(1)}, bf16[256,1024]{1,0:T(8,128)(2,1)}, u32[]{:S(2)}) copy-start(bf16[256,1024]{1,0:T(8,128)(2,1)} %param.11) | copy-start | bytes 1572868
  0.6 4.7 %copy-start.8 = (bf16[256,256]{1,0:T(8,128)(2,1)S(1)}, bf16[256,256]{1,0:T(8,128)(2,1)}, u32[]{:S(2)}) copy-start(bf16[256,256]{1,0:T(8,128)(2,1)} %param.12) | copy-start | bytes 393220
  0.7 4.8 %copy-start.9 = (bf16[256,256]{1,0:T(8,128)(2,1)S(1)}, bf16[256,256]{1,0:T(8,128)(2,1)}, u32[]{:S(2)}) copy-start(bf16[256,256]{1,0:T(8,128)(2,1)} %param.13) | copy-start | bytes 393220
  0.7 4.9 %copy-start.10 = (bf16[256,256]{1,0:T(8,128)(2,1)S(1)}, bf16[256,256]{1,0:T(8,128)(2,1)}, u32[]{:S(2)}) copy-start(bf16[256,256]{1,0:T(8,128)(2,1)} %param.14) | copy-start | bytes 393220
  0.7 5.0 %copy-start.1 = (bf16[256,128]{1,0:T(8,128)(2,1)S(1)}, bf16[256,128]{1,0:T(8,128)(2,1)}, u32[]{:S(2)}) copy-start(bf16[256,128]{1,0:T(8,128)(2,1)} %param.16) | copy-start | bytes 196612
  0.7 5.0 %copy-start.2 = (bf16[256,128]{1,0:T(8,128)(2,1)S(1)}, bf16[256,128]{1,0:T(8,128)(2,1)}, u32[]{:S(2)}) copy-start(bf16[256,128]{1,0:T(8,128)(2,1)} %param.15) | copy-start | bytes 196612
  2.9 3.0 %copy-start.4 = (f32[1,4,128,64]{2,3,1,0:T(8,128)S(1)}, f32[1,4,128,64]{2,3,1,0:T(8,128)}, u32[]{:S(2)}) copy-start(f32[1,4,128,64]{2,3,1,0:T(8,128)} %param.18) | copy-start | bytes 393220
  3.1 3.2 %collective-permute-start.1 = (f32[4]{0:T(128)S(1)}, f32[4]{0:T(128)S(1)}, u32[]{:S(2)}, u32[]{:S(2)}) collective-permute-start(f32[4]{0:T(128)S(1)} %fusion.50), channel_id=1, source_target_pairs={{0,8},{8,0},{1,9},{9,1},{2,10},{10,2},{3,11},{11,3},{4,12},{12,4},... | collective-permute-start | bytes 56 | tf_op jit(solution)/shard_map/ppermute | solution.py:23
  5.1 8.3 %copy-start.13 = (pred[256,256]{1,0:T(8,128)(4,1)}, pred[256,256]{1,0:T(8,128)(4,1)S(1)}, u32[]{:S(2)}) copy-start(pred[256,256]{1,0:T(8,128)(4,1)S(1)} %iota_compare_fusion) | copy-start | bytes 196612
  6.3 10.1 %copy-start.15 = (f32[4]{0:T(128)}, f32[4]{0:T(128)S(1)}, u32[]{:S(2)}) copy-start(f32[4]{0:T(128)S(1)} %get-tuple-element.53) | copy-start | bytes 52
  6.6 3.4 %collective-permute-start = (f32[4,128,64]{1,2,0:T(8,128)S(1)}, f32[4,128,64]{1,2,0:T(8,128)S(1)}, u32[]{:S(2)}, u32[]{:S(2)}) collective-permute-start(f32[4,128,64]{1,2,0:T(8,128)S(1)} %fusion.13), channel_id=1, source_target_pairs={{0,8},{8,0},{1,9},{9,1},{2,10},{10,2},{3,11},{11,3},{4,12},{12,4},... | collective-permute-start | bytes 393224 | tf_op jit(solution)/shard_map/ppermute | solution.py:23
  9.0 4.4 %copy-start.3 = (bf16[1024,256]{1,0:T(8,128)(2,1)S(1)}, bf16[1024,256]{1,0:T(8,128)(2,1)}, u32[]{:S(2)}) copy-start(bf16[1024,256]{1,0:T(8,128)(2,1)} %param.19) | copy-start | bytes 1572868
  10.0 3.3 %copy-start.11 = (bf16[1,256,4,64]{1,3,2,0:T(8,128)(2,1)}, bf16[1,256,4,64]{1,3,2,0:T(8,128)(2,1)S(1)}, u32[]{:S(2)}) copy-start(bf16[1,256,4,64]{1,3,2,0:T(8,128)(2,1)S(1)} %fusion.12) | copy-start | bytes 393220
  10.1 9.7 %collective-permute-start.2 = (f32[4,128,64]{1,2,0:T(8,128)S(1)}, f32[4,128,64]{1,2,0:T(8,128)S(1)}, u32[]{:S(2)}, u32[]{:S(2)}) collective-permute-start(f32[4,128,64]{1,2,0:T(8,128)S(1)} %add_select_fusion), channel_id=1, source_target_pairs={{0,16},{16,0},{1,17},{17,1},{2,18},{18,2},{3,19},{19,3},{4,20},{20... | collective-permute-start | bytes 393224 | tf_op jit(solution)/shard_map/ppermute | solution.py:23
  13.4 20.3 %copy-start.14 = (pred[256,256]{1,0:T(8,128)(4,1)S(1)}, pred[256,256]{1,0:T(8,128)(4,1)}, u32[]{:S(2)}) copy-start(pred[256,256]{1,0:T(8,128)(4,1)} %copy-done.13) | copy-start | bytes 196612
  13.8 5.5 %collective-permute-start.3 = (f32[4]{0:T(128)S(1)}, f32[4]{0:T(128)S(1)}, u32[]{:S(2)}, u32[]{:S(2)}) collective-permute-start(f32[4]{0:T(128)S(1)} %get-tuple-element.53), channel_id=1, source_target_pairs={{0,16},{16,0},{1,17},{17,1},{2,18},{18,2},{3,19},{19,3},{4,20},{20... | collective-permute-start | bytes 56 | tf_op jit(solution)/shard_map/ppermute | solution.py:23
  19.8 13.9 %copy-start.6 = (f32[4,128,64]{1,2,0:T(8,128)}, f32[4,128,64]{1,2,0:T(8,128)S(1)}, u32[]{:S(2)}) copy-start(f32[4,128,64]{1,2,0:T(8,128)S(1)} %collective-permute-done.2) | copy-start | bytes 393220
  21.1 11.2 %collective-permute-start.6 = (f32[128,64]{0,1:T(8,128)S(1)}, f32[128,64]{0,1:T(8,128)S(1)}, u32[]{:S(2)}, u32[]{:S(2)}) collective-permute-start(f32[128,64]{0,1:T(8,128)S(1)} %select_bitcast_fusion), channel_id=1, source_target_pairs={{64,0},{96,32},{128,64},{160,96},{192,128},{224,160},{256,192},{28... | collective-permute-start | bytes 98312 | tf_op jit(solution)/shard_map/ppermute | solution.py:28
  22.4 9.9 %collective-permute-start.4 = (f32[128,64]{0,1:T(8,128)S(1)}, f32[128,64]{0,1:T(8,128)S(1)}, u32[]{:S(2)}, u32[]{:S(2)}) collective-permute-start(f32[128,64]{0,1:T(8,128)S(1)} %select_bitcast_fusion), channel_id=1, source_target_pairs={{32,0},{64,32},{96,64},{128,96},{160,128},{192,160},{224,192},{256... | collective-permute-start | bytes 98312 | tf_op jit(solution)/shard_map/ppermute | solution.py:28
  25.5 6.2 %collective-permute-start.5 = (f32[]{:T(128)}, f32[]{:T(128)}, u32[]{:S(2)}, u32[]{:S(2)}) collective-permute-start(f32[]{:T(128)} %bitcast.34), channel_id=1, source_target_pairs={{32,0},{64,32},{96,64},{128,96},{160,128},{192,160},{224,192},{256... | collective-permute-start | bytes 20 | tf_op jit(solution)/shard_map/ppermute | solution.py:28
  32.4 11.0 %collective-permute-start.8 = (f32[128,64]{0,1:T(8,128)S(1)}, f32[128,64]{0,1:T(8,128)S(1)}, u32[]{:S(2)}, u32[]{:S(2)}) collective-permute-start(f32[128,64]{0,1:T(8,128)S(1)} %multiply_add_fusion), channel_id=1, source_target_pairs={{64,0},{96,32},{128,64},{160,96},{192,128},{224,160},{256,192},{28... | collective-permute-start | bytes 98312 | tf_op jit(solution)/shard_map/ppermute | solution.py:28
  34.5 8.1 %collective-permute-start.7 = (f32[]{:T(128)}, f32[]{:T(128)}, u32[]{:S(2)}, u32[]{:S(2)}) collective-permute-start(f32[]{:T(128)} %bitcast.34), channel_id=1, source_target_pairs={{64,0},{96,32},{128,64},{160,96},{192,128},{224,160},{256,192},{28... | collective-permute-start | bytes 20 | tf_op jit(solution)/shard_map/ppermute | solution.py:28
  43.4 11.0 %collective-permute-start.10 = (f32[128,64]{0,1:T(8,128)S(1)}, f32[128,64]{0,1:T(8,128)S(1)}, u32[]{:S(2)}, u32[]{:S(2)}) collective-permute-start(f32[128,64]{0,1:T(8,128)S(1)} %add_select_fusion.3), channel_id=1, source_target_pairs={{128,0},{160,32},{192,64},{224,96},{256,128},{288,160},{320,192},{... | collective-permute-start | bytes 98312 | tf_op jit(solution)/shard_map/ppermute | solution.py:28
  45.1 7.9 %collective-permute-start.9 = (f32[]{:T(128)}, f32[]{:T(128)}, u32[]{:S(2)}, u32[]{:S(2)}) collective-permute-start(f32[]{:T(128)} %mul.306), channel_id=1, source_target_pairs={{64,0},{96,32},{128,64},{160,96},{192,128},{224,160},{256,192},{28... | collective-permute-start | bytes 20 | tf_op jit(solution)/shard_map/ppermute | solution.py:28
  54.4 16.2 %collective-permute-start.12 = (f32[128,64]{0,1:T(8,128)S(1)}, f32[128,64]{0,1:T(8,128)S(1)}, u32[]{:S(2)}, u32[]{:S(2)}) collective-permute-start(f32[128,64]{0,1:T(8,128)S(1)} %add_select_fusion.2), channel_id=1, source_target_pairs={{256,0},{288,32},{320,64},{352,96},{384,128},{416,160},{448,192},{... | collective-permute-start | bytes 98312 | tf_op jit(solution)/shard_map/ppermute | solution.py:28
  56.0 10.6 %collective-permute-start.11 = (f32[]{:T(128)}, f32[]{:T(128)}, u32[]{:S(2)}, u32[]{:S(2)}) collective-permute-start(f32[]{:T(128)} %select_n.187), channel_id=1, source_target_pairs={{128,0},{160,32},{192,64},{224,96},{256,128},{288,160},{320,192},{... | collective-permute-start | bytes 20 | tf_op jit(solution)/shard_map/ppermute | solution.py:28
  70.7 3.1 %collective-permute-start.13 = (f32[128,64]{0,1:T(8,128)S(1)}, f32[128,64]{0,1:T(8,128)S(1)}, u32[]{:S(2)}, u32[]{:S(2)}) collective-permute-start(f32[128,64]{0,1:T(8,128)S(1)} %add_select_fusion.1), channel_id=1, source_target_pairs={{0,8},{8,0},{1,9},{9,1},{2,10},{10,2},{3,11},{11,3},{4,12},{12,4},... | collective-permute-start | bytes 98312 | tf_op jit(solution)/shard_map/ppermute | solution.py:23
  73.8 6.4 %copy-start.7 = (f32[4,128,64]{1,2,0:T(8,128)S(1)}, f32[4,128,64]{1,2,0:T(8,128)}, u32[]{:S(2)}) copy-start(f32[4,128,64]{1,2,0:T(8,128)} %copy-done.6) | copy-start | bytes 393220
  73.8 6.4 %collective-permute-start.14 = (f32[2,128,64]{1,2,0:T(8,128)S(1)}, f32[2,128,64]{1,2,0:T(8,128)}, u32[]{:S(2)}, u32[]{:S(2)}) collective-permute-start(f32[2,128,64]{1,2,0:T(8,128)S(1)} %maximum_select_fusion.1), channel_id=1, source_target_pairs={{0,16},{16,0},{1,17},{17,1},{2,18},{18,2},{3,19},{19,3},{4,20},{20... | collective-permute-start | bytes 196616 | tf_op jit(solution)/shard_map/ppermute | solution.py:23
  80.2 10.7 %copy-start.5 = (bf16[1024,256]{1,0:T(8,128)(2,1)S(1)}, bf16[1024,256]{1,0:T(8,128)(2,1)}, u32[]{:S(2)}) copy-start(bf16[1024,256]{1,0:T(8,128)(2,1)} %param.20) | copy-start | bytes 1572868
  83.6 13.1 %all-to-all-start = ((f32[256,8,32]{0,2,1:T(8,128)}), f32[256,8,32]{0,2,1:T(8,128)S(1)}, u32[]{:S(2)}, u32[]{:S(2)}) async-start(f32[256,8,32]{0,2,1:T(8,128)} %pad_maximum_fusion), calls=%async_computation | async-start | bytes 524288 | tf_op jit(solution)/shard_map/all_to_all | solution.py:176
  98.0 34.5 %copy-start.12 = (bf16[1,256,4,64]{1,3,2,0:T(8,128)(2,1)S(1)}, bf16[1,256,4,64]{1,3,2,0:T(8,128)(2,1)}, u32[]{:S(2)}) copy-start(bf16[1,256,4,64]{1,3,2,0:T(8,128)(2,1)} %copy-done.11) | copy-start | bytes 393220
  99.2 22.2 %collective-permute-start.21 = (bf16[256,128]{1,0:T(8,128)(2,1)S(1)}, bf16[256,128]{1,0:T(8,128)(2,1)S(1)}, u32[]{:S(2)}, u32[]{:S(2)}) collective-permute-start(bf16[256,128]{1,0:T(8,128)(2,1)S(1)} %bitcast.214), channel_id=1, source_target_pairs={{0,1},{1,2},{2,3},{3,4},{4,5},{5,6},{6,7},{7,0},{8,9},{9,10},{10,1... | collective-permute-start | bytes 196616 | tf_op jit(solution)/shard_map/ppermute | solution.py:190
  102.0 23.8 %collective-permute-start.15 = (bf16[256,128]{1,0:T(8,128)(2,1)S(1)}, bf16[256,128]{1,0:T(8,128)(2,1)S(1)}, u32[]{:S(2)}, u32[]{:S(2)}) collective-permute-start(bf16[256,128]{1,0:T(8,128)(2,1)S(1)} %bitcast.213), channel_id=1, source_target_pairs={{0,7},{1,0},{2,1},{3,2},{4,3},{5,4},{6,5},{7,6},{8,15},{9,8},{10,9... | collective-permute-start | bytes 196616 | tf_op jit(solution)/shard_map/ppermute | solution.py:190
  111.9 31.7 %collective-permute-start.16 = (bf16[256,128]{1,0:T(8,128)(2,1)}, bf16[256,128]{1,0:T(8,128)(2,1)}, u32[]{:S(2)}, u32[]{:S(2)}) collective-permute-start(bf16[256,128]{1,0:T(8,128)(2,1)} %bitcast.184), channel_id=1, source_target_pairs={{0,6},{1,7},{2,0},{3,1},{4,2},{5,3},{6,4},{7,5},{8,14},{9,15},{10,... | collective-permute-start | bytes 196616 | tf_op jit(solution)/shard_map/ppermute | solution.py:190
  113.8 29.8 %collective-permute-start.17 = (bf16[256,128]{1,0:T(8,128)(2,1)}, bf16[256,128]{1,0:T(8,128)(2,1)}, u32[]{:S(2)}, u32[]{:S(2)}) collective-permute-start(bf16[256,128]{1,0:T(8,128)(2,1)} %bitcast.183), channel_id=1, source_target_pairs={{0,5},{1,6},{2,7},{3,0},{4,1},{5,2},{6,3},{7,4},{8,13},{9,14},{10,... | collective-permute-start | bytes 196616 | tf_op jit(solution)/shard_map/ppermute | solution.py:190
  119.0 24.6 %collective-permute-start.18 = (bf16[256,128]{1,0:T(8,128)(2,1)}, bf16[256,128]{1,0:T(8,128)(2,1)}, u32[]{:S(2)}, u32[]{:S(2)}) collective-permute-start(bf16[256,128]{1,0:T(8,128)(2,1)} %bitcast.182), channel_id=1, source_target_pairs={{0,4},{1,5},{2,6},{3,7},{4,0},{5,1},{6,2},{7,3},{8,12},{9,13},{10,... | collective-permute-start | bytes 196616 | tf_op jit(solution)/shard_map/ppermute | solution.py:190
  121.5 22.1 %collective-permute-start.19 = (bf16[256,128]{1,0:T(8,128)(2,1)}, bf16[256,128]{1,0:T(8,128)(2,1)}, u32[]{:S(2)}, u32[]{:S(2)}) collective-permute-start(bf16[256,128]{1,0:T(8,128)(2,1)} %bitcast.181), channel_id=1, source_target_pairs={{0,3},{1,4},{2,5},{3,6},{4,7},{5,0},{6,1},{7,2},{8,11},{9,12},{10,... | collective-permute-start | bytes 196616 | tf_op jit(solution)/shard_map/ppermute | solution.py:190
  125.8 17.8 %collective-permute-start.20 = (bf16[256,128]{1,0:T(8,128)(2,1)}, bf16[256,128]{1,0:T(8,128)(2,1)}, u32[]{:S(2)}, u32[]{:S(2)}) collective-permute-start(bf16[256,128]{1,0:T(8,128)(2,1)} %bitcast.180), channel_id=1, source_target_pairs={{0,2},{1,3},{2,4},{3,5},{4,6},{5,7},{6,0},{7,1},{8,10},{9,11},{10,... | collective-permute-start | bytes 196616 | tf_op jit(solution)/shard_map/ppermute | solution.py:190
  140.1 13.5 %all-to-all-start.2 = ((bf16[16,2,1,16,544]{4,3,0,2,1:T(8,128)(2,1)}), bf16[16,2,1,16,544]{4,3,0,2,1:T(8,128)(2,1)S(1)}, u32[]{:S(2)}, u32[]{:S(2)}) async-start(bf16[16,2,1,16,544]{4,3,0,2,1:T(8,128)(2,1)} %copy.84), calls=%async_computation.2 | async-start | bytes 1310720 | tf_op jit(solution)/shard_map/all_to_all | solution.py:176

commit v11 on v5

--- a/solution.py
+++ b/solution.py
@@ -211,7 +211,7 @@
     block_log = partials[10]
     incoming = suffix_scan((jnp.exp(block_log), block_sum))
     grad_z, grad_x, grad_bc_part = finish_block(partials, incoming)
-    grad_bc = summed_over(grad_bc_part, HEAD, 1).astype(jnp.bfloat16)
+    grad_bc = summed_over(grad_bc_part.astype(jnp.bfloat16), HEAD, 1).astype(jnp.bfloat16)
     input_part = (
         times_rows(grad_z, w_gate) + times_rows(grad_x, w_value) + times_rows(grad_bc, w_shared)
     )

time: 168 us -> 167 us (level)
  no operation moved by 1% of the time
where the time goes in v11:
time: 167 us; the launch traced here: 166 us
  starting transfers between devices  77.8 us (47%)
  waiting for transfers between devices  46.7 us (28%)
  blocking collectives  17.3 us (10%)
  local copies, waits for them, and re-layouts  7.44 us (4%)
  matrix products  6.7 us (4%)
  other arithmetic  6.01 us (4%)
  between operations  4.11 us (2%)
    ppermute x9, waiting for transfers between devices, shift(): return jax.tree.map(lambda a: lax.ppermute(a, axis, pairs), tree)  28.8 us
    ppermute x7, starting transfers between devices, spread_sum(): total = total + lax.ppermute(piece, axis, pairs).astype(jnp.float32)  27.5 us
    all_to_all x2, blocking collectives, summed_over(): gathered = lax.all_to_all(part, axis, split, split, tiled=True)  17.3 us
    all_to_all x2, starting transfers between devices, summed_over(): gathered = lax.all_to_all(part, axis, split, split, tiled=True)  17.2 us
    ppermute x9, starting transfers between devices, shift(): return jax.tree.map(lambda a: lax.ppermute(a, axis, pairs), tree)  16.8 us
    ppermute x6, starting transfers between devices, swap(): return jax.tree.map(lambda a: lax.ppermute(a, axis, [(0, 1), (1, 0)]), tree)  16.3 us
    all_to_all x2, waiting for transfers between devices, summed_over(): gathered = lax.all_to_all(part, axis, split, split, tiled=True)  7.81 us
    ppermute x6, waiting for transfers between devices, swap(): return jax.tree.map(lambda a: lax.ppermute(a, axis, [(0, 1), (1, 0)]), tree)  5.47 us
  transfers between devices with their start and end apart: 24, of which 13 were waited for; matrix products, arithmetic and copies ran while one was open for 6% of the time, Pallas kernels for 0%

profile of v11, /device:TPU:32, one launch (start us, length us, event | category | flops | bytes accessed | tf_op | source)
XLA Modules:
  0.0 166.1 jit_solution(14321603239620751087)
XLA Ops:
  0.7 0.8 reshape.420
  1.5 1.2 reduce-window.6
  3.1 1.9 %collective-permute-start.1 = (f32[4]{0:T(128)S(1)}, f32[4]{0:T(128)S(1)}, u32[]{:S(2)}, u32[]{:S(2)}) collective-permute-start(f32[4]{0:T(128)S(1)} %fusion.52), channel_id=1, source_target_pairs={{0,8},{8,0},{1,9},{9,1},{2,10},{10,2},{3,11},{11,3},{4,12},{12,4},... | collective-permute-start | bytes 56 | tf_op jit(solution)/shard_map/ppermute | solution.py:23
  6.2 0.3 fusion.13
  6.4 2.4 %collective-permute-start = (f32[4,128,64]{1,2,0:T(8,128)S(1)}, f32[4,128,64]{1,2,0:T(8,128)S(1)}, u32[]{:S(2)}, u32[]{:S(2)}) collective-permute-start(f32[4,128,64]{1,2,0:T(8,128)S(1)} %fusion.13), channel_id=1, source_target_pairs={{0,8},{8,0},{1,9},{9,1},{2,10},{10,2},{3,11},{11,3},{4,12},{12,4},... | collective-permute-start | bytes 393224 | tf_op jit(solution)/shard_map/ppermute | solution.py:23
  9.0 0.8 collective-permute-done
  9.9 3.5 %collective-permute-start.2 = (f32[4,128,64]{1,2,0:T(8,128)S(1)}, f32[4,128,64]{1,2,0:T(8,128)S(1)}, u32[]{:S(2)}, u32[]{:S(2)}) collective-permute-start(f32[4,128,64]{1,2,0:T(8,128)S(1)} %add_select_fusion), channel_id=1, source_target_pairs={{0,16},{16,0},{1,17},{17,1},{2,18},{18,2},{3,19},{19,3},{4,20},{20... | collective-permute-start | bytes 393224 | tf_op jit(solution)/shard_map/ppermute | solution.py:23
  13.4 1.0 fusion.12
  14.4 2.4 %collective-permute-start.3 = (f32[4]{0:T(128)S(1)}, f32[4]{0:T(128)S(1)}, u32[]{:S(2)}, u32[]{:S(2)}) collective-permute-start(f32[4]{0:T(128)S(1)} %get-tuple-element.51), channel_id=1, source_target_pairs={{0,16},{16,0},{1,17},{17,1},{2,18},{18,2},{3,19},{19,3},{4,20},{20... | collective-permute-start | bytes 56 | tf_op jit(solution)/shard_map/ppermute | solution.py:23
  16.7 0.6 dynamic-slice.34
  17.3 2.5 %collective-permute-done.3 = f32[4]{0:T(128)S(1)} collective-permute-done((f32[4]{0:T(128)S(1)}, f32[4]{0:T(128)S(1)}, u32[]{:S(2)}, u32[]{:S(2)}) %collective-permute-start.3) | collective-permute-done | bytes 48 | tf_op jit(solution)/shard_map/ppermute | solution.py:23
  19.8 0.6 dynamic-slice.35
  20.4 1.3 select_bitcast_fusion
  21.7 1.3 collective-permute-start.6
  23.0 5.8 %collective-permute-start.4 = (f32[128,64]{0,1:T(8,128)S(1)}, f32[128,64]{0,1:T(8,128)S(1)}, u32[]{:S(2)}, u32[]{:S(2)}) collective-permute-start(f32[128,64]{0,1:T(8,128)S(1)} %select_bitcast_fusion), channel_id=1, source_target_pairs={{32,0},{64,32},{96,64},{128,96},{160,128},{192,160},{224,192},{256... | collective-permute-start | bytes 98312 | tf_op jit(solution)/shard_map/ppermute | solution.py:28
  28.8 0.6 dynamic_slice.31
  29.4 1.9 %collective-permute-start.5 = (f32[]{:T(128)}, f32[]{:T(128)}, u32[]{:S(2)}, u32[]{:S(2)}) collective-permute-start(f32[]{:T(128)} %bitcast.34), channel_id=1, source_target_pairs={{32,0},{64,32},{96,64},{128,96},{160,128},{192,160},{224,192},{256... | collective-permute-start | bytes 20 | tf_op jit(solution)/shard_map/ppermute | solution.py:28
  31.4 3.7 %collective-permute-done.5 = f32[]{:T(128)} collective-permute-done((f32[]{:T(128)}, f32[]{:T(128)}, u32[]{:S(2)}, u32[]{:S(2)}) %collective-permute-start.5) | collective-permute-done | bytes 36 | tf_op jit(solution)/shard_map/ppermute | solution.py:28
  35.7 1.3 collective-permute-start.8
  37.0 0.8 fusion.2
  37.9 1.3 collective-permute-start.7
  39.2 7.5 %collective-permute-done.7 = f32[]{:T(128)} collective-permute-done((f32[]{:T(128)}, f32[]{:T(128)}, u32[]{:S(2)}, u32[]{:S(2)}) %collective-permute-start.7) | collective-permute-done | bytes 36 | tf_op jit(solution)/shard_map/ppermute | solution.py:28
  47.4 1.3 collective-permute-start.10
  48.7 0.4 convolution_bitcast_fusion.3
  49.1 1.3 collective-permute-start.9
  50.4 6.2 %collective-permute-done.9 = f32[]{:T(128)} collective-permute-done((f32[]{:T(128)}, f32[]{:T(128)}, u32[]{:S(2)}, u32[]{:S(2)}) %collective-permute-start.9) | collective-permute-done | bytes 36 | tf_op jit(solution)/shard_map/ppermute | solution.py:28
  57.2 0.4 collective-permute-done.10
  57.6 1.3 collective-permute-start.12
  58.9 0.3 fusion.16
  59.2 1.3 collective-permute-start.11
  60.5 8.3 %collective-permute-done.11 = f32[]{:T(128)} collective-permute-done((f32[]{:T(128)}, f32[]{:T(128)}, u32[]{:S(2)}, u32[]{:S(2)}) %collective-permute-start.11) | collective-permute-done | bytes 36 | tf_op jit(solution)/shard_map/ppermute | solution.py:28
  69.5 2.7 %collective-permute-done.12 = f32[128,64]{0,1:T(8,128)S(1)} collective-permute-done((f32[128,64]{0,1:T(8,128)S(1)}, f32[128,64]{0,1:T(8,128)S(1)}, u32[]{:S(2)}, u32[]{:S(2)}) %collective-permute-start.12) | collective-permute-done | bytes 32800 | tf_op jit(solution)/shard_map/ppermute | solution.py:28
  72.2 1.9 %collective-permute-start.13 = (f32[128,64]{0,1:T(8,128)S(1)}, f32[128,64]{0,1:T(8,128)S(1)}, u32[]{:S(2)}, u32[]{:S(2)}) collective-permute-start(f32[128,64]{0,1:T(8,128)S(1)} %add_select_fusion.1), channel_id=1, source_target_pairs={{0,8},{8,0},{1,9},{9,1},{2,10},{10,2},{3,11},{11,3},{4,12},{12,4},... | collective-permute-start | bytes 98312 | tf_op jit(solution)/shard_map/ppermute | solution.py:23
  74.4 0.9 collective-permute-done.13
  75.3 4.3 %collective-permute-start.14 = (f32[2,128,64]{1,2,0:T(8,128)S(1)}, f32[2,128,64]{1,2,0:T(8,128)S(1)}, u32[]{:S(2)}, u32[]{:S(2)}) collective-permute-start(f32[2,128,64]{1,2,0:T(8,128)S(1)} %maximum_select_fusion.1), channel_id=1, source_target_pairs={{0,16},{16,0},{1,17},{17,1},{2,18},{18,2},{3,19},{19,3},{4,20},{20... | collective-permute-start | bytes 196616 | tf_op jit(solution)/shard_map/ppermute | solution.py:23
  79.6 1.1 convolution_bitcast_fusion.1
  80.8 1.2 collective-permute-done.14
  82.1 0.4 fusion.15
  82.5 0.7 pad_maximum_fusion
  83.1 5.3 %all-to-all-start = ((bf16[256,8,32]{0,2,1:T(8,128)(2,1)}), bf16[256,8,32]{0,2,1:T(8,128)(2,1)S(1)}, u32[]{:S(2)}, u32[]{:S(2)}) async-start(bf16[256,8,32]{0,2,1:T(8,128)(2,1)} %pad_maximum_fusion), calls=%async_computation | async-start | bytes 262144 | tf_op jit(solution)/shard_map/all_to_all | solution.py:176
  88.7 7.8 %all-to-all-done = bf16[256,8,32]{0,2,1:T(8,128)(2,1)S(1)} async-done(((bf16[256,8,32]{0,2,1:T(8,128)(2,1)}), bf16[256,8,32]{0,2,1:T(8,128)(2,1)S(1)}, u32[]{:S(2)}, u32[]{:S(2)}) %all-to-all-start) | async-done | bytes 131104 | tf_op jit(solution)/shard_map/all_to_all | solution.py:176
  96.5 0.5 fusion
  97.0 0.7 copy.90
  97.9 4.8 %all_to_all.21 = bf16[16,2,2,16,544]{4,3,1,0,2:T(8,128)(2,1)S(1)} all-to-all(bf16[16,2,2,16,544]{4,3,1,0,2:T(8,128)(2,1)S(1)} %copy.91), channel_id=1, replica_groups=mesh['z'=16,'y_lo'=2,'core'=2,'y_hi'=2,'x'=4] {'core'}, dimensions={2} | all-to-all | bytes 2228224 | tf_op jit(solution)/shard_map/all_to_all | solution.py:176
  102.6 0.6 reduce_sum.64
  103.3 12.5 %all_to_all.22 = bf16[16,2,1,16,544]{4,3,0,2,1:T(8,128)(2,1)S(1)} all-to-all(bf16[16,2,1,16,544]{4,3,0,2,1:T(8,128)(2,1)S(1)} %copy.92), channel_id=1, replica_groups=mesh['z'=16,'y_lo'=2,'core'=2,'y_hi'=2,'x'=4] {'y_lo'}, dimensions={1} | all-to-all | bytes 1114112 | tf_op jit(solution)/shard_map/all_to_all | solution.py:176
  115.9 0.9 reduce_sum.65
  116.8 11.9 %all-to-all-start.3 = ((bf16[16,1,1,16,544]{4,3,2,1,0:T(8,128)(2,1)}), bf16[16,1,1,16,544]{4,3,2,1,0:T(8,128)(2,1)S(1)}, u32[]{:S(2)}, u32[]{:S(2)}) async-start(bf16[16,1,1,16,544]{4,3,2,1,0:T(8,128)(2,1)} %bitcast.58), calls=%async_computation.3 | async-start | bytes 655360 | tf_op jit(solution)/shard_map/all_to_all | solution.py:176
  128.7 0.3 fusion.56
  129.3 0.4 convolution_add_fusion.1
  129.6 0.5 copy-done.9
  130.1 0.3 fusion.3
  130.5 1.2 constant_dynamic-slice_fusion.7
  131.8 2.8 %collective-permute-start.21 = (bf16[256,128]{1,0:T(8,128)(2,1)S(1)}, bf16[256,128]{1,0:T(8,128)(2,1)S(1)}, u32[]{:S(2)}, u32[]{:S(2)}) collective-permute-start(bf16[256,128]{1,0:T(8,128)(2,1)S(1)} %bitcast.219), channel_id=1, source_target_pairs={{0,1},{1,2},{2,3},{3,4},{4,5},{5,6},{6,7},{7,0},{8,9},{9,10},{10,1... | collective-permute-start | bytes 196616 | tf_op jit(solution)/shard_map/ppermute | solution.py:190
  134.6 6.7 %collective-permute-start.15 = (bf16[256,128]{1,0:T(8,128)(2,1)S(1)}, bf16[256,128]{1,0:T(8,128)(2,1)S(1)}, u32[]{:S(2)}, u32[]{:S(2)}) collective-permute-start(bf16[256,128]{1,0:T(8,128)(2,1)S(1)} %bitcast.217), channel_id=1, source_target_pairs={{0,7},{1,0},{2,1},{3,2},{4,3},{5,4},{6,5},{7,6},{8,15},{9,8},{10,9... | collective-permute-start | bytes 196616 | tf_op jit(solution)/shard_map/ppermute | solution.py:190
  141.4 1.9 %collective-permute-start.16 = (bf16[256,128]{1,0:T(8,128)(2,1)S(1)}, bf16[256,128]{1,0:T(8,128)(2,1)S(1)}, u32[]{:S(2)}, u32[]{:S(2)}) collective-permute-start(bf16[256,128]{1,0:T(8,128)(2,1)S(1)} %bitcast.220), channel_id=1, source_target_pairs={{0,6},{1,7},{2,0},{3,1},{4,2},{5,3},{6,4},{7,5},{8,14},{9,15},{10,... | collective-permute-start | bytes 196616 | tf_op jit(solution)/shard_map/ppermute | solution.py:190
  143.3 2.8 %collective-permute-start.17 = (bf16[256,128]{1,0:T(8,128)(2,1)S(1)}, bf16[256,128]{1,0:T(8,128)(2,1)S(1)}, u32[]{:S(2)}, u32[]{:S(2)}) collective-permute-start(bf16[256,128]{1,0:T(8,128)(2,1)S(1)} %bitcast.218), channel_id=1, source_target_pairs={{0,5},{1,6},{2,7},{3,0},{4,1},{5,2},{6,3},{7,4},{8,13},{9,14},{10,... | collective-permute-start | bytes 196616 | tf_op jit(solution)/shard_map/ppermute | solution.py:190
  146.1 4.8 %collective-permute-start.18 = (bf16[256,128]{1,0:T(8,128)(2,1)S(1)}, bf16[256,128]{1,0:T(8,128)(2,1)S(1)}, u32[]{:S(2)}, u32[]{:S(2)}) collective-permute-start(bf16[256,128]{1,0:T(8,128)(2,1)S(1)} %bitcast.216), channel_id=1, source_target_pairs={{0,4},{1,5},{2,6},{3,7},{4,0},{5,1},{6,2},{7,3},{8,12},{9,13},{10,... | collective-permute-start | bytes 196616 | tf_op jit(solution)/shard_map/ppermute | solution.py:190
  151.0 1.9 %collective-permute-start.19 = (bf16[256,128]{1,0:T(8,128)(2,1)S(1)}, bf16[256,128]{1,0:T(8,128)(2,1)S(1)}, u32[]{:S(2)}, u32[]{:S(2)}) collective-permute-start(bf16[256,128]{1,0:T(8,128)(2,1)S(1)} %bitcast.215), channel_id=1, source_target_pairs={{0,3},{1,4},{2,5},{3,6},{4,7},{5,0},{6,1},{7,2},{8,11},{9,12},{10,... | collective-permute-start | bytes 196616 | tf_op jit(solution)/shard_map/ppermute | solution.py:190
  152.9 6.6 %collective-permute-start.20 = (bf16[256,128]{1,0:T(8,128)(2,1)S(1)}, bf16[256,128]{1,0:T(8,128)(2,1)S(1)}, u32[]{:S(2)}, u32[]{:S(2)}) collective-permute-start(bf16[256,128]{1,0:T(8,128)(2,1)S(1)} %bitcast.214), channel_id=1, source_target_pairs={{0,2},{1,3},{2,4},{3,5},{4,6},{5,7},{6,0},{7,1},{8,10},{9,11},{10,... | collective-permute-start | bytes 196616 | tf_op jit(solution)/shard_map/ppermute | solution.py:190
  159.5 4.6 %collective-permute-done.20 = bf16[256,128]{1,0:T(8,128)(2,1)S(1)} collective-permute-done((bf16[256,128]{1,0:T(8,128)(2,1)S(1)}, bf16[256,128]{1,0:T(8,128)(2,1)S(1)}, u32[]{:S(2)}, u32[]{:S(2)}) %collective-permute-start.20) | collective-permute-done | bytes 65568 | tf_op jit(solution)/shard_map/ppermute | solution.py:190
  164.1 0.7 fusion.44
  164.9 0.6 slice.28
  165.5 0.6 fusion.53
  (76 shorter events, 2.9 us)
Async XLA Ops:
  0.6 95.9 %copy-start = (bf16[256,1024]{1,0:T(8,128)(2,1)S(1)}, bf16[256,1024]{1,0:T(8,128)(2,1)}, u32[]{:S(2)}) copy-start(bf16[256,1024]{1,0:T(8,128)(2,1)} %param.11) | copy-start | bytes 1572868
  0.6 4.6 %copy-start.6 = (bf16[256,256]{1,0:T(8,128)(2,1)S(1)}, bf16[256,256]{1,0:T(8,128)(2,1)}, u32[]{:S(2)}) copy-start(bf16[256,256]{1,0:T(8,128)(2,1)} %param.13) | copy-start | bytes 393220
  0.7 4.7 %copy-start.7 = (bf16[256,256]{1,0:T(8,128)(2,1)S(1)}, bf16[256,256]{1,0:T(8,128)(2,1)}, u32[]{:S(2)}) copy-start(bf16[256,256]{1,0:T(8,128)(2,1)} %param.14) | copy-start | bytes 393220
  0.7 4.8 %copy-start.1 = (bf16[256,128]{1,0:T(8,128)(2,1)S(1)}, bf16[256,128]{1,0:T(8,128)(2,1)}, u32[]{:S(2)}) copy-start(bf16[256,128]{1,0:T(8,128)(2,1)} %param.16) | copy-start | bytes 196612
  0.7 4.8 %copy-start.2 = (bf16[256,128]{1,0:T(8,128)(2,1)S(1)}, bf16[256,128]{1,0:T(8,128)(2,1)}, u32[]{:S(2)}) copy-start(bf16[256,128]{1,0:T(8,128)(2,1)} %param.15) | copy-start | bytes 196612
  0.7 5.0 %copy-start.4 = (f32[1,4,128,64]{2,3,1,0:T(8,128)S(1)}, f32[1,4,128,64]{2,3,1,0:T(8,128)}, u32[]{:S(2)}) copy-start(f32[1,4,128,64]{2,3,1,0:T(8,128)} %param.18) | copy-start | bytes 393220
  3.1 3.1 %collective-permute-start.1 = (f32[4]{0:T(128)S(1)}, f32[4]{0:T(128)S(1)}, u32[]{:S(2)}, u32[]{:S(2)}) collective-permute-start(f32[4]{0:T(128)S(1)} %fusion.52), channel_id=1, source_target_pairs={{0,8},{8,0},{1,9},{9,1},{2,10},{10,2},{3,11},{11,3},{4,12},{12,4},... | collective-permute-start | bytes 56 | tf_op jit(solution)/shard_map/ppermute | solution.py:23
  5.3 3.6 %copy-start.8 = (bf16[256,256]{1,0:T(8,128)(2,1)S(1)}, bf16[256,256]{1,0:T(8,128)(2,1)}, u32[]{:S(2)}) copy-start(bf16[256,256]{1,0:T(8,128)(2,1)} %param.12) | copy-start | bytes 393220
  6.4 3.3 %collective-permute-start = (f32[4,128,64]{1,2,0:T(8,128)S(1)}, f32[4,128,64]{1,2,0:T(8,128)S(1)}, u32[]{:S(2)}, u32[]{:S(2)}) collective-permute-start(f32[4,128,64]{1,2,0:T(8,128)S(1)} %fusion.13), channel_id=1, source_target_pairs={{0,8},{8,0},{1,9},{9,1},{2,10},{10,2},{3,11},{11,3},{4,12},{12,4},... | collective-permute-start | bytes 393224 | tf_op jit(solution)/shard_map/ppermute | solution.py:23
  9.9 10.5 %collective-permute-start.2 = (f32[4,128,64]{1,2,0:T(8,128)S(1)}, f32[4,128,64]{1,2,0:T(8,128)S(1)}, u32[]{:S(2)}, u32[]{:S(2)}) collective-permute-start(f32[4,128,64]{1,2,0:T(8,128)S(1)} %add_select_fusion), channel_id=1, source_target_pairs={{0,16},{16,0},{1,17},{17,1},{2,18},{18,2},{3,19},{19,3},{4,20},{20... | collective-permute-start | bytes 393224 | tf_op jit(solution)/shard_map/ppermute | solution.py:23
  14.4 5.5 %collective-permute-start.3 = (f32[4]{0:T(128)S(1)}, f32[4]{0:T(128)S(1)}, u32[]{:S(2)}, u32[]{:S(2)}) collective-permute-start(f32[4]{0:T(128)S(1)} %get-tuple-element.51), channel_id=1, source_target_pairs={{0,16},{16,0},{1,17},{17,1},{2,18},{18,2},{3,19},{19,3},{4,20},{20... | collective-permute-start | bytes 56 | tf_op jit(solution)/shard_map/ppermute | solution.py:23
  21.7 14.0 %collective-permute-start.6 = (f32[128,64]{0,1:T(8,128)S(1)}, f32[128,64]{0,1:T(8,128)S(1)}, u32[]{:S(2)}, u32[]{:S(2)}) collective-permute-start(f32[128,64]{0,1:T(8,128)S(1)} %select_bitcast_fusion), channel_id=1, source_target_pairs={{64,0},{96,32},{128,64},{160,96},{192,128},{224,160},{256,192},{28... | collective-permute-start | bytes 98312 | tf_op jit(solution)/shard_map/ppermute | solution.py:28
  23.0 12.7 %collective-permute-start.4 = (f32[128,64]{0,1:T(8,128)S(1)}, f32[128,64]{0,1:T(8,128)S(1)}, u32[]{:S(2)}, u32[]{:S(2)}) collective-permute-start(f32[128,64]{0,1:T(8,128)S(1)} %select_bitcast_fusion), channel_id=1, source_target_pairs={{32,0},{64,32},{96,64},{128,96},{160,128},{192,160},{224,192},{256... | collective-permute-start | bytes 98312 | tf_op jit(solution)/shard_map/ppermute | solution.py:28
  29.4 5.6 %collective-permute-start.5 = (f32[]{:T(128)}, f32[]{:T(128)}, u32[]{:S(2)}, u32[]{:S(2)}) collective-permute-start(f32[]{:T(128)} %bitcast.34), channel_id=1, source_target_pairs={{32,0},{64,32},{96,64},{128,96},{160,128},{192,160},{224,192},{256... | collective-permute-start | bytes 20 | tf_op jit(solution)/shard_map/ppermute | solution.py:28
  35.7 11.6 %collective-permute-start.8 = (f32[128,64]{0,1:T(8,128)S(1)}, f32[128,64]{0,1:T(8,128)S(1)}, u32[]{:S(2)}, u32[]{:S(2)}) collective-permute-start(f32[128,64]{0,1:T(8,128)S(1)} %multiply_add_fusion), channel_id=1, source_target_pairs={{64,0},{96,32},{128,64},{160,96},{192,128},{224,160},{256,192},{28... | collective-permute-start | bytes 98312 | tf_op jit(solution)/shard_map/ppermute | solution.py:28
  37.9 8.8 %collective-permute-start.7 = (f32[]{:T(128)}, f32[]{:T(128)}, u32[]{:S(2)}, u32[]{:S(2)}) collective-permute-start(f32[]{:T(128)} %bitcast.34), channel_id=1, source_target_pairs={{64,0},{96,32},{128,64},{160,96},{192,128},{224,160},{256,192},{28... | collective-permute-start | bytes 20 | tf_op jit(solution)/shard_map/ppermute | solution.py:28
  47.4 10.3 %collective-permute-start.10 = (f32[128,64]{0,1:T(8,128)S(1)}, f32[128,64]{0,1:T(8,128)S(1)}, u32[]{:S(2)}, u32[]{:S(2)}) collective-permute-start(f32[128,64]{0,1:T(8,128)S(1)} %add_select_fusion.3), channel_id=1, source_target_pairs={{128,0},{160,32},{192,64},{224,96},{256,128},{288,160},{320,192},{... | collective-permute-start | bytes 98312 | tf_op jit(solution)/shard_map/ppermute | solution.py:28
  49.1 7.5 %collective-permute-start.9 = (f32[]{:T(128)}, f32[]{:T(128)}, u32[]{:S(2)}, u32[]{:S(2)}) collective-permute-start(f32[]{:T(128)} %mul.306), channel_id=1, source_target_pairs={{64,0},{96,32},{128,64},{160,96},{192,128},{224,160},{256,192},{28... | collective-permute-start | bytes 20 | tf_op jit(solution)/shard_map/ppermute | solution.py:28
  57.6 14.5 %collective-permute-start.12 = (f32[128,64]{0,1:T(8,128)S(1)}, f32[128,64]{0,1:T(8,128)S(1)}, u32[]{:S(2)}, u32[]{:S(2)}) collective-permute-start(f32[128,64]{0,1:T(8,128)S(1)} %add_select_fusion.2), channel_id=1, source_target_pairs={{256,0},{288,32},{320,64},{352,96},{384,128},{416,160},{448,192},{... | collective-permute-start | bytes 98312 | tf_op jit(solution)/shard_map/ppermute | solution.py:28
  59.2 9.6 %collective-permute-start.11 = (f32[]{:T(128)}, f32[]{:T(128)}, u32[]{:S(2)}, u32[]{:S(2)}) collective-permute-start(f32[]{:T(128)} %select_n.187), channel_id=1, source_target_pairs={{128,0},{160,32},{192,64},{224,96},{256,128},{288,160},{320,192},{... | collective-permute-start | bytes 20 | tf_op jit(solution)/shard_map/ppermute | solution.py:28
  72.2 3.1 %collective-permute-start.13 = (f32[128,64]{0,1:T(8,128)S(1)}, f32[128,64]{0,1:T(8,128)S(1)}, u32[]{:S(2)}, u32[]{:S(2)}) collective-permute-start(f32[128,64]{0,1:T(8,128)S(1)} %add_select_fusion.1), channel_id=1, source_target_pairs={{0,8},{8,0},{1,9},{9,1},{2,10},{10,2},{3,11},{11,3},{4,12},{12,4},... | collective-permute-start | bytes 98312 | tf_op jit(solution)/shard_map/ppermute | solution.py:23
  75.3 6.7 %collective-permute-start.14 = (f32[2,128,64]{1,2,0:T(8,128)S(1)}, f32[2,128,64]{1,2,0:T(8,128)S(1)}, u32[]{:S(2)}, u32[]{:S(2)}) collective-permute-start(f32[2,128,64]{1,2,0:T(8,128)S(1)} %maximum_select_fusion.1), channel_id=1, source_target_pairs={{0,16},{16,0},{1,17},{17,1},{2,18},{18,2},{3,19},{19,3},{4,20},{20... | collective-permute-start | bytes 196616 | tf_op jit(solution)/shard_map/ppermute | solution.py:23
  83.1 13.4 %all-to-all-start = ((bf16[256,8,32]{0,2,1:T(8,128)(2,1)}), bf16[256,8,32]{0,2,1:T(8,128)(2,1)S(1)}, u32[]{:S(2)}, u32[]{:S(2)}) async-start(bf16[256,8,32]{0,2,1:T(8,128)(2,1)} %pad_maximum_fusion), calls=%async_computation | async-start | bytes 262144 | tf_op jit(solution)/shard_map/all_to_all | solution.py:176
  103.3 25.4 %copy-start.3 = (bf16[1024,256]{1,0:T(8,128)(2,1)S(1)}, bf16[1024,256]{1,0:T(8,128)(2,1)}, u32[]{:S(2)}) copy-start(bf16[1024,256]{1,0:T(8,128)(2,1)} %param.19) | copy-start | bytes 1572868
  116.8 12.5 %copy-start.5 = (bf16[1024,256]{1,0:T(8,128)(2,1)S(1)}, bf16[1024,256]{1,0:T(8,128)(2,1)}, u32[]{:S(2)}) copy-start(bf16[1024,256]{1,0:T(8,128)(2,1)} %param.20) | copy-start | bytes 1572868
  116.8 48.0 %all-to-all-start.3 = ((bf16[16,1,1,16,544]{4,3,2,1,0:T(8,128)(2,1)}), bf16[16,1,1,16,544]{4,3,2,1,0:T(8,128)(2,1)S(1)}, u32[]{:S(2)}, u32[]{:S(2)}) async-start(bf16[16,1,1,16,544]{4,3,2,1,0:T(8,128)(2,1)} %bitcast.58), calls=%async_computation.3 | async-start | bytes 655360 | tf_op jit(solution)/shard_map/all_to_all | solution.py:176
  129.3 0.8 copy-start.9
  131.8 19.2 %collective-permute-start.21 = (bf16[256,128]{1,0:T(8,128)(2,1)S(1)}, bf16[256,128]{1,0:T(8,128)(2,1)S(1)}, u32[]{:S(2)}, u32[]{:S(2)}) collective-permute-start(bf16[256,128]{1,0:T(8,128)(2,1)S(1)} %bitcast.219), channel_id=1, source_target_pairs={{0,1},{1,2},{2,3},{3,4},{4,5},{5,6},{6,7},{7,0},{8,9},{9,10},{10,1... | collective-permute-start | bytes 196616 | tf_op jit(solution)/shard_map/ppermute | solution.py:190
  134.6 18.3 %collective-permute-start.15 = (bf16[256,128]{1,0:T(8,128)(2,1)S(1)}, bf16[256,128]{1,0:T(8,128)(2,1)S(1)}, u32[]{:S(2)}, u32[]{:S(2)}) collective-permute-start(bf16[256,128]{1,0:T(8,128)(2,1)S(1)} %bitcast.217), channel_id=1, source_target_pairs={{0,7},{1,0},{2,1},{3,2},{4,3},{5,4},{6,5},{7,6},{8,15},{9,8},{10,9... | collective-permute-start | bytes 196616 | tf_op jit(solution)/shard_map/ppermute | solution.py:190
  141.4 18.1 %collective-permute-start.16 = (bf16[256,128]{1,0:T(8,128)(2,1)S(1)}, bf16[256,128]{1,0:T(8,128)(2,1)S(1)}, u32[]{:S(2)}, u32[]{:S(2)}) collective-permute-start(bf16[256,128]{1,0:T(8,128)(2,1)S(1)} %bitcast.220), channel_id=1, source_target_pairs={{0,6},{1,7},{2,0},{3,1},{4,2},{5,3},{6,4},{7,5},{8,14},{9,15},{10,... | collective-permute-start | bytes 196616 | tf_op jit(solution)/shard_map/ppermute | solution.py:190
  143.3 16.2 %collective-permute-start.17 = (bf16[256,128]{1,0:T(8,128)(2,1)S(1)}, bf16[256,128]{1,0:T(8,128)(2,1)S(1)}, u32[]{:S(2)}, u32[]{:S(2)}) collective-permute-start(bf16[256,128]{1,0:T(8,128)(2,1)S(1)} %bitcast.218), channel_id=1, source_target_pairs={{0,5},{1,6},{2,7},{3,0},{4,1},{5,2},{6,3},{7,4},{8,13},{9,14},{10,... | collective-permute-start | bytes 196616 | tf_op jit(solution)/shard_map/ppermute | solution.py:190
  146.1 13.4 %collective-permute-start.18 = (bf16[256,128]{1,0:T(8,128)(2,1)S(1)}, bf16[256,128]{1,0:T(8,128)(2,1)S(1)}, u32[]{:S(2)}, u32[]{:S(2)}) collective-permute-start(bf16[256,128]{1,0:T(8,128)(2,1)S(1)} %bitcast.216), channel_id=1, source_target_pairs={{0,4},{1,5},{2,6},{3,7},{4,0},{5,1},{6,2},{7,3},{8,12},{9,13},{10,... | collective-permute-start | bytes 196616 | tf_op jit(solution)/shard_map/ppermute | solution.py:190
  151.0 8.6 %collective-permute-start.19 = (bf16[256,128]{1,0:T(8,128)(2,1)S(1)}, bf16[256,128]{1,0:T(8,128)(2,1)S(1)}, u32[]{:S(2)}, u32[]{:S(2)}) collective-permute-start(bf16[256,128]{1,0:T(8,128)(2,1)S(1)} %bitcast.215), channel_id=1, source_target_pairs={{0,3},{1,4},{2,5},{3,6},{4,7},{5,0},{6,1},{7,2},{8,11},{9,12},{10,... | collective-permute-start | bytes 196616 | tf_op jit(solution)/shard_map/ppermute | solution.py:190
  152.9 11.2 %collective-permute-start.20 = (bf16[256,128]{1,0:T(8,128)(2,1)S(1)}, bf16[256,128]{1,0:T(8,128)(2,1)S(1)}, u32[]{:S(2)}, u32[]{:S(2)}) collective-permute-start(bf16[256,128]{1,0:T(8,128)(2,1)S(1)} %bitcast.214), channel_id=1, source_target_pairs={{0,2},{1,3},{2,4},{3,5},{4,6},{5,7},{6,0},{7,1},{8,10},{9,11},{10,... | collective-permute-start | bytes 196616 | tf_op jit(solution)/shard_map/ppermute | solution.py:190

commit v12 on v9

--- a/solution.py
+++ b/solution.py
@@ -218,7 +218,7 @@
     block_log = partials[10]
     incoming = suffix_scan((jnp.exp(block_log), block_sum))
     grad_z, grad_x, grad_bc_part = finish_block(partials, incoming)
-    grad_bc = summed_over(grad_bc_part, HEAD, 1).astype(jnp.bfloat16)
+    grad_bc = summed_over(grad_bc_part.astype(jnp.bfloat16), HEAD, 1).astype(jnp.bfloat16)
     input_part = (
         times_rows(grad_z, w_gate) + times_rows(grad_x, w_value) + times_rows(grad_bc, w_shared)
     )
@@ -230,7 +230,7 @@
     sizes = [lax.axis_size(name) for name in CTX]
     rows = rows.reshape(*sizes, rows.shape[0] // math.prod(sizes), rows.shape[1])
     for level in reversed(range(len(CTX))):
-        if level > 0:
+        if level == len(CTX) - 1:
             rows = swap_sum(rows, CTX[level], level)
         else:
             rows = summed_over(rows.astype(jnp.bfloat16), CTX[level], level)

time: 173 us -> 172 us (level)
  the two profiles are of different devices: /device:TPU:38 before, /device:TPU:6 now
where the time goes in v12:
time: 172 us; the launch traced here: 171 us
  starting transfers between devices  74.8 us (43%)
  waiting for transfers between devices  54.8 us (32%)
  blocking collectives  12.5 us (7%)
  local copies, waits for them, and re-layouts  9.61 us (6%)
  matrix products  8.52 us (5%)
  other arithmetic  6.86 us (4%)
  between operations  3.91 us (2%)
    ppermute x9, waiting for transfers between devices, shift(): return jax.tree.map(lambda a: lax.ppermute(a, axis, pairs), tree)  32.2 us
    ppermute x7, starting transfers between devices, spread_sum(): total = total + lax.ppermute(piece, axis, pairs).astype(jnp.float32)  26.3 us
    all_to_all x2, starting transfers between devices, summed_over(): gathered = lax.all_to_all(part, axis, split, split, tiled=True)  20.4 us
    ppermute x7, starting transfers between devices, swap(): return jax.tree.map(lambda a: lax.ppermute(a, axis, [(0, 1), (1, 0)]), tree)  16.5 us
    all_to_all x1, blocking collectives, summed_over(): gathered = lax.all_to_all(part, axis, split, split, tiled=True)  12.5 us
    ppermute x9, starting transfers between devices, shift(): return jax.tree.map(lambda a: lax.ppermute(a, axis, pairs), tree)  11.6 us
    ppermute x7, waiting for transfers between devices, swap(): return jax.tree.map(lambda a: lax.ppermute(a, axis, [(0, 1), (1, 0)]), tree)  8.86 us
    ppermute x7, waiting for transfers between devices, spread_sum(): total = total + lax.ppermute(piece, axis, pairs).astype(jnp.float32)  7.83 us
  transfers between devices with their start and end apart: 25, of which 14 were waited for; matrix products, arithmetic and copies ran while one was open for 7% of the time, Pallas kernels for 0%

profile of v12, /device:TPU:6, one launch (start us, length us, event | category | flops | bytes accessed | tf_op | source)
XLA Modules:
  0.0 171.0 jit_solution(2188318366697326257)
XLA Ops:
  0.7 0.8 reshape.410
  1.5 1.2 reduce-window.6
  3.1 1.9 %collective-permute-start.1 = (f32[4]{0:T(128)S(1)}, f32[4]{0:T(128)S(1)}, u32[]{:S(2)}, u32[]{:S(2)}) collective-permute-start(f32[4]{0:T(128)S(1)} %fusion.51), channel_id=1, source_target_pairs={{0,8},{8,0},{1,9},{9,1},{2,10},{10,2},{3,11},{11,3},{4,12},{12,4},... | collective-permute-start | bytes 56 | tf_op jit(solution)/shard_map/ppermute | solution.py:23
  5.1 1.1 fusion.53
  6.2 1.2 fusion.54
  8.2 2.4 %collective-permute-start = (f32[4,128,64]{1,2,0:T(8,128)S(1)}, f32[4,128,64]{1,2,0:T(8,128)S(1)}, u32[]{:S(2)}, u32[]{:S(2)}) collective-permute-start(f32[4,128,64]{1,2,0:T(8,128)S(1)} %fusion.12), channel_id=1, source_target_pairs={{0,8},{8,0},{1,9},{9,1},{2,10},{10,2},{3,11},{11,3},{4,12},{12,4},... | collective-permute-start | bytes 393224 | tf_op jit(solution)/shard_map/ppermute | solution.py:23
  10.8 0.8 collective-permute-done
  11.7 3.5 %collective-permute-start.2 = (f32[4,128,64]{1,2,0:T(8,128)S(1)}, f32[4,128,64]{1,2,0:T(8,128)S(1)}, u32[]{:S(2)}, u32[]{:S(2)}) collective-permute-start(f32[4,128,64]{1,2,0:T(8,128)S(1)} %add_select_fusion), channel_id=1, source_target_pairs={{0,16},{16,0},{1,17},{17,1},{2,18},{18,2},{3,19},{19,3},{4,20},{20... | collective-permute-start | bytes 393224 | tf_op jit(solution)/shard_map/ppermute | solution.py:23
  15.2 1.0 fusion.11
  16.2 2.5 %collective-permute-start.3 = (f32[4]{0:T(128)S(1)}, f32[4]{0:T(128)S(1)}, u32[]{:S(2)}, u32[]{:S(2)}) collective-permute-start(f32[4]{0:T(128)S(1)} %get-tuple-element.51), channel_id=1, source_target_pairs={{0,16},{16,0},{1,17},{17,1},{2,18},{18,2},{3,19},{19,3},{4,20},{20... | collective-permute-start | bytes 56 | tf_op jit(solution)/shard_map/ppermute | solution.py:23
  18.7 0.6 dynamic-slice.34
  19.3 2.5 %collective-permute-done.3 = f32[4]{0:T(128)S(1)} collective-permute-done((f32[4]{0:T(128)S(1)}, f32[4]{0:T(128)S(1)}, u32[]{:S(2)}, u32[]{:S(2)}) %collective-permute-start.3) | collective-permute-done | bytes 48 | tf_op jit(solution)/shard_map/ppermute | solution.py:23
  21.8 0.6 dynamic-slice.35
  22.4 1.3 select_bitcast_fusion
  23.7 1.3 collective-permute-start.6
  25.0 1.3 collective-permute-start.4
  26.3 0.6 dynamic_slice.38
  26.9 1.3 collective-permute-start.5
  28.2 5.0 %collective-permute-done.5 = f32[]{:T(128)} collective-permute-done((f32[]{:T(128)}, f32[]{:T(128)}, u32[]{:S(2)}, u32[]{:S(2)}) %collective-permute-start.5) | collective-permute-done | bytes 36 | tf_op jit(solution)/shard_map/ppermute | solution.py:28
  33.8 1.3 collective-permute-start.8
  35.1 0.8 fusion.1
  35.9 1.3 collective-permute-start.7
  37.2 7.0 %collective-permute-done.7 = f32[]{:T(128)} collective-permute-done((f32[]{:T(128)}, f32[]{:T(128)}, u32[]{:S(2)}, u32[]{:S(2)}) %collective-permute-start.7) | collective-permute-done | bytes 36 | tf_op jit(solution)/shard_map/ppermute | solution.py:28
  44.8 1.3 collective-permute-start.10
  46.1 0.4 convolution_bitcast_fusion.3
  46.5 1.3 collective-permute-start.9
  47.8 6.8 %collective-permute-done.9 = f32[]{:T(128)} collective-permute-done((f32[]{:T(128)}, f32[]{:T(128)}, u32[]{:S(2)}, u32[]{:S(2)}) %collective-permute-start.9) | collective-permute-done | bytes 36 | tf_op jit(solution)/shard_map/ppermute | solution.py:28
  55.2 0.8 collective-permute-done.10
  56.0 1.3 collective-permute-start.12
  57.6 1.3 collective-permute-start.11
  58.9 9.4 %collective-permute-done.11 = f32[]{:T(128)} collective-permute-done((f32[]{:T(128)}, f32[]{:T(128)}, u32[]{:S(2)}, u32[]{:S(2)}) %collective-permute-start.11) | collective-permute-done | bytes 36 | tf_op jit(solution)/shard_map/ppermute | solution.py:28
  68.9 3.3 %collective-permute-done.12 = f32[128,64]{0,1:T(8,128)S(1)} collective-permute-done((f32[128,64]{0,1:T(8,128)S(1)}, f32[128,64]{0,1:T(8,128)S(1)}, u32[]{:S(2)}, u32[]{:S(2)}) %collective-permute-start.12) | collective-permute-done | bytes 32800 | tf_op jit(solution)/shard_map/ppermute | solution.py:28
  72.2 1.9 %collective-permute-start.13 = (f32[128,64]{0,1:T(8,128)S(1)}, f32[128,64]{0,1:T(8,128)S(1)}, u32[]{:S(2)}, u32[]{:S(2)}) collective-permute-start(f32[128,64]{0,1:T(8,128)S(1)} %add_select_fusion.1), channel_id=1, source_target_pairs={{0,8},{8,0},{1,9},{9,1},{2,10},{10,2},{3,11},{11,3},{4,12},{12,4},... | collective-permute-start | bytes 98312 | tf_op jit(solution)/shard_map/ppermute | solution.py:23
  74.4 0.9 collective-permute-done.13
  75.3 2.4 %collective-permute-start.14 = (f32[2,128,64]{1,2,0:T(8,128)S(1)}, f32[2,128,64]{1,2,0:T(8,128)S(1)}, u32[]{:S(2)}, u32[]{:S(2)}) collective-permute-start(f32[2,128,64]{1,2,0:T(8,128)S(1)} %maximum_select_fusion.1), channel_id=1, source_target_pairs={{0,16},{16,0},{1,17},{17,1},{2,18},{18,2},{3,19},{19,3},{4,20},{20... | collective-permute-start | bytes 196616 | tf_op jit(solution)/shard_map/ppermute | solution.py:23
  77.7 1.1 convolution_bitcast_fusion.1
  78.8 2.6 %collective-permute-done.14 = f32[2,128,64]{1,2,0:T(8,128)S(1)} collective-permute-done((f32[2,128,64]{1,2,0:T(8,128)S(1)}, f32[2,128,64]{1,2,0:T(8,128)S(1)}, u32[]{:S(2)}, u32[]{:S(2)}) %collective-permute-start.14) | collective-permute-done | bytes 65568 | tf_op jit(solution)/shard_map/ppermute | solution.py:23
  81.5 0.4 fusion.14
  81.9 0.7 pad_maximum_fusion
  82.6 7.1 %all-to-all-start = ((bf16[256,8,32]{0,2,1:T(8,128)(2,1)}), bf16[256,8,32]{0,2,1:T(8,128)(2,1)S(1)}, u32[]{:S(2)}, u32[]{:S(2)}) async-start(bf16[256,8,32]{0,2,1:T(8,128)(2,1)} %pad_maximum_fusion), calls=%async_computation | async-start | bytes 262144 | tf_op jit(solution)/shard_map/all_to_all | solution.py:176
  90.0 5.9 %all-to-all-done = bf16[256,8,32]{0,2,1:T(8,128)(2,1)S(1)} async-done(((bf16[256,8,32]{0,2,1:T(8,128)(2,1)}), bf16[256,8,32]{0,2,1:T(8,128)(2,1)S(1)}, u32[]{:S(2)}, u32[]{:S(2)}) %all-to-all-start) | async-done | bytes 131104 | tf_op jit(solution)/shard_map/all_to_all | solution.py:176
  95.9 0.5 multiply_bitcast_fusion
  96.4 2.1 %copy.70 = f32[1024,544]{1,0:T(8,128)} copy(f32[1024,544]{0,1:T(8,128)S(1)} %multiply_bitcast_fusion) | data formatting | bytes 4456448 | tf_op jit(solution)/shard_map/mul | solution.py:168
  98.4 1.4 dynamic-slice_convert_fusion
  99.8 1.9 %collective-permute-start.22 = (bf16[16,2,1,16,544]{4,3,2,1,0:T(8,128)(2,1)S(1)}, bf16[16,2,1,16,544]{4,3,2,1,0:T(8,128)(2,1)S(1)}, u32[]{:S(2)}, u32[]{:S(2)}) collective-permute-start(bf16[16,2,1,16,544]{4,3,2,1,0:T(8,128)(2,1)S(1)} %dynamic-slice_convert_fusion), channel_id=1, source_target_pairs={{0,8},{8,0},{1,9},{9,1},{2,10},{10,2},{3,11},{11,3},{4,12},{12,4},... | collective-permute-start | bytes 1671176 | tf_op jit(solution)/shard_map/ppermute | solution.py:23
  101.8 2.1 %collective-permute-done.22 = bf16[16,2,1,16,544]{4,3,2,1,0:T(8,128)(2,1)S(1)} collective-permute-done((bf16[16,2,1,16,544]{4,3,2,1,0:T(8,128)(2,1)S(1)}, bf16[16,2,1,16,544]{4,3,2,1,0:T(8,128)(2,1)S(1)}, u32[]{:S(2)}, u32[]{:S(2)}) %collective-permute-start.22) | collective-permute-done | bytes 557088 | tf_op jit(solution)/shard_map/ppermute | solution.py:23
  103.8 1.5 add_convert_fusion
  105.4 12.5 %all_to_all.16 = bf16[16,2,1,16,544]{4,3,2,0,1:T(8,128)(2,1)S(1)} all-to-all(bf16[16,2,1,16,544]{4,3,2,0,1:T(8,128)(2,1)S(1)} %copy.71), channel_id=1, replica_groups=mesh['z'=16,'y_lo'=2,'core'=2,'y_hi'=2,'x'=4] {'y_lo'}, dimensions={1} | all-to-all | bytes 1114112 | tf_op jit(solution)/shard_map/all_to_all | solution.py:176
  117.9 0.9 reduce_sum.52
  118.8 13.3 %all-to-all-start.2 = ((bf16[16,1,1,16,544]{4,3,2,1,0:T(8,128)(2,1)}), bf16[16,1,1,16,544]{4,3,2,1,0:T(8,128)(2,1)S(1)}, u32[]{:S(2)}, u32[]{:S(2)}) async-start(bf16[16,1,1,16,544]{4,3,2,1,0:T(8,128)(2,1)} %bitcast.57), calls=%async_computation.2 | async-start | bytes 655360 | tf_op jit(solution)/shard_map/all_to_all | solution.py:176
  132.7 0.4 convolution_add_fusion.1
  133.5 1.2 constant_dynamic-slice_fusion.7
  134.7 3.9 %collective-permute-start.21 = (bf16[256,128]{1,0:T(8,128)(2,1)S(1)}, bf16[256,128]{1,0:T(8,128)(2,1)S(1)}, u32[]{:S(2)}, u32[]{:S(2)}) collective-permute-start(bf16[256,128]{1,0:T(8,128)(2,1)S(1)} %bitcast.216), channel_id=1, source_target_pairs={{0,1},{1,2},{2,3},{3,4},{4,5},{5,6},{6,7},{7,0},{8,9},{9,10},{10,1... | collective-permute-start | bytes 196616 | tf_op jit(solution)/shard_map/ppermute | solution.py:190
  138.6 2.4 %collective-permute-start.20 = (bf16[256,128]{1,0:T(8,128)(2,1)S(1)}, bf16[256,128]{1,0:T(8,128)(2,1)S(1)}, u32[]{:S(2)}, u32[]{:S(2)}) collective-permute-start(bf16[256,128]{1,0:T(8,128)(2,1)S(1)} %bitcast.214), channel_id=1, source_target_pairs={{0,2},{1,3},{2,4},{3,5},{4,6},{5,7},{6,0},{7,1},{8,10},{9,11},{10,... | collective-permute-start | bytes 196616 | tf_op jit(solution)/shard_map/ppermute | solution.py:190
  141.1 5.5 %collective-permute-start.19 = (bf16[256,128]{1,0:T(8,128)(2,1)S(1)}, bf16[256,128]{1,0:T(8,128)(2,1)S(1)}, u32[]{:S(2)}, u32[]{:S(2)}) collective-permute-start(bf16[256,128]{1,0:T(8,128)(2,1)S(1)} %bitcast.213), channel_id=1, source_target_pairs={{0,3},{1,4},{2,5},{3,6},{4,7},{5,0},{6,1},{7,2},{8,11},{9,12},{10,... | collective-permute-start | bytes 196616 | tf_op jit(solution)/shard_map/ppermute | solution.py:190
  146.6 2.5 %collective-permute-start.18 = (bf16[256,128]{1,0:T(8,128)(2,1)S(1)}, bf16[256,128]{1,0:T(8,128)(2,1)S(1)}, u32[]{:S(2)}, u32[]{:S(2)}) collective-permute-start(bf16[256,128]{1,0:T(8,128)(2,1)S(1)} %bitcast.215), channel_id=1, source_target_pairs={{0,4},{1,5},{2,6},{3,7},{4,0},{5,1},{6,2},{7,3},{8,12},{9,13},{10,... | collective-permute-start | bytes 196616 | tf_op jit(solution)/shard_map/ppermute | solution.py:190
  149.1 3.9 %collective-permute-start.17 = (bf16[256,128]{1,0:T(8,128)(2,1)S(1)}, bf16[256,128]{1,0:T(8,128)(2,1)S(1)}, u32[]{:S(2)}, u32[]{:S(2)}) collective-permute-start(bf16[256,128]{1,0:T(8,128)(2,1)S(1)} %bitcast.217), channel_id=1, source_target_pairs={{0,5},{1,6},{2,7},{3,0},{4,1},{5,2},{6,3},{7,4},{8,13},{9,14},{10,... | collective-permute-start | bytes 196616 | tf_op jit(solution)/shard_map/ppermute | solution.py:190
  153.1 6.1 %collective-permute-start.16 = (bf16[256,128]{1,0:T(8,128)(2,1)S(1)}, bf16[256,128]{1,0:T(8,128)(2,1)S(1)}, u32[]{:S(2)}, u32[]{:S(2)}) collective-permute-start(bf16[256,128]{1,0:T(8,128)(2,1)S(1)} %bitcast.219), channel_id=1, source_target_pairs={{0,6},{1,7},{2,0},{3,1},{4,2},{5,3},{6,4},{7,5},{8,14},{9,15},{10,... | collective-permute-start | bytes 196616 | tf_op jit(solution)/shard_map/ppermute | solution.py:190
  159.2 1.9 %collective-permute-start.15 = (bf16[256,128]{1,0:T(8,128)(2,1)S(1)}, bf16[256,128]{1,0:T(8,128)(2,1)S(1)}, u32[]{:S(2)}, u32[]{:S(2)}) collective-permute-start(bf16[256,128]{1,0:T(8,128)(2,1)S(1)} %bitcast.218), channel_id=1, source_target_pairs={{0,7},{1,0},{2,1},{3,2},{4,3},{5,4},{6,5},{7,6},{8,15},{9,8},{10,9... | collective-permute-start | bytes 196616 | tf_op jit(solution)/shard_map/ppermute | solution.py:190
  161.2 2.0 %collective-permute-done.16 = bf16[256,128]{1,0:T(8,128)(2,1)S(1)} collective-permute-done((bf16[256,128]{1,0:T(8,128)(2,1)S(1)}, bf16[256,128]{1,0:T(8,128)(2,1)S(1)}, u32[]{:S(2)}, u32[]{:S(2)}) %collective-permute-start.16) | collective-permute-done | bytes 65568 | tf_op jit(solution)/shard_map/ppermute | solution.py:190
  163.2 5.9 %collective-permute-done.15 = bf16[256,128]{1,0:T(8,128)(2,1)S(1)} collective-permute-done((bf16[256,128]{1,0:T(8,128)(2,1)S(1)}, bf16[256,128]{1,0:T(8,128)(2,1)S(1)}, u32[]{:S(2)}, u32[]{:S(2)}) %collective-permute-start.15) | collective-permute-done | bytes 65568 | tf_op jit(solution)/shard_map/ppermute | solution.py:190
  169.0 0.7 fusion.43
  169.8 0.6 fusion.52
  170.4 0.6 slice.28
  (77 shorter events, 3.5 us)
Async XLA Ops:
  0.6 95.3 %copy-start = (bf16[256,1024]{1,0:T(8,128)(2,1)S(1)}, bf16[256,1024]{1,0:T(8,128)(2,1)}, u32[]{:S(2)}) copy-start(bf16[256,1024]{1,0:T(8,128)(2,1)} %param.11) | copy-start | bytes 1572868
  0.6 7.3 %copy-start.1 = (bf16[256,128]{1,0:T(8,128)(2,1)S(1)}, bf16[256,128]{1,0:T(8,128)(2,1)}, u32[]{:S(2)}) copy-start(bf16[256,128]{1,0:T(8,128)(2,1)} %param.16) | copy-start | bytes 196612
  0.7 6.9 %copy-start.6 = (bf16[256,256]{1,0:T(8,128)(2,1)S(1)}, bf16[256,256]{1,0:T(8,128)(2,1)}, u32[]{:S(2)}) copy-start(bf16[256,256]{1,0:T(8,128)(2,1)} %param.13) | copy-start | bytes 393220
  0.7 7.0 %copy-start.7 = (bf16[256,256]{1,0:T(8,128)(2,1)S(1)}, bf16[256,256]{1,0:T(8,128)(2,1)}, u32[]{:S(2)}) copy-start(bf16[256,256]{1,0:T(8,128)(2,1)} %param.14) | copy-start | bytes 393220
  0.7 9.9 %copy-start.8 = (bf16[256,256]{1,0:T(8,128)(2,1)S(1)}, bf16[256,256]{1,0:T(8,128)(2,1)}, u32[]{:S(2)}) copy-start(bf16[256,256]{1,0:T(8,128)(2,1)} %param.12) | copy-start | bytes 393220
  3.1 4.8 %collective-permute-start.1 = (f32[4]{0:T(128)S(1)}, f32[4]{0:T(128)S(1)}, u32[]{:S(2)}, u32[]{:S(2)}) collective-permute-start(f32[4]{0:T(128)S(1)} %fusion.51), channel_id=1, source_target_pairs={{0,8},{8,0},{1,9},{9,1},{2,10},{10,2},{3,11},{11,3},{4,12},{12,4},... | collective-permute-start | bytes 56 | tf_op jit(solution)/shard_map/ppermute | solution.py:23
  8.2 3.4 %collective-permute-start = (f32[4,128,64]{1,2,0:T(8,128)S(1)}, f32[4,128,64]{1,2,0:T(8,128)S(1)}, u32[]{:S(2)}, u32[]{:S(2)}) collective-permute-start(f32[4,128,64]{1,2,0:T(8,128)S(1)} %fusion.12), channel_id=1, source_target_pairs={{0,8},{8,0},{1,9},{9,1},{2,10},{10,2},{3,11},{11,3},{4,12},{12,4},... | collective-permute-start | bytes 393224 | tf_op jit(solution)/shard_map/ppermute | solution.py:23
  11.7 10.7 %collective-permute-start.2 = (f32[4,128,64]{1,2,0:T(8,128)S(1)}, f32[4,128,64]{1,2,0:T(8,128)S(1)}, u32[]{:S(2)}, u32[]{:S(2)}) collective-permute-start(f32[4,128,64]{1,2,0:T(8,128)S(1)} %add_select_fusion), channel_id=1, source_target_pairs={{0,16},{16,0},{1,17},{17,1},{2,18},{18,2},{3,19},{19,3},{4,20},{20... | collective-permute-start | bytes 393224 | tf_op jit(solution)/shard_map/ppermute | solution.py:23
  15.2 31.0 %copy-start.4 = (f32[1,4,128,64]{2,3,1,0:T(8,128)S(1)}, f32[1,4,128,64]{2,3,1,0:T(8,128)}, u32[]{:S(2)}) copy-start(f32[1,4,128,64]{2,3,1,0:T(8,128)} %param.18) | copy-start | bytes 393220
  16.2 41.1 %copy-start.2 = (bf16[256,128]{1,0:T(8,128)(2,1)S(1)}, bf16[256,128]{1,0:T(8,128)(2,1)}, u32[]{:S(2)}) copy-start(bf16[256,128]{1,0:T(8,128)(2,1)} %param.15) | copy-start | bytes 196612
  16.2 5.6 %collective-permute-start.3 = (f32[4]{0:T(128)S(1)}, f32[4]{0:T(128)S(1)}, u32[]{:S(2)}, u32[]{:S(2)}) collective-permute-start(f32[4]{0:T(128)S(1)} %get-tuple-element.51), channel_id=1, source_target_pairs={{0,16},{16,0},{1,17},{17,1},{2,18},{18,2},{3,19},{19,3},{4,20},{20... | collective-permute-start | bytes 56 | tf_op jit(solution)/shard_map/ppermute | solution.py:23
  23.7 10.1 %collective-permute-start.6 = (f32[128,64]{0,1:T(8,128)S(1)}, f32[128,64]{0,1:T(8,128)S(1)}, u32[]{:S(2)}, u32[]{:S(2)}) collective-permute-start(f32[128,64]{0,1:T(8,128)S(1)} %select_bitcast_fusion), channel_id=1, source_target_pairs={{64,0},{96,32},{128,64},{160,96},{192,128},{224,160},{256,192},{28... | collective-permute-start | bytes 98312 | tf_op jit(solution)/shard_map/ppermute | solution.py:28
  25.0 8.8 %collective-permute-start.4 = (f32[128,64]{0,1:T(8,128)S(1)}, f32[128,64]{0,1:T(8,128)S(1)}, u32[]{:S(2)}, u32[]{:S(2)}) collective-permute-start(f32[128,64]{0,1:T(8,128)S(1)} %select_bitcast_fusion), channel_id=1, source_target_pairs={{32,0},{64,32},{96,64},{128,96},{160,128},{192,160},{224,192},{256... | collective-permute-start | bytes 98312 | tf_op jit(solution)/shard_map/ppermute | solution.py:28
  26.9 6.3 %collective-permute-start.5 = (f32[]{:T(128)}, f32[]{:T(128)}, u32[]{:S(2)}, u32[]{:S(2)}) collective-permute-start(f32[]{:T(128)} %bitcast.34), channel_id=1, source_target_pairs={{32,0},{64,32},{96,64},{128,96},{160,128},{192,160},{224,192},{256... | collective-permute-start | bytes 20 | tf_op jit(solution)/shard_map/ppermute | solution.py:28
  33.8 11.0 %collective-permute-start.8 = (f32[128,64]{0,1:T(8,128)S(1)}, f32[128,64]{0,1:T(8,128)S(1)}, u32[]{:S(2)}, u32[]{:S(2)}) collective-permute-start(f32[128,64]{0,1:T(8,128)S(1)} %multiply_add_fusion), channel_id=1, source_target_pairs={{64,0},{96,32},{128,64},{160,96},{192,128},{224,160},{256,192},{28... | collective-permute-start | bytes 98312 | tf_op jit(solution)/shard_map/ppermute | solution.py:28
  35.9 8.3 %collective-permute-start.7 = (f32[]{:T(128)}, f32[]{:T(128)}, u32[]{:S(2)}, u32[]{:S(2)}) collective-permute-start(f32[]{:T(128)} %bitcast.34), channel_id=1, source_target_pairs={{64,0},{96,32},{128,64},{160,96},{192,128},{224,160},{256,192},{28... | collective-permute-start | bytes 20 | tf_op jit(solution)/shard_map/ppermute | solution.py:28
  44.8 11.2 %collective-permute-start.10 = (f32[128,64]{0,1:T(8,128)S(1)}, f32[128,64]{0,1:T(8,128)S(1)}, u32[]{:S(2)}, u32[]{:S(2)}) collective-permute-start(f32[128,64]{0,1:T(8,128)S(1)} %add_select_fusion.3), channel_id=1, source_target_pairs={{128,0},{160,32},{192,64},{224,96},{256,128},{288,160},{320,192},{... | collective-permute-start | bytes 98312 | tf_op jit(solution)/shard_map/ppermute | solution.py:28
  46.5 8.1 %collective-permute-start.9 = (f32[]{:T(128)}, f32[]{:T(128)}, u32[]{:S(2)}, u32[]{:S(2)}) collective-permute-start(f32[]{:T(128)} %mul.308), channel_id=1, source_target_pairs={{64,0},{96,32},{128,64},{160,96},{192,128},{224,160},{256,192},{28... | collective-permute-start | bytes 20 | tf_op jit(solution)/shard_map/ppermute | solution.py:28
  56.0 16.2 %collective-permute-start.12 = (f32[128,64]{0,1:T(8,128)S(1)}, f32[128,64]{0,1:T(8,128)S(1)}, u32[]{:S(2)}, u32[]{:S(2)}) collective-permute-start(f32[128,64]{0,1:T(8,128)S(1)} %add_select_fusion.2), channel_id=1, source_target_pairs={{256,0},{288,32},{320,64},{352,96},{384,128},{416,160},{448,192},{... | collective-permute-start | bytes 98312 | tf_op jit(solution)/shard_map/ppermute | solution.py:28
  57.6 10.7 %collective-permute-start.11 = (f32[]{:T(128)}, f32[]{:T(128)}, u32[]{:S(2)}, u32[]{:S(2)}) collective-permute-start(f32[]{:T(128)} %select_n.194), channel_id=1, source_target_pairs={{128,0},{160,32},{192,64},{224,96},{256,128},{288,160},{320,192},{... | collective-permute-start | bytes 20 | tf_op jit(solution)/shard_map/ppermute | solution.py:28
  72.2 3.1 %collective-permute-start.13 = (f32[128,64]{0,1:T(8,128)S(1)}, f32[128,64]{0,1:T(8,128)S(1)}, u32[]{:S(2)}, u32[]{:S(2)}) collective-permute-start(f32[128,64]{0,1:T(8,128)S(1)} %add_select_fusion.1), channel_id=1, source_target_pairs={{0,8},{8,0},{1,9},{9,1},{2,10},{10,2},{3,11},{11,3},{4,12},{12,4},... | collective-permute-start | bytes 98312 | tf_op jit(solution)/shard_map/ppermute | solution.py:23
  75.3 6.2 %collective-permute-start.14 = (f32[2,128,64]{1,2,0:T(8,128)S(1)}, f32[2,128,64]{1,2,0:T(8,128)S(1)}, u32[]{:S(2)}, u32[]{:S(2)}) collective-permute-start(f32[2,128,64]{1,2,0:T(8,128)S(1)} %maximum_select_fusion.1), channel_id=1, source_target_pairs={{0,16},{16,0},{1,17},{17,1},{2,18},{18,2},{3,19},{19,3},{4,20},{20... | collective-permute-start | bytes 196616 | tf_op jit(solution)/shard_map/ppermute | solution.py:23
  82.6 13.3 %all-to-all-start = ((bf16[256,8,32]{0,2,1:T(8,128)(2,1)}), bf16[256,8,32]{0,2,1:T(8,128)(2,1)S(1)}, u32[]{:S(2)}, u32[]{:S(2)}) async-start(bf16[256,8,32]{0,2,1:T(8,128)(2,1)} %pad_maximum_fusion), calls=%async_computation | async-start | bytes 262144 | tf_op jit(solution)/shard_map/all_to_all | solution.py:176
  99.8 4.0 %collective-permute-start.22 = (bf16[16,2,1,16,544]{4,3,2,1,0:T(8,128)(2,1)S(1)}, bf16[16,2,1,16,544]{4,3,2,1,0:T(8,128)(2,1)S(1)}, u32[]{:S(2)}, u32[]{:S(2)}) collective-permute-start(bf16[16,2,1,16,544]{4,3,2,1,0:T(8,128)(2,1)S(1)} %dynamic-slice_convert_fusion), channel_id=1, source_target_pairs={{0,8},{8,0},{1,9},{9,1},{2,10},{10,2},{3,11},{11,3},{4,12},{12,4},... | collective-permute-start | bytes 1671176 | tf_op jit(solution)/shard_map/ppermute | solution.py:23
  105.3 26.8 %copy-start.3 = (bf16[1024,256]{1,0:T(8,128)(2,1)S(1)}, bf16[1024,256]{1,0:T(8,128)(2,1)}, u32[]{:S(2)}) copy-start(bf16[1024,256]{1,0:T(8,128)(2,1)} %param.19) | copy-start | bytes 1572868
  105.4 27.3 %copy-start.5 = (bf16[1024,256]{1,0:T(8,128)(2,1)S(1)}, bf16[1024,256]{1,0:T(8,128)(2,1)}, u32[]{:S(2)}) copy-start(bf16[1024,256]{1,0:T(8,128)(2,1)} %param.20) | copy-start | bytes 1572868
  118.8 50.9 %all-to-all-start.2 = ((bf16[16,1,1,16,544]{4,3,2,1,0:T(8,128)(2,1)}), bf16[16,1,1,16,544]{4,3,2,1,0:T(8,128)(2,1)S(1)}, u32[]{:S(2)}, u32[]{:S(2)}) async-start(bf16[16,1,1,16,544]{4,3,2,1,0:T(8,128)(2,1)} %bitcast.57), calls=%async_computation.2 | async-start | bytes 655360 | tf_op jit(solution)/shard_map/all_to_all | solution.py:176
  132.1 0.9 copy-start.9
  134.7 18.4 %collective-permute-start.21 = (bf16[256,128]{1,0:T(8,128)(2,1)S(1)}, bf16[256,128]{1,0:T(8,128)(2,1)S(1)}, u32[]{:S(2)}, u32[]{:S(2)}) collective-permute-start(bf16[256,128]{1,0:T(8,128)(2,1)S(1)} %bitcast.216), channel_id=1, source_target_pairs={{0,1},{1,2},{2,3},{3,4},{4,5},{5,6},{6,7},{7,0},{8,9},{9,10},{10,1... | collective-permute-start | bytes 196616 | tf_op jit(solution)/shard_map/ppermute | solution.py:190
  138.6 20.6 %collective-permute-start.20 = (bf16[256,128]{1,0:T(8,128)(2,1)S(1)}, bf16[256,128]{1,0:T(8,128)(2,1)S(1)}, u32[]{:S(2)}, u32[]{:S(2)}) collective-permute-start(bf16[256,128]{1,0:T(8,128)(2,1)S(1)} %bitcast.214), channel_id=1, source_target_pairs={{0,2},{1,3},{2,4},{3,5},{4,6},{5,7},{6,0},{7,1},{8,10},{9,11},{10,... | collective-permute-start | bytes 196616 | tf_op jit(solution)/shard_map/ppermute | solution.py:190
  141.1 20.1 %collective-permute-start.19 = (bf16[256,128]{1,0:T(8,128)(2,1)S(1)}, bf16[256,128]{1,0:T(8,128)(2,1)S(1)}, u32[]{:S(2)}, u32[]{:S(2)}) collective-permute-start(bf16[256,128]{1,0:T(8,128)(2,1)S(1)} %bitcast.213), channel_id=1, source_target_pairs={{0,3},{1,4},{2,5},{3,6},{4,7},{5,0},{6,1},{7,2},{8,11},{9,12},{10,... | collective-permute-start | bytes 196616 | tf_op jit(solution)/shard_map/ppermute | solution.py:190
  146.6 14.6 %collective-permute-start.18 = (bf16[256,128]{1,0:T(8,128)(2,1)S(1)}, bf16[256,128]{1,0:T(8,128)(2,1)S(1)}, u32[]{:S(2)}, u32[]{:S(2)}) collective-permute-start(bf16[256,128]{1,0:T(8,128)(2,1)S(1)} %bitcast.215), channel_id=1, source_target_pairs={{0,4},{1,5},{2,6},{3,7},{4,0},{5,1},{6,2},{7,3},{8,12},{9,13},{10,... | collective-permute-start | bytes 196616 | tf_op jit(solution)/shard_map/ppermute | solution.py:190
  149.1 12.1 %collective-permute-start.17 = (bf16[256,128]{1,0:T(8,128)(2,1)S(1)}, bf16[256,128]{1,0:T(8,128)(2,1)S(1)}, u32[]{:S(2)}, u32[]{:S(2)}) collective-permute-start(bf16[256,128]{1,0:T(8,128)(2,1)S(1)} %bitcast.217), channel_id=1, source_target_pairs={{0,5},{1,6},{2,7},{3,0},{4,1},{5,2},{6,3},{7,4},{8,13},{9,14},{10,... | collective-permute-start | bytes 196616 | tf_op jit(solution)/shard_map/ppermute | solution.py:190
  153.1 10.1 %collective-permute-start.16 = (bf16[256,128]{1,0:T(8,128)(2,1)S(1)}, bf16[256,128]{1,0:T(8,128)(2,1)S(1)}, u32[]{:S(2)}, u32[]{:S(2)}) collective-permute-start(bf16[256,128]{1,0:T(8,128)(2,1)S(1)} %bitcast.219), channel_id=1, source_target_pairs={{0,6},{1,7},{2,0},{3,1},{4,2},{5,3},{6,4},{7,5},{8,14},{9,15},{10,... | collective-permute-start | bytes 196616 | tf_op jit(solution)/shard_map/ppermute | solution.py:190
  159.2 9.8 %collective-permute-start.15 = (bf16[256,128]{1,0:T(8,128)(2,1)S(1)}, bf16[256,128]{1,0:T(8,128)(2,1)S(1)}, u32[]{:S(2)}, u32[]{:S(2)}) collective-permute-start(bf16[256,128]{1,0:T(8,128)(2,1)S(1)} %bitcast.218), channel_id=1, source_target_pairs={{0,7},{1,0},{2,1},{3,2},{4,3},{5,4},{6,5},{7,6},{8,15},{9,8},{10,9... | collective-permute-start | bytes 196616 | tf_op jit(solution)/shard_map/ppermute | solution.py:190

commit v13 on v11

--- a/solution.py
+++ b/solution.py
@@ -222,8 +222,10 @@
     rows = row_term(events, projected, norm_scale)
     sizes = [lax.axis_size(name) for name in CTX]
     rows = rows.reshape(*sizes, rows.shape[0] // math.prod(sizes), rows.shape[1])
-    for level in reversed(range(len(CTX))):
+    for level in reversed(range(1, len(CTX))):
         rows = summed_over(rows.astype(jnp.bfloat16), CTX[level], level)
+    flat = rows.reshape(rows.shape[0], -1).astype(jnp.bfloat16)
+    rows = summed_over(flat, CTX[0], 0).reshape(1, 1, 1, rows.shape[-2], rows.shape[-1])
     reduced = rows.reshape(rows.shape[-2], rows.shape[-1])
     grad_w_gate = reduced[:, :head_cols]
     grad_w_value = reduced[:, head_cols : 2 * head_cols]

time: 167 us -> 172 us (1.030)
  local copies, waits for them, and re-layouts: 7.44 us -> 9.74 us
  other arithmetic: 6.01 us -> 8.02 us
    convert_element_type x0 -> x1, other arithmetic: none -> 2.27 us  [per_device(): flat = rows.reshape(rows.shape[0], -1).astype(jnp.bfloat16)]
where the time goes in v13:
time: 172 us; the launch traced here: 171 us
  starting transfers between devices  77.9 us (45%)
  waiting for transfers between devices  46.6 us (27%)
  blocking collectives  17.2 us (10%)
  local copies, waits for them, and re-layouts  9.74 us (6%)
  other arithmetic  8.02 us (5%)
  matrix products  6.71 us (4%)
  between operations  4.4 us (3%)
    ppermute x9, waiting for transfers between devices, shift(): return jax.tree.map(lambda a: lax.ppermute(a, axis, pairs), tree)  28.7 us
    ppermute x7, starting transfers between devices, spread_sum(): total = total + lax.ppermute(piece, axis, pairs).astype(jnp.float32)  27.5 us
    all_to_all x2, starting transfers between devices, summed_over(): gathered = lax.all_to_all(part, axis, split, split, tiled=True)  17.3 us
    all_to_all x2, blocking collectives, summed_over(): gathered = lax.all_to_all(part, axis, split, split, tiled=True)  17.2 us
    ppermute x9, starting transfers between devices, shift(): return jax.tree.map(lambda a: lax.ppermute(a, axis, pairs), tree)  16.8 us
    ppermute x6, starting transfers between devices, swap(): return jax.tree.map(lambda a: lax.ppermute(a, axis, [(0, 1), (1, 0)]), tree)  16.3 us
    all_to_all x2, waiting for transfers between devices, summed_over(): gathered = lax.all_to_all(part, axis, split, split, tiled=True)  7.81 us
    ppermute x6, waiting for transfers between devices, swap(): return jax.tree.map(lambda a: lax.ppermute(a, axis, [(0, 1), (1, 0)]), tree)  5.47 us
  transfers between devices with their start and end apart: 24, of which 13 were waited for; matrix products, arithmetic and copies ran while one was open for 6% of the time, Pallas kernels for 0%

profile of v13, /device:TPU:32, one launch (start us, length us, event | category | flops | bytes accessed | tf_op | source)
XLA Modules:
  0.0 170.6 jit_solution(17952285636225169744)
XLA Ops:
  0.7 0.8 reshape.425
  1.5 1.2 reduce-window.6
  3.1 1.9 %collective-permute-start.1 = (f32[4]{0:T(128)S(1)}, f32[4]{0:T(128)S(1)}, u32[]{:S(2)}, u32[]{:S(2)}) collective-permute-start(f32[4]{0:T(128)S(1)} %fusion.52), channel_id=1, source_target_pairs={{0,8},{8,0},{1,9},{9,1},{2,10},{10,2},{3,11},{11,3},{4,12},{12,4},... | collective-permute-start | bytes 56 | tf_op jit(solution)/shard_map/ppermute | solution.py:23
  6.4 2.4 %collective-permute-start = (f32[4,128,64]{1,2,0:T(8,128)S(1)}, f32[4,128,64]{1,2,0:T(8,128)S(1)}, u32[]{:S(2)}, u32[]{:S(2)}) collective-permute-start(f32[4,128,64]{1,2,0:T(8,128)S(1)} %fusion.13), channel_id=1, source_target_pairs={{0,8},{8,0},{1,9},{9,1},{2,10},{10,2},{3,11},{11,3},{4,12},{12,4},... | collective-permute-start | bytes 393224 | tf_op jit(solution)/shard_map/ppermute | solution.py:23
  9.0 0.8 collective-permute-done
  9.9 3.5 %collective-permute-start.2 = (f32[4,128,64]{1,2,0:T(8,128)S(1)}, f32[4,128,64]{1,2,0:T(8,128)S(1)}, u32[]{:S(2)}, u32[]{:S(2)}) collective-permute-start(f32[4,128,64]{1,2,0:T(8,128)S(1)} %add_select_fusion), channel_id=1, source_target_pairs={{0,16},{16,0},{1,17},{17,1},{2,18},{18,2},{3,19},{19,3},{4,20},{20... | collective-permute-start | bytes 393224 | tf_op jit(solution)/shard_map/ppermute | solution.py:23
  13.4 1.0 fusion.12
  14.4 2.4 %collective-permute-start.3 = (f32[4]{0:T(128)S(1)}, f32[4]{0:T(128)S(1)}, u32[]{:S(2)}, u32[]{:S(2)}) collective-permute-start(f32[4]{0:T(128)S(1)} %get-tuple-element.51), channel_id=1, source_target_pairs={{0,16},{16,0},{1,17},{17,1},{2,18},{18,2},{3,19},{19,3},{4,20},{20... | collective-permute-start | bytes 56 | tf_op jit(solution)/shard_map/ppermute | solution.py:23
  16.7 0.6 dynamic-slice.34
  17.3 2.5 %collective-permute-done.3 = f32[4]{0:T(128)S(1)} collective-permute-done((f32[4]{0:T(128)S(1)}, f32[4]{0:T(128)S(1)}, u32[]{:S(2)}, u32[]{:S(2)}) %collective-permute-start.3) | collective-permute-done | bytes 48 | tf_op jit(solution)/shard_map/ppermute | solution.py:23
  19.8 0.6 dynamic-slice.35
  20.4 1.3 select_bitcast_fusion
  21.7 1.3 collective-permute-start.6
  23.0 5.8 %collective-permute-start.4 = (f32[128,64]{0,1:T(8,128)S(1)}, f32[128,64]{0,1:T(8,128)S(1)}, u32[]{:S(2)}, u32[]{:S(2)}) collective-permute-start(f32[128,64]{0,1:T(8,128)S(1)} %select_bitcast_fusion), channel_id=1, source_target_pairs={{32,0},{64,32},{96,64},{128,96},{160,128},{192,160},{224,192},{256... | collective-permute-start | bytes 98312 | tf_op jit(solution)/shard_map/ppermute | solution.py:28
  28.9 0.6 dynamic_slice.31
  29.4 1.9 %collective-permute-start.5 = (f32[]{:T(128)}, f32[]{:T(128)}, u32[]{:S(2)}, u32[]{:S(2)}) collective-permute-start(f32[]{:T(128)} %bitcast.34), channel_id=1, source_target_pairs={{32,0},{64,32},{96,64},{128,96},{160,128},{192,160},{224,192},{256... | collective-permute-start | bytes 20 | tf_op jit(solution)/shard_map/ppermute | solution.py:28
  31.4 3.7 %collective-permute-done.5 = f32[]{:T(128)} collective-permute-done((f32[]{:T(128)}, f32[]{:T(128)}, u32[]{:S(2)}, u32[]{:S(2)}) %collective-permute-start.5) | collective-permute-done | bytes 36 | tf_op jit(solution)/shard_map/ppermute | solution.py:28
  35.8 1.3 collective-permute-start.8
  37.1 0.8 fusion.2
  37.9 1.3 collective-permute-start.7
  39.2 7.5 %collective-permute-done.7 = f32[]{:T(128)} collective-permute-done((f32[]{:T(128)}, f32[]{:T(128)}, u32[]{:S(2)}, u32[]{:S(2)}) %collective-permute-start.7) | collective-permute-done | bytes 36 | tf_op jit(solution)/shard_map/ppermute | solution.py:28
  47.5 1.3 collective-permute-start.10
  48.8 0.4 convolution_bitcast_fusion.3
  49.2 1.3 collective-permute-start.9
  50.5 6.2 %collective-permute-done.9 = f32[]{:T(128)} collective-permute-done((f32[]{:T(128)}, f32[]{:T(128)}, u32[]{:S(2)}, u32[]{:S(2)}) %collective-permute-start.9) | collective-permute-done | bytes 36 | tf_op jit(solution)/shard_map/ppermute | solution.py:28
  57.8 1.3 collective-permute-start.12
  59.4 1.3 collective-permute-start.11
  60.7 8.3 %collective-permute-done.11 = f32[]{:T(128)} collective-permute-done((f32[]{:T(128)}, f32[]{:T(128)}, u32[]{:S(2)}, u32[]{:S(2)}) %collective-permute-start.11) | collective-permute-done | bytes 36 | tf_op jit(solution)/shard_map/ppermute | solution.py:28
  69.7 2.6 %collective-permute-done.12 = f32[128,64]{0,1:T(8,128)S(1)} collective-permute-done((f32[128,64]{0,1:T(8,128)S(1)}, f32[128,64]{0,1:T(8,128)S(1)}, u32[]{:S(2)}, u32[]{:S(2)}) %collective-permute-start.12) | collective-permute-done | bytes 32800 | tf_op jit(solution)/shard_map/ppermute | solution.py:28
  72.3 1.9 %collective-permute-start.13 = (f32[128,64]{0,1:T(8,128)S(1)}, f32[128,64]{0,1:T(8,128)S(1)}, u32[]{:S(2)}, u32[]{:S(2)}) collective-permute-start(f32[128,64]{0,1:T(8,128)S(1)} %add_select_fusion.1), channel_id=1, source_target_pairs={{0,8},{8,0},{1,9},{9,1},{2,10},{10,2},{3,11},{11,3},{4,12},{12,4},... | collective-permute-start | bytes 98312 | tf_op jit(solution)/shard_map/ppermute | solution.py:23
  74.5 0.9 collective-permute-done.13
  75.4 4.3 %collective-permute-start.14 = (f32[2,128,64]{1,2,0:T(8,128)S(1)}, f32[2,128,64]{1,2,0:T(8,128)S(1)}, u32[]{:S(2)}, u32[]{:S(2)}) collective-permute-start(f32[2,128,64]{1,2,0:T(8,128)S(1)} %maximum_select_fusion.1), channel_id=1, source_target_pairs={{0,16},{16,0},{1,17},{17,1},{2,18},{18,2},{3,19},{19,3},{4,20},{20... | collective-permute-start | bytes 196616 | tf_op jit(solution)/shard_map/ppermute | solution.py:23
  79.7 1.1 convolution_bitcast_fusion.1
  80.9 1.2 collective-permute-done.14
  82.2 0.4 fusion.15
  82.6 0.7 pad_maximum_fusion
  83.3 5.3 %all-to-all-start = ((bf16[256,8,32]{0,2,1:T(8,128)(2,1)}), bf16[256,8,32]{0,2,1:T(8,128)(2,1)S(1)}, u32[]{:S(2)}, u32[]{:S(2)}) async-start(bf16[256,8,32]{0,2,1:T(8,128)(2,1)} %pad_maximum_fusion), calls=%async_computation | async-start | bytes 262144 | tf_op jit(solution)/shard_map/all_to_all | solution.py:176
  88.9 7.8 %all-to-all-done = bf16[256,8,32]{0,2,1:T(8,128)(2,1)S(1)} async-done(((bf16[256,8,32]{0,2,1:T(8,128)(2,1)}), bf16[256,8,32]{0,2,1:T(8,128)(2,1)S(1)}, u32[]{:S(2)}, u32[]{:S(2)}) %all-to-all-start) | async-done | bytes 131104 | tf_op jit(solution)/shard_map/all_to_all | solution.py:176
  96.7 0.5 fusion
  97.2 0.7 copy.111
  98.0 4.8 %all_to_all.22 = bf16[16,2,2,16,544]{4,3,1,0,2:T(8,128)(2,1)S(1)} all-to-all(bf16[16,2,2,16,544]{4,3,1,0,2:T(8,128)(2,1)S(1)} %copy.112), channel_id=1, replica_groups=mesh['z'=16,'y_lo'=2,'core'=2,'y_hi'=2,'x'=4] {'core'}, dimensions={2} | all-to-all | bytes 2228224 | tf_op jit(solution)/shard_map/all_to_all | solution.py:176
  102.8 0.6 reduce_sum.64
  103.5 12.4 %all_to_all.23 = bf16[16,2,1,16,544]{4,3,0,2,1:T(8,128)(2,1)S(1)} all-to-all(bf16[16,2,1,16,544]{4,3,0,2,1:T(8,128)(2,1)S(1)} %copy.113), channel_id=1, replica_groups=mesh['z'=16,'y_lo'=2,'core'=2,'y_hi'=2,'x'=4] {'y_lo'}, dimensions={1} | all-to-all | bytes 1114112 | tf_op jit(solution)/shard_map/all_to_all | solution.py:176
  116.0 0.7 convert_element_type.124
  116.7 0.5 broadcast.192
  117.3 2.3 %reduce.10 = bf16[16,8704]{1,0:T(8,128)(2,1)S(1)} reduce(bf16[16,1,8704]{2,1,0:T(2,128)(2,1)S(1)} %convert_element_type.124, bf16[]{:T(256)} %broadcast.192), dimensions={1}, to_apply=%convert_element_type.124.reduce_sub_computation | reduce | bytes 557058 | tf_op jit(solution)/shard_map/convert_element_type | solution.py:227
  119.5 0.8 reshape.445
  120.3 12.0 %all-to-all-start.3 = ((bf16[16,2,4352]{2,1,0:T(2,128)(2,1)}), bf16[16,2,4352]{2,1,0:T(2,128)(2,1)S(1)}, u32[]{:S(2)}, u32[]{:S(2)}) async-start(bf16[16,2,4352]{2,1,0:T(2,128)(2,1)} %reshape.445), calls=%async_computation.3 | async-start | bytes 557056 | tf_op jit(solution)/shard_map/all_to_all | solution.py:176
  132.3 0.3 fusion.56
  132.9 0.4 convolution_add_fusion.1
  133.2 0.5 copy-done.9
  134.1 1.2 constant_dynamic-slice_fusion.7
  135.4 2.8 %collective-permute-start.21 = (bf16[256,128]{1,0:T(8,128)(2,1)S(1)}, bf16[256,128]{1,0:T(8,128)(2,1)S(1)}, u32[]{:S(2)}, u32[]{:S(2)}) collective-permute-start(bf16[256,128]{1,0:T(8,128)(2,1)S(1)} %bitcast.218), channel_id=1, source_target_pairs={{0,1},{1,2},{2,3},{3,4},{4,5},{5,6},{6,7},{7,0},{8,9},{9,10},{10,1... | collective-permute-start | bytes 196616 | tf_op jit(solution)/shard_map/ppermute | solution.py:190
  138.2 6.7 %collective-permute-start.15 = (bf16[256,128]{1,0:T(8,128)(2,1)S(1)}, bf16[256,128]{1,0:T(8,128)(2,1)S(1)}, u32[]{:S(2)}, u32[]{:S(2)}) collective-permute-start(bf16[256,128]{1,0:T(8,128)(2,1)S(1)} %bitcast.216), channel_id=1, source_target_pairs={{0,7},{1,0},{2,1},{3,2},{4,3},{5,4},{6,5},{7,6},{8,15},{9,8},{10,9... | collective-permute-start | bytes 196616 | tf_op jit(solution)/shard_map/ppermute | solution.py:190
  145.0 1.9 %collective-permute-start.16 = (bf16[256,128]{1,0:T(8,128)(2,1)S(1)}, bf16[256,128]{1,0:T(8,128)(2,1)S(1)}, u32[]{:S(2)}, u32[]{:S(2)}) collective-permute-start(bf16[256,128]{1,0:T(8,128)(2,1)S(1)} %bitcast.219), channel_id=1, source_target_pairs={{0,6},{1,7},{2,0},{3,1},{4,2},{5,3},{6,4},{7,5},{8,14},{9,15},{10,... | collective-permute-start | bytes 196616 | tf_op jit(solution)/shard_map/ppermute | solution.py:190
  146.9 2.8 %collective-permute-start.17 = (bf16[256,128]{1,0:T(8,128)(2,1)S(1)}, bf16[256,128]{1,0:T(8,128)(2,1)S(1)}, u32[]{:S(2)}, u32[]{:S(2)}) collective-permute-start(bf16[256,128]{1,0:T(8,128)(2,1)S(1)} %bitcast.217), channel_id=1, source_target_pairs={{0,5},{1,6},{2,7},{3,0},{4,1},{5,2},{6,3},{7,4},{8,13},{9,14},{10,... | collective-permute-start | bytes 196616 | tf_op jit(solution)/shard_map/ppermute | solution.py:190
  149.7 4.8 %collective-permute-start.18 = (bf16[256,128]{1,0:T(8,128)(2,1)S(1)}, bf16[256,128]{1,0:T(8,128)(2,1)S(1)}, u32[]{:S(2)}, u32[]{:S(2)}) collective-permute-start(bf16[256,128]{1,0:T(8,128)(2,1)S(1)} %bitcast.215), channel_id=1, source_target_pairs={{0,4},{1,5},{2,6},{3,7},{4,0},{5,1},{6,2},{7,3},{8,12},{9,13},{10,... | collective-permute-start | bytes 196616 | tf_op jit(solution)/shard_map/ppermute | solution.py:190
  154.6 1.9 %collective-permute-start.19 = (bf16[256,128]{1,0:T(8,128)(2,1)S(1)}, bf16[256,128]{1,0:T(8,128)(2,1)S(1)}, u32[]{:S(2)}, u32[]{:S(2)}) collective-permute-start(bf16[256,128]{1,0:T(8,128)(2,1)S(1)} %bitcast.214), channel_id=1, source_target_pairs={{0,3},{1,4},{2,5},{3,6},{4,7},{5,0},{6,1},{7,2},{8,11},{9,12},{10,... | collective-permute-start | bytes 196616 | tf_op jit(solution)/shard_map/ppermute | solution.py:190
  156.5 6.6 %collective-permute-start.20 = (bf16[256,128]{1,0:T(8,128)(2,1)S(1)}, bf16[256,128]{1,0:T(8,128)(2,1)S(1)}, u32[]{:S(2)}, u32[]{:S(2)}) collective-permute-start(bf16[256,128]{1,0:T(8,128)(2,1)S(1)} %bitcast.213), channel_id=1, source_target_pairs={{0,2},{1,3},{2,4},{3,5},{4,6},{5,7},{6,0},{7,1},{8,10},{9,11},{10,... | collective-permute-start | bytes 196616 | tf_op jit(solution)/shard_map/ppermute | solution.py:190
  163.1 4.6 %collective-permute-done.20 = bf16[256,128]{1,0:T(8,128)(2,1)S(1)} collective-permute-done((bf16[256,128]{1,0:T(8,128)(2,1)S(1)}, bf16[256,128]{1,0:T(8,128)(2,1)S(1)}, u32[]{:S(2)}, u32[]{:S(2)}) %collective-permute-start.20) | collective-permute-done | bytes 65568 | tf_op jit(solution)/shard_map/ppermute | solution.py:190
  167.7 0.7 fusion.44
  168.7 0.6 convert_reduce_fusion
  169.3 0.6 slice.28
  169.9 0.6 fusion.53
  (82 shorter events, 4.6 us)
Async XLA Ops:
  0.6 96.1 %copy-start = (bf16[256,1024]{1,0:T(8,128)(2,1)S(1)}, bf16[256,1024]{1,0:T(8,128)(2,1)}, u32[]{:S(2)}) copy-start(bf16[256,1024]{1,0:T(8,128)(2,1)} %param.11) | copy-start | bytes 1572868
  0.6 4.6 %copy-start.6 = (bf16[256,256]{1,0:T(8,128)(2,1)S(1)}, bf16[256,256]{1,0:T(8,128)(2,1)}, u32[]{:S(2)}) copy-start(bf16[256,256]{1,0:T(8,128)(2,1)} %param.13) | copy-start | bytes 393220
  0.7 4.7 %copy-start.7 = (bf16[256,256]{1,0:T(8,128)(2,1)S(1)}, bf16[256,256]{1,0:T(8,128)(2,1)}, u32[]{:S(2)}) copy-start(bf16[256,256]{1,0:T(8,128)(2,1)} %param.14) | copy-start | bytes 393220
  0.7 4.8 %copy-start.1 = (bf16[256,128]{1,0:T(8,128)(2,1)S(1)}, bf16[256,128]{1,0:T(8,128)(2,1)}, u32[]{:S(2)}) copy-start(bf16[256,128]{1,0:T(8,128)(2,1)} %param.16) | copy-start | bytes 196612
  0.7 4.8 %copy-start.2 = (bf16[256,128]{1,0:T(8,128)(2,1)S(1)}, bf16[256,128]{1,0:T(8,128)(2,1)}, u32[]{:S(2)}) copy-start(bf16[256,128]{1,0:T(8,128)(2,1)} %param.15) | copy-start | bytes 196612
  0.7 5.0 %copy-start.4 = (f32[1,4,128,64]{2,3,1,0:T(8,128)S(1)}, f32[1,4,128,64]{2,3,1,0:T(8,128)}, u32[]{:S(2)}) copy-start(f32[1,4,128,64]{2,3,1,0:T(8,128)} %param.18) | copy-start | bytes 393220
  3.1 3.1 %collective-permute-start.1 = (f32[4]{0:T(128)S(1)}, f32[4]{0:T(128)S(1)}, u32[]{:S(2)}, u32[]{:S(2)}) collective-permute-start(f32[4]{0:T(128)S(1)} %fusion.52), channel_id=1, source_target_pairs={{0,8},{8,0},{1,9},{9,1},{2,10},{10,2},{3,11},{11,3},{4,12},{12,4},... | collective-permute-start | bytes 56 | tf_op jit(solution)/shard_map/ppermute | solution.py:23
  5.3 3.6 %copy-start.8 = (bf16[256,256]{1,0:T(8,128)(2,1)S(1)}, bf16[256,256]{1,0:T(8,128)(2,1)}, u32[]{:S(2)}) copy-start(bf16[256,256]{1,0:T(8,128)(2,1)} %param.12) | copy-start | bytes 393220
  6.4 3.3 %collective-permute-start = (f32[4,128,64]{1,2,0:T(8,128)S(1)}, f32[4,128,64]{1,2,0:T(8,128)S(1)}, u32[]{:S(2)}, u32[]{:S(2)}) collective-permute-start(f32[4,128,64]{1,2,0:T(8,128)S(1)} %fusion.13), channel_id=1, source_target_pairs={{0,8},{8,0},{1,9},{9,1},{2,10},{10,2},{3,11},{11,3},{4,12},{12,4},... | collective-permute-start | bytes 393224 | tf_op jit(solution)/shard_map/ppermute | solution.py:23
  9.9 10.5 %collective-permute-start.2 = (f32[4,128,64]{1,2,0:T(8,128)S(1)}, f32[4,128,64]{1,2,0:T(8,128)S(1)}, u32[]{:S(2)}, u32[]{:S(2)}) collective-permute-start(f32[4,128,64]{1,2,0:T(8,128)S(1)} %add_select_fusion), channel_id=1, source_target_pairs={{0,16},{16,0},{1,17},{17,1},{2,18},{18,2},{3,19},{19,3},{4,20},{20... | collective-permute-start | bytes 393224 | tf_op jit(solution)/shard_map/ppermute | solution.py:23
  14.4 5.5 %collective-permute-start.3 = (f32[4]{0:T(128)S(1)}, f32[4]{0:T(128)S(1)}, u32[]{:S(2)}, u32[]{:S(2)}) collective-permute-start(f32[4]{0:T(128)S(1)} %get-tuple-element.51), channel_id=1, source_target_pairs={{0,16},{16,0},{1,17},{17,1},{2,18},{18,2},{3,19},{19,3},{4,20},{20... | collective-permute-start | bytes 56 | tf_op jit(solution)/shard_map/ppermute | solution.py:23
  21.7 14.0 %collective-permute-start.6 = (f32[128,64]{0,1:T(8,128)S(1)}, f32[128,64]{0,1:T(8,128)S(1)}, u32[]{:S(2)}, u32[]{:S(2)}) collective-permute-start(f32[128,64]{0,1:T(8,128)S(1)} %select_bitcast_fusion), channel_id=1, source_target_pairs={{64,0},{96,32},{128,64},{160,96},{192,128},{224,160},{256,192},{28... | collective-permute-start | bytes 98312 | tf_op jit(solution)/shard_map/ppermute | solution.py:28
  23.0 12.7 %collective-permute-start.4 = (f32[128,64]{0,1:T(8,128)S(1)}, f32[128,64]{0,1:T(8,128)S(1)}, u32[]{:S(2)}, u32[]{:S(2)}) collective-permute-start(f32[128,64]{0,1:T(8,128)S(1)} %select_bitcast_fusion), channel_id=1, source_target_pairs={{32,0},{64,32},{96,64},{128,96},{160,128},{192,160},{224,192},{256... | collective-permute-start | bytes 98312 | tf_op jit(solution)/shard_map/ppermute | solution.py:28
  29.4 5.6 %collective-permute-start.5 = (f32[]{:T(128)}, f32[]{:T(128)}, u32[]{:S(2)}, u32[]{:S(2)}) collective-permute-start(f32[]{:T(128)} %bitcast.34), channel_id=1, source_target_pairs={{32,0},{64,32},{96,64},{128,96},{160,128},{192,160},{224,192},{256... | collective-permute-start | bytes 20 | tf_op jit(solution)/shard_map/ppermute | solution.py:28
  35.8 11.7 %collective-permute-start.8 = (f32[128,64]{0,1:T(8,128)S(1)}, f32[128,64]{0,1:T(8,128)S(1)}, u32[]{:S(2)}, u32[]{:S(2)}) collective-permute-start(f32[128,64]{0,1:T(8,128)S(1)} %multiply_add_fusion), channel_id=1, source_target_pairs={{64,0},{96,32},{128,64},{160,96},{192,128},{224,160},{256,192},{28... | collective-permute-start | bytes 98312 | tf_op jit(solution)/shard_map/ppermute | solution.py:28
  37.9 8.8 %collective-permute-start.7 = (f32[]{:T(128)}, f32[]{:T(128)}, u32[]{:S(2)}, u32[]{:S(2)}) collective-permute-start(f32[]{:T(128)} %bitcast.34), channel_id=1, source_target_pairs={{64,0},{96,32},{128,64},{160,96},{192,128},{224,160},{256,192},{28... | collective-permute-start | bytes 20 | tf_op jit(solution)/shard_map/ppermute | solution.py:28
  47.5 10.3 %collective-permute-start.10 = (f32[128,64]{0,1:T(8,128)S(1)}, f32[128,64]{0,1:T(8,128)S(1)}, u32[]{:S(2)}, u32[]{:S(2)}) collective-permute-start(f32[128,64]{0,1:T(8,128)S(1)} %add_select_fusion.3), channel_id=1, source_target_pairs={{128,0},{160,32},{192,64},{224,96},{256,128},{288,160},{320,192},{... | collective-permute-start | bytes 98312 | tf_op jit(solution)/shard_map/ppermute | solution.py:28
  49.2 7.5 %collective-permute-start.9 = (f32[]{:T(128)}, f32[]{:T(128)}, u32[]{:S(2)}, u32[]{:S(2)}) collective-permute-start(f32[]{:T(128)} %mul.306), channel_id=1, source_target_pairs={{64,0},{96,32},{128,64},{160,96},{192,128},{224,160},{256,192},{28... | collective-permute-start | bytes 20 | tf_op jit(solution)/shard_map/ppermute | solution.py:28
  57.8 14.5 %collective-permute-start.12 = (f32[128,64]{0,1:T(8,128)S(1)}, f32[128,64]{0,1:T(8,128)S(1)}, u32[]{:S(2)}, u32[]{:S(2)}) collective-permute-start(f32[128,64]{0,1:T(8,128)S(1)} %add_select_fusion.2), channel_id=1, source_target_pairs={{256,0},{288,32},{320,64},{352,96},{384,128},{416,160},{448,192},{... | collective-permute-start | bytes 98312 | tf_op jit(solution)/shard_map/ppermute | solution.py:28
  59.4 9.6 %collective-permute-start.11 = (f32[]{:T(128)}, f32[]{:T(128)}, u32[]{:S(2)}, u32[]{:S(2)}) collective-permute-start(f32[]{:T(128)} %select_n.187), channel_id=1, source_target_pairs={{128,0},{160,32},{192,64},{224,96},{256,128},{288,160},{320,192},{... | collective-permute-start | bytes 20 | tf_op jit(solution)/shard_map/ppermute | solution.py:28
  72.3 3.1 %collective-permute-start.13 = (f32[128,64]{0,1:T(8,128)S(1)}, f32[128,64]{0,1:T(8,128)S(1)}, u32[]{:S(2)}, u32[]{:S(2)}) collective-permute-start(f32[128,64]{0,1:T(8,128)S(1)} %add_select_fusion.1), channel_id=1, source_target_pairs={{0,8},{8,0},{1,9},{9,1},{2,10},{10,2},{3,11},{11,3},{4,12},{12,4},... | collective-permute-start | bytes 98312 | tf_op jit(solution)/shard_map/ppermute | solution.py:23
  75.4 6.7 %collective-permute-start.14 = (f32[2,128,64]{1,2,0:T(8,128)S(1)}, f32[2,128,64]{1,2,0:T(8,128)S(1)}, u32[]{:S(2)}, u32[]{:S(2)}) collective-permute-start(f32[2,128,64]{1,2,0:T(8,128)S(1)} %maximum_select_fusion.1), channel_id=1, source_target_pairs={{0,16},{16,0},{1,17},{17,1},{2,18},{18,2},{3,19},{19,3},{4,20},{20... | collective-permute-start | bytes 196616 | tf_op jit(solution)/shard_map/ppermute | solution.py:23
  83.3 13.4 %all-to-all-start = ((bf16[256,8,32]{0,2,1:T(8,128)(2,1)}), bf16[256,8,32]{0,2,1:T(8,128)(2,1)S(1)}, u32[]{:S(2)}, u32[]{:S(2)}) async-start(bf16[256,8,32]{0,2,1:T(8,128)(2,1)} %pad_maximum_fusion), calls=%async_computation | async-start | bytes 262144 | tf_op jit(solution)/shard_map/all_to_all | solution.py:176
  116.0 16.3 %copy-start.3 = (bf16[1024,256]{1,0:T(8,128)(2,1)S(1)}, bf16[1024,256]{1,0:T(8,128)(2,1)}, u32[]{:S(2)}) copy-start(bf16[1024,256]{1,0:T(8,128)(2,1)} %param.19) | copy-start | bytes 1572868
  120.3 12.5 %copy-start.5 = (bf16[1024,256]{1,0:T(8,128)(2,1)S(1)}, bf16[1024,256]{1,0:T(8,128)(2,1)}, u32[]{:S(2)}) copy-start(bf16[1024,256]{1,0:T(8,128)(2,1)} %param.20) | copy-start | bytes 1572868
  120.3 48.1 %all-to-all-start.3 = ((bf16[16,2,4352]{2,1,0:T(2,128)(2,1)}), bf16[16,2,4352]{2,1,0:T(2,128)(2,1)S(1)}, u32[]{:S(2)}, u32[]{:S(2)}) async-start(bf16[16,2,4352]{2,1,0:T(2,128)(2,1)} %reshape.445), calls=%async_computation.3 | async-start | bytes 557056 | tf_op jit(solution)/shard_map/all_to_all | solution.py:176
  132.8 0.8 copy-start.9
  135.4 19.2 %collective-permute-start.21 = (bf16[256,128]{1,0:T(8,128)(2,1)S(1)}, bf16[256,128]{1,0:T(8,128)(2,1)S(1)}, u32[]{:S(2)}, u32[]{:S(2)}) collective-permute-start(bf16[256,128]{1,0:T(8,128)(2,1)S(1)} %bitcast.218), channel_id=1, source_target_pairs={{0,1},{1,2},{2,3},{3,4},{4,5},{5,6},{6,7},{7,0},{8,9},{9,10},{10,1... | collective-permute-start | bytes 196616 | tf_op jit(solution)/shard_map/ppermute | solution.py:190
  138.2 18.3 %collective-permute-start.15 = (bf16[256,128]{1,0:T(8,128)(2,1)S(1)}, bf16[256,128]{1,0:T(8,128)(2,1)S(1)}, u32[]{:S(2)}, u32[]{:S(2)}) collective-permute-start(bf16[256,128]{1,0:T(8,128)(2,1)S(1)} %bitcast.216), channel_id=1, source_target_pairs={{0,7},{1,0},{2,1},{3,2},{4,3},{5,4},{6,5},{7,6},{8,15},{9,8},{10,9... | collective-permute-start | bytes 196616 | tf_op jit(solution)/shard_map/ppermute | solution.py:190
  145.0 18.1 %collective-permute-start.16 = (bf16[256,128]{1,0:T(8,128)(2,1)S(1)}, bf16[256,128]{1,0:T(8,128)(2,1)S(1)}, u32[]{:S(2)}, u32[]{:S(2)}) collective-permute-start(bf16[256,128]{1,0:T(8,128)(2,1)S(1)} %bitcast.219), channel_id=1, source_target_pairs={{0,6},{1,7},{2,0},{3,1},{4,2},{5,3},{6,4},{7,5},{8,14},{9,15},{10,... | collective-permute-start | bytes 196616 | tf_op jit(solution)/shard_map/ppermute | solution.py:190
  146.9 16.2 %collective-permute-start.17 = (bf16[256,128]{1,0:T(8,128)(2,1)S(1)}, bf16[256,128]{1,0:T(8,128)(2,1)S(1)}, u32[]{:S(2)}, u32[]{:S(2)}) collective-permute-start(bf16[256,128]{1,0:T(8,128)(2,1)S(1)} %bitcast.217), channel_id=1, source_target_pairs={{0,5},{1,6},{2,7},{3,0},{4,1},{5,2},{6,3},{7,4},{8,13},{9,14},{10,... | collective-permute-start | bytes 196616 | tf_op jit(solution)/shard_map/ppermute | solution.py:190
  149.7 13.4 %collective-permute-start.18 = (bf16[256,128]{1,0:T(8,128)(2,1)S(1)}, bf16[256,128]{1,0:T(8,128)(2,1)S(1)}, u32[]{:S(2)}, u32[]{:S(2)}) collective-permute-start(bf16[256,128]{1,0:T(8,128)(2,1)S(1)} %bitcast.215), channel_id=1, source_target_pairs={{0,4},{1,5},{2,6},{3,7},{4,0},{5,1},{6,2},{7,3},{8,12},{9,13},{10,... | collective-permute-start | bytes 196616 | tf_op jit(solution)/shard_map/ppermute | solution.py:190
  154.6 8.6 %collective-permute-start.19 = (bf16[256,128]{1,0:T(8,128)(2,1)S(1)}, bf16[256,128]{1,0:T(8,128)(2,1)S(1)}, u32[]{:S(2)}, u32[]{:S(2)}) collective-permute-start(bf16[256,128]{1,0:T(8,128)(2,1)S(1)} %bitcast.214), channel_id=1, source_target_pairs={{0,3},{1,4},{2,5},{3,6},{4,7},{5,0},{6,1},{7,2},{8,11},{9,12},{10,... | collective-permute-start | bytes 196616 | tf_op jit(solution)/shard_map/ppermute | solution.py:190
  156.5 11.2 %collective-permute-start.20 = (bf16[256,128]{1,0:T(8,128)(2,1)S(1)}, bf16[256,128]{1,0:T(8,128)(2,1)S(1)}, u32[]{:S(2)}, u32[]{:S(2)}) collective-permute-start(bf16[256,128]{1,0:T(8,128)(2,1)S(1)} %bitcast.213), channel_id=1, source_target_pairs={{0,2},{1,3},{2,4},{3,5},{4,6},{5,7},{6,0},{7,1},{8,10},{9,11},{10,... | collective-permute-start | bytes 196616 | tf_op jit(solution)/shard_map/ppermute | solution.py:190
